TPU v7x, 32 devices: a whole 2x2x4 slice. The times are simulated.
32 devices in a mesh: dom: 32 (over z, y, x, core).
Axes of the slice: x: 2, y: 2, z: 4, core: 2. Of those that a mesh axis runs over, the one named last changes fastest.
Arguments:
- x_block: float32 [8, 49152], P(None, 'dom'), may hold values from -18 to 18
- p_block: float32 [8, 49152], P(None, 'dom'), may hold values from -18 to 18
- stiff_elem: float32 [20, 20, 8192], P(None, None, 'dom'), may hold values from -6 to 12.4, as said below
- mass_elem: float32 [20, 20, 8192], P(None, None, 'dom'), may hold values from -0.03 to 0.7, as said below
- node_elem: float32 [10, 10, 8192], P(None, None, 'dom'), may hold values from -1 to 6.1, as said below
- elem_edge: int32 [20, 8192], P(None, 'dom'), may hold values from 0 to 1919, as said below
- elem_node: int32 [10, 8192], P(None, 'dom'), may hold values from 0 to 575, as said below
- send_edge: int32 [6, 2048], P(None, 'dom'), may hold values from 0 to 1535, as said below
- send_node: int32 [6, 1024], P(None, 'dom'), may hold values from 0 to 383, as said below
- grad_pairs: int32 [2, 49152], P(None, 'dom'), may hold values from 0 to 575, as said below
Outputs:
- w_block: float32 [8, 49152], P(None, 'dom')
- gram_stiff: float32 [24, 24], replicated
- gram_mass: float32 [24, 24], replicated
Inputs may be any that keep to these rules, and one draw needn't show every extreme that they name: `stiff_elem`: each element's matrix is symmetric and positive definite. `mass_elem`: each element's matrix is symmetric and positive definite. `node_elem`: each element's matrix is symmetric and positive definite. `elem_edge`: the 20 entries of one element are distinct, and every entry of a subdomain's extended edge list is used by some element of that subdomain. `elem_node`: the 10 entries of one element are distinct, and every entry of a subdomain's extended nodal list is used by some element of that subdomain. `send_edge`: the 64 entries of one direction of one subdomain are distinct. `send_node`: the 32 entries of one direction of one subdomain are distinct. `grad_pairs`: the tail and head of one edge unknown differ.
All inputs are finite; a program needn't handle non-finite values.
Results may differ from a plain program's by a relative error of at most 0.0001.
Values sent between devices are 32-bit elements; how exact they have to be, the bound alone decides.
No kernel may reach another device: no remote copies, remote signals or barrier semaphores. Data moves between devices by JAX's collectives and lax.ppermute only.
A program may use at most 128 MiB of HBM per device.

v0:
```python
import jax
import jax.numpy as jnp
from jax import lax
from jax.sharding import PartitionSpec as P

CHEB_DEG = 3
NNODE = 384
LANES = 128


highest = lax.Precision.HIGHEST
OFFSETS = (1, -1, 4, -4, 16, -16)
interval_low = 0.3
interval_high = 1.7
jacobi_weight = 0.7


def from_behind(shard, axis, by):
    length = lax.axis_size(axis)
    return lax.ppermute(shard, axis, [(i, (i + by) % length) for i in range(length)])


def shift_pieces(pieces, offsets):
    length = lax.axis_size("dom")
    out = [None] * len(pieces)
    targets = {}
    for number, offset in enumerate(offsets):
        targets.setdefault(offset % length, []).append(number)
    for offset, numbers in targets.items():
        sizes = [pieces[number].shape[1] for number in numbers]
        moved = from_behind(jnp.concatenate([pieces[number] for number in numbers], axis=1), "dom", offset)
        start = 0
        for number, size in zip(numbers, sizes):
            out[number] = moved[:, start : start + size]
            start += size
    return out


def all_sum(value):
    length = lax.axis_size("dom")
    if length & (length - 1):
        return lax.psum(value, "dom")
    stride = 1
    while stride < length:
        value = value + lax.ppermute(value, "dom", [(i, i ^ stride) for i in range(length)])
        stride *= 2
    return value


def index_table(index, length):
    groups = -(-length // LANES)
    lo = index % LANES
    hi = index // LANES
    lo_hot = (lo[:, None] == jnp.arange(LANES, dtype=jnp.int32)[None, :]).astype(jnp.float32)
    hi_mask = (hi[None, :] == jnp.arange(groups, dtype=jnp.int32)[:, None]).astype(jnp.float32)
    return lo_hot, hi_mask, length


def gather_cols(values, table):
    lo_hot, hi_mask, length = table
    groups = hi_mask.shape[0]
    rows = values.shape[0]
    padded = jnp.pad(values, ((0, 0), (0, groups * LANES - length)))
    split = padded.reshape(rows, groups, LANES)
    picked = jnp.einsum("rab,nb->ran", split, lo_hot, precision=highest)
    return jnp.sum(picked * hi_mask[None], axis=1)


def scatter_cols(terms, table):
    lo_hot, hi_mask, length = table
    groups = hi_mask.shape[0]
    rows = terms.shape[0]
    spread = terms[:, None, :] * hi_mask[None]
    summed = jnp.einsum("ran,nb->rab", spread, lo_hot, precision=highest)
    return summed.reshape(rows, groups * LANES)[:, :length]


def extend_pieces(values, send_table):
    outgoing = gather_cols(values, send_table)
    ghosts = outgoing.shape[1] // 6
    return [outgoing[:, d * ghosts : (d + 1) * ghosts] for d in range(6)], list(OFFSETS)


def extend_finish(values, moved):
    return jnp.concatenate([values] + moved, axis=1)


def give_back_pieces(extended, send_table):
    owned = send_table[2]
    ghosts = (extended.shape[1] - owned) // 6
    pieces = [extended[:, owned + d * ghosts : owned + (d + 1) * ghosts] for d in range(6)]
    return pieces, [-offset for offset in OFFSETS]


def give_back_finish(extended, moved, send_table):
    owned = send_table[2]
    return extended[:, :owned] + scatter_cols(jnp.concatenate(moved, axis=1), send_table)


def exchange(*groups):
    pieces, offsets, bounds = [], [], []
    flat = len({piece.shape[0] for group_pieces, _ in groups for piece in group_pieces}) > 1
    for group_pieces, group_offsets in groups:
        bounds.append((len(pieces), len(group_pieces)))
        pieces += [piece.reshape(1, -1) if flat else piece for piece in group_pieces]
        offsets += group_offsets
    moved = shift_pieces(pieces, offsets)
    out = []
    for (start, count), (group_pieces, _) in zip(bounds, groups):
        out.append([m.reshape(p.shape) for m, p in zip(moved[start : start + count], group_pieces)])
    return out


def extend(values, send_table):
    (moved,) = exchange(extend_pieces(values, send_table))
    return extend_finish(values, moved)


def give_back(extended, send_table):
    (moved,) = exchange(give_back_pieces(extended, send_table))
    return give_back_finish(extended, moved, send_table)


def element_terms(matrices, values):
    return jnp.sum(matrices[None, :, :, :] * values[:, None, :, :], axis=2)


def inner_elements(left, right):
    return jnp.einsum("cke,dke->cd", left, right, precision=highest)


def arrange(pair_part, row_part, modes):
    mode_mode = pair_part[:, :modes, :modes]
    mode_prev = pair_part[:, :modes, modes:]
    prev_mode = pair_part[:, modes:, :modes]
    prev_prev = pair_part[:, modes:, modes:]
    new_mode = jnp.swapaxes(row_part[:, :, :modes], 1, 2)
    new_prev = jnp.swapaxes(row_part[:, :, 2 * modes :], 1, 2)
    upper = jnp.concatenate([mode_mode, new_mode, mode_prev], axis=2)
    lower = jnp.concatenate([prev_mode, new_prev, prev_prev], axis=2)
    return jnp.concatenate([upper, row_part, lower], axis=1)


def shards(
    x_block,
    p_block,
    stiff_elem,
    mass_elem,
    node_elem,
    elem_edge,
    elem_node,
    send_edge,
    send_node,
    grad_pairs,
):
    modes = x_block.shape[0]
    owned_edges = x_block.shape[1]
    edofs, elements = elem_edge.shape
    ndofs = elem_node.shape[0]
    edge_length = owned_edges + 6 * send_edge.shape[1]
    node_length = NNODE + 6 * send_node.shape[1]

    edge_table = index_table(elem_edge.reshape(-1), edge_length)
    node_table = index_table(elem_node.reshape(-1), node_length)
    send_edge_table = index_table(send_edge.reshape(-1), owned_edges)
    send_node_table = index_table(send_node.reshape(-1), NNODE)
    tails = grad_pairs[0]
    heads = grad_pairs[1]
    grad_table = index_table(jnp.concatenate([heads, tails]), node_length)

    def edge_values(extended):
        return gather_cols(extended, edge_table).reshape(extended.shape[0], edofs, elements)

    def edge_sum(terms):
        return scatter_cols(terms.reshape(terms.shape[0], -1), edge_table)

    pair = jnp.concatenate([x_block, p_block], axis=0)
    node_diag_local = scatter_cols(jnp.einsum("jje->je", node_elem).reshape(1, -1), node_table)
    pair_moved, node_diag_moved = exchange(
        extend_pieces(pair, send_edge_table), give_back_pieces(node_diag_local, send_node_table)
    )
    pair_values = edge_values(extend_finish(pair, pair_moved))
    node_diag = give_back_finish(node_diag_local, node_diag_moved, send_node_table)[0]
    stiff_pair = element_terms(stiff_elem, pair_values)
    mass_pair = element_terms(mass_elem, pair_values)
    edge_diag_terms = jnp.einsum("jje->je", stiff_elem)[None]
    images = give_back(
        edge_sum(jnp.concatenate([stiff_pair[:modes], mass_pair[:modes], edge_diag_terms], axis=0)),
        send_edge_table,
    )
    stiff_x = images[:modes]
    mass_x = images[modes : 2 * modes]
    edge_diag = images[2 * modes]
    numerator, denominator = all_sum(
        jnp.stack([jnp.sum(x_block * stiff_x, axis=1), jnp.sum(x_block * mass_x, axis=1)])
    )
    quotient = numerator / denominator
    residual = stiff_x - quotient[:, None] * mass_x

    def stiff_image(vectors):
        values = edge_values(extend(vectors, send_edge_table))
        return give_back(edge_sum(element_terms(stiff_elem, values)), send_edge_table)

    center = 0.5 * (interval_high + interval_low)
    spread = 0.5 * (interval_high - interval_low)
    sigma = center / spread
    rho_now = 1.0 / sigma
    step_dir = residual / (center * edge_diag)
    smooth = step_dir
    for turn in range(CHEB_DEG - 1):
        rho_next = 1.0 / (2.0 * sigma - rho_now)
        remain = residual - stiff_image(smooth)
        step_dir = rho_next * rho_now * step_dir + 2.0 * rho_next / spread * remain / edge_diag
        smooth = smooth + step_dir
        rho_now = rho_next
    after = residual - stiff_image(smooth)
    gathered_res = scatter_cols(jnp.concatenate([after, -after], axis=1), grad_table)
    nodal_res = give_back(gathered_res, send_node_table)
    first = jacobi_weight * nodal_res / node_diag
    first_values = gather_cols(extend(first, send_node_table), node_table).reshape(modes, ndofs, elements)
    node_image = give_back(
        scatter_cols(element_terms(node_elem, first_values).reshape(modes, -1), node_table),
        send_node_table,
    )
    second = first + jacobi_weight * (nodal_res - node_image) / node_diag
    ends = gather_cols(extend(second, send_node_table), grad_table)
    w_block = smooth + ends[:, :owned_edges] - ends[:, owned_edges:]
    w_values = edge_values(extend(w_block, send_edge_table))
    stiff_wterm = element_terms(stiff_elem, w_values)
    mass_wterm = element_terms(mass_elem, w_values)
    basis_values = jnp.concatenate([pair_values[:modes], w_values, pair_values[modes:]], axis=0)
    w_rows = jnp.stack(
        [inner_elements(stiff_wterm, basis_values), inner_elements(mass_wterm, basis_values)]
    )
    stiff_part = inner_elements(pair_values, stiff_pair)
    mass_part = inner_elements(pair_values, mass_pair)
    full_gram = all_sum(arrange(jnp.stack([stiff_part, mass_part]), w_rows, modes))
    total_edges = owned_edges * lax.axis_size("dom")
    return (w_block, full_gram[0] / total_edges, full_gram[1] / total_edges)


def solution(mesh):
    in_specs = (
        P(None, "dom"),
        P(None, "dom"),
        P(None, None, "dom"),
        P(None, None, "dom"),
        P(None, None, "dom"),
        P(None, "dom"),
        P(None, "dom"),
        P(None, "dom"),
        P(None, "dom"),
        P(None, "dom"),
    )
    out_specs = (P(None, "dom"), P(), P())
    return jax.shard_map(shards, mesh=mesh, in_specs=in_specs, out_specs=out_specs, check_vma=False)
```

profile of v0, /device:TPU:0, one launch (start us, length us, event | category | flops | bytes accessed | tf_op | source)
XLA Modules:
  0.0 258.5 jit_solution(13556081949529517190)
XLA Ops:
  5.2 6.0 %collective-permute-start.1 = (f32[1,1056]{1,0:T(1,128)S(1)}, f32[1,1056]{1,0:T(1,128)S(1)}, u32[]{:S(2)}, u32[]{:S(2)}) collective-permute-start(f32[1,1056]{1,0:T(1,128)S(1)} %pad_maximum_fusion.7), channel_id=1, source_target_pairs={{0,31},{1,0},{2,1},{3,2},{4,3},{5,4},{6,5},{7,6},{8,7},{9,8},{10,9... | collective-permute-start | bytes 12680 | tf_op jit(solution)/shard_map/ppermute | solution.py:20
  11.4 4.8 %collective-permute-start.3 = (f32[1,1056]{1,0:T(1,128)S(1)}, f32[1,1056]{1,0:T(1,128)S(1)}, u32[]{:S(2)}, u32[]{:S(2)}) collective-permute-start(f32[1,1056]{1,0:T(1,128)S(1)} %pad_maximum_fusion.9), channel_id=1, source_target_pairs={{0,28},{1,29},{2,30},{3,31},{4,0},{5,1},{6,2},{7,3},{8,4},{9,5},{1... | collective-permute-start | bytes 12680 | tf_op jit(solution)/shard_map/ppermute | solution.py:20
  31.1 4.7 %collective-permute-start.7 = (f32[17,64]{1,0:T(8,128)S(1)}, f32[17,64]{1,0:T(8,128)S(1)}, u32[]{:S(2)}, u32[]{:S(2)}) collective-permute-start(f32[17,64]{1,0:T(8,128)S(1)} %get-tuple-element.20), channel_id=1, source_target_pairs={{0,28},{1,29},{2,30},{3,31},{4,0},{5,1},{6,2},{7,3},{8,4},{9,5},{1... | collective-permute-start | bytes 13064 | tf_op jit(solution)/shard_map/ppermute | solution.py:20
  35.8 5.3 %collective-permute-start.5 = (f32[17,64]{1,0:T(8,128)S(1)}, f32[17,64]{1,0:T(8,128)S(1)}, u32[]{:S(2)}, u32[]{:S(2)}) collective-permute-start(f32[17,64]{1,0:T(8,128)S(1)} %get-tuple-element.22), channel_id=1, source_target_pairs={{0,31},{1,0},{2,1},{3,2},{4,3},{5,4},{6,5},{7,6},{8,7},{9,8},{10,9... | collective-permute-start | bytes 13064 | tf_op jit(solution)/shard_map/ppermute | solution.py:20
  65.6 5.0 %collective-permute-done.17 = f32[8,64]{1,0:T(8,128)S(1)} collective-permute-done((f32[8,64]{1,0:T(8,128)S(1)}, f32[8,64]{1,0:T(8,128)S(1)}, u32[]{:S(2)}, u32[]{:S(2)}) %collective-permute-start.17) | collective-permute-done | bytes 2080 | tf_op jit(solution)/shard_map/ppermute | solution.py:20
  78.0 4.7 %collective-permute-start.22 = (f32[8,64]{1,0:T(8,128)S(1)}, f32[8,64]{1,0:T(8,128)S(1)}, u32[]{:S(2)}, u32[]{:S(2)}) collective-permute-start(f32[8,64]{1,0:T(8,128)S(1)} %get-tuple-element.32), channel_id=1, source_target_pairs={{0,28},{1,29},{2,30},{3,31},{4,0},{5,1},{6,2},{7,3},{8,4},{9,5},{1... | collective-permute-start | bytes 6152 | tf_op jit(solution)/shard_map/ppermute | solution.py:20
  82.7 5.3 %collective-permute-start.20 = (f32[8,64]{1,0:T(8,128)S(1)}, f32[8,64]{1,0:T(8,128)S(1)}, u32[]{:S(2)}, u32[]{:S(2)}) collective-permute-start(f32[8,64]{1,0:T(8,128)S(1)} %get-tuple-element.34), channel_id=1, source_target_pairs={{0,31},{1,0},{2,1},{3,2},{4,3},{5,4},{6,5},{7,6},{8,7},{9,8},{10,9... | collective-permute-start | bytes 6152 | tf_op jit(solution)/shard_map/ppermute | solution.py:20
  92.3 7.4 %collective-permute-start.26 = (f32[8,64]{1,0:T(8,128)S(1)}, f32[8,64]{1,0:T(8,128)S(1)}, u32[]{:S(2)}, u32[]{:S(2)}) collective-permute-start(f32[8,64]{1,0:T(8,128)S(1)} %get-tuple-element.68), channel_id=1, source_target_pairs={{0,31},{1,0},{2,1},{3,2},{4,3},{5,4},{6,5},{7,6},{8,7},{9,8},{10,9... | collective-permute-start | bytes 6152 | tf_op jit(solution)/shard_map/ppermute | solution.py:20
  101.1 5.3 %collective-permute-done.25 = f32[8,64]{1,0:T(8,128)S(1)} collective-permute-done((f32[8,64]{1,0:T(8,128)S(1)}, f32[8,64]{1,0:T(8,128)S(1)}, u32[]{:S(2)}, u32[]{:S(2)}) %collective-permute-start.25) | collective-permute-done | bytes 2080 | tf_op jit(solution)/shard_map/ppermute | solution.py:20
  112.5 4.7 %collective-permute-start.32 = (f32[8,64]{1,0:T(8,128)S(1)}, f32[8,64]{1,0:T(8,128)S(1)}, u32[]{:S(2)}, u32[]{:S(2)}) collective-permute-start(f32[8,64]{1,0:T(8,128)S(1)} %get-tuple-element.28), channel_id=1, source_target_pairs={{0,28},{1,29},{2,30},{3,31},{4,0},{5,1},{6,2},{7,3},{8,4},{9,5},{1... | collective-permute-start | bytes 6152 | tf_op jit(solution)/shard_map/ppermute | solution.py:20
  117.3 5.3 %collective-permute-start.30 = (f32[8,64]{1,0:T(8,128)S(1)}, f32[8,64]{1,0:T(8,128)S(1)}, u32[]{:S(2)}, u32[]{:S(2)}) collective-permute-start(f32[8,64]{1,0:T(8,128)S(1)} %get-tuple-element.30), channel_id=1, source_target_pairs={{0,31},{1,0},{2,1},{3,2},{4,3},{5,4},{6,5},{7,6},{8,7},{9,8},{10,9... | collective-permute-start | bytes 6152 | tf_op jit(solution)/shard_map/ppermute | solution.py:20
  126.9 7.4 %collective-permute-start.36 = (f32[8,64]{1,0:T(8,128)S(1)}, f32[8,64]{1,0:T(8,128)S(1)}, u32[]{:S(2)}, u32[]{:S(2)}) collective-permute-start(f32[8,64]{1,0:T(8,128)S(1)} %get-tuple-element.64), channel_id=1, source_target_pairs={{0,31},{1,0},{2,1},{3,2},{4,3},{5,4},{6,5},{7,6},{8,7},{9,8},{10,9... | collective-permute-start | bytes 6152 | tf_op jit(solution)/shard_map/ppermute | solution.py:20
  135.6 5.3 %collective-permute-done.35 = f32[8,64]{1,0:T(8,128)S(1)} collective-permute-done((f32[8,64]{1,0:T(8,128)S(1)}, f32[8,64]{1,0:T(8,128)S(1)}, u32[]{:S(2)}, u32[]{:S(2)}) %collective-permute-start.35) | collective-permute-done | bytes 2080 | tf_op jit(solution)/shard_map/ppermute | solution.py:20
  147.1 4.7 %collective-permute-start.42 = (f32[8,64]{1,0:T(8,128)S(1)}, f32[8,64]{1,0:T(8,128)S(1)}, u32[]{:S(2)}, u32[]{:S(2)}) collective-permute-start(f32[8,64]{1,0:T(8,128)S(1)} %get-tuple-element.24), channel_id=1, source_target_pairs={{0,28},{1,29},{2,30},{3,31},{4,0},{5,1},{6,2},{7,3},{8,4},{9,5},{1... | collective-permute-start | bytes 6152 | tf_op jit(solution)/shard_map/ppermute | solution.py:20
  151.8 5.3 %collective-permute-start.40 = (f32[8,64]{1,0:T(8,128)S(1)}, f32[8,64]{1,0:T(8,128)S(1)}, u32[]{:S(2)}, u32[]{:S(2)}) collective-permute-start(f32[8,64]{1,0:T(8,128)S(1)} %get-tuple-element.26), channel_id=1, source_target_pairs={{0,31},{1,0},{2,1},{3,2},{4,3},{5,4},{6,5},{7,6},{8,7},{9,8},{10,9... | collective-permute-start | bytes 6152 | tf_op jit(solution)/shard_map/ppermute | solution.py:20
  164.6 5.3 %collective-permute-start.45 = (f32[8,32]{1,0:T(8,128)S(1)}, f32[8,32]{1,0:T(8,128)S(1)}, u32[]{:S(2)}, u32[]{:S(2)}) collective-permute-start(f32[8,32]{1,0:T(8,128)S(1)} %get-tuple-element.50), channel_id=1, source_target_pairs={{0,31},{1,0},{2,1},{3,2},{4,3},{5,4},{6,5},{7,6},{8,7},{9,8},{10,9... | collective-permute-start | bytes 3080 | tf_op jit(solution)/shard_map/ppermute | solution.py:20
  174.0 7.4 %collective-permute-start.51 = (f32[8,32]{1,0:T(8,128)S(1)}, f32[8,32]{1,0:T(8,128)S(1)}, u32[]{:S(2)}, u32[]{:S(2)}) collective-permute-start(f32[8,32]{1,0:T(8,128)S(1)} %get-tuple-element.84), channel_id=1, source_target_pairs={{0,31},{1,0},{2,1},{3,2},{4,3},{5,4},{6,5},{7,6},{8,7},{9,8},{10,9... | collective-permute-start | bytes 3080 | tf_op jit(solution)/shard_map/ppermute | solution.py:20
  182.8 5.3 %collective-permute-done.50 = f32[8,32]{1,0:T(8,128)S(1)} collective-permute-done((f32[8,32]{1,0:T(8,128)S(1)}, f32[8,32]{1,0:T(8,128)S(1)}, u32[]{:S(2)}, u32[]{:S(2)}) %collective-permute-start.50) | collective-permute-done | bytes 1056 | tf_op jit(solution)/shard_map/ppermute | solution.py:20
  191.0 4.7 %collective-permute-start.57 = (f32[8,32]{1,0:T(8,128)S(1)}, f32[8,32]{1,0:T(8,128)S(1)}, u32[]{:S(2)}, u32[]{:S(2)}) collective-permute-start(f32[8,32]{1,0:T(8,128)S(1)} %get-tuple-element.44), channel_id=1, source_target_pairs={{0,28},{1,29},{2,30},{3,31},{4,0},{5,1},{6,2},{7,3},{8,4},{9,5},{1... | collective-permute-start | bytes 3080 | tf_op jit(solution)/shard_map/ppermute | solution.py:20
  195.7 5.3 %collective-permute-start.55 = (f32[8,32]{1,0:T(8,128)S(1)}, f32[8,32]{1,0:T(8,128)S(1)}, u32[]{:S(2)}, u32[]{:S(2)}) collective-permute-start(f32[8,32]{1,0:T(8,128)S(1)} %get-tuple-element.46), channel_id=1, source_target_pairs={{0,31},{1,0},{2,1},{3,2},{4,3},{5,4},{6,5},{7,6},{8,7},{9,8},{10,9... | collective-permute-start | bytes 3080 | tf_op jit(solution)/shard_map/ppermute | solution.py:20
  205.1 7.4 %collective-permute-start.61 = (f32[8,32]{1,0:T(8,128)S(1)}, f32[8,32]{1,0:T(8,128)S(1)}, u32[]{:S(2)}, u32[]{:S(2)}) collective-permute-start(f32[8,32]{1,0:T(8,128)S(1)} %get-tuple-element.80), channel_id=1, source_target_pairs={{0,31},{1,0},{2,1},{3,2},{4,3},{5,4},{6,5},{7,6},{8,7},{9,8},{10,9... | collective-permute-start | bytes 3080 | tf_op jit(solution)/shard_map/ppermute | solution.py:20
  213.9 5.3 %collective-permute-done.60 = f32[8,32]{1,0:T(8,128)S(1)} collective-permute-done((f32[8,32]{1,0:T(8,128)S(1)}, f32[8,32]{1,0:T(8,128)S(1)}, u32[]{:S(2)}, u32[]{:S(2)}) %collective-permute-start.60) | collective-permute-done | bytes 1056 | tf_op jit(solution)/shard_map/ppermute | solution.py:20
  229.4 5.3 %collective-permute-done.65 = f32[8,64]{1,0:T(8,128)S(1)} collective-permute-done((f32[8,64]{1,0:T(8,128)S(1)}, f32[8,64]{1,0:T(8,128)S(1)}, u32[]{:S(2)}, u32[]{:S(2)}) %collective-permute-start.65) | collective-permute-done | bytes 2080 | tf_op jit(solution)/shard_map/ppermute | solution.py:20
  253.1 4.7 %collective-permute-done.74 = f32[2,24,24]{2,1,0:T(8,128)S(1)} collective-permute-done((f32[2,24,24]{2,1,0:T(8,128)S(1)}, f32[2,24,24]{2,1,0:T(8,128)S(1)}, u32[]{:S(2)}, u32[]{:S(2)}) %collective-permute-start.74) | collective-permute-done | bytes 4640 | tf_op jit(solution)/shard_map/ppermute | solution.py:45
  (315 shorter events, 124.4 us)
Async XLA Ops:
  4.6 12.1 %collective-permute-start = (f32[1,1056]{1,0:T(1,128)S(1)}, f32[1,1056]{1,0:T(1,128)S(1)}, u32[]{:S(2)}, u32[]{:S(2)}) collective-permute-start(f32[1,1056]{1,0:T(1,128)S(1)} %pad_maximum_fusion.6), channel_id=1, source_target_pairs={{0,1},{1,2},{2,3},{3,4},{4,5},{5,6},{6,7},{7,8},{8,9},{9,10},{10,1... | collective-permute-start | bytes 12680 | tf_op jit(solution)/shard_map/ppermute | solution.py:20
  5.2 11.6 %collective-permute-start.1 = (f32[1,1056]{1,0:T(1,128)S(1)}, f32[1,1056]{1,0:T(1,128)S(1)}, u32[]{:S(2)}, u32[]{:S(2)}) collective-permute-start(f32[1,1056]{1,0:T(1,128)S(1)} %pad_maximum_fusion.7), channel_id=1, source_target_pairs={{0,31},{1,0},{2,1},{3,2},{4,3},{5,4},{6,5},{7,6},{8,7},{9,8},{10,9... | collective-permute-start | bytes 12680 | tf_op jit(solution)/shard_map/ppermute | solution.py:20
  30.9 11.6 %collective-permute-start.9 = (f32[17,128]{1,0:T(8,128)S(1)}, f32[17,128]{1,0:T(8,128)S(1)}, u32[]{:S(2)}, u32[]{:S(2)}) collective-permute-start(f32[17,128]{1,0:T(8,128)S(1)} %concatenate.212), channel_id=1, source_target_pairs={{0,16},{1,17},{2,18},{3,19},{4,20},{5,21},{6,22},{7,23},{8,24},{9,... | collective-permute-start | bytes 26120 | tf_op jit(solution)/shard_map/ppermute | solution.py:20
  31.0 10.1 %collective-permute-start.8 = (f32[17,64]{1,0:T(8,128)S(1)}, f32[17,64]{1,0:T(8,128)S(1)}, u32[]{:S(2)}, u32[]{:S(2)}) collective-permute-start(f32[17,64]{1,0:T(8,128)S(1)} %get-tuple-element.19), channel_id=1, source_target_pairs={{0,4},{1,5},{2,6},{3,7},{4,8},{5,9},{6,10},{7,11},{8,12},{9,13},{1... | collective-permute-start | bytes 13064 | tf_op jit(solution)/shard_map/ppermute | solution.py:20
  31.1 10.1 %collective-permute-start.7 = (f32[17,64]{1,0:T(8,128)S(1)}, f32[17,64]{1,0:T(8,128)S(1)}, u32[]{:S(2)}, u32[]{:S(2)}) collective-permute-start(f32[17,64]{1,0:T(8,128)S(1)} %get-tuple-element.20), channel_id=1, source_target_pairs={{0,28},{1,29},{2,30},{3,31},{4,0},{5,1},{6,2},{7,3},{8,4},{9,5},{1... | collective-permute-start | bytes 13064 | tf_op jit(solution)/shard_map/ppermute | solution.py:20
  77.9 11.5 %collective-permute-start.24 = (f32[8,128]{1,0:T(8,128)S(1)}, f32[8,128]{1,0:T(8,128)S(1)}, u32[]{:S(2)}, u32[]{:S(2)}) collective-permute-start(f32[8,128]{1,0:T(8,128)S(1)} %concatenate.214), channel_id=1, source_target_pairs={{0,16},{1,17},{2,18},{3,19},{4,20},{5,21},{6,22},{7,23},{8,24},{9,... | collective-permute-start | bytes 12296 | tf_op jit(solution)/shard_map/ppermute | solution.py:20
  78.0 10.1 %collective-permute-start.23 = (f32[8,64]{1,0:T(8,128)S(1)}, f32[8,64]{1,0:T(8,128)S(1)}, u32[]{:S(2)}, u32[]{:S(2)}) collective-permute-start(f32[8,64]{1,0:T(8,128)S(1)} %get-tuple-element.31), channel_id=1, source_target_pairs={{0,4},{1,5},{2,6},{3,7},{4,8},{5,9},{6,10},{7,11},{8,12},{9,13},{1... | collective-permute-start | bytes 6152 | tf_op jit(solution)/shard_map/ppermute | solution.py:20
  78.0 10.1 %collective-permute-start.22 = (f32[8,64]{1,0:T(8,128)S(1)}, f32[8,64]{1,0:T(8,128)S(1)}, u32[]{:S(2)}, u32[]{:S(2)}) collective-permute-start(f32[8,64]{1,0:T(8,128)S(1)} %get-tuple-element.32), channel_id=1, source_target_pairs={{0,28},{1,29},{2,30},{3,31},{4,0},{5,1},{6,2},{7,3},{8,4},{9,5},{1... | collective-permute-start | bytes 6152 | tf_op jit(solution)/shard_map/ppermute | solution.py:20
  112.5 11.5 %collective-permute-start.34 = (f32[8,128]{1,0:T(8,128)S(1)}, f32[8,128]{1,0:T(8,128)S(1)}, u32[]{:S(2)}, u32[]{:S(2)}) collective-permute-start(f32[8,128]{1,0:T(8,128)S(1)} %concatenate.216), channel_id=1, source_target_pairs={{0,16},{1,17},{2,18},{3,19},{4,20},{5,21},{6,22},{7,23},{8,24},{9,... | collective-permute-start | bytes 12296 | tf_op jit(solution)/shard_map/ppermute | solution.py:20
  112.5 10.1 %collective-permute-start.33 = (f32[8,64]{1,0:T(8,128)S(1)}, f32[8,64]{1,0:T(8,128)S(1)}, u32[]{:S(2)}, u32[]{:S(2)}) collective-permute-start(f32[8,64]{1,0:T(8,128)S(1)} %get-tuple-element.27), channel_id=1, source_target_pairs={{0,4},{1,5},{2,6},{3,7},{4,8},{5,9},{6,10},{7,11},{8,12},{9,13},{1... | collective-permute-start | bytes 6152 | tf_op jit(solution)/shard_map/ppermute | solution.py:20
  112.5 10.1 %collective-permute-start.32 = (f32[8,64]{1,0:T(8,128)S(1)}, f32[8,64]{1,0:T(8,128)S(1)}, u32[]{:S(2)}, u32[]{:S(2)}) collective-permute-start(f32[8,64]{1,0:T(8,128)S(1)} %get-tuple-element.28), channel_id=1, source_target_pairs={{0,28},{1,29},{2,30},{3,31},{4,0},{5,1},{6,2},{7,3},{8,4},{9,5},{1... | collective-permute-start | bytes 6152 | tf_op jit(solution)/shard_map/ppermute | solution.py:20
  124.8 9.6 %collective-permute-start.38 = (f32[8,64]{1,0:T(8,128)S(1)}, f32[8,64]{1,0:T(8,128)S(1)}, u32[]{:S(2)}, u32[]{:S(2)}) collective-permute-start(f32[8,64]{1,0:T(8,128)S(1)} %get-tuple-element.62), channel_id=1, source_target_pairs={{0,28},{1,29},{2,30},{3,31},{4,0},{5,1},{6,2},{7,3},{8,4},{9,5},{1... | collective-permute-start | bytes 6152 | tf_op jit(solution)/shard_map/ppermute | solution.py:20
  124.8 9.6 %collective-permute-start.37 = (f32[8,64]{1,0:T(8,128)S(1)}, f32[8,64]{1,0:T(8,128)S(1)}, u32[]{:S(2)}, u32[]{:S(2)}) collective-permute-start(f32[8,64]{1,0:T(8,128)S(1)} %get-tuple-element.63), channel_id=1, source_target_pairs={{0,4},{1,5},{2,6},{3,7},{4,8},{5,9},{6,10},{7,11},{8,12},{9,13},{1... | collective-permute-start | bytes 6152 | tf_op jit(solution)/shard_map/ppermute | solution.py:20
  147.0 11.5 %collective-permute-start.44 = (f32[8,128]{1,0:T(8,128)S(1)}, f32[8,128]{1,0:T(8,128)S(1)}, u32[]{:S(2)}, u32[]{:S(2)}) collective-permute-start(f32[8,128]{1,0:T(8,128)S(1)} %concatenate.218), channel_id=1, source_target_pairs={{0,16},{1,17},{2,18},{3,19},{4,20},{5,21},{6,22},{7,23},{8,24},{9,... | collective-permute-start | bytes 12296 | tf_op jit(solution)/shard_map/ppermute | solution.py:20
  147.0 10.3 %collective-permute-start.43 = (f32[8,64]{1,0:T(8,128)S(1)}, f32[8,64]{1,0:T(8,128)S(1)}, u32[]{:S(2)}, u32[]{:S(2)}) collective-permute-start(f32[8,64]{1,0:T(8,128)S(1)} %get-tuple-element.23), channel_id=1, source_target_pairs={{0,4},{1,5},{2,6},{3,7},{4,8},{5,9},{6,10},{7,11},{8,12},{9,13},{1... | collective-permute-start | bytes 6152 | tf_op jit(solution)/shard_map/ppermute | solution.py:20
  147.1 10.3 %collective-permute-start.42 = (f32[8,64]{1,0:T(8,128)S(1)}, f32[8,64]{1,0:T(8,128)S(1)}, u32[]{:S(2)}, u32[]{:S(2)}) collective-permute-start(f32[8,64]{1,0:T(8,128)S(1)} %get-tuple-element.24), channel_id=1, source_target_pairs={{0,28},{1,29},{2,30},{3,31},{4,0},{5,1},{6,2},{7,3},{8,4},{9,5},{1... | collective-permute-start | bytes 6152 | tf_op jit(solution)/shard_map/ppermute | solution.py:20
  159.8 11.5 %collective-permute-start.49 = (f32[8,64]{1,0:T(8,128)S(1)}, f32[8,64]{1,0:T(8,128)S(1)}, u32[]{:S(2)}, u32[]{:S(2)}) collective-permute-start(f32[8,64]{1,0:T(8,128)S(1)} %concatenate.219), channel_id=1, source_target_pairs={{0,16},{1,17},{2,18},{3,19},{4,20},{5,21},{6,22},{7,23},{8,24},{9,... | collective-permute-start | bytes 6152 | tf_op jit(solution)/shard_map/ppermute | solution.py:20
  159.8 10.1 %collective-permute-start.48 = (f32[8,32]{1,0:T(8,128)S(1)}, f32[8,32]{1,0:T(8,128)S(1)}, u32[]{:S(2)}, u32[]{:S(2)}) collective-permute-start(f32[8,32]{1,0:T(8,128)S(1)} %get-tuple-element.47), channel_id=1, source_target_pairs={{0,4},{1,5},{2,6},{3,7},{4,8},{5,9},{6,10},{7,11},{8,12},{9,13},{1... | collective-permute-start | bytes 3080 | tf_op jit(solution)/shard_map/ppermute | solution.py:20
  159.9 10.1 %collective-permute-start.47 = (f32[8,32]{1,0:T(8,128)S(1)}, f32[8,32]{1,0:T(8,128)S(1)}, u32[]{:S(2)}, u32[]{:S(2)}) collective-permute-start(f32[8,32]{1,0:T(8,128)S(1)} %get-tuple-element.48), channel_id=1, source_target_pairs={{0,28},{1,29},{2,30},{3,31},{4,0},{5,1},{6,2},{7,3},{8,4},{9,5},{1... | collective-permute-start | bytes 3080 | tf_op jit(solution)/shard_map/ppermute | solution.py:20
  190.9 11.5 %collective-permute-start.59 = (f32[8,64]{1,0:T(8,128)S(1)}, f32[8,64]{1,0:T(8,128)S(1)}, u32[]{:S(2)}, u32[]{:S(2)}) collective-permute-start(f32[8,64]{1,0:T(8,128)S(1)} %concatenate.221), channel_id=1, source_target_pairs={{0,16},{1,17},{2,18},{3,19},{4,20},{5,21},{6,22},{7,23},{8,24},{9,... | collective-permute-start | bytes 6152 | tf_op jit(solution)/shard_map/ppermute | solution.py:20
  190.9 10.6 %collective-permute-start.58 = (f32[8,32]{1,0:T(8,128)S(1)}, f32[8,32]{1,0:T(8,128)S(1)}, u32[]{:S(2)}, u32[]{:S(2)}) collective-permute-start(f32[8,32]{1,0:T(8,128)S(1)} %get-tuple-element.43), channel_id=1, source_target_pairs={{0,4},{1,5},{2,6},{3,7},{4,8},{5,9},{6,10},{7,11},{8,12},{9,13},{1... | collective-permute-start | bytes 3080 | tf_op jit(solution)/shard_map/ppermute | solution.py:20
  191.0 10.6 %collective-permute-start.57 = (f32[8,32]{1,0:T(8,128)S(1)}, f32[8,32]{1,0:T(8,128)S(1)}, u32[]{:S(2)}, u32[]{:S(2)}) collective-permute-start(f32[8,32]{1,0:T(8,128)S(1)} %get-tuple-element.44), channel_id=1, source_target_pairs={{0,28},{1,29},{2,30},{3,31},{4,0},{5,1},{6,2},{7,3},{8,4},{9,5},{1... | collective-permute-start | bytes 3080 | tf_op jit(solution)/shard_map/ppermute | solution.py:20
  203.1 10.0 %collective-permute-start.63 = (f32[8,32]{1,0:T(8,128)S(1)}, f32[8,32]{1,0:T(8,128)S(1)}, u32[]{:S(2)}, u32[]{:S(2)}) collective-permute-start(f32[8,32]{1,0:T(8,128)S(1)} %get-tuple-element.78), channel_id=1, source_target_pairs={{0,28},{1,29},{2,30},{3,31},{4,0},{5,1},{6,2},{7,3},{8,4},{9,5},{1... | collective-permute-start | bytes 3080 | tf_op jit(solution)/shard_map/ppermute | solution.py:20
  203.1 10.0 %collective-permute-start.62 = (f32[8,32]{1,0:T(8,128)S(1)}, f32[8,32]{1,0:T(8,128)S(1)}, u32[]{:S(2)}, u32[]{:S(2)}) collective-permute-start(f32[8,32]{1,0:T(8,128)S(1)} %get-tuple-element.79), channel_id=1, source_target_pairs={{0,4},{1,5},{2,6},{3,7},{4,8},{5,9},{6,10},{7,11},{8,12},{9,13},{1... | collective-permute-start | bytes 3080 | tf_op jit(solution)/shard_map/ppermute | solution.py:20
  (60 other events, 409.9 us)
where the time goes:
time: 259 us; the launch traced here: 258 us
  starting transfers between devices  122 us (47%)
  waiting for transfers between devices  82.4 us (32%)
  matrix products  40.7 us (16%)
  local copies, waits for them, and re-layouts  6.32 us (2%)
  other arithmetic  4.83 us (2%)
    ppermute x65, starting transfers between devices, from_behind(): lax.ppermute(shard, axis, [(i, (i + by) % length) for i in range(length)])  121 us
    ppermute x65, waiting for transfers between devices, from_behind(): lax.ppermute(shard, axis, [(i, (i + by) % length) for i in range(length)])  49.9 us
    ppermute x10, waiting for transfers between devices, all_sum(): lax.ppermute(value, 'dom', [(i, i ^ stride) for i in range(length)])  32.5 us
    dot_general x14, matrix products, gather_cols(): picked = jnp.einsum('rab,nb->ran', split, lo_hot, precision=highest)  25.6 us
    dot_general x14, matrix products, scatter_cols(): summed = jnp.einsum('ran,nb->rab', spread, lo_hot, precision=highest)  13 us
  transfers between devices with their start and end apart: 75, of which 31 were waited for; matrix products, arithmetic and copies ran while one was open for 1% of the time, Pallas kernels for 0%

commit v1 on v0

--- a/solution.py
+++ b/solution.py
@@ -51,9 +51,17 @@
     groups = -(-length // LANES)
     lo = index % LANES
     hi = index // LANES
-    lo_hot = (lo[:, None] == jnp.arange(LANES, dtype=jnp.int32)[None, :]).astype(jnp.float32)
+    lo_hot = (lo[:, None] == jnp.arange(LANES, dtype=jnp.int32)[None, :]).astype(jnp.bfloat16)
     hi_mask = (hi[None, :] == jnp.arange(groups, dtype=jnp.int32)[:, None]).astype(jnp.float32)
     return lo_hot, hi_mask, length
+
+
+def three_parts(values, axis):
+    first = lax.reduce_precision(values, exponent_bits=8, mantissa_bits=7)
+    rest = values - first
+    second = lax.reduce_precision(rest, exponent_bits=8, mantissa_bits=7)
+    third = rest - second
+    return jnp.concatenate([first, second, third], axis=axis).astype(jnp.bfloat16)
 
 
 def gather_cols(values, table):
@@ -61,8 +69,10 @@
     groups = hi_mask.shape[0]
     rows = values.shape[0]
     padded = jnp.pad(values, ((0, 0), (0, groups * LANES - length)))
-    split = padded.reshape(rows, groups, LANES)
-    picked = jnp.einsum("rab,nb->ran", split, lo_hot, precision=highest)
+    split = three_parts(padded.reshape(rows, groups, LANES), 2)
+    picked = jnp.einsum(
+        "rak,nk->ran", split, jnp.concatenate([lo_hot] * 3, axis=1), preferred_element_type=jnp.float32
+    )
     return jnp.sum(picked * hi_mask[None], axis=1)
 
 
@@ -70,8 +80,10 @@
     lo_hot, hi_mask, length = table
     groups = hi_mask.shape[0]
     rows = terms.shape[0]
-    spread = terms[:, None, :] * hi_mask[None]
-    summed = jnp.einsum("ran,nb->rab", spread, lo_hot, precision=highest)
+    spread = three_parts(terms[:, None, :] * hi_mask[None], 2)
+    summed = jnp.einsum(
+        "ran,nb->rab", spread, jnp.concatenate([lo_hot] * 3, axis=0), preferred_element_type=jnp.float32
+    )
     return summed.reshape(rows, groups * LANES)[:, :length]
 
 

time: 259 us -> 263 us (1.015)
  starting transfers between devices: 122 us -> 104 us
  other arithmetic: 4.83 us -> 19.1 us
  local copies, waits for them, and re-layouts: 6.32 us -> 15.6 us
    ppermute x65, starting transfers between devices: 121 us -> 98.9 us  [from_behind(): lax.ppermute(shard, axis, [(i, (i + by) % length) for i in range(length)])]
    convert_element_type x0 -> x5, other arithmetic: none -> 6.46 us  [index_table(): (lo[:, None] == jnp.arange(LANES, dtype=jnp.int32)[None, :]).astype(jnp.b...]
    another operation x0 -> x31, other arithmetic: none -> 6.07 us
    slice x10 -> x11, local copies, waits for them, and re-layouts: 0.1 us -> 4.36 us  [shift_pieces(): out[number] = moved[:, start:start + size]]
    ppermute x10, starting transfers between devices: 1.25 us -> 4.78 us  [all_sum(): lax.ppermute(value, 'dom', [(i, i ^ stride) for i in range(length)])]
    ppermute x10, waiting for transfers between devices: 32.5 us -> 29.7 us  [all_sum(): lax.ppermute(value, 'dom', [(i, i ^ stride) for i in range(length)])]
    concatenate x7, local copies, waits for them, and re-layouts: 0.57 us -> 3.21 us  [give_back_finish(): jnp.concatenate(moved, axis=1)]
  transfers between devices with their start and end apart: 75 -> 75, of which waited for: 31 -> 30; matrix products, arithmetic and copies ran while one was open for 1% -> 6% of each run, Pallas kernels for 0% -> 0%
where the time goes in v1:
time: 263 us; the launch traced here: 262 us
  starting transfers between devices  104 us (40%)
  waiting for transfers between devices  79.8 us (30%)
  matrix products  41.3 us (16%)
  other arithmetic  19.1 us (7%)
  local copies, waits for them, and re-layouts  15.6 us (6%)
    ppermute x65, starting transfers between devices, from_behind(): lax.ppermute(shard, axis, [(i, (i + by) % length) for i in range(length)])  98.9 us
    ppermute x65, waiting for transfers between devices, from_behind(): lax.ppermute(shard, axis, [(i, (i + by) % length) for i in range(length)])  50.2 us
    ppermute x10, waiting for transfers between devices, all_sum(): lax.ppermute(value, 'dom', [(i, i ^ stride) for i in range(length)])  29.7 us
    dot_general x14, matrix products, gather_cols(): jnp.einsum('rak,nk->ran', split, jnp.concatenate([lo_hot] * 3, axis=1), p...  27 us
    dot_general x14, matrix products, scatter_cols(): jnp.einsum('ran,nb->rab', spread, jnp.concatenate([lo_hot] * 3, axis=0),...  12.1 us
    convert_element_type x5, other arithmetic, index_table(): (lo[:, None] == jnp.arange(LANES, dtype=jnp.int32)[None, :]).astype(jnp.b...  6.46 us
    another operation x31, other arithmetic  6.07 us
  transfers between devices with their start and end apart: 75, of which 30 were waited for; matrix products, arithmetic and copies ran while one was open for 6% of the time, Pallas kernels for 0%

profile of v1, /device:TPU:0, one launch (start us, length us, event | category | flops | bytes accessed | tf_op | source)
XLA Modules:
  0.0 261.7 jit_solution(16311048393353343928)
XLA Ops:
  7.2 4.1 %collective-permute-start.4 = (f32[1,2112]{1,0:T(1,128)S(1)}, f32[1,2112]{1,0:T(1,128)S(1)}, u32[]{:S(2)}, u32[]{:S(2)}) collective-permute-start(f32[1,2112]{1,0:T(1,128)S(1)} %pad_maximum_fusion.21), channel_id=1, source_target_pairs={{0,16},{1,17},{2,18},{3,19},{4,20},{5,21},{6,22},{7,23},{8,24},{9,... | collective-permute-start | bytes 25352 | tf_op jit(solution)/shard_map/ppermute | solution.py:20
  16.6 5.4 %collective-permute-start.1 = (f32[1,1056]{1,0:T(1,128)S(1)}, f32[1,1056]{1,0:T(1,128)S(1)}, u32[]{:S(2)}, u32[]{:S(2)}) collective-permute-start(f32[1,1056]{1,0:T(1,128)S(1)} %pad_maximum_fusion.24), channel_id=1, source_target_pairs={{0,31},{1,0},{2,1},{3,2},{4,3},{5,4},{6,5},{7,6},{8,7},{9,8},{10,9... | collective-permute-start | bytes 12680 | tf_op jit(solution)/shard_map/ppermute | solution.py:20
  26.1 4.1 %fusion.40 = f32[16,5120]{1,0:T(8,128)S(1)} fusion(f32[15,5120]{1,0:T(8,128)S(1)} %fusion.96, bf16[5120,128]{1,0:T(8,128)(2,1)} %fusion.28, bf16[16,15,128]{2,0,1:T(8,128)(2,1)S(1)} %get-tuple-element.48, bf16[16,15,128]{2,0,1:T(8,128)(2,1)S(1)} %get-tuple-element.49, bf16[16,15,128]{2,0,1:T(8,128)(2,1)S(1)} %get-tuple-element.47), kind=kOutput, calls=%fused_computation.77 | convolution fusion | flops 958443520 | bytes 2129920 | tf_op jit(solution)/shard_map/rak,nk->ran/dot_general | solution.py:73
  41.0 4.7 %collective-permute-done.6 = f32[17,64]{1,0:T(8,128)S(1)} collective-permute-done((f32[17,64]{1,0:T(8,128)S(1)}, f32[17,64]{1,0:T(8,128)S(1)}, u32[]{:S(2)}, u32[]{:S(2)}) %collective-permute-start.6) | collective-permute-done | bytes 4384 | tf_op jit(solution)/shard_map/ppermute | solution.py:20
  48.0 4.6 %collective-permute-start.11 = (f32[2,8]{1,0:T(2,128)S(1)}, f32[2,8]{1,0:T(2,128)S(1)}, u32[]{:S(2)}, u32[]{:S(2)}) collective-permute-start(f32[2,8]{1,0:T(2,128)S(1)} %fusion.255), channel_id=1, source_target_pairs={{0,2},{1,3},{2,0},{3,1},{4,6},{5,7},{6,4},{7,5},{8,10},{9,11},{10,... | collective-permute-start | bytes 200 | tf_op jit(solution)/shard_map/ppermute | solution.py:45
  61.4 4.4 %collective-permute-done.14 = f32[2,8]{1,0:T(2,128)S(1)} collective-permute-done((f32[2,8]{1,0:T(2,128)S(1)}, f32[2,8]{1,0:T(2,128)S(1)}, u32[]{:S(2)}, u32[]{:S(2)}) %collective-permute-start.14) | collective-permute-done | bytes 96 | tf_op jit(solution)/shard_map/ppermute | solution.py:45
  66.4 5.3 %collective-permute-start.16 = (f32[8,64]{1,0:T(8,128)S(1)}, f32[8,64]{1,0:T(8,128)S(1)}, u32[]{:S(2)}, u32[]{:S(2)}) collective-permute-start(f32[8,64]{1,0:T(8,128)S(1)} %get-tuple-element.155), channel_id=1, source_target_pairs={{0,31},{1,0},{2,1},{3,2},{4,3},{5,4},{6,5},{7,6},{8,7},{9,8},{10,9... | collective-permute-start | bytes 6152 | tf_op jit(solution)/shard_map/ppermute | solution.py:20
  71.7 4.7 %collective-permute-start.18 = (f32[8,64]{1,0:T(8,128)S(1)}, f32[8,64]{1,0:T(8,128)S(1)}, u32[]{:S(2)}, u32[]{:S(2)}) collective-permute-start(f32[8,64]{1,0:T(8,128)S(1)} %get-tuple-element.153), channel_id=1, source_target_pairs={{0,28},{1,29},{2,30},{3,31},{4,0},{5,1},{6,2},{7,3},{8,4},{9,5},{1... | collective-permute-start | bytes 6152 | tf_op jit(solution)/shard_map/ppermute | solution.py:20
  99.0 5.3 %collective-permute-start.26 = (f32[8,64]{1,0:T(8,128)S(1)}, f32[8,64]{1,0:T(8,128)S(1)}, u32[]{:S(2)}, u32[]{:S(2)}) collective-permute-start(f32[8,64]{1,0:T(8,128)S(1)} %get-tuple-element.151), channel_id=1, source_target_pairs={{0,31},{1,0},{2,1},{3,2},{4,3},{5,4},{6,5},{7,6},{8,7},{9,8},{10,9... | collective-permute-start | bytes 6152 | tf_op jit(solution)/shard_map/ppermute | solution.py:20
  104.3 4.7 %collective-permute-start.28 = (f32[8,64]{1,0:T(8,128)S(1)}, f32[8,64]{1,0:T(8,128)S(1)}, u32[]{:S(2)}, u32[]{:S(2)}) collective-permute-start(f32[8,64]{1,0:T(8,128)S(1)} %get-tuple-element.149), channel_id=1, source_target_pairs={{0,28},{1,29},{2,30},{3,31},{4,0},{5,1},{6,2},{7,3},{8,4},{9,5},{1... | collective-permute-start | bytes 6152 | tf_op jit(solution)/shard_map/ppermute | solution.py:20
  131.6 6.7 %collective-permute-start.36 = (f32[8,64]{1,0:T(8,128)S(1)}, f32[8,64]{1,0:T(8,128)S(1)}, u32[]{:S(2)}, u32[]{:S(2)}) collective-permute-start(f32[8,64]{1,0:T(8,128)S(1)} %get-tuple-element.147), channel_id=1, source_target_pairs={{0,31},{1,0},{2,1},{3,2},{4,3},{5,4},{6,5},{7,6},{8,7},{9,8},{10,9... | collective-permute-start | bytes 6152 | tf_op jit(solution)/shard_map/ppermute | solution.py:20
  138.2 4.7 %collective-permute-start.38 = (f32[8,64]{1,0:T(8,128)S(1)}, f32[8,64]{1,0:T(8,128)S(1)}, u32[]{:S(2)}, u32[]{:S(2)}) collective-permute-start(f32[8,64]{1,0:T(8,128)S(1)} %get-tuple-element.145), channel_id=1, source_target_pairs={{0,28},{1,29},{2,30},{3,31},{4,0},{5,1},{6,2},{7,3},{8,4},{9,5},{1... | collective-permute-start | bytes 6152 | tf_op jit(solution)/shard_map/ppermute | solution.py:20
  164.5 4.4 %collective-permute-start.45 = (f32[8,32]{1,0:T(8,128)S(1)}, f32[8,32]{1,0:T(8,128)S(1)}, u32[]{:S(2)}, u32[]{:S(2)}) collective-permute-start(f32[8,32]{1,0:T(8,128)S(1)} %get-tuple-element.121), channel_id=1, source_target_pairs={{0,31},{1,0},{2,1},{3,2},{4,3},{5,4},{6,5},{7,6},{8,7},{9,8},{10,9... | collective-permute-start | bytes 3080 | tf_op jit(solution)/shard_map/ppermute | solution.py:20
  171.0 4.6 %collective-permute-done.46 = f32[8,32]{1,0:T(8,128)S(1)} collective-permute-done((f32[8,32]{1,0:T(8,128)S(1)}, f32[8,32]{1,0:T(8,128)S(1)}, u32[]{:S(2)}, u32[]{:S(2)}) %collective-permute-start.46) | collective-permute-done | bytes 1056 | tf_op jit(solution)/shard_map/ppermute | solution.py:20
  176.2 6.3 %collective-permute-start.51 = (f32[8,32]{1,0:T(8,128)S(1)}, f32[8,32]{1,0:T(8,128)S(1)}, u32[]{:S(2)}, u32[]{:S(2)}) collective-permute-start(f32[8,32]{1,0:T(8,128)S(1)} %get-tuple-element.167), channel_id=1, source_target_pairs={{0,31},{1,0},{2,1},{3,2},{4,3},{5,4},{6,5},{7,6},{8,7},{9,8},{10,9... | collective-permute-start | bytes 3080 | tf_op jit(solution)/shard_map/ppermute | solution.py:20
  182.4 4.7 %collective-permute-start.53 = (f32[8,32]{1,0:T(8,128)S(1)}, f32[8,32]{1,0:T(8,128)S(1)}, u32[]{:S(2)}, u32[]{:S(2)}) collective-permute-start(f32[8,32]{1,0:T(8,128)S(1)} %get-tuple-element.165), channel_id=1, source_target_pairs={{0,28},{1,29},{2,30},{3,31},{4,0},{5,1},{6,2},{7,3},{8,4},{9,5},{1... | collective-permute-start | bytes 3080 | tf_op jit(solution)/shard_map/ppermute | solution.py:20
  206.2 5.3 %collective-permute-start.61 = (f32[8,32]{1,0:T(8,128)S(1)}, f32[8,32]{1,0:T(8,128)S(1)}, u32[]{:S(2)}, u32[]{:S(2)}) collective-permute-start(f32[8,32]{1,0:T(8,128)S(1)} %get-tuple-element.163), channel_id=1, source_target_pairs={{0,31},{1,0},{2,1},{3,2},{4,3},{5,4},{6,5},{7,6},{8,7},{9,8},{10,9... | collective-permute-start | bytes 3080 | tf_op jit(solution)/shard_map/ppermute | solution.py:20
  211.5 4.7 %collective-permute-start.63 = (f32[8,32]{1,0:T(8,128)S(1)}, f32[8,32]{1,0:T(8,128)S(1)}, u32[]{:S(2)}, u32[]{:S(2)}) collective-permute-start(f32[8,32]{1,0:T(8,128)S(1)} %get-tuple-element.161), channel_id=1, source_target_pairs={{0,28},{1,29},{2,30},{3,31},{4,0},{5,1},{6,2},{7,3},{8,4},{9,5},{1... | collective-permute-start | bytes 3080 | tf_op jit(solution)/shard_map/ppermute | solution.py:20
  223.1 5.3 %collective-permute-start.66 = (f32[8,64]{1,0:T(8,128)S(1)}, f32[8,64]{1,0:T(8,128)S(1)}, u32[]{:S(2)}, u32[]{:S(2)}) collective-permute-start(f32[8,64]{1,0:T(8,128)S(1)} %get-tuple-element.134), channel_id=1, source_target_pairs={{0,31},{1,0},{2,1},{3,2},{4,3},{5,4},{6,5},{7,6},{8,7},{9,8},{10,9... | collective-permute-start | bytes 6152 | tf_op jit(solution)/shard_map/ppermute | solution.py:20
  228.4 4.7 %collective-permute-start.68 = (f32[8,64]{1,0:T(8,128)S(1)}, f32[8,64]{1,0:T(8,128)S(1)}, u32[]{:S(2)}, u32[]{:S(2)}) collective-permute-start(f32[8,64]{1,0:T(8,128)S(1)} %get-tuple-element.132), channel_id=1, source_target_pairs={{0,28},{1,29},{2,30},{3,31},{4,0},{5,1},{6,2},{7,3},{8,4},{9,5},{1... | collective-permute-start | bytes 6152 | tf_op jit(solution)/shard_map/ppermute | solution.py:20
  244.9 3.8 %collective-permute-done.71 = f32[2,24,24]{2,1,0:T(8,128)S(1)} collective-permute-done((f32[2,24,24]{2,1,0:T(8,128)S(1)}, f32[2,24,24]{2,1,0:T(8,128)S(1)}, u32[]{:S(2)}, u32[]{:S(2)}) %collective-permute-start.71) | collective-permute-done | bytes 4640 | tf_op jit(solution)/shard_map/ppermute | solution.py:45
  248.7 3.8 %collective-permute-done.72 = f32[2,24,24]{2,1,0:T(8,128)S(1)} collective-permute-done((f32[2,24,24]{2,1,0:T(8,128)S(1)}, f32[2,24,24]{2,1,0:T(8,128)S(1)}, u32[]{:S(2)}, u32[]{:S(2)}) %collective-permute-start.72) | collective-permute-done | bytes 4640 | tf_op jit(solution)/shard_map/ppermute | solution.py:45
  252.5 3.8 %collective-permute-done.73 = f32[2,24,24]{2,1,0:T(8,128)S(1)} collective-permute-done((f32[2,24,24]{2,1,0:T(8,128)S(1)}, f32[2,24,24]{2,1,0:T(8,128)S(1)}, u32[]{:S(2)}, u32[]{:S(2)}) %collective-permute-start.73) | collective-permute-done | bytes 4640 | tf_op jit(solution)/shard_map/ppermute | solution.py:45
  256.4 4.7 %collective-permute-done.74 = f32[2,24,24]{2,1,0:T(8,128)S(1)} collective-permute-done((f32[2,24,24]{2,1,0:T(8,128)S(1)}, f32[2,24,24]{2,1,0:T(8,128)S(1)}, u32[]{:S(2)}, u32[]{:S(2)}) %collective-permute-start.74) | collective-permute-done | bytes 4640 | tf_op jit(solution)/shard_map/ppermute | solution.py:45
  (420 shorter events, 144.7 us)
Async XLA Ops:
  7.2 18.6 %collective-permute-start.4 = (f32[1,2112]{1,0:T(1,128)S(1)}, f32[1,2112]{1,0:T(1,128)S(1)}, u32[]{:S(2)}, u32[]{:S(2)}) collective-permute-start(f32[1,2112]{1,0:T(1,128)S(1)} %pad_maximum_fusion.21), channel_id=1, source_target_pairs={{0,16},{1,17},{2,18},{3,19},{4,20},{5,21},{6,22},{7,23},{8,24},{9,... | collective-permute-start | bytes 25352 | tf_op jit(solution)/shard_map/ppermute | solution.py:20
  11.5 13.9 %collective-permute-start.2 = (f32[1,1056]{1,0:T(1,128)S(1)}, f32[1,1056]{1,0:T(1,128)S(1)}, u32[]{:S(2)}, u32[]{:S(2)}) collective-permute-start(f32[1,1056]{1,0:T(1,128)S(1)} %pad_maximum_fusion.25), channel_id=1, source_target_pairs={{0,4},{1,5},{2,6},{3,7},{4,8},{5,9},{6,10},{7,11},{8,12},{9,13},{1... | collective-permute-start | bytes 12680 | tf_op jit(solution)/shard_map/ppermute | solution.py:20
  13.1 12.3 %collective-permute-start.3 = (f32[1,1056]{1,0:T(1,128)S(1)}, f32[1,1056]{1,0:T(1,128)S(1)}, u32[]{:S(2)}, u32[]{:S(2)}) collective-permute-start(f32[1,1056]{1,0:T(1,128)S(1)} %pad_maximum_fusion.26), channel_id=1, source_target_pairs={{0,28},{1,29},{2,30},{3,31},{4,0},{5,1},{6,2},{7,3},{8,4},{9,5},{1... | collective-permute-start | bytes 12680 | tf_op jit(solution)/shard_map/ppermute | solution.py:20
  16.5 9.0 %collective-permute-start = (f32[1,1056]{1,0:T(1,128)S(1)}, f32[1,1056]{1,0:T(1,128)S(1)}, u32[]{:S(2)}, u32[]{:S(2)}) collective-permute-start(f32[1,1056]{1,0:T(1,128)S(1)} %pad_maximum_fusion.23), channel_id=1, source_target_pairs={{0,1},{1,2},{2,3},{3,4},{4,5},{5,6},{6,7},{7,8},{8,9},{9,10},{10,1... | collective-permute-start | bytes 12680 | tf_op jit(solution)/shard_map/ppermute | solution.py:20
  16.6 8.9 %collective-permute-start.1 = (f32[1,1056]{1,0:T(1,128)S(1)}, f32[1,1056]{1,0:T(1,128)S(1)}, u32[]{:S(2)}, u32[]{:S(2)}) collective-permute-start(f32[1,1056]{1,0:T(1,128)S(1)} %pad_maximum_fusion.24), channel_id=1, source_target_pairs={{0,31},{1,0},{2,1},{3,2},{4,3},{5,4},{6,5},{7,6},{8,7},{9,8},{10,9... | collective-permute-start | bytes 12680 | tf_op jit(solution)/shard_map/ppermute | solution.py:20
  39.0 6.7 %collective-permute-start.6 = (f32[17,64]{1,0:T(8,128)S(1)}, f32[17,64]{1,0:T(8,128)S(1)}, u32[]{:S(2)}, u32[]{:S(2)}) collective-permute-start(f32[17,64]{1,0:T(8,128)S(1)} %get-tuple-element.42), channel_id=1, source_target_pairs={{0,1},{1,2},{2,3},{3,4},{4,5},{5,6},{6,7},{7,8},{8,9},{9,10},{10,1... | collective-permute-start | bytes 13064 | tf_op jit(solution)/shard_map/ppermute | solution.py:20
  39.0 6.7 %collective-permute-start.7 = (f32[17,64]{1,0:T(8,128)S(1)}, f32[17,64]{1,0:T(8,128)S(1)}, u32[]{:S(2)}, u32[]{:S(2)}) collective-permute-start(f32[17,64]{1,0:T(8,128)S(1)} %get-tuple-element.41), channel_id=1, source_target_pairs={{0,28},{1,29},{2,30},{3,31},{4,0},{5,1},{6,2},{7,3},{8,4},{9,5},{1... | collective-permute-start | bytes 13064 | tf_op jit(solution)/shard_map/ppermute | solution.py:20
  39.0 6.7 %collective-permute-start.8 = (f32[17,64]{1,0:T(8,128)S(1)}, f32[17,64]{1,0:T(8,128)S(1)}, u32[]{:S(2)}, u32[]{:S(2)}) collective-permute-start(f32[17,64]{1,0:T(8,128)S(1)} %get-tuple-element.40), channel_id=1, source_target_pairs={{0,4},{1,5},{2,6},{3,7},{4,8},{5,9},{6,10},{7,11},{8,12},{9,13},{1... | collective-permute-start | bytes 13064 | tf_op jit(solution)/shard_map/ppermute | solution.py:20
  66.3 10.1 %collective-permute-start.15 = (f32[8,64]{1,0:T(8,128)S(1)}, f32[8,64]{1,0:T(8,128)S(1)}, u32[]{:S(2)}, u32[]{:S(2)}) collective-permute-start(f32[8,64]{1,0:T(8,128)S(1)} %get-tuple-element.156), channel_id=1, source_target_pairs={{0,1},{1,2},{2,3},{3,4},{4,5},{5,6},{6,7},{7,8},{8,9},{9,10},{10,1... | collective-permute-start | bytes 6152 | tf_op jit(solution)/shard_map/ppermute | solution.py:20
  66.4 10.1 %collective-permute-start.16 = (f32[8,64]{1,0:T(8,128)S(1)}, f32[8,64]{1,0:T(8,128)S(1)}, u32[]{:S(2)}, u32[]{:S(2)}) collective-permute-start(f32[8,64]{1,0:T(8,128)S(1)} %get-tuple-element.155), channel_id=1, source_target_pairs={{0,31},{1,0},{2,1},{3,2},{4,3},{5,4},{6,5},{7,6},{8,7},{9,8},{10,9... | collective-permute-start | bytes 6152 | tf_op jit(solution)/shard_map/ppermute | solution.py:20
  98.9 10.8 %collective-permute-start.25 = (f32[8,64]{1,0:T(8,128)S(1)}, f32[8,64]{1,0:T(8,128)S(1)}, u32[]{:S(2)}, u32[]{:S(2)}) collective-permute-start(f32[8,64]{1,0:T(8,128)S(1)} %get-tuple-element.152), channel_id=1, source_target_pairs={{0,1},{1,2},{2,3},{3,4},{4,5},{5,6},{6,7},{7,8},{8,9},{9,10},{10,1... | collective-permute-start | bytes 6152 | tf_op jit(solution)/shard_map/ppermute | solution.py:20
  99.0 10.8 %collective-permute-start.26 = (f32[8,64]{1,0:T(8,128)S(1)}, f32[8,64]{1,0:T(8,128)S(1)}, u32[]{:S(2)}, u32[]{:S(2)}) collective-permute-start(f32[8,64]{1,0:T(8,128)S(1)} %get-tuple-element.151), channel_id=1, source_target_pairs={{0,31},{1,0},{2,1},{3,2},{4,3},{5,4},{6,5},{7,6},{8,7},{9,8},{10,9... | collective-permute-start | bytes 6152 | tf_op jit(solution)/shard_map/ppermute | solution.py:20
  120.0 8.2 %collective-permute-start.30 = (f32[8,64]{1,0:T(8,128)S(1)}, f32[8,64]{1,0:T(8,128)S(1)}, u32[]{:S(2)}, u32[]{:S(2)}) collective-permute-start(f32[8,64]{1,0:T(8,128)S(1)} %get-tuple-element.66), channel_id=1, source_target_pairs={{0,31},{1,0},{2,1},{3,2},{4,3},{5,4},{6,5},{7,6},{8,7},{9,8},{10,9... | collective-permute-start | bytes 6152 | tf_op jit(solution)/shard_map/ppermute | solution.py:20
  120.1 8.2 %collective-permute-start.31 = (f32[8,64]{1,0:T(8,128)S(1)}, f32[8,64]{1,0:T(8,128)S(1)}, u32[]{:S(2)}, u32[]{:S(2)}) collective-permute-start(f32[8,64]{1,0:T(8,128)S(1)} %get-tuple-element.65), channel_id=1, source_target_pairs={{0,1},{1,2},{2,3},{3,4},{4,5},{5,6},{6,7},{7,8},{8,9},{9,10},{10,1... | collective-permute-start | bytes 6152 | tf_op jit(solution)/shard_map/ppermute | solution.py:20
  120.6 7.7 %collective-permute-start.32 = (f32[8,64]{1,0:T(8,128)S(1)}, f32[8,64]{1,0:T(8,128)S(1)}, u32[]{:S(2)}, u32[]{:S(2)}) collective-permute-start(f32[8,64]{1,0:T(8,128)S(1)} %get-tuple-element.64), channel_id=1, source_target_pairs={{0,28},{1,29},{2,30},{3,31},{4,0},{5,1},{6,2},{7,3},{8,4},{9,5},{1... | collective-permute-start | bytes 6152 | tf_op jit(solution)/shard_map/ppermute | solution.py:20
  131.6 12.7 %collective-permute-start.35 = (f32[8,64]{1,0:T(8,128)S(1)}, f32[8,64]{1,0:T(8,128)S(1)}, u32[]{:S(2)}, u32[]{:S(2)}) collective-permute-start(f32[8,64]{1,0:T(8,128)S(1)} %get-tuple-element.148), channel_id=1, source_target_pairs={{0,1},{1,2},{2,3},{3,4},{4,5},{5,6},{6,7},{7,8},{8,9},{9,10},{10,1... | collective-permute-start | bytes 6152 | tf_op jit(solution)/shard_map/ppermute | solution.py:20
  131.6 12.7 %collective-permute-start.36 = (f32[8,64]{1,0:T(8,128)S(1)}, f32[8,64]{1,0:T(8,128)S(1)}, u32[]{:S(2)}, u32[]{:S(2)}) collective-permute-start(f32[8,64]{1,0:T(8,128)S(1)} %get-tuple-element.147), channel_id=1, source_target_pairs={{0,31},{1,0},{2,1},{3,2},{4,3},{5,4},{6,5},{7,6},{8,7},{9,8},{10,9... | collective-permute-start | bytes 6152 | tf_op jit(solution)/shard_map/ppermute | solution.py:20
  176.1 11.0 %collective-permute-start.50 = (f32[8,32]{1,0:T(8,128)S(1)}, f32[8,32]{1,0:T(8,128)S(1)}, u32[]{:S(2)}, u32[]{:S(2)}) collective-permute-start(f32[8,32]{1,0:T(8,128)S(1)} %get-tuple-element.168), channel_id=1, source_target_pairs={{0,1},{1,2},{2,3},{3,4},{4,5},{5,6},{6,7},{7,8},{8,9},{9,10},{10,1... | collective-permute-start | bytes 3080 | tf_op jit(solution)/shard_map/ppermute | solution.py:20
  176.2 11.0 %collective-permute-start.51 = (f32[8,32]{1,0:T(8,128)S(1)}, f32[8,32]{1,0:T(8,128)S(1)}, u32[]{:S(2)}, u32[]{:S(2)}) collective-permute-start(f32[8,32]{1,0:T(8,128)S(1)} %get-tuple-element.167), channel_id=1, source_target_pairs={{0,31},{1,0},{2,1},{3,2},{4,3},{5,4},{6,5},{7,6},{8,7},{9,8},{10,9... | collective-permute-start | bytes 3080 | tf_op jit(solution)/shard_map/ppermute | solution.py:20
  197.5 6.7 %collective-permute-start.59 = (f32[8,64]{1,0:T(8,128)S(1)}, f32[8,64]{1,0:T(8,128)}, u32[]{:S(2)}, u32[]{:S(2)}) collective-permute-start(f32[8,64]{1,0:T(8,128)S(1)} %concatenate.425), channel_id=1, source_target_pairs={{0,16},{1,17},{2,18},{3,19},{4,20},{5,21},{6,22},{7,23},{8,24},{9,... | collective-permute-start | bytes 6152 | tf_op jit(solution)/shard_map/ppermute | solution.py:20
  206.2 10.6 %collective-permute-start.60 = (f32[8,32]{1,0:T(8,128)S(1)}, f32[8,32]{1,0:T(8,128)S(1)}, u32[]{:S(2)}, u32[]{:S(2)}) collective-permute-start(f32[8,32]{1,0:T(8,128)S(1)} %get-tuple-element.164), channel_id=1, source_target_pairs={{0,1},{1,2},{2,3},{3,4},{4,5},{5,6},{6,7},{7,8},{8,9},{9,10},{10,1... | collective-permute-start | bytes 3080 | tf_op jit(solution)/shard_map/ppermute | solution.py:20
  206.2 10.6 %collective-permute-start.61 = (f32[8,32]{1,0:T(8,128)S(1)}, f32[8,32]{1,0:T(8,128)S(1)}, u32[]{:S(2)}, u32[]{:S(2)}) collective-permute-start(f32[8,32]{1,0:T(8,128)S(1)} %get-tuple-element.163), channel_id=1, source_target_pairs={{0,31},{1,0},{2,1},{3,2},{4,3},{5,4},{6,5},{7,6},{8,7},{9,8},{10,9... | collective-permute-start | bytes 3080 | tf_op jit(solution)/shard_map/ppermute | solution.py:20
  223.0 10.1 %collective-permute-start.65 = (f32[8,64]{1,0:T(8,128)S(1)}, f32[8,64]{1,0:T(8,128)S(1)}, u32[]{:S(2)}, u32[]{:S(2)}) collective-permute-start(f32[8,64]{1,0:T(8,128)S(1)} %get-tuple-element.135), channel_id=1, source_target_pairs={{0,1},{1,2},{2,3},{3,4},{4,5},{5,6},{6,7},{7,8},{8,9},{9,10},{10,1... | collective-permute-start | bytes 6152 | tf_op jit(solution)/shard_map/ppermute | solution.py:20
  223.1 10.1 %collective-permute-start.66 = (f32[8,64]{1,0:T(8,128)S(1)}, f32[8,64]{1,0:T(8,128)S(1)}, u32[]{:S(2)}, u32[]{:S(2)}) collective-permute-start(f32[8,64]{1,0:T(8,128)S(1)} %get-tuple-element.134), channel_id=1, source_target_pairs={{0,31},{1,0},{2,1},{3,2},{4,3},{5,4},{6,5},{7,6},{8,7},{9,8},{10,9... | collective-permute-start | bytes 6152 | tf_op jit(solution)/shard_map/ppermute | solution.py:20
  (93 other events, 746.5 us)

commit v2 on v0

--- a/solution.py
+++ b/solution.py
@@ -191,8 +191,10 @@
     stiff_x = images[:modes]
     mass_x = images[modes : 2 * modes]
     edge_diag = images[2 * modes]
+    stiff_part = inner_elements(pair_values, stiff_pair)
+    mass_part = inner_elements(pair_values, mass_pair)
     numerator, denominator = all_sum(
-        jnp.stack([jnp.sum(x_block * stiff_x, axis=1), jnp.sum(x_block * mass_x, axis=1)])
+        jnp.stack([jnp.diagonal(stiff_part)[:modes], jnp.diagonal(mass_part)[:modes]])
     )
     quotient = numerator / denominator
     residual = stiff_x - quotient[:, None] * mass_x
@@ -232,8 +234,6 @@
     w_rows = jnp.stack(
         [inner_elements(stiff_wterm, basis_values), inner_elements(mass_wterm, basis_values)]
     )
-    stiff_part = inner_elements(pair_values, stiff_pair)
-    mass_part = inner_elements(pair_values, mass_pair)
     full_gram = all_sum(arrange(jnp.stack([stiff_part, mass_part]), w_rows, modes))
     total_edges = owned_edges * lax.axis_size("dom")
     return (w_block, full_gram[0] / total_edges, full_gram[1] / total_edges)

time: 259 us -> 243 us (0.938)
  starting transfers between devices: 122 us -> 103 us
  waiting for transfers between devices: 82.4 us -> 85.9 us
    ppermute x65, starting transfers between devices: 121 us -> 102 us  [from_behind(): lax.ppermute(shard, axis, [(i, (i + by) % length) for i in range(length)])]
    ppermute x65, waiting for transfers between devices: 49.9 us -> 60.7 us  [from_behind(): lax.ppermute(shard, axis, [(i, (i + by) % length) for i in range(length)])]
    ppermute x10, waiting for transfers between devices: 32.5 us -> 25.2 us  [all_sum(): lax.ppermute(value, 'dom', [(i, i ^ stride) for i in range(length)])]
  transfers between devices with their start and end apart: 75 -> 75, of which waited for: 31 -> 32; matrix products, arithmetic and copies ran while one was open for 1% -> 2% of each run, Pallas kernels for 0% -> 0%
where the time goes in v2:
time: 243 us
  starting transfers between devices  103 us (42%)
  waiting for transfers between devices  85.9 us (35%)
  matrix products  40.8 us (17%)
  local copies, waits for them, and re-layouts  8.58 us (4%)
  other arithmetic  3.77 us (2%)
    ppermute x65, starting transfers between devices, from_behind(): lax.ppermute(shard, axis, [(i, (i + by) % length) for i in range(length)])  102 us
    ppermute x65, waiting for transfers between devices, from_behind(): lax.ppermute(shard, axis, [(i, (i + by) % length) for i in range(length)])  60.7 us
    dot_general x14, matrix products, gather_cols(): picked = jnp.einsum('rab,nb->ran', split, lo_hot, precision=highest)  25.6 us
    ppermute x10, waiting for transfers between devices, all_sum(): lax.ppermute(value, 'dom', [(i, i ^ stride) for i in range(length)])  25.2 us
    dot_general x14, matrix products, scatter_cols(): summed = jnp.einsum('ran,nb->rab', spread, lo_hot, precision=highest)  13 us
  transfers between devices with their start and end apart: 75, of which 32 were waited for; matrix products, arithmetic and copies ran while one was open for 2% of the time, Pallas kernels for 0%

profile of v2, /device:TPU:0, one launch (start us, length us, event | category | flops | bytes accessed | tf_op | source)
XLA Modules:
  0.0 243.2 jit_solution(15596331673774222613)
XLA Ops:
  4.6 4.1 %collective-permute-start.4 = (f32[1,2112]{1,0:T(1,128)S(1)}, f32[1,2112]{1,0:T(1,128)S(1)}, u32[]{:S(2)}, u32[]{:S(2)}) collective-permute-start(f32[1,2112]{1,0:T(1,128)S(1)} %pad_maximum_fusion.4), channel_id=1, source_target_pairs={{0,16},{1,17},{2,18},{3,19},{4,20},{5,21},{6,22},{7,23},{8,24},{9,... | collective-permute-start | bytes 25352 | tf_op jit(solution)/shard_map/ppermute | solution.py:20
  9.0 5.4 %collective-permute-start.1 = (f32[1,1056]{1,0:T(1,128)S(1)}, f32[1,1056]{1,0:T(1,128)S(1)}, u32[]{:S(2)}, u32[]{:S(2)}) collective-permute-start(f32[1,1056]{1,0:T(1,128)S(1)} %pad_maximum_fusion.7), channel_id=1, source_target_pairs={{0,31},{1,0},{2,1},{3,2},{4,3},{5,4},{6,5},{7,6},{8,7},{9,8},{10,9... | collective-permute-start | bytes 12680 | tf_op jit(solution)/shard_map/ppermute | solution.py:20
  14.7 4.8 %collective-permute-start.3 = (f32[1,1056]{1,0:T(1,128)S(1)}, f32[1,1056]{1,0:T(1,128)S(1)}, u32[]{:S(2)}, u32[]{:S(2)}) collective-permute-start(f32[1,1056]{1,0:T(1,128)S(1)} %pad_maximum_fusion.9), channel_id=1, source_target_pairs={{0,28},{1,29},{2,30},{3,31},{4,0},{5,1},{6,2},{7,3},{8,4},{9,5},{1... | collective-permute-start | bytes 12680 | tf_op jit(solution)/shard_map/ppermute | solution.py:20
  21.5 4.3 %fusion.20 = f32[16,5120]{1,0:T(8,128)S(1)} fusion(f32[15,5120]{1,0:T(8,128)S(1)} %fusion.109, s32[5120]{0:T(1024)S(1)} %get-tuple-element.49, f32[16,1920]{1,0:T(8,128)S(1)} %concatenate.178), kind=kOutput, calls=%fused_computation.28 | convolution fusion | flops 1890467840 | bytes 778240 | tf_op jit(solution)/shard_map/rab,nb->ran/dot_general | solution.py:65
  33.8 6.1 %collective-permute-start.5 = (f32[17,64]{1,0:T(8,128)S(1)}, f32[17,64]{1,0:T(8,128)S(1)}, u32[]{:S(2)}, u32[]{:S(2)}) collective-permute-start(f32[17,64]{1,0:T(8,128)S(1)} %get-tuple-element.20), channel_id=1, source_target_pairs={{0,31},{1,0},{2,1},{3,2},{4,3},{5,4},{6,5},{7,6},{8,7},{9,8},{10,9... | collective-permute-start | bytes 13064 | tf_op jit(solution)/shard_map/ppermute | solution.py:20
  57.3 5.3 %collective-permute-start.16 = (f32[8,64]{1,0:T(8,128)S(1)}, f32[8,64]{1,0:T(8,128)S(1)}, u32[]{:S(2)}, u32[]{:S(2)}) collective-permute-start(f32[8,64]{1,0:T(8,128)S(1)} %get-tuple-element.70), channel_id=1, source_target_pairs={{0,31},{1,0},{2,1},{3,2},{4,3},{5,4},{6,5},{7,6},{8,7},{9,8},{10,9... | collective-permute-start | bytes 6152 | tf_op jit(solution)/shard_map/ppermute | solution.py:20
  62.7 4.7 %collective-permute-start.18 = (f32[8,64]{1,0:T(8,128)S(1)}, f32[8,64]{1,0:T(8,128)S(1)}, u32[]{:S(2)}, u32[]{:S(2)}) collective-permute-start(f32[8,64]{1,0:T(8,128)S(1)} %get-tuple-element.68), channel_id=1, source_target_pairs={{0,28},{1,29},{2,30},{3,31},{4,0},{5,1},{6,2},{7,3},{8,4},{9,5},{1... | collective-permute-start | bytes 6152 | tf_op jit(solution)/shard_map/ppermute | solution.py:20
  80.6 4.1 %collective-permute-done.21 = f32[8,64]{1,0:T(8,128)S(1)} collective-permute-done((f32[8,64]{1,0:T(8,128)S(1)}, f32[8,64]{1,0:T(8,128)S(1)}, u32[]{:S(2)}, u32[]{:S(2)}) %collective-permute-start.21) | collective-permute-done | bytes 2080 | tf_op jit(solution)/shard_map/ppermute | solution.py:20
  87.5 5.3 %collective-permute-start.26 = (f32[8,64]{1,0:T(8,128)S(1)}, f32[8,64]{1,0:T(8,128)S(1)}, u32[]{:S(2)}, u32[]{:S(2)}) collective-permute-start(f32[8,64]{1,0:T(8,128)S(1)} %get-tuple-element.66), channel_id=1, source_target_pairs={{0,31},{1,0},{2,1},{3,2},{4,3},{5,4},{6,5},{7,6},{8,7},{9,8},{10,9... | collective-permute-start | bytes 6152 | tf_op jit(solution)/shard_map/ppermute | solution.py:20
  92.8 4.7 %collective-permute-start.28 = (f32[8,64]{1,0:T(8,128)S(1)}, f32[8,64]{1,0:T(8,128)S(1)}, u32[]{:S(2)}, u32[]{:S(2)}) collective-permute-start(f32[8,64]{1,0:T(8,128)S(1)} %get-tuple-element.64), channel_id=1, source_target_pairs={{0,28},{1,29},{2,30},{3,31},{4,0},{5,1},{6,2},{7,3},{8,4},{9,5},{1... | collective-permute-start | bytes 6152 | tf_op jit(solution)/shard_map/ppermute | solution.py:20
  110.7 4.1 %collective-permute-done.31 = f32[8,64]{1,0:T(8,128)S(1)} collective-permute-done((f32[8,64]{1,0:T(8,128)S(1)}, f32[8,64]{1,0:T(8,128)S(1)}, u32[]{:S(2)}, u32[]{:S(2)}) %collective-permute-start.31) | collective-permute-done | bytes 2080 | tf_op jit(solution)/shard_map/ppermute | solution.py:20
  117.6 5.3 %collective-permute-start.36 = (f32[8,64]{1,0:T(8,128)S(1)}, f32[8,64]{1,0:T(8,128)S(1)}, u32[]{:S(2)}, u32[]{:S(2)}) collective-permute-start(f32[8,64]{1,0:T(8,128)S(1)} %get-tuple-element.62), channel_id=1, source_target_pairs={{0,31},{1,0},{2,1},{3,2},{4,3},{5,4},{6,5},{7,6},{8,7},{9,8},{10,9... | collective-permute-start | bytes 6152 | tf_op jit(solution)/shard_map/ppermute | solution.py:20
  123.0 4.7 %collective-permute-start.38 = (f32[8,64]{1,0:T(8,128)S(1)}, f32[8,64]{1,0:T(8,128)S(1)}, u32[]{:S(2)}, u32[]{:S(2)}) collective-permute-start(f32[8,64]{1,0:T(8,128)S(1)} %get-tuple-element.60), channel_id=1, source_target_pairs={{0,28},{1,29},{2,30},{3,31},{4,0},{5,1},{6,2},{7,3},{8,4},{9,5},{1... | collective-permute-start | bytes 6152 | tf_op jit(solution)/shard_map/ppermute | solution.py:20
  141.0 3.9 %collective-permute-done.41 = f32[8,64]{1,0:T(8,128)S(1)} collective-permute-done((f32[8,64]{1,0:T(8,128)S(1)}, f32[8,64]{1,0:T(8,128)S(1)}, u32[]{:S(2)}, u32[]{:S(2)}) %collective-permute-start.41) | collective-permute-done | bytes 2080 | tf_op jit(solution)/shard_map/ppermute | solution.py:20
  148.2 4.3 %collective-permute-start.45 = (f32[8,32]{1,0:T(8,128)S(1)}, f32[8,32]{1,0:T(8,128)S(1)}, u32[]{:S(2)}, u32[]{:S(2)}) collective-permute-start(f32[8,32]{1,0:T(8,128)S(1)} %get-tuple-element.48), channel_id=1, source_target_pairs={{0,31},{1,0},{2,1},{3,2},{4,3},{5,4},{6,5},{7,6},{8,7},{9,8},{10,9... | collective-permute-start | bytes 3080 | tf_op jit(solution)/shard_map/ppermute | solution.py:20
  154.6 4.6 %collective-permute-done.46 = f32[8,32]{1,0:T(8,128)S(1)} collective-permute-done((f32[8,32]{1,0:T(8,128)S(1)}, f32[8,32]{1,0:T(8,128)S(1)}, u32[]{:S(2)}, u32[]{:S(2)}) %collective-permute-start.46) | collective-permute-done | bytes 1056 | tf_op jit(solution)/shard_map/ppermute | solution.py:20
  159.9 6.3 %collective-permute-start.51 = (f32[8,32]{1,0:T(8,128)S(1)}, f32[8,32]{1,0:T(8,128)S(1)}, u32[]{:S(2)}, u32[]{:S(2)}) collective-permute-start(f32[8,32]{1,0:T(8,128)S(1)} %get-tuple-element.82), channel_id=1, source_target_pairs={{0,31},{1,0},{2,1},{3,2},{4,3},{5,4},{6,5},{7,6},{8,7},{9,8},{10,9... | collective-permute-start | bytes 3080 | tf_op jit(solution)/shard_map/ppermute | solution.py:20
  166.2 4.7 %collective-permute-start.53 = (f32[8,32]{1,0:T(8,128)S(1)}, f32[8,32]{1,0:T(8,128)S(1)}, u32[]{:S(2)}, u32[]{:S(2)}) collective-permute-start(f32[8,32]{1,0:T(8,128)S(1)} %get-tuple-element.80), channel_id=1, source_target_pairs={{0,28},{1,29},{2,30},{3,31},{4,0},{5,1},{6,2},{7,3},{8,4},{9,5},{1... | collective-permute-start | bytes 3080 | tf_op jit(solution)/shard_map/ppermute | solution.py:20
  180.8 4.1 %collective-permute-done.56 = f32[8,32]{1,0:T(8,128)S(1)} collective-permute-done((f32[8,32]{1,0:T(8,128)S(1)}, f32[8,32]{1,0:T(8,128)S(1)}, u32[]{:S(2)}, u32[]{:S(2)}) %collective-permute-start.56) | collective-permute-done | bytes 1056 | tf_op jit(solution)/shard_map/ppermute | solution.py:20
  187.6 5.3 %collective-permute-start.61 = (f32[8,32]{1,0:T(8,128)S(1)}, f32[8,32]{1,0:T(8,128)S(1)}, u32[]{:S(2)}, u32[]{:S(2)}) collective-permute-start(f32[8,32]{1,0:T(8,128)S(1)} %get-tuple-element.78), channel_id=1, source_target_pairs={{0,31},{1,0},{2,1},{3,2},{4,3},{5,4},{6,5},{7,6},{8,7},{9,8},{10,9... | collective-permute-start | bytes 3080 | tf_op jit(solution)/shard_map/ppermute | solution.py:20
  192.9 4.7 %collective-permute-start.63 = (f32[8,32]{1,0:T(8,128)S(1)}, f32[8,32]{1,0:T(8,128)S(1)}, u32[]{:S(2)}, u32[]{:S(2)}) collective-permute-start(f32[8,32]{1,0:T(8,128)S(1)} %get-tuple-element.76), channel_id=1, source_target_pairs={{0,28},{1,29},{2,30},{3,31},{4,0},{5,1},{6,2},{7,3},{8,4},{9,5},{1... | collective-permute-start | bytes 3080 | tf_op jit(solution)/shard_map/ppermute | solution.py:20
  204.9 5.3 %collective-permute-start.66 = (f32[8,64]{1,0:T(8,128)S(1)}, f32[8,64]{1,0:T(8,128)S(1)}, u32[]{:S(2)}, u32[]{:S(2)}) collective-permute-start(f32[8,64]{1,0:T(8,128)S(1)} %get-tuple-element.58), channel_id=1, source_target_pairs={{0,31},{1,0},{2,1},{3,2},{4,3},{5,4},{6,5},{7,6},{8,7},{9,8},{10,9... | collective-permute-start | bytes 6152 | tf_op jit(solution)/shard_map/ppermute | solution.py:20
  210.2 4.7 %collective-permute-start.68 = (f32[8,64]{1,0:T(8,128)S(1)}, f32[8,64]{1,0:T(8,128)S(1)}, u32[]{:S(2)}, u32[]{:S(2)}) collective-permute-start(f32[8,64]{1,0:T(8,128)S(1)} %get-tuple-element.56), channel_id=1, source_target_pairs={{0,28},{1,29},{2,30},{3,31},{4,0},{5,1},{6,2},{7,3},{8,4},{9,5},{1... | collective-permute-start | bytes 6152 | tf_op jit(solution)/shard_map/ppermute | solution.py:20
  237.9 4.7 %collective-permute-done.74 = f32[2,24,24]{2,1,0:T(8,128)S(1)} collective-permute-done((f32[2,24,24]{2,1,0:T(8,128)S(1)}, f32[2,24,24]{2,1,0:T(8,128)S(1)}, u32[]{:S(2)}, u32[]{:S(2)}) %collective-permute-start.74) | collective-permute-done | bytes 4640 | tf_op jit(solution)/shard_map/ppermute | solution.py:45
  (316 shorter events, 125.8 us)
Async XLA Ops:
  4.6 16.6 %collective-permute-start.4 = (f32[1,2112]{1,0:T(1,128)S(1)}, f32[1,2112]{1,0:T(1,128)S(1)}, u32[]{:S(2)}, u32[]{:S(2)}) collective-permute-start(f32[1,2112]{1,0:T(1,128)S(1)} %pad_maximum_fusion.4), channel_id=1, source_target_pairs={{0,16},{1,17},{2,18},{3,19},{4,20},{5,21},{6,22},{7,23},{8,24},{9,... | collective-permute-start | bytes 25352 | tf_op jit(solution)/shard_map/ppermute | solution.py:20
  8.9 10.9 %collective-permute-start = (f32[1,1056]{1,0:T(1,128)S(1)}, f32[1,1056]{1,0:T(1,128)S(1)}, u32[]{:S(2)}, u32[]{:S(2)}) collective-permute-start(f32[1,1056]{1,0:T(1,128)S(1)} %pad_maximum_fusion.6), channel_id=1, source_target_pairs={{0,1},{1,2},{2,3},{3,4},{4,5},{5,6},{6,7},{7,8},{8,9},{9,10},{10,1... | collective-permute-start | bytes 12680 | tf_op jit(solution)/shard_map/ppermute | solution.py:20
  9.0 10.7 %collective-permute-start.1 = (f32[1,1056]{1,0:T(1,128)S(1)}, f32[1,1056]{1,0:T(1,128)S(1)}, u32[]{:S(2)}, u32[]{:S(2)}) collective-permute-start(f32[1,1056]{1,0:T(1,128)S(1)} %pad_maximum_fusion.7), channel_id=1, source_target_pairs={{0,31},{1,0},{2,1},{3,2},{4,3},{5,4},{6,5},{7,6},{8,7},{9,8},{10,9... | collective-permute-start | bytes 12680 | tf_op jit(solution)/shard_map/ppermute | solution.py:20
  33.8 17.8 %collective-permute-start.5 = (f32[17,64]{1,0:T(8,128)S(1)}, f32[17,64]{1,0:T(8,128)S(1)}, u32[]{:S(2)}, u32[]{:S(2)}) collective-permute-start(f32[17,64]{1,0:T(8,128)S(1)} %get-tuple-element.20), channel_id=1, source_target_pairs={{0,31},{1,0},{2,1},{3,2},{4,3},{5,4},{6,5},{7,6},{8,7},{9,8},{10,9... | collective-permute-start | bytes 13064 | tf_op jit(solution)/shard_map/ppermute | solution.py:20
  40.0 11.6 %collective-permute-start.6 = (f32[17,64]{1,0:T(8,128)S(1)}, f32[17,64]{1,0:T(8,128)S(1)}, u32[]{:S(2)}, u32[]{:S(2)}) collective-permute-start(f32[17,64]{1,0:T(8,128)S(1)} %get-tuple-element.19), channel_id=1, source_target_pairs={{0,1},{1,2},{2,3},{3,4},{4,5},{5,6},{6,7},{7,8},{8,9},{9,10},{10,1... | collective-permute-start | bytes 13064 | tf_op jit(solution)/shard_map/ppermute | solution.py:20
  43.6 8.1 %collective-permute-start.7 = (f32[17,64]{1,0:T(8,128)S(1)}, f32[17,64]{1,0:T(8,128)S(1)}, u32[]{:S(2)}, u32[]{:S(2)}) collective-permute-start(f32[17,64]{1,0:T(8,128)S(1)} %get-tuple-element.18), channel_id=1, source_target_pairs={{0,28},{1,29},{2,30},{3,31},{4,0},{5,1},{6,2},{7,3},{8,4},{9,5},{1... | collective-permute-start | bytes 13064 | tf_op jit(solution)/shard_map/ppermute | solution.py:20
  57.3 10.1 %collective-permute-start.15 = (f32[8,64]{1,0:T(8,128)S(1)}, f32[8,64]{1,0:T(8,128)S(1)}, u32[]{:S(2)}, u32[]{:S(2)}) collective-permute-start(f32[8,64]{1,0:T(8,128)S(1)} %get-tuple-element.71), channel_id=1, source_target_pairs={{0,1},{1,2},{2,3},{3,4},{4,5},{5,6},{6,7},{7,8},{8,9},{9,10},{10,1... | collective-permute-start | bytes 6152 | tf_op jit(solution)/shard_map/ppermute | solution.py:20
  57.3 10.1 %collective-permute-start.16 = (f32[8,64]{1,0:T(8,128)S(1)}, f32[8,64]{1,0:T(8,128)S(1)}, u32[]{:S(2)}, u32[]{:S(2)}) collective-permute-start(f32[8,64]{1,0:T(8,128)S(1)} %get-tuple-element.70), channel_id=1, source_target_pairs={{0,31},{1,0},{2,1},{3,2},{4,3},{5,4},{6,5},{7,6},{8,7},{9,8},{10,9... | collective-permute-start | bytes 6152 | tf_op jit(solution)/shard_map/ppermute | solution.py:20
  78.0 6.7 %collective-permute-start.21 = (f32[8,64]{1,0:T(8,128)S(1)}, f32[8,64]{1,0:T(8,128)S(1)}, u32[]{:S(2)}, u32[]{:S(2)}) collective-permute-start(f32[8,64]{1,0:T(8,128)S(1)} %get-tuple-element.31), channel_id=1, source_target_pairs={{0,1},{1,2},{2,3},{3,4},{4,5},{5,6},{6,7},{7,8},{8,9},{9,10},{10,1... | collective-permute-start | bytes 6152 | tf_op jit(solution)/shard_map/ppermute | solution.py:20
  87.5 10.2 %collective-permute-start.25 = (f32[8,64]{1,0:T(8,128)S(1)}, f32[8,64]{1,0:T(8,128)S(1)}, u32[]{:S(2)}, u32[]{:S(2)}) collective-permute-start(f32[8,64]{1,0:T(8,128)S(1)} %get-tuple-element.67), channel_id=1, source_target_pairs={{0,1},{1,2},{2,3},{3,4},{4,5},{5,6},{6,7},{7,8},{8,9},{9,10},{10,1... | collective-permute-start | bytes 6152 | tf_op jit(solution)/shard_map/ppermute | solution.py:20
  87.5 10.2 %collective-permute-start.26 = (f32[8,64]{1,0:T(8,128)S(1)}, f32[8,64]{1,0:T(8,128)S(1)}, u32[]{:S(2)}, u32[]{:S(2)}) collective-permute-start(f32[8,64]{1,0:T(8,128)S(1)} %get-tuple-element.66), channel_id=1, source_target_pairs={{0,31},{1,0},{2,1},{3,2},{4,3},{5,4},{6,5},{7,6},{8,7},{9,8},{10,9... | collective-permute-start | bytes 6152 | tf_op jit(solution)/shard_map/ppermute | solution.py:20
  108.1 6.7 %collective-permute-start.31 = (f32[8,64]{1,0:T(8,128)S(1)}, f32[8,64]{1,0:T(8,128)S(1)}, u32[]{:S(2)}, u32[]{:S(2)}) collective-permute-start(f32[8,64]{1,0:T(8,128)S(1)} %get-tuple-element.27), channel_id=1, source_target_pairs={{0,1},{1,2},{2,3},{3,4},{4,5},{5,6},{6,7},{7,8},{8,9},{9,10},{10,1... | collective-permute-start | bytes 6152 | tf_op jit(solution)/shard_map/ppermute | solution.py:20
  117.6 10.2 %collective-permute-start.35 = (f32[8,64]{1,0:T(8,128)S(1)}, f32[8,64]{1,0:T(8,128)S(1)}, u32[]{:S(2)}, u32[]{:S(2)}) collective-permute-start(f32[8,64]{1,0:T(8,128)S(1)} %get-tuple-element.63), channel_id=1, source_target_pairs={{0,1},{1,2},{2,3},{3,4},{4,5},{5,6},{6,7},{7,8},{8,9},{9,10},{10,1... | collective-permute-start | bytes 6152 | tf_op jit(solution)/shard_map/ppermute | solution.py:20
  117.6 10.2 %collective-permute-start.36 = (f32[8,64]{1,0:T(8,128)S(1)}, f32[8,64]{1,0:T(8,128)S(1)}, u32[]{:S(2)}, u32[]{:S(2)}) collective-permute-start(f32[8,64]{1,0:T(8,128)S(1)} %get-tuple-element.62), channel_id=1, source_target_pairs={{0,31},{1,0},{2,1},{3,2},{4,3},{5,4},{6,5},{7,6},{8,7},{9,8},{10,9... | collective-permute-start | bytes 6152 | tf_op jit(solution)/shard_map/ppermute | solution.py:20
  138.3 6.7 %collective-permute-start.41 = (f32[8,64]{1,0:T(8,128)S(1)}, f32[8,64]{1,0:T(8,128)S(1)}, u32[]{:S(2)}, u32[]{:S(2)}) collective-permute-start(f32[8,64]{1,0:T(8,128)S(1)} %get-tuple-element.23), channel_id=1, source_target_pairs={{0,1},{1,2},{2,3},{3,4},{4,5},{5,6},{6,7},{7,8},{8,9},{9,10},{10,1... | collective-permute-start | bytes 6152 | tf_op jit(solution)/shard_map/ppermute | solution.py:20
  152.5 6.6 %collective-permute-start.48 = (f32[8,32]{1,0:T(8,128)S(1)}, f32[8,32]{1,0:T(8,128)S(1)}, u32[]{:S(2)}, u32[]{:S(2)}) collective-permute-start(f32[8,32]{1,0:T(8,128)S(1)} %get-tuple-element.45), channel_id=1, source_target_pairs={{0,4},{1,5},{2,6},{3,7},{4,8},{5,9},{6,10},{7,11},{8,12},{9,13},{1... | collective-permute-start | bytes 3080 | tf_op jit(solution)/shard_map/ppermute | solution.py:20
  159.9 11.0 %collective-permute-start.50 = (f32[8,32]{1,0:T(8,128)S(1)}, f32[8,32]{1,0:T(8,128)S(1)}, u32[]{:S(2)}, u32[]{:S(2)}) collective-permute-start(f32[8,32]{1,0:T(8,128)S(1)} %get-tuple-element.83), channel_id=1, source_target_pairs={{0,1},{1,2},{2,3},{3,4},{4,5},{5,6},{6,7},{7,8},{8,9},{9,10},{10,1... | collective-permute-start | bytes 3080 | tf_op jit(solution)/shard_map/ppermute | solution.py:20
  159.9 11.0 %collective-permute-start.51 = (f32[8,32]{1,0:T(8,128)S(1)}, f32[8,32]{1,0:T(8,128)S(1)}, u32[]{:S(2)}, u32[]{:S(2)}) collective-permute-start(f32[8,32]{1,0:T(8,128)S(1)} %get-tuple-element.82), channel_id=1, source_target_pairs={{0,31},{1,0},{2,1},{3,2},{4,3},{5,4},{6,5},{7,6},{8,7},{9,8},{10,9... | collective-permute-start | bytes 3080 | tf_op jit(solution)/shard_map/ppermute | solution.py:20
  178.1 8.8 %collective-permute-start.59 = (f32[8,64]{1,0:T(8,128)S(1)}, f32[8,64]{1,0:T(8,128)S(1)}, u32[]{:S(2)}, u32[]{:S(2)}) collective-permute-start(f32[8,64]{1,0:T(8,128)S(1)} %concatenate.231), channel_id=1, source_target_pairs={{0,16},{1,17},{2,18},{3,19},{4,20},{5,21},{6,22},{7,23},{8,24},{9,... | collective-permute-start | bytes 6152 | tf_op jit(solution)/shard_map/ppermute | solution.py:20
  178.3 6.7 %collective-permute-start.56 = (f32[8,32]{1,0:T(8,128)S(1)}, f32[8,32]{1,0:T(8,128)S(1)}, u32[]{:S(2)}, u32[]{:S(2)}) collective-permute-start(f32[8,32]{1,0:T(8,128)S(1)} %get-tuple-element.43), channel_id=1, source_target_pairs={{0,1},{1,2},{2,3},{3,4},{4,5},{5,6},{6,7},{7,8},{8,9},{9,10},{10,1... | collective-permute-start | bytes 3080 | tf_op jit(solution)/shard_map/ppermute | solution.py:20
  187.6 10.1 %collective-permute-start.60 = (f32[8,32]{1,0:T(8,128)S(1)}, f32[8,32]{1,0:T(8,128)S(1)}, u32[]{:S(2)}, u32[]{:S(2)}) collective-permute-start(f32[8,32]{1,0:T(8,128)S(1)} %get-tuple-element.79), channel_id=1, source_target_pairs={{0,1},{1,2},{2,3},{3,4},{4,5},{5,6},{6,7},{7,8},{8,9},{9,10},{10,1... | collective-permute-start | bytes 3080 | tf_op jit(solution)/shard_map/ppermute | solution.py:20
  187.6 10.1 %collective-permute-start.61 = (f32[8,32]{1,0:T(8,128)S(1)}, f32[8,32]{1,0:T(8,128)S(1)}, u32[]{:S(2)}, u32[]{:S(2)}) collective-permute-start(f32[8,32]{1,0:T(8,128)S(1)} %get-tuple-element.78), channel_id=1, source_target_pairs={{0,31},{1,0},{2,1},{3,2},{4,3},{5,4},{6,5},{7,6},{8,7},{9,8},{10,9... | collective-permute-start | bytes 3080 | tf_op jit(solution)/shard_map/ppermute | solution.py:20
  204.8 10.1 %collective-permute-start.65 = (f32[8,64]{1,0:T(8,128)S(1)}, f32[8,64]{1,0:T(8,128)S(1)}, u32[]{:S(2)}, u32[]{:S(2)}) collective-permute-start(f32[8,64]{1,0:T(8,128)S(1)} %get-tuple-element.59), channel_id=1, source_target_pairs={{0,1},{1,2},{2,3},{3,4},{4,5},{5,6},{6,7},{7,8},{8,9},{9,10},{10,1... | collective-permute-start | bytes 6152 | tf_op jit(solution)/shard_map/ppermute | solution.py:20
  204.9 10.1 %collective-permute-start.66 = (f32[8,64]{1,0:T(8,128)S(1)}, f32[8,64]{1,0:T(8,128)S(1)}, u32[]{:S(2)}, u32[]{:S(2)}) collective-permute-start(f32[8,64]{1,0:T(8,128)S(1)} %get-tuple-element.58), channel_id=1, source_target_pairs={{0,31},{1,0},{2,1},{3,2},{4,3},{5,4},{6,5},{7,6},{8,7},{9,8},{10,9... | collective-permute-start | bytes 6152 | tf_op jit(solution)/shard_map/ppermute | solution.py:20
  (59 other events, 361.0 us)

commit v3 on v2

--- a/solution.py
+++ b/solution.py
@@ -40,10 +40,21 @@
     length = lax.axis_size("dom")
     if length & (length - 1):
         return lax.psum(value, "dom")
-    stride = 1
-    while stride < length:
-        value = value + lax.ppermute(value, "dom", [(i, i ^ stride) for i in range(length)])
-        stride *= 2
+    me = lax.axis_index("dom")
+    shift = 0
+    while (1 << shift) < length:
+        bits = 2 if (4 << shift) <= length else 1
+        size = 1 << bits
+        got = [value] + [
+            lax.ppermute(value, "dom", [(i, i ^ (t << shift)) for i in range(length)])
+            for t in range(1, size)
+        ]
+        digit = (me >> shift) & (size - 1)
+        ordered = jnp.take(jnp.stack(got), jnp.arange(size) ^ digit, axis=0)
+        while ordered.shape[0] > 1:
+            ordered = ordered[0::2] + ordered[1::2]
+        value = ordered[0]
+        shift += bits
     return value
 
 
@@ -191,6 +202,7 @@
     stiff_x = images[:modes]
     mass_x = images[modes : 2 * modes]
     edge_diag = images[2 * modes]
+    images_ext = extend(images, send_edge_table)
     stiff_part = inner_elements(pair_values, stiff_pair)
     mass_part = inner_elements(pair_values, mass_pair)
     numerator, denominator = all_sum(
@@ -199,8 +211,10 @@
     quotient = numerator / denominator
     residual = stiff_x - quotient[:, None] * mass_x
 
-    def stiff_image(vectors):
-        values = edge_values(extend(vectors, send_edge_table))
+    def stiff_image(vectors, extended=None):
+        if extended is None:
+            extended = extend(vectors, send_edge_table)
+        values = edge_values(extended)
         return give_back(edge_sum(element_terms(stiff_elem, values)), send_edge_table)
 
     center = 0.5 * (interval_high + interval_low)
@@ -209,9 +223,11 @@
     rho_now = 1.0 / sigma
     step_dir = residual / (center * edge_diag)
     smooth = step_dir
+    residual_ext = images_ext[:modes] - quotient[:, None] * images_ext[modes : 2 * modes]
+    smooth_ext = residual_ext / (center * images_ext[2 * modes])
     for turn in range(CHEB_DEG - 1):
         rho_next = 1.0 / (2.0 * sigma - rho_now)
-        remain = residual - stiff_image(smooth)
+        remain = residual - stiff_image(smooth, smooth_ext if turn == 0 else None)
         step_dir = rho_next * rho_now * step_dir + 2.0 * rho_next / spread * remain / edge_diag
         smooth = smooth + step_dir
         rho_now = rho_next

time: 243 us -> 246 us (1.012)
  waiting for transfers between devices: 85.9 us -> 77.1 us
  starting transfers between devices: 103 us -> 109 us
  local copies, waits for them, and re-layouts: 8.58 us -> 12 us
    ppermute x10 -> x14, starting transfers between devices: 0.29 us -> 10.6 us  [all_sum(): lax.ppermute(value, 'dom', [(i, i ^ t << shift) for i in range(length)])]
    ppermute x10 -> x14, waiting for transfers between devices: 25.2 us -> 17.2 us  [all_sum(): lax.ppermute(value, 'dom', [(i, i ^ t << shift) for i in range(length)])]
    gather x0 -> x6, local copies, waits for them, and re-layouts: none -> 3.37 us  [all_sum(): ordered = jnp.take(jnp.stack(got), jnp.arange(size) ^ digit, axis=0)]
    ppermute x65, starting transfers between devices: 102 us -> 98.8 us  [from_behind(): lax.ppermute(shard, axis, [(i, (i + by) % length) for i in range(length)])]
  transfers between devices with their start and end apart: 75 -> 79, of which waited for: 32 -> 32; matrix products, arithmetic and copies ran while one was open for 2% -> 3% of each run, Pallas kernels for 0% -> 0%
where the time goes in v3:
time: 246 us
  starting transfers between devices  109 us (44%)
  waiting for transfers between devices  77.1 us (31%)
  matrix products  40.9 us (17%)
  local copies, waits for them, and re-layouts  12 us (5%)
  other arithmetic  4.4 us (2%)
    ppermute x65, starting transfers between devices, from_behind(): lax.ppermute(shard, axis, [(i, (i + by) % length) for i in range(length)])  98.8 us
    ppermute x65, waiting for transfers between devices, from_behind(): lax.ppermute(shard, axis, [(i, (i + by) % length) for i in range(length)])  59.9 us
    dot_general x14, matrix products, gather_cols(): picked = jnp.einsum('rab,nb->ran', split, lo_hot, precision=highest)  25.7 us
    ppermute x14, waiting for transfers between devices, all_sum(): lax.ppermute(value, 'dom', [(i, i ^ t << shift) for i in range(length)])  17.2 us
    dot_general x14, matrix products, scatter_cols(): summed = jnp.einsum('ran,nb->rab', spread, lo_hot, precision=highest)  13 us
    ppermute x14, starting transfers between devices, all_sum(): lax.ppermute(value, 'dom', [(i, i ^ t << shift) for i in range(length)])  10.6 us
  transfers between devices with their start and end apart: 79, of which 32 were waited for; matrix products, arithmetic and copies ran while one was open for 3% of the time, Pallas kernels for 0%

profile of v3, /device:TPU:0, one launch (start us, length us, event | category | flops | bytes accessed | tf_op | source)
XLA Modules:
  0.0 245.6 jit_solution(17830237556113315554)
XLA Ops:
  4.6 4.1 %collective-permute-start.4 = (f32[1,2112]{1,0:T(1,128)S(1)}, f32[1,2112]{1,0:T(1,128)S(1)}, u32[]{:S(2)}, u32[]{:S(2)}) collective-permute-start(f32[1,2112]{1,0:T(1,128)S(1)} %pad_maximum_fusion.7), channel_id=1, source_target_pairs={{0,16},{1,17},{2,18},{3,19},{4,20},{5,21},{6,22},{7,23},{8,24},{9,... | collective-permute-start | bytes 25352 | tf_op jit(solution)/shard_map/ppermute | solution.py:20
  9.0 5.4 %collective-permute-start.1 = (f32[1,1056]{1,0:T(1,128)S(1)}, f32[1,1056]{1,0:T(1,128)S(1)}, u32[]{:S(2)}, u32[]{:S(2)}) collective-permute-start(f32[1,1056]{1,0:T(1,128)S(1)} %pad_maximum_fusion.10), channel_id=1, source_target_pairs={{0,31},{1,0},{2,1},{3,2},{4,3},{5,4},{6,5},{7,6},{8,7},{9,8},{10,9... | collective-permute-start | bytes 12680 | tf_op jit(solution)/shard_map/ppermute | solution.py:20
  14.7 4.8 %collective-permute-start.3 = (f32[1,1056]{1,0:T(1,128)S(1)}, f32[1,1056]{1,0:T(1,128)S(1)}, u32[]{:S(2)}, u32[]{:S(2)}) collective-permute-start(f32[1,1056]{1,0:T(1,128)S(1)} %pad_maximum_fusion.12), channel_id=1, source_target_pairs={{0,28},{1,29},{2,30},{3,31},{4,0},{5,1},{6,2},{7,3},{8,4},{9,5},{1... | collective-permute-start | bytes 12680 | tf_op jit(solution)/shard_map/ppermute | solution.py:20
  21.5 4.3 %fusion.20 = f32[16,5120]{1,0:T(8,128)S(1)} fusion(f32[15,5120]{1,0:T(8,128)S(1)} %fusion.109, s32[5120]{0:T(1024)S(1)} %get-tuple-element.55, f32[16,1920]{1,0:T(8,128)S(1)} %concatenate.178), kind=kOutput, calls=%fused_computation.34 | convolution fusion | flops 1890467840 | bytes 778240 | tf_op jit(solution)/shard_map/rab,nb->ran/dot_general | solution.py:76
  35.6 4.3 %collective-permute-start.5 = (f32[17,64]{1,0:T(8,128)S(1)}, f32[17,64]{1,0:T(8,128)S(1)}, u32[]{:S(2)}, u32[]{:S(2)}) collective-permute-start(f32[17,64]{1,0:T(8,128)S(1)} %get-tuple-element.22), channel_id=1, source_target_pairs={{0,31},{1,0},{2,1},{3,2},{4,3},{5,4},{6,5},{7,6},{8,7},{9,8},{10,9... | collective-permute-start | bytes 13064 | tf_op jit(solution)/shard_map/ppermute | solution.py:20
  50.5 4.4 %collective-permute-done.16 = f32[2,8]{1,0:T(2,128)S(1)} collective-permute-done((f32[2,8]{1,0:T(2,128)S(1)}, f32[2,8]{1,0:T(2,128)S(1)}, u32[]{:S(2)}, u32[]{:S(2)}) %collective-permute-start.16) | collective-permute-done | bytes 96 | tf_op jit(solution)/shard_map/ppermute | solution.py:49
  60.7 5.3 %collective-permute-start.18 = (f32[17,64]{1,0:T(8,128)S(1)}, f32[17,64]{1,0:T(8,128)S(1)}, u32[]{:S(2)}, u32[]{:S(2)}) collective-permute-start(f32[17,64]{1,0:T(8,128)S(1)} %get-tuple-element.37), channel_id=1, source_target_pairs={{0,31},{1,0},{2,1},{3,2},{4,3},{5,4},{6,5},{7,6},{8,7},{9,8},{10,9... | collective-permute-start | bytes 13064 | tf_op jit(solution)/shard_map/ppermute | solution.py:20
  66.0 4.7 %collective-permute-start.20 = (f32[17,64]{1,0:T(8,128)S(1)}, f32[17,64]{1,0:T(8,128)S(1)}, u32[]{:S(2)}, u32[]{:S(2)}) collective-permute-start(f32[17,64]{1,0:T(8,128)S(1)} %get-tuple-element.35), channel_id=1, source_target_pairs={{0,28},{1,29},{2,30},{3,31},{4,0},{5,1},{6,2},{7,3},{8,4},{9,5},{1... | collective-permute-start | bytes 13064 | tf_op jit(solution)/shard_map/ppermute | solution.py:20
  84.2 4.0 %collective-permute-done.23 = f32[8,64]{1,0:T(8,128)S(1)} collective-permute-done((f32[8,64]{1,0:T(8,128)S(1)}, f32[8,64]{1,0:T(8,128)S(1)}, u32[]{:S(2)}, u32[]{:S(2)}) %collective-permute-start.23) | collective-permute-done | bytes 2080 | tf_op jit(solution)/shard_map/ppermute | solution.py:20
  91.1 5.3 %collective-permute-start.28 = (f32[8,64]{1,0:T(8,128)S(1)}, f32[8,64]{1,0:T(8,128)S(1)}, u32[]{:S(2)}, u32[]{:S(2)}) collective-permute-start(f32[8,64]{1,0:T(8,128)S(1)} %get-tuple-element.72), channel_id=1, source_target_pairs={{0,31},{1,0},{2,1},{3,2},{4,3},{5,4},{6,5},{7,6},{8,7},{9,8},{10,9... | collective-permute-start | bytes 6152 | tf_op jit(solution)/shard_map/ppermute | solution.py:20
  96.4 4.7 %collective-permute-start.30 = (f32[8,64]{1,0:T(8,128)S(1)}, f32[8,64]{1,0:T(8,128)S(1)}, u32[]{:S(2)}, u32[]{:S(2)}) collective-permute-start(f32[8,64]{1,0:T(8,128)S(1)} %get-tuple-element.70), channel_id=1, source_target_pairs={{0,28},{1,29},{2,30},{3,31},{4,0},{5,1},{6,2},{7,3},{8,4},{9,5},{1... | collective-permute-start | bytes 6152 | tf_op jit(solution)/shard_map/ppermute | solution.py:20
  114.3 4.1 %collective-permute-done.33 = f32[8,64]{1,0:T(8,128)S(1)} collective-permute-done((f32[8,64]{1,0:T(8,128)S(1)}, f32[8,64]{1,0:T(8,128)S(1)}, u32[]{:S(2)}, u32[]{:S(2)}) %collective-permute-start.33) | collective-permute-done | bytes 2080 | tf_op jit(solution)/shard_map/ppermute | solution.py:20
  121.2 5.3 %collective-permute-start.38 = (f32[8,64]{1,0:T(8,128)S(1)}, f32[8,64]{1,0:T(8,128)S(1)}, u32[]{:S(2)}, u32[]{:S(2)}) collective-permute-start(f32[8,64]{1,0:T(8,128)S(1)} %get-tuple-element.68), channel_id=1, source_target_pairs={{0,31},{1,0},{2,1},{3,2},{4,3},{5,4},{6,5},{7,6},{8,7},{9,8},{10,9... | collective-permute-start | bytes 6152 | tf_op jit(solution)/shard_map/ppermute | solution.py:20
  126.5 4.7 %collective-permute-start.40 = (f32[8,64]{1,0:T(8,128)S(1)}, f32[8,64]{1,0:T(8,128)S(1)}, u32[]{:S(2)}, u32[]{:S(2)}) collective-permute-start(f32[8,64]{1,0:T(8,128)S(1)} %get-tuple-element.66), channel_id=1, source_target_pairs={{0,28},{1,29},{2,30},{3,31},{4,0},{5,1},{6,2},{7,3},{8,4},{9,5},{1... | collective-permute-start | bytes 6152 | tf_op jit(solution)/shard_map/ppermute | solution.py:20
  144.6 3.9 %collective-permute-done.43 = f32[8,64]{1,0:T(8,128)S(1)} collective-permute-done((f32[8,64]{1,0:T(8,128)S(1)}, f32[8,64]{1,0:T(8,128)S(1)}, u32[]{:S(2)}, u32[]{:S(2)}) %collective-permute-start.43) | collective-permute-done | bytes 2080 | tf_op jit(solution)/shard_map/ppermute | solution.py:20
  151.8 4.3 %collective-permute-start.47 = (f32[8,32]{1,0:T(8,128)S(1)}, f32[8,32]{1,0:T(8,128)S(1)}, u32[]{:S(2)}, u32[]{:S(2)}) collective-permute-start(f32[8,32]{1,0:T(8,128)S(1)} %get-tuple-element.54), channel_id=1, source_target_pairs={{0,31},{1,0},{2,1},{3,2},{4,3},{5,4},{6,5},{7,6},{8,7},{9,8},{10,9... | collective-permute-start | bytes 3080 | tf_op jit(solution)/shard_map/ppermute | solution.py:20
  158.2 4.6 %collective-permute-done.48 = f32[8,32]{1,0:T(8,128)S(1)} collective-permute-done((f32[8,32]{1,0:T(8,128)S(1)}, f32[8,32]{1,0:T(8,128)S(1)}, u32[]{:S(2)}, u32[]{:S(2)}) %collective-permute-start.48) | collective-permute-done | bytes 1056 | tf_op jit(solution)/shard_map/ppermute | solution.py:20
  163.5 6.3 %collective-permute-start.53 = (f32[8,32]{1,0:T(8,128)S(1)}, f32[8,32]{1,0:T(8,128)S(1)}, u32[]{:S(2)}, u32[]{:S(2)}) collective-permute-start(f32[8,32]{1,0:T(8,128)S(1)} %get-tuple-element.84), channel_id=1, source_target_pairs={{0,31},{1,0},{2,1},{3,2},{4,3},{5,4},{6,5},{7,6},{8,7},{9,8},{10,9... | collective-permute-start | bytes 3080 | tf_op jit(solution)/shard_map/ppermute | solution.py:20
  169.7 4.7 %collective-permute-start.55 = (f32[8,32]{1,0:T(8,128)S(1)}, f32[8,32]{1,0:T(8,128)S(1)}, u32[]{:S(2)}, u32[]{:S(2)}) collective-permute-start(f32[8,32]{1,0:T(8,128)S(1)} %get-tuple-element.82), channel_id=1, source_target_pairs={{0,28},{1,29},{2,30},{3,31},{4,0},{5,1},{6,2},{7,3},{8,4},{9,5},{1... | collective-permute-start | bytes 3080 | tf_op jit(solution)/shard_map/ppermute | solution.py:20
  184.4 4.1 %collective-permute-done.58 = f32[8,32]{1,0:T(8,128)S(1)} collective-permute-done((f32[8,32]{1,0:T(8,128)S(1)}, f32[8,32]{1,0:T(8,128)S(1)}, u32[]{:S(2)}, u32[]{:S(2)}) %collective-permute-start.58) | collective-permute-done | bytes 1056 | tf_op jit(solution)/shard_map/ppermute | solution.py:20
  191.2 5.3 %collective-permute-start.63 = (f32[8,32]{1,0:T(8,128)S(1)}, f32[8,32]{1,0:T(8,128)S(1)}, u32[]{:S(2)}, u32[]{:S(2)}) collective-permute-start(f32[8,32]{1,0:T(8,128)S(1)} %get-tuple-element.80), channel_id=1, source_target_pairs={{0,31},{1,0},{2,1},{3,2},{4,3},{5,4},{6,5},{7,6},{8,7},{9,8},{10,9... | collective-permute-start | bytes 3080 | tf_op jit(solution)/shard_map/ppermute | solution.py:20
  196.5 4.7 %collective-permute-start.65 = (f32[8,32]{1,0:T(8,128)S(1)}, f32[8,32]{1,0:T(8,128)S(1)}, u32[]{:S(2)}, u32[]{:S(2)}) collective-permute-start(f32[8,32]{1,0:T(8,128)S(1)} %get-tuple-element.78), channel_id=1, source_target_pairs={{0,28},{1,29},{2,30},{3,31},{4,0},{5,1},{6,2},{7,3},{8,4},{9,5},{1... | collective-permute-start | bytes 3080 | tf_op jit(solution)/shard_map/ppermute | solution.py:20
  208.4 5.3 %collective-permute-start.68 = (f32[8,64]{1,0:T(8,128)S(1)}, f32[8,64]{1,0:T(8,128)S(1)}, u32[]{:S(2)}, u32[]{:S(2)}) collective-permute-start(f32[8,64]{1,0:T(8,128)S(1)} %get-tuple-element.64), channel_id=1, source_target_pairs={{0,31},{1,0},{2,1},{3,2},{4,3},{5,4},{6,5},{7,6},{8,7},{9,8},{10,9... | collective-permute-start | bytes 6152 | tf_op jit(solution)/shard_map/ppermute | solution.py:20
  213.8 4.7 %collective-permute-start.70 = (f32[8,64]{1,0:T(8,128)S(1)}, f32[8,64]{1,0:T(8,128)S(1)}, u32[]{:S(2)}, u32[]{:S(2)}) collective-permute-start(f32[8,64]{1,0:T(8,128)S(1)} %get-tuple-element.62), channel_id=1, source_target_pairs={{0,28},{1,29},{2,30},{3,31},{4,0},{5,1},{6,2},{7,3},{8,4},{9,5},{1... | collective-permute-start | bytes 6152 | tf_op jit(solution)/shard_map/ppermute | solution.py:20
  (356 shorter events, 130.3 us)
Async XLA Ops:
  4.6 16.6 %collective-permute-start.4 = (f32[1,2112]{1,0:T(1,128)S(1)}, f32[1,2112]{1,0:T(1,128)S(1)}, u32[]{:S(2)}, u32[]{:S(2)}) collective-permute-start(f32[1,2112]{1,0:T(1,128)S(1)} %pad_maximum_fusion.7), channel_id=1, source_target_pairs={{0,16},{1,17},{2,18},{3,19},{4,20},{5,21},{6,22},{7,23},{8,24},{9,... | collective-permute-start | bytes 25352 | tf_op jit(solution)/shard_map/ppermute | solution.py:20
  8.9 11.0 %collective-permute-start = (f32[1,1056]{1,0:T(1,128)S(1)}, f32[1,1056]{1,0:T(1,128)S(1)}, u32[]{:S(2)}, u32[]{:S(2)}) collective-permute-start(f32[1,1056]{1,0:T(1,128)S(1)} %pad_maximum_fusion.9), channel_id=1, source_target_pairs={{0,1},{1,2},{2,3},{3,4},{4,5},{5,6},{6,7},{7,8},{8,9},{9,10},{10,1... | collective-permute-start | bytes 12680 | tf_op jit(solution)/shard_map/ppermute | solution.py:20
  9.0 10.9 %collective-permute-start.1 = (f32[1,1056]{1,0:T(1,128)S(1)}, f32[1,1056]{1,0:T(1,128)S(1)}, u32[]{:S(2)}, u32[]{:S(2)}) collective-permute-start(f32[1,1056]{1,0:T(1,128)S(1)} %pad_maximum_fusion.10), channel_id=1, source_target_pairs={{0,31},{1,0},{2,1},{3,2},{4,3},{5,4},{6,5},{7,6},{8,7},{9,8},{10,9... | collective-permute-start | bytes 12680 | tf_op jit(solution)/shard_map/ppermute | solution.py:20
  30.3 9.6 %collective-permute-start.10 = (f32[2,8]{1,0:T(2,128)S(1)}, f32[2,8]{1,0:T(2,128)S(1)}, u32[]{:S(2)}, u32[]{:S(2)}) collective-permute-start(f32[2,8]{1,0:T(2,128)S(1)} %get-tuple-element.95), channel_id=1, source_target_pairs={{0,1},{1,0},{2,3},{3,2},{4,5},{5,4},{6,7},{7,6},{8,9},{9,8},{10,11... | collective-permute-start | bytes 200 | tf_op jit(solution)/shard_map/ppermute | solution.py:49
  30.3 10.6 %collective-permute-start.11 = (f32[2,8]{1,0:T(2,128)S(1)}, f32[2,8]{1,0:T(2,128)S(1)}, u32[]{:S(2)}, u32[]{:S(2)}) collective-permute-start(f32[2,8]{1,0:T(2,128)S(1)} %get-tuple-element.95), channel_id=1, source_target_pairs={{0,2},{1,3},{2,0},{3,1},{4,6},{5,7},{6,4},{7,5},{8,10},{9,11},{10,... | collective-permute-start | bytes 200 | tf_op jit(solution)/shard_map/ppermute | solution.py:49
  30.4 10.5 %collective-permute-start.12 = (f32[2,8]{1,0:T(2,128)S(1)}, f32[2,8]{1,0:T(2,128)S(1)}, u32[]{:S(2)}, u32[]{:S(2)}) collective-permute-start(f32[2,8]{1,0:T(2,128)S(1)} %get-tuple-element.95), channel_id=1, source_target_pairs={{0,3},{1,2},{2,1},{3,0},{4,7},{5,6},{6,5},{7,4},{8,11},{9,10},{10,... | collective-permute-start | bytes 200 | tf_op jit(solution)/shard_map/ppermute | solution.py:49
  35.6 20.0 %collective-permute-start.5 = (f32[17,64]{1,0:T(8,128)S(1)}, f32[17,64]{1,0:T(8,128)S(1)}, u32[]{:S(2)}, u32[]{:S(2)}) collective-permute-start(f32[17,64]{1,0:T(8,128)S(1)} %get-tuple-element.22), channel_id=1, source_target_pairs={{0,31},{1,0},{2,1},{3,2},{4,3},{5,4},{6,5},{7,6},{8,7},{9,8},{10,9... | collective-permute-start | bytes 13064 | tf_op jit(solution)/shard_map/ppermute | solution.py:20
  39.9 15.7 %collective-permute-start.6 = (f32[17,64]{1,0:T(8,128)S(1)}, f32[17,64]{1,0:T(8,128)S(1)}, u32[]{:S(2)}, u32[]{:S(2)}) collective-permute-start(f32[17,64]{1,0:T(8,128)S(1)} %get-tuple-element.21), channel_id=1, source_target_pairs={{0,1},{1,2},{2,3},{3,4},{4,5},{5,6},{6,7},{7,8},{8,9},{9,10},{10,1... | collective-permute-start | bytes 13064 | tf_op jit(solution)/shard_map/ppermute | solution.py:20
  39.9 15.7 %collective-permute-start.7 = (f32[17,64]{1,0:T(8,128)S(1)}, f32[17,64]{1,0:T(8,128)S(1)}, u32[]{:S(2)}, u32[]{:S(2)}) collective-permute-start(f32[17,64]{1,0:T(8,128)S(1)} %get-tuple-element.20), channel_id=1, source_target_pairs={{0,28},{1,29},{2,30},{3,31},{4,0},{5,1},{6,2},{7,3},{8,4},{9,5},{1... | collective-permute-start | bytes 13064 | tf_op jit(solution)/shard_map/ppermute | solution.py:20
  46.3 9.3 %collective-permute-start.8 = (f32[17,64]{1,0:T(8,128)S(1)}, f32[17,64]{1,0:T(8,128)S(1)}, u32[]{:S(2)}, u32[]{:S(2)}) collective-permute-start(f32[17,64]{1,0:T(8,128)S(1)} %get-tuple-element.19), channel_id=1, source_target_pairs={{0,4},{1,5},{2,6},{3,7},{4,8},{5,9},{6,10},{7,11},{8,12},{9,13},{1... | collective-permute-start | bytes 13064 | tf_op jit(solution)/shard_map/ppermute | solution.py:20
  60.7 10.1 %collective-permute-start.17 = (f32[17,64]{1,0:T(8,128)S(1)}, f32[17,64]{1,0:T(8,128)S(1)}, u32[]{:S(2)}, u32[]{:S(2)}) collective-permute-start(f32[17,64]{1,0:T(8,128)S(1)} %get-tuple-element.38), channel_id=1, source_target_pairs={{0,1},{1,2},{2,3},{3,4},{4,5},{5,6},{6,7},{7,8},{8,9},{9,10},{10,1... | collective-permute-start | bytes 13064 | tf_op jit(solution)/shard_map/ppermute | solution.py:20
  60.7 10.1 %collective-permute-start.18 = (f32[17,64]{1,0:T(8,128)S(1)}, f32[17,64]{1,0:T(8,128)S(1)}, u32[]{:S(2)}, u32[]{:S(2)}) collective-permute-start(f32[17,64]{1,0:T(8,128)S(1)} %get-tuple-element.37), channel_id=1, source_target_pairs={{0,31},{1,0},{2,1},{3,2},{4,3},{5,4},{6,5},{7,6},{8,7},{9,8},{10,9... | collective-permute-start | bytes 13064 | tf_op jit(solution)/shard_map/ppermute | solution.py:20
  81.5 6.7 %collective-permute-start.23 = (f32[8,64]{1,0:T(8,128)S(1)}, f32[8,64]{1,0:T(8,128)S(1)}, u32[]{:S(2)}, u32[]{:S(2)}) collective-permute-start(f32[8,64]{1,0:T(8,128)S(1)} %get-tuple-element.33), channel_id=1, source_target_pairs={{0,1},{1,2},{2,3},{3,4},{4,5},{5,6},{6,7},{7,8},{8,9},{9,10},{10,1... | collective-permute-start | bytes 6152 | tf_op jit(solution)/shard_map/ppermute | solution.py:20
  91.0 10.2 %collective-permute-start.27 = (f32[8,64]{1,0:T(8,128)S(1)}, f32[8,64]{1,0:T(8,128)S(1)}, u32[]{:S(2)}, u32[]{:S(2)}) collective-permute-start(f32[8,64]{1,0:T(8,128)S(1)} %get-tuple-element.73), channel_id=1, source_target_pairs={{0,1},{1,2},{2,3},{3,4},{4,5},{5,6},{6,7},{7,8},{8,9},{9,10},{10,1... | collective-permute-start | bytes 6152 | tf_op jit(solution)/shard_map/ppermute | solution.py:20
  91.1 10.2 %collective-permute-start.28 = (f32[8,64]{1,0:T(8,128)S(1)}, f32[8,64]{1,0:T(8,128)S(1)}, u32[]{:S(2)}, u32[]{:S(2)}) collective-permute-start(f32[8,64]{1,0:T(8,128)S(1)} %get-tuple-element.72), channel_id=1, source_target_pairs={{0,31},{1,0},{2,1},{3,2},{4,3},{5,4},{6,5},{7,6},{8,7},{9,8},{10,9... | collective-permute-start | bytes 6152 | tf_op jit(solution)/shard_map/ppermute | solution.py:20
  121.2 10.2 %collective-permute-start.37 = (f32[8,64]{1,0:T(8,128)S(1)}, f32[8,64]{1,0:T(8,128)S(1)}, u32[]{:S(2)}, u32[]{:S(2)}) collective-permute-start(f32[8,64]{1,0:T(8,128)S(1)} %get-tuple-element.69), channel_id=1, source_target_pairs={{0,1},{1,2},{2,3},{3,4},{4,5},{5,6},{6,7},{7,8},{8,9},{9,10},{10,1... | collective-permute-start | bytes 6152 | tf_op jit(solution)/shard_map/ppermute | solution.py:20
  121.2 10.2 %collective-permute-start.38 = (f32[8,64]{1,0:T(8,128)S(1)}, f32[8,64]{1,0:T(8,128)S(1)}, u32[]{:S(2)}, u32[]{:S(2)}) collective-permute-start(f32[8,64]{1,0:T(8,128)S(1)} %get-tuple-element.68), channel_id=1, source_target_pairs={{0,31},{1,0},{2,1},{3,2},{4,3},{5,4},{6,5},{7,6},{8,7},{9,8},{10,9... | collective-permute-start | bytes 6152 | tf_op jit(solution)/shard_map/ppermute | solution.py:20
  163.4 11.0 %collective-permute-start.52 = (f32[8,32]{1,0:T(8,128)S(1)}, f32[8,32]{1,0:T(8,128)S(1)}, u32[]{:S(2)}, u32[]{:S(2)}) collective-permute-start(f32[8,32]{1,0:T(8,128)S(1)} %get-tuple-element.85), channel_id=1, source_target_pairs={{0,1},{1,2},{2,3},{3,4},{4,5},{5,6},{6,7},{7,8},{8,9},{9,10},{10,1... | collective-permute-start | bytes 3080 | tf_op jit(solution)/shard_map/ppermute | solution.py:20
  163.5 11.0 %collective-permute-start.53 = (f32[8,32]{1,0:T(8,128)S(1)}, f32[8,32]{1,0:T(8,128)S(1)}, u32[]{:S(2)}, u32[]{:S(2)}) collective-permute-start(f32[8,32]{1,0:T(8,128)S(1)} %get-tuple-element.84), channel_id=1, source_target_pairs={{0,31},{1,0},{2,1},{3,2},{4,3},{5,4},{6,5},{7,6},{8,7},{9,8},{10,9... | collective-permute-start | bytes 3080 | tf_op jit(solution)/shard_map/ppermute | solution.py:20
  181.7 8.8 %collective-permute-start.61 = (f32[8,64]{1,0:T(8,128)S(1)}, f32[8,64]{1,0:T(8,128)S(1)}, u32[]{:S(2)}, u32[]{:S(2)}) collective-permute-start(f32[8,64]{1,0:T(8,128)S(1)} %concatenate.231), channel_id=1, source_target_pairs={{0,16},{1,17},{2,18},{3,19},{4,20},{5,21},{6,22},{7,23},{8,24},{9,... | collective-permute-start | bytes 6152 | tf_op jit(solution)/shard_map/ppermute | solution.py:20
  191.2 10.1 %collective-permute-start.62 = (f32[8,32]{1,0:T(8,128)S(1)}, f32[8,32]{1,0:T(8,128)S(1)}, u32[]{:S(2)}, u32[]{:S(2)}) collective-permute-start(f32[8,32]{1,0:T(8,128)S(1)} %get-tuple-element.81), channel_id=1, source_target_pairs={{0,1},{1,2},{2,3},{3,4},{4,5},{5,6},{6,7},{7,8},{8,9},{9,10},{10,1... | collective-permute-start | bytes 3080 | tf_op jit(solution)/shard_map/ppermute | solution.py:20
  191.2 10.1 %collective-permute-start.63 = (f32[8,32]{1,0:T(8,128)S(1)}, f32[8,32]{1,0:T(8,128)S(1)}, u32[]{:S(2)}, u32[]{:S(2)}) collective-permute-start(f32[8,32]{1,0:T(8,128)S(1)} %get-tuple-element.80), channel_id=1, source_target_pairs={{0,31},{1,0},{2,1},{3,2},{4,3},{5,4},{6,5},{7,6},{8,7},{9,8},{10,9... | collective-permute-start | bytes 3080 | tf_op jit(solution)/shard_map/ppermute | solution.py:20
  208.4 10.1 %collective-permute-start.67 = (f32[8,64]{1,0:T(8,128)S(1)}, f32[8,64]{1,0:T(8,128)S(1)}, u32[]{:S(2)}, u32[]{:S(2)}) collective-permute-start(f32[8,64]{1,0:T(8,128)S(1)} %get-tuple-element.65), channel_id=1, source_target_pairs={{0,1},{1,2},{2,3},{3,4},{4,5},{5,6},{6,7},{7,8},{8,9},{9,10},{10,1... | collective-permute-start | bytes 6152 | tf_op jit(solution)/shard_map/ppermute | solution.py:20
  208.4 10.1 %collective-permute-start.68 = (f32[8,64]{1,0:T(8,128)S(1)}, f32[8,64]{1,0:T(8,128)S(1)}, u32[]{:S(2)}, u32[]{:S(2)}) collective-permute-start(f32[8,64]{1,0:T(8,128)S(1)} %get-tuple-element.64), channel_id=1, source_target_pairs={{0,31},{1,0},{2,1},{3,2},{4,3},{5,4},{6,5},{7,6},{8,7},{9,8},{10,9... | collective-permute-start | bytes 6152 | tf_op jit(solution)/shard_map/ppermute | solution.py:20
  (63 other events, 387.2 us)

commit v4 on v3

--- a/solution.py
+++ b/solution.py
@@ -50,9 +50,14 @@
             for t in range(1, size)
         ]
         digit = (me >> shift) & (size - 1)
-        ordered = jnp.take(jnp.stack(got), jnp.arange(size) ^ digit, axis=0)
-        while ordered.shape[0] > 1:
-            ordered = ordered[0::2] + ordered[1::2]
+        ordered = []
+        for member in range(size):
+            pick = got[0]
+            for t in range(1, size):
+                pick = jnp.where((member ^ digit) == t, got[t], pick)
+            ordered.append(pick)
+        while len(ordered) > 1:
+            ordered = [ordered[k] + ordered[k + 1] for k in range(0, len(ordered), 2)]
         value = ordered[0]
         shift += bits
     return value
@@ -202,7 +207,6 @@
     stiff_x = images[:modes]
     mass_x = images[modes : 2 * modes]
     edge_diag = images[2 * modes]
-    images_ext = extend(images, send_edge_table)
     stiff_part = inner_elements(pair_values, stiff_pair)
     mass_part = inner_elements(pair_values, mass_pair)
     numerator, denominator = all_sum(
@@ -211,10 +215,8 @@
     quotient = numerator / denominator
     residual = stiff_x - quotient[:, None] * mass_x
 
-    def stiff_image(vectors, extended=None):
-        if extended is None:
-            extended = extend(vectors, send_edge_table)
-        values = edge_values(extended)
+    def stiff_image(vectors):
+        values = edge_values(extend(vectors, send_edge_table))
         return give_back(edge_sum(element_terms(stiff_elem, values)), send_edge_table)
 
     center = 0.5 * (interval_high + interval_low)
@@ -223,11 +225,9 @@
     rho_now = 1.0 / sigma
     step_dir = residual / (center * edge_diag)
     smooth = step_dir
-    residual_ext = images_ext[:modes] - quotient[:, None] * images_ext[modes : 2 * modes]
-    smooth_ext = residual_ext / (center * images_ext[2 * modes])
     for turn in range(CHEB_DEG - 1):
         rho_next = 1.0 / (2.0 * sigma - rho_now)
-        remain = residual - stiff_image(smooth, smooth_ext if turn == 0 else None)
+        remain = residual - stiff_image(smooth)
         step_dir = rho_next * rho_now * step_dir + 2.0 * rho_next / spread * remain / edge_diag
         smooth = smooth + step_dir
         rho_now = rho_next

time: 246 us -> 242 us (0.984)
  local copies, waits for them, and re-layouts: 12 us -> 8.56 us
  starting transfers between devices: 109 us -> 112 us
    gather x6 -> x0, local copies, waits for them, and re-layouts: 3.37 us -> none  [all_sum(): ordered = jnp.take(jnp.stack(got), jnp.arange(size) ^ digit, axis=0)]
  transfers between devices with their start and end apart: 79 -> 79, of which waited for: 32 -> 32; matrix products, arithmetic and copies ran while one was open for 3% -> 2% of each run, Pallas kernels for 0% -> 0%
where the time goes in v4:
time: 242 us
  starting transfers between devices  112 us (46%)
  waiting for transfers between devices  75.6 us (31%)
  matrix products  40.8 us (17%)
  local copies, waits for them, and re-layouts  8.56 us (4%)
  other arithmetic  3.83 us (2%)
    ppermute x65, starting transfers between devices, from_behind(): lax.ppermute(shard, axis, [(i, (i + by) % length) for i in range(length)])  99.1 us
    ppermute x65, waiting for transfers between devices, from_behind(): lax.ppermute(shard, axis, [(i, (i + by) % length) for i in range(length)])  60.6 us
    dot_general x14, matrix products, gather_cols(): picked = jnp.einsum('rab,nb->ran', split, lo_hot, precision=highest)  25.6 us
    ppermute x14, waiting for transfers between devices, all_sum(): lax.ppermute(value, 'dom', [(i, i ^ t << shift) for i in range(length)])  15 us
    dot_general x14, matrix products, scatter_cols(): summed = jnp.einsum('ran,nb->rab', spread, lo_hot, precision=highest)  13 us
    ppermute x14, starting transfers between devices, all_sum(): lax.ppermute(value, 'dom', [(i, i ^ t << shift) for i in range(length)])  12.5 us
  transfers between devices with their start and end apart: 79, of which 32 were waited for; matrix products, arithmetic and copies ran while one was open for 2% of the time, Pallas kernels for 0%

profile of v4, /device:TPU:0, one launch (start us, length us, event | category | flops | bytes accessed | tf_op | source)
XLA Modules:
  0.0 242.1 jit_solution(8622591851191162917)
XLA Ops:
  4.6 4.1 %collective-permute-start.4 = (f32[1,2112]{1,0:T(1,128)S(1)}, f32[1,2112]{1,0:T(1,128)S(1)}, u32[]{:S(2)}, u32[]{:S(2)}) collective-permute-start(f32[1,2112]{1,0:T(1,128)S(1)} %pad_maximum_fusion.4), channel_id=1, source_target_pairs={{0,16},{1,17},{2,18},{3,19},{4,20},{5,21},{6,22},{7,23},{8,24},{9,... | collective-permute-start | bytes 25352 | tf_op jit(solution)/shard_map/ppermute | solution.py:20
  9.0 5.4 %collective-permute-start.1 = (f32[1,1056]{1,0:T(1,128)S(1)}, f32[1,1056]{1,0:T(1,128)S(1)}, u32[]{:S(2)}, u32[]{:S(2)}) collective-permute-start(f32[1,1056]{1,0:T(1,128)S(1)} %pad_maximum_fusion.7), channel_id=1, source_target_pairs={{0,31},{1,0},{2,1},{3,2},{4,3},{5,4},{6,5},{7,6},{8,7},{9,8},{10,9... | collective-permute-start | bytes 12680 | tf_op jit(solution)/shard_map/ppermute | solution.py:20
  14.7 4.8 %collective-permute-start.3 = (f32[1,1056]{1,0:T(1,128)S(1)}, f32[1,1056]{1,0:T(1,128)S(1)}, u32[]{:S(2)}, u32[]{:S(2)}) collective-permute-start(f32[1,1056]{1,0:T(1,128)S(1)} %pad_maximum_fusion.9), channel_id=1, source_target_pairs={{0,28},{1,29},{2,30},{3,31},{4,0},{5,1},{6,2},{7,3},{8,4},{9,5},{1... | collective-permute-start | bytes 12680 | tf_op jit(solution)/shard_map/ppermute | solution.py:20
  21.5 4.3 %fusion.20 = f32[16,5120]{1,0:T(8,128)S(1)} fusion(f32[15,5120]{1,0:T(8,128)S(1)} %fusion.109, s32[5120]{0:T(1024)S(1)} %get-tuple-element.49, f32[16,1920]{1,0:T(8,128)S(1)} %concatenate.178), kind=kOutput, calls=%fused_computation.28 | convolution fusion | flops 1890467840 | bytes 778240 | tf_op jit(solution)/shard_map/rab,nb->ran/dot_general | solution.py:81
  35.6 4.6 %collective-permute-start.5 = (f32[17,64]{1,0:T(8,128)S(1)}, f32[17,64]{1,0:T(8,128)S(1)}, u32[]{:S(2)}, u32[]{:S(2)}) collective-permute-start(f32[17,64]{1,0:T(8,128)S(1)} %get-tuple-element.20), channel_id=1, source_target_pairs={{0,31},{1,0},{2,1},{3,2},{4,3},{5,4},{6,5},{7,6},{8,7},{9,8},{10,9... | collective-permute-start | bytes 13064 | tf_op jit(solution)/shard_map/ppermute | solution.py:20
  59.3 5.3 %collective-permute-start.18 = (f32[8,64]{1,0:T(8,128)S(1)}, f32[8,64]{1,0:T(8,128)S(1)}, u32[]{:S(2)}, u32[]{:S(2)}) collective-permute-start(f32[8,64]{1,0:T(8,128)S(1)} %get-tuple-element.70), channel_id=1, source_target_pairs={{0,31},{1,0},{2,1},{3,2},{4,3},{5,4},{6,5},{7,6},{8,7},{9,8},{10,9... | collective-permute-start | bytes 6152 | tf_op jit(solution)/shard_map/ppermute | solution.py:20
  64.7 4.7 %collective-permute-start.20 = (f32[8,64]{1,0:T(8,128)S(1)}, f32[8,64]{1,0:T(8,128)S(1)}, u32[]{:S(2)}, u32[]{:S(2)}) collective-permute-start(f32[8,64]{1,0:T(8,128)S(1)} %get-tuple-element.68), channel_id=1, source_target_pairs={{0,28},{1,29},{2,30},{3,31},{4,0},{5,1},{6,2},{7,3},{8,4},{9,5},{1... | collective-permute-start | bytes 6152 | tf_op jit(solution)/shard_map/ppermute | solution.py:20
  82.6 4.1 %collective-permute-done.23 = f32[8,64]{1,0:T(8,128)S(1)} collective-permute-done((f32[8,64]{1,0:T(8,128)S(1)}, f32[8,64]{1,0:T(8,128)S(1)}, u32[]{:S(2)}, u32[]{:S(2)}) %collective-permute-start.23) | collective-permute-done | bytes 2080 | tf_op jit(solution)/shard_map/ppermute | solution.py:20
  89.5 5.3 %collective-permute-start.28 = (f32[8,64]{1,0:T(8,128)S(1)}, f32[8,64]{1,0:T(8,128)S(1)}, u32[]{:S(2)}, u32[]{:S(2)}) collective-permute-start(f32[8,64]{1,0:T(8,128)S(1)} %get-tuple-element.66), channel_id=1, source_target_pairs={{0,31},{1,0},{2,1},{3,2},{4,3},{5,4},{6,5},{7,6},{8,7},{9,8},{10,9... | collective-permute-start | bytes 6152 | tf_op jit(solution)/shard_map/ppermute | solution.py:20
  94.8 4.7 %collective-permute-start.30 = (f32[8,64]{1,0:T(8,128)S(1)}, f32[8,64]{1,0:T(8,128)S(1)}, u32[]{:S(2)}, u32[]{:S(2)}) collective-permute-start(f32[8,64]{1,0:T(8,128)S(1)} %get-tuple-element.64), channel_id=1, source_target_pairs={{0,28},{1,29},{2,30},{3,31},{4,0},{5,1},{6,2},{7,3},{8,4},{9,5},{1... | collective-permute-start | bytes 6152 | tf_op jit(solution)/shard_map/ppermute | solution.py:20
  112.7 4.1 %collective-permute-done.33 = f32[8,64]{1,0:T(8,128)S(1)} collective-permute-done((f32[8,64]{1,0:T(8,128)S(1)}, f32[8,64]{1,0:T(8,128)S(1)}, u32[]{:S(2)}, u32[]{:S(2)}) %collective-permute-start.33) | collective-permute-done | bytes 2080 | tf_op jit(solution)/shard_map/ppermute | solution.py:20
  119.7 5.3 %collective-permute-start.38 = (f32[8,64]{1,0:T(8,128)S(1)}, f32[8,64]{1,0:T(8,128)S(1)}, u32[]{:S(2)}, u32[]{:S(2)}) collective-permute-start(f32[8,64]{1,0:T(8,128)S(1)} %get-tuple-element.62), channel_id=1, source_target_pairs={{0,31},{1,0},{2,1},{3,2},{4,3},{5,4},{6,5},{7,6},{8,7},{9,8},{10,9... | collective-permute-start | bytes 6152 | tf_op jit(solution)/shard_map/ppermute | solution.py:20
  125.0 4.7 %collective-permute-start.40 = (f32[8,64]{1,0:T(8,128)S(1)}, f32[8,64]{1,0:T(8,128)S(1)}, u32[]{:S(2)}, u32[]{:S(2)}) collective-permute-start(f32[8,64]{1,0:T(8,128)S(1)} %get-tuple-element.60), channel_id=1, source_target_pairs={{0,28},{1,29},{2,30},{3,31},{4,0},{5,1},{6,2},{7,3},{8,4},{9,5},{1... | collective-permute-start | bytes 6152 | tf_op jit(solution)/shard_map/ppermute | solution.py:20
  143.0 3.9 %collective-permute-done.43 = f32[8,64]{1,0:T(8,128)S(1)} collective-permute-done((f32[8,64]{1,0:T(8,128)S(1)}, f32[8,64]{1,0:T(8,128)S(1)}, u32[]{:S(2)}, u32[]{:S(2)}) %collective-permute-start.43) | collective-permute-done | bytes 2080 | tf_op jit(solution)/shard_map/ppermute | solution.py:20
  150.2 4.3 %collective-permute-start.47 = (f32[8,32]{1,0:T(8,128)S(1)}, f32[8,32]{1,0:T(8,128)S(1)}, u32[]{:S(2)}, u32[]{:S(2)}) collective-permute-start(f32[8,32]{1,0:T(8,128)S(1)} %get-tuple-element.48), channel_id=1, source_target_pairs={{0,31},{1,0},{2,1},{3,2},{4,3},{5,4},{6,5},{7,6},{8,7},{9,8},{10,9... | collective-permute-start | bytes 3080 | tf_op jit(solution)/shard_map/ppermute | solution.py:20
  156.6 4.6 %collective-permute-done.48 = f32[8,32]{1,0:T(8,128)S(1)} collective-permute-done((f32[8,32]{1,0:T(8,128)S(1)}, f32[8,32]{1,0:T(8,128)S(1)}, u32[]{:S(2)}, u32[]{:S(2)}) %collective-permute-start.48) | collective-permute-done | bytes 1056 | tf_op jit(solution)/shard_map/ppermute | solution.py:20
  161.9 6.3 %collective-permute-start.53 = (f32[8,32]{1,0:T(8,128)S(1)}, f32[8,32]{1,0:T(8,128)S(1)}, u32[]{:S(2)}, u32[]{:S(2)}) collective-permute-start(f32[8,32]{1,0:T(8,128)S(1)} %get-tuple-element.82), channel_id=1, source_target_pairs={{0,31},{1,0},{2,1},{3,2},{4,3},{5,4},{6,5},{7,6},{8,7},{9,8},{10,9... | collective-permute-start | bytes 3080 | tf_op jit(solution)/shard_map/ppermute | solution.py:20
  168.2 4.7 %collective-permute-start.55 = (f32[8,32]{1,0:T(8,128)S(1)}, f32[8,32]{1,0:T(8,128)S(1)}, u32[]{:S(2)}, u32[]{:S(2)}) collective-permute-start(f32[8,32]{1,0:T(8,128)S(1)} %get-tuple-element.80), channel_id=1, source_target_pairs={{0,28},{1,29},{2,30},{3,31},{4,0},{5,1},{6,2},{7,3},{8,4},{9,5},{1... | collective-permute-start | bytes 3080 | tf_op jit(solution)/shard_map/ppermute | solution.py:20
  182.8 4.1 %collective-permute-done.58 = f32[8,32]{1,0:T(8,128)S(1)} collective-permute-done((f32[8,32]{1,0:T(8,128)S(1)}, f32[8,32]{1,0:T(8,128)S(1)}, u32[]{:S(2)}, u32[]{:S(2)}) %collective-permute-start.58) | collective-permute-done | bytes 1056 | tf_op jit(solution)/shard_map/ppermute | solution.py:20
  189.6 5.3 %collective-permute-start.63 = (f32[8,32]{1,0:T(8,128)S(1)}, f32[8,32]{1,0:T(8,128)S(1)}, u32[]{:S(2)}, u32[]{:S(2)}) collective-permute-start(f32[8,32]{1,0:T(8,128)S(1)} %get-tuple-element.78), channel_id=1, source_target_pairs={{0,31},{1,0},{2,1},{3,2},{4,3},{5,4},{6,5},{7,6},{8,7},{9,8},{10,9... | collective-permute-start | bytes 3080 | tf_op jit(solution)/shard_map/ppermute | solution.py:20
  194.9 4.7 %collective-permute-start.65 = (f32[8,32]{1,0:T(8,128)S(1)}, f32[8,32]{1,0:T(8,128)S(1)}, u32[]{:S(2)}, u32[]{:S(2)}) collective-permute-start(f32[8,32]{1,0:T(8,128)S(1)} %get-tuple-element.76), channel_id=1, source_target_pairs={{0,28},{1,29},{2,30},{3,31},{4,0},{5,1},{6,2},{7,3},{8,4},{9,5},{1... | collective-permute-start | bytes 3080 | tf_op jit(solution)/shard_map/ppermute | solution.py:20
  206.9 5.3 %collective-permute-start.68 = (f32[8,64]{1,0:T(8,128)S(1)}, f32[8,64]{1,0:T(8,128)S(1)}, u32[]{:S(2)}, u32[]{:S(2)}) collective-permute-start(f32[8,64]{1,0:T(8,128)S(1)} %get-tuple-element.58), channel_id=1, source_target_pairs={{0,31},{1,0},{2,1},{3,2},{4,3},{5,4},{6,5},{7,6},{8,7},{9,8},{10,9... | collective-permute-start | bytes 6152 | tf_op jit(solution)/shard_map/ppermute | solution.py:20
  212.2 4.7 %collective-permute-start.70 = (f32[8,64]{1,0:T(8,128)S(1)}, f32[8,64]{1,0:T(8,128)S(1)}, u32[]{:S(2)}, u32[]{:S(2)}) collective-permute-start(f32[8,64]{1,0:T(8,128)S(1)} %get-tuple-element.56), channel_id=1, source_target_pairs={{0,28},{1,29},{2,30},{3,31},{4,0},{5,1},{6,2},{7,3},{8,4},{9,5},{1... | collective-permute-start | bytes 6152 | tf_op jit(solution)/shard_map/ppermute | solution.py:20
  237.4 4.1 %collective-permute-done.78 = f32[2,24,24]{2,1,0:T(8,128)S(1)} collective-permute-done((f32[2,24,24]{2,1,0:T(8,128)S(1)}, f32[2,24,24]{2,1,0:T(8,128)S(1)}, u32[]{:S(2)}, u32[]{:S(2)}) %collective-permute-start.78) | collective-permute-done | bytes 4640 | tf_op jit(solution)/shard_map/ppermute | solution.py:49
  (320 shorter events, 126.8 us)
Async XLA Ops:
  4.6 16.6 %collective-permute-start.4 = (f32[1,2112]{1,0:T(1,128)S(1)}, f32[1,2112]{1,0:T(1,128)S(1)}, u32[]{:S(2)}, u32[]{:S(2)}) collective-permute-start(f32[1,2112]{1,0:T(1,128)S(1)} %pad_maximum_fusion.4), channel_id=1, source_target_pairs={{0,16},{1,17},{2,18},{3,19},{4,20},{5,21},{6,22},{7,23},{8,24},{9,... | collective-permute-start | bytes 25352 | tf_op jit(solution)/shard_map/ppermute | solution.py:20
  8.9 10.9 %collective-permute-start = (f32[1,1056]{1,0:T(1,128)S(1)}, f32[1,1056]{1,0:T(1,128)S(1)}, u32[]{:S(2)}, u32[]{:S(2)}) collective-permute-start(f32[1,1056]{1,0:T(1,128)S(1)} %pad_maximum_fusion.6), channel_id=1, source_target_pairs={{0,1},{1,2},{2,3},{3,4},{4,5},{5,6},{6,7},{7,8},{8,9},{9,10},{10,1... | collective-permute-start | bytes 12680 | tf_op jit(solution)/shard_map/ppermute | solution.py:20
  9.0 10.8 %collective-permute-start.1 = (f32[1,1056]{1,0:T(1,128)S(1)}, f32[1,1056]{1,0:T(1,128)S(1)}, u32[]{:S(2)}, u32[]{:S(2)}) collective-permute-start(f32[1,1056]{1,0:T(1,128)S(1)} %pad_maximum_fusion.7), channel_id=1, source_target_pairs={{0,31},{1,0},{2,1},{3,2},{4,3},{5,4},{6,5},{7,6},{8,7},{9,8},{10,9... | collective-permute-start | bytes 12680 | tf_op jit(solution)/shard_map/ppermute | solution.py:20
  30.3 9.9 %collective-permute-start.10 = (f32[2,8]{1,0:T(2,128)S(1)}, f32[2,8]{1,0:T(2,128)S(1)}, u32[]{:S(2)}, u32[]{:S(2)}) collective-permute-start(f32[2,8]{1,0:T(2,128)S(1)} %pad_maximum_fusion.10), channel_id=1, source_target_pairs={{0,3},{1,2},{2,1},{3,0},{4,7},{5,6},{6,5},{7,4},{8,11},{9,10},{10,... | collective-permute-start | bytes 200 | tf_op jit(solution)/shard_map/ppermute | solution.py:49
  30.3 10.6 %collective-permute-start.11 = (f32[2,8]{1,0:T(2,128)S(1)}, f32[2,8]{1,0:T(2,128)S(1)}, u32[]{:S(2)}, u32[]{:S(2)}) collective-permute-start(f32[2,8]{1,0:T(2,128)S(1)} %pad_maximum_fusion.10), channel_id=1, source_target_pairs={{0,2},{1,3},{2,0},{3,1},{4,6},{5,7},{6,4},{7,5},{8,10},{9,11},{10,... | collective-permute-start | bytes 200 | tf_op jit(solution)/shard_map/ppermute | solution.py:49
  30.4 10.5 %collective-permute-start.12 = (f32[2,8]{1,0:T(2,128)S(1)}, f32[2,8]{1,0:T(2,128)S(1)}, u32[]{:S(2)}, u32[]{:S(2)}) collective-permute-start(f32[2,8]{1,0:T(2,128)S(1)} %pad_maximum_fusion.10), channel_id=1, source_target_pairs={{0,1},{1,0},{2,3},{3,2},{4,5},{5,4},{6,7},{7,6},{8,9},{9,8},{10,11... | collective-permute-start | bytes 200 | tf_op jit(solution)/shard_map/ppermute | solution.py:49
  35.6 18.1 %collective-permute-start.5 = (f32[17,64]{1,0:T(8,128)S(1)}, f32[17,64]{1,0:T(8,128)S(1)}, u32[]{:S(2)}, u32[]{:S(2)}) collective-permute-start(f32[17,64]{1,0:T(8,128)S(1)} %get-tuple-element.20), channel_id=1, source_target_pairs={{0,31},{1,0},{2,1},{3,2},{4,3},{5,4},{6,5},{7,6},{8,7},{9,8},{10,9... | collective-permute-start | bytes 13064 | tf_op jit(solution)/shard_map/ppermute | solution.py:20
  40.2 13.4 %collective-permute-start.6 = (f32[17,64]{1,0:T(8,128)S(1)}, f32[17,64]{1,0:T(8,128)S(1)}, u32[]{:S(2)}, u32[]{:S(2)}) collective-permute-start(f32[17,64]{1,0:T(8,128)S(1)} %get-tuple-element.19), channel_id=1, source_target_pairs={{0,1},{1,2},{2,3},{3,4},{4,5},{5,6},{6,7},{7,8},{8,9},{9,10},{10,1... | collective-permute-start | bytes 13064 | tf_op jit(solution)/shard_map/ppermute | solution.py:20
  40.2 13.4 %collective-permute-start.7 = (f32[17,64]{1,0:T(8,128)S(1)}, f32[17,64]{1,0:T(8,128)S(1)}, u32[]{:S(2)}, u32[]{:S(2)}) collective-permute-start(f32[17,64]{1,0:T(8,128)S(1)} %get-tuple-element.18), channel_id=1, source_target_pairs={{0,28},{1,29},{2,30},{3,31},{4,0},{5,1},{6,2},{7,3},{8,4},{9,5},{1... | collective-permute-start | bytes 13064 | tf_op jit(solution)/shard_map/ppermute | solution.py:20
  59.3 10.1 %collective-permute-start.17 = (f32[8,64]{1,0:T(8,128)S(1)}, f32[8,64]{1,0:T(8,128)S(1)}, u32[]{:S(2)}, u32[]{:S(2)}) collective-permute-start(f32[8,64]{1,0:T(8,128)S(1)} %get-tuple-element.71), channel_id=1, source_target_pairs={{0,1},{1,2},{2,3},{3,4},{4,5},{5,6},{6,7},{7,8},{8,9},{9,10},{10,1... | collective-permute-start | bytes 6152 | tf_op jit(solution)/shard_map/ppermute | solution.py:20
  59.3 10.1 %collective-permute-start.18 = (f32[8,64]{1,0:T(8,128)S(1)}, f32[8,64]{1,0:T(8,128)S(1)}, u32[]{:S(2)}, u32[]{:S(2)}) collective-permute-start(f32[8,64]{1,0:T(8,128)S(1)} %get-tuple-element.70), channel_id=1, source_target_pairs={{0,31},{1,0},{2,1},{3,2},{4,3},{5,4},{6,5},{7,6},{8,7},{9,8},{10,9... | collective-permute-start | bytes 6152 | tf_op jit(solution)/shard_map/ppermute | solution.py:20
  80.0 6.7 %collective-permute-start.23 = (f32[8,64]{1,0:T(8,128)S(1)}, f32[8,64]{1,0:T(8,128)S(1)}, u32[]{:S(2)}, u32[]{:S(2)}) collective-permute-start(f32[8,64]{1,0:T(8,128)S(1)} %get-tuple-element.31), channel_id=1, source_target_pairs={{0,1},{1,2},{2,3},{3,4},{4,5},{5,6},{6,7},{7,8},{8,9},{9,10},{10,1... | collective-permute-start | bytes 6152 | tf_op jit(solution)/shard_map/ppermute | solution.py:20
  89.5 10.2 %collective-permute-start.27 = (f32[8,64]{1,0:T(8,128)S(1)}, f32[8,64]{1,0:T(8,128)S(1)}, u32[]{:S(2)}, u32[]{:S(2)}) collective-permute-start(f32[8,64]{1,0:T(8,128)S(1)} %get-tuple-element.67), channel_id=1, source_target_pairs={{0,1},{1,2},{2,3},{3,4},{4,5},{5,6},{6,7},{7,8},{8,9},{9,10},{10,1... | collective-permute-start | bytes 6152 | tf_op jit(solution)/shard_map/ppermute | solution.py:20
  89.5 10.2 %collective-permute-start.28 = (f32[8,64]{1,0:T(8,128)S(1)}, f32[8,64]{1,0:T(8,128)S(1)}, u32[]{:S(2)}, u32[]{:S(2)}) collective-permute-start(f32[8,64]{1,0:T(8,128)S(1)} %get-tuple-element.66), channel_id=1, source_target_pairs={{0,31},{1,0},{2,1},{3,2},{4,3},{5,4},{6,5},{7,6},{8,7},{9,8},{10,9... | collective-permute-start | bytes 6152 | tf_op jit(solution)/shard_map/ppermute | solution.py:20
  110.1 6.7 %collective-permute-start.33 = (f32[8,64]{1,0:T(8,128)S(1)}, f32[8,64]{1,0:T(8,128)S(1)}, u32[]{:S(2)}, u32[]{:S(2)}) collective-permute-start(f32[8,64]{1,0:T(8,128)S(1)} %get-tuple-element.27), channel_id=1, source_target_pairs={{0,1},{1,2},{2,3},{3,4},{4,5},{5,6},{6,7},{7,8},{8,9},{9,10},{10,1... | collective-permute-start | bytes 6152 | tf_op jit(solution)/shard_map/ppermute | solution.py:20
  119.6 10.2 %collective-permute-start.37 = (f32[8,64]{1,0:T(8,128)S(1)}, f32[8,64]{1,0:T(8,128)S(1)}, u32[]{:S(2)}, u32[]{:S(2)}) collective-permute-start(f32[8,64]{1,0:T(8,128)S(1)} %get-tuple-element.63), channel_id=1, source_target_pairs={{0,1},{1,2},{2,3},{3,4},{4,5},{5,6},{6,7},{7,8},{8,9},{9,10},{10,1... | collective-permute-start | bytes 6152 | tf_op jit(solution)/shard_map/ppermute | solution.py:20
  119.7 10.2 %collective-permute-start.38 = (f32[8,64]{1,0:T(8,128)S(1)}, f32[8,64]{1,0:T(8,128)S(1)}, u32[]{:S(2)}, u32[]{:S(2)}) collective-permute-start(f32[8,64]{1,0:T(8,128)S(1)} %get-tuple-element.62), channel_id=1, source_target_pairs={{0,31},{1,0},{2,1},{3,2},{4,3},{5,4},{6,5},{7,6},{8,7},{9,8},{10,9... | collective-permute-start | bytes 6152 | tf_op jit(solution)/shard_map/ppermute | solution.py:20
  161.9 11.0 %collective-permute-start.52 = (f32[8,32]{1,0:T(8,128)S(1)}, f32[8,32]{1,0:T(8,128)S(1)}, u32[]{:S(2)}, u32[]{:S(2)}) collective-permute-start(f32[8,32]{1,0:T(8,128)S(1)} %get-tuple-element.83), channel_id=1, source_target_pairs={{0,1},{1,2},{2,3},{3,4},{4,5},{5,6},{6,7},{7,8},{8,9},{9,10},{10,1... | collective-permute-start | bytes 3080 | tf_op jit(solution)/shard_map/ppermute | solution.py:20
  161.9 11.0 %collective-permute-start.53 = (f32[8,32]{1,0:T(8,128)S(1)}, f32[8,32]{1,0:T(8,128)S(1)}, u32[]{:S(2)}, u32[]{:S(2)}) collective-permute-start(f32[8,32]{1,0:T(8,128)S(1)} %get-tuple-element.82), channel_id=1, source_target_pairs={{0,31},{1,0},{2,1},{3,2},{4,3},{5,4},{6,5},{7,6},{8,7},{9,8},{10,9... | collective-permute-start | bytes 3080 | tf_op jit(solution)/shard_map/ppermute | solution.py:20
  180.1 8.8 %collective-permute-start.61 = (f32[8,64]{1,0:T(8,128)S(1)}, f32[8,64]{1,0:T(8,128)S(1)}, u32[]{:S(2)}, u32[]{:S(2)}) collective-permute-start(f32[8,64]{1,0:T(8,128)S(1)} %concatenate.231), channel_id=1, source_target_pairs={{0,16},{1,17},{2,18},{3,19},{4,20},{5,21},{6,22},{7,23},{8,24},{9,... | collective-permute-start | bytes 6152 | tf_op jit(solution)/shard_map/ppermute | solution.py:20
  189.6 10.1 %collective-permute-start.62 = (f32[8,32]{1,0:T(8,128)S(1)}, f32[8,32]{1,0:T(8,128)S(1)}, u32[]{:S(2)}, u32[]{:S(2)}) collective-permute-start(f32[8,32]{1,0:T(8,128)S(1)} %get-tuple-element.79), channel_id=1, source_target_pairs={{0,1},{1,2},{2,3},{3,4},{4,5},{5,6},{6,7},{7,8},{8,9},{9,10},{10,1... | collective-permute-start | bytes 3080 | tf_op jit(solution)/shard_map/ppermute | solution.py:20
  189.6 10.1 %collective-permute-start.63 = (f32[8,32]{1,0:T(8,128)S(1)}, f32[8,32]{1,0:T(8,128)S(1)}, u32[]{:S(2)}, u32[]{:S(2)}) collective-permute-start(f32[8,32]{1,0:T(8,128)S(1)} %get-tuple-element.78), channel_id=1, source_target_pairs={{0,31},{1,0},{2,1},{3,2},{4,3},{5,4},{6,5},{7,6},{8,7},{9,8},{10,9... | collective-permute-start | bytes 3080 | tf_op jit(solution)/shard_map/ppermute | solution.py:20
  206.9 10.1 %collective-permute-start.67 = (f32[8,64]{1,0:T(8,128)S(1)}, f32[8,64]{1,0:T(8,128)S(1)}, u32[]{:S(2)}, u32[]{:S(2)}) collective-permute-start(f32[8,64]{1,0:T(8,128)S(1)} %get-tuple-element.59), channel_id=1, source_target_pairs={{0,1},{1,2},{2,3},{3,4},{4,5},{5,6},{6,7},{7,8},{8,9},{9,10},{10,1... | collective-permute-start | bytes 6152 | tf_op jit(solution)/shard_map/ppermute | solution.py:20
  206.9 10.1 %collective-permute-start.68 = (f32[8,64]{1,0:T(8,128)S(1)}, f32[8,64]{1,0:T(8,128)S(1)}, u32[]{:S(2)}, u32[]{:S(2)}) collective-permute-start(f32[8,64]{1,0:T(8,128)S(1)} %get-tuple-element.58), channel_id=1, source_target_pairs={{0,31},{1,0},{2,1},{3,2},{4,3},{5,4},{6,5},{7,6},{8,7},{9,8},{10,9... | collective-permute-start | bytes 6152 | tf_op jit(solution)/shard_map/ppermute | solution.py:20
  (63 other events, 391.5 us)

commit v5 on v4

--- a/solution.py
+++ b/solution.py
@@ -78,7 +78,7 @@
     rows = values.shape[0]
     padded = jnp.pad(values, ((0, 0), (0, groups * LANES - length)))
     split = padded.reshape(rows, groups, LANES)
-    picked = jnp.einsum("rab,nb->ran", split, lo_hot, precision=highest)
+    picked = jnp.einsum("rab,nb->ran", split, lo_hot, precision=lax.Precision.HIGH)
     return jnp.sum(picked * hi_mask[None], axis=1)
 
 
@@ -87,7 +87,7 @@
     groups = hi_mask.shape[0]
     rows = terms.shape[0]
     spread = terms[:, None, :] * hi_mask[None]
-    summed = jnp.einsum("ran,nb->rab", spread, lo_hot, precision=highest)
+    summed = jnp.einsum("ran,nb->rab", spread, lo_hot, precision=lax.Precision.HIGH)
     return summed.reshape(rows, groups * LANES)[:, :length]
 
 

time: 242 us -> 236 us (0.975)
  matrix products: 40.8 us -> 34.4 us
    dot_general x28, matrix products: 38.6 us -> 32.1 us  [the longest x14 22.6 us: gather_cols(): jnp.einsum('rab,nb->ran', split, lo_hot, precision=lax.Precision.HIGH)]
where the time goes in v5:
time: 236 us
  starting transfers between devices  112 us (47%)
  waiting for transfers between devices  75.6 us (32%)
  matrix products  34.4 us (15%)
  local copies, waits for them, and re-layouts  8.56 us (4%)
  other arithmetic  3.83 us (2%)
    ppermute x65, starting transfers between devices, from_behind(): lax.ppermute(shard, axis, [(i, (i + by) % length) for i in range(length)])  99.1 us
    ppermute x65, waiting for transfers between devices, from_behind(): lax.ppermute(shard, axis, [(i, (i + by) % length) for i in range(length)])  60.6 us
    dot_general x14, matrix products, gather_cols(): jnp.einsum('rab,nb->ran', split, lo_hot, precision=lax.Precision.HIGH)  22.6 us
    ppermute x14, waiting for transfers between devices, all_sum(): lax.ppermute(value, 'dom', [(i, i ^ t << shift) for i in range(length)])  15 us
    ppermute x14, starting transfers between devices, all_sum(): lax.ppermute(value, 'dom', [(i, i ^ t << shift) for i in range(length)])  12.5 us
    dot_general x14, matrix products, scatter_cols(): jnp.einsum('ran,nb->rab', spread, lo_hot, precision=lax.Precision.HIGH)  9.56 us
  transfers between devices with their start and end apart: 79, of which 32 were waited for; matrix products, arithmetic and copies ran while one was open for 2% of the time, Pallas kernels for 0%

profile of v5, /device:TPU:0, one launch (start us, length us, event | category | flops | bytes accessed | tf_op | source)
XLA Modules:
  0.0 235.7 jit_solution(17126229612699876224)
XLA Ops:
  4.5 4.1 %collective-permute-start.4 = (f32[1,2112]{1,0:T(1,128)S(1)}, f32[1,2112]{1,0:T(1,128)S(1)}, u32[]{:S(2)}, u32[]{:S(2)}) collective-permute-start(f32[1,2112]{1,0:T(1,128)S(1)} %pad_maximum_fusion.4), channel_id=1, source_target_pairs={{0,16},{1,17},{2,18},{3,19},{4,20},{5,21},{6,22},{7,23},{8,24},{9,... | collective-permute-start | bytes 25352 | tf_op jit(solution)/shard_map/ppermute | solution.py:20
  8.9 5.4 %collective-permute-start.1 = (f32[1,1056]{1,0:T(1,128)S(1)}, f32[1,1056]{1,0:T(1,128)S(1)}, u32[]{:S(2)}, u32[]{:S(2)}) collective-permute-start(f32[1,1056]{1,0:T(1,128)S(1)} %pad_maximum_fusion.7), channel_id=1, source_target_pairs={{0,31},{1,0},{2,1},{3,2},{4,3},{5,4},{6,5},{7,6},{8,7},{9,8},{10,9... | collective-permute-start | bytes 12680 | tf_op jit(solution)/shard_map/ppermute | solution.py:20
  14.5 4.8 %collective-permute-start.3 = (f32[1,1056]{1,0:T(1,128)S(1)}, f32[1,1056]{1,0:T(1,128)S(1)}, u32[]{:S(2)}, u32[]{:S(2)}) collective-permute-start(f32[1,1056]{1,0:T(1,128)S(1)} %pad_maximum_fusion.9), channel_id=1, source_target_pairs={{0,28},{1,29},{2,30},{3,31},{4,0},{5,1},{6,2},{7,3},{8,4},{9,5},{1... | collective-permute-start | bytes 12680 | tf_op jit(solution)/shard_map/ppermute | solution.py:20
  21.3 3.7 %fusion.20 = f32[16,5120]{1,0:T(8,128)S(1)} fusion(f32[15,5120]{1,0:T(8,128)S(1)} %fusion.109, s32[5120]{0:T(1024)S(1)} %get-tuple-element.49, f32[16,1920]{1,0:T(8,128)S(1)} %concatenate.178), kind=kOutput, calls=%fused_computation.28 | convolution fusion | flops 946749440 | bytes 778240 | tf_op jit(solution)/shard_map/rab,nb->ran/dot_general | solution.py:81
  33.4 4.6 %collective-permute-start.5 = (f32[17,64]{1,0:T(8,128)S(1)}, f32[17,64]{1,0:T(8,128)S(1)}, u32[]{:S(2)}, u32[]{:S(2)}) collective-permute-start(f32[17,64]{1,0:T(8,128)S(1)} %get-tuple-element.20), channel_id=1, source_target_pairs={{0,31},{1,0},{2,1},{3,2},{4,3},{5,4},{6,5},{7,6},{8,7},{9,8},{10,9... | collective-permute-start | bytes 13064 | tf_op jit(solution)/shard_map/ppermute | solution.py:20
  57.0 5.3 %collective-permute-start.18 = (f32[8,64]{1,0:T(8,128)S(1)}, f32[8,64]{1,0:T(8,128)S(1)}, u32[]{:S(2)}, u32[]{:S(2)}) collective-permute-start(f32[8,64]{1,0:T(8,128)S(1)} %get-tuple-element.70), channel_id=1, source_target_pairs={{0,31},{1,0},{2,1},{3,2},{4,3},{5,4},{6,5},{7,6},{8,7},{9,8},{10,9... | collective-permute-start | bytes 6152 | tf_op jit(solution)/shard_map/ppermute | solution.py:20
  62.4 4.7 %collective-permute-start.20 = (f32[8,64]{1,0:T(8,128)S(1)}, f32[8,64]{1,0:T(8,128)S(1)}, u32[]{:S(2)}, u32[]{:S(2)}) collective-permute-start(f32[8,64]{1,0:T(8,128)S(1)} %get-tuple-element.68), channel_id=1, source_target_pairs={{0,28},{1,29},{2,30},{3,31},{4,0},{5,1},{6,2},{7,3},{8,4},{9,5},{1... | collective-permute-start | bytes 6152 | tf_op jit(solution)/shard_map/ppermute | solution.py:20
  79.3 4.1 %collective-permute-done.23 = f32[8,64]{1,0:T(8,128)S(1)} collective-permute-done((f32[8,64]{1,0:T(8,128)S(1)}, f32[8,64]{1,0:T(8,128)S(1)}, u32[]{:S(2)}, u32[]{:S(2)}) %collective-permute-start.23) | collective-permute-done | bytes 2080 | tf_op jit(solution)/shard_map/ppermute | solution.py:20
  86.2 5.3 %collective-permute-start.28 = (f32[8,64]{1,0:T(8,128)S(1)}, f32[8,64]{1,0:T(8,128)S(1)}, u32[]{:S(2)}, u32[]{:S(2)}) collective-permute-start(f32[8,64]{1,0:T(8,128)S(1)} %get-tuple-element.66), channel_id=1, source_target_pairs={{0,31},{1,0},{2,1},{3,2},{4,3},{5,4},{6,5},{7,6},{8,7},{9,8},{10,9... | collective-permute-start | bytes 6152 | tf_op jit(solution)/shard_map/ppermute | solution.py:20
  91.5 4.7 %collective-permute-start.30 = (f32[8,64]{1,0:T(8,128)S(1)}, f32[8,64]{1,0:T(8,128)S(1)}, u32[]{:S(2)}, u32[]{:S(2)}) collective-permute-start(f32[8,64]{1,0:T(8,128)S(1)} %get-tuple-element.64), channel_id=1, source_target_pairs={{0,28},{1,29},{2,30},{3,31},{4,0},{5,1},{6,2},{7,3},{8,4},{9,5},{1... | collective-permute-start | bytes 6152 | tf_op jit(solution)/shard_map/ppermute | solution.py:20
  108.5 4.1 %collective-permute-done.33 = f32[8,64]{1,0:T(8,128)S(1)} collective-permute-done((f32[8,64]{1,0:T(8,128)S(1)}, f32[8,64]{1,0:T(8,128)S(1)}, u32[]{:S(2)}, u32[]{:S(2)}) %collective-permute-start.33) | collective-permute-done | bytes 2080 | tf_op jit(solution)/shard_map/ppermute | solution.py:20
  115.4 5.3 %collective-permute-start.38 = (f32[8,64]{1,0:T(8,128)S(1)}, f32[8,64]{1,0:T(8,128)S(1)}, u32[]{:S(2)}, u32[]{:S(2)}) collective-permute-start(f32[8,64]{1,0:T(8,128)S(1)} %get-tuple-element.62), channel_id=1, source_target_pairs={{0,31},{1,0},{2,1},{3,2},{4,3},{5,4},{6,5},{7,6},{8,7},{9,8},{10,9... | collective-permute-start | bytes 6152 | tf_op jit(solution)/shard_map/ppermute | solution.py:20
  120.7 4.7 %collective-permute-start.40 = (f32[8,64]{1,0:T(8,128)S(1)}, f32[8,64]{1,0:T(8,128)S(1)}, u32[]{:S(2)}, u32[]{:S(2)}) collective-permute-start(f32[8,64]{1,0:T(8,128)S(1)} %get-tuple-element.60), channel_id=1, source_target_pairs={{0,28},{1,29},{2,30},{3,31},{4,0},{5,1},{6,2},{7,3},{8,4},{9,5},{1... | collective-permute-start | bytes 6152 | tf_op jit(solution)/shard_map/ppermute | solution.py:20
  137.8 3.9 %collective-permute-done.43 = f32[8,64]{1,0:T(8,128)S(1)} collective-permute-done((f32[8,64]{1,0:T(8,128)S(1)}, f32[8,64]{1,0:T(8,128)S(1)}, u32[]{:S(2)}, u32[]{:S(2)}) %collective-permute-start.43) | collective-permute-done | bytes 2080 | tf_op jit(solution)/shard_map/ppermute | solution.py:20
  144.9 4.3 %collective-permute-start.47 = (f32[8,32]{1,0:T(8,128)S(1)}, f32[8,32]{1,0:T(8,128)S(1)}, u32[]{:S(2)}, u32[]{:S(2)}) collective-permute-start(f32[8,32]{1,0:T(8,128)S(1)} %get-tuple-element.48), channel_id=1, source_target_pairs={{0,31},{1,0},{2,1},{3,2},{4,3},{5,4},{6,5},{7,6},{8,7},{9,8},{10,9... | collective-permute-start | bytes 3080 | tf_op jit(solution)/shard_map/ppermute | solution.py:20
  151.3 4.6 %collective-permute-done.48 = f32[8,32]{1,0:T(8,128)S(1)} collective-permute-done((f32[8,32]{1,0:T(8,128)S(1)}, f32[8,32]{1,0:T(8,128)S(1)}, u32[]{:S(2)}, u32[]{:S(2)}) %collective-permute-start.48) | collective-permute-done | bytes 1056 | tf_op jit(solution)/shard_map/ppermute | solution.py:20
  156.5 6.3 %collective-permute-start.53 = (f32[8,32]{1,0:T(8,128)S(1)}, f32[8,32]{1,0:T(8,128)S(1)}, u32[]{:S(2)}, u32[]{:S(2)}) collective-permute-start(f32[8,32]{1,0:T(8,128)S(1)} %get-tuple-element.82), channel_id=1, source_target_pairs={{0,31},{1,0},{2,1},{3,2},{4,3},{5,4},{6,5},{7,6},{8,7},{9,8},{10,9... | collective-permute-start | bytes 3080 | tf_op jit(solution)/shard_map/ppermute | solution.py:20
  162.8 4.7 %collective-permute-start.55 = (f32[8,32]{1,0:T(8,128)S(1)}, f32[8,32]{1,0:T(8,128)S(1)}, u32[]{:S(2)}, u32[]{:S(2)}) collective-permute-start(f32[8,32]{1,0:T(8,128)S(1)} %get-tuple-element.80), channel_id=1, source_target_pairs={{0,28},{1,29},{2,30},{3,31},{4,0},{5,1},{6,2},{7,3},{8,4},{9,5},{1... | collective-permute-start | bytes 3080 | tf_op jit(solution)/shard_map/ppermute | solution.py:20
  177.1 4.1 %collective-permute-done.58 = f32[8,32]{1,0:T(8,128)S(1)} collective-permute-done((f32[8,32]{1,0:T(8,128)S(1)}, f32[8,32]{1,0:T(8,128)S(1)}, u32[]{:S(2)}, u32[]{:S(2)}) %collective-permute-start.58) | collective-permute-done | bytes 1056 | tf_op jit(solution)/shard_map/ppermute | solution.py:20
  183.8 5.3 %collective-permute-start.63 = (f32[8,32]{1,0:T(8,128)S(1)}, f32[8,32]{1,0:T(8,128)S(1)}, u32[]{:S(2)}, u32[]{:S(2)}) collective-permute-start(f32[8,32]{1,0:T(8,128)S(1)} %get-tuple-element.78), channel_id=1, source_target_pairs={{0,31},{1,0},{2,1},{3,2},{4,3},{5,4},{6,5},{7,6},{8,7},{9,8},{10,9... | collective-permute-start | bytes 3080 | tf_op jit(solution)/shard_map/ppermute | solution.py:20
  189.1 4.7 %collective-permute-start.65 = (f32[8,32]{1,0:T(8,128)S(1)}, f32[8,32]{1,0:T(8,128)S(1)}, u32[]{:S(2)}, u32[]{:S(2)}) collective-permute-start(f32[8,32]{1,0:T(8,128)S(1)} %get-tuple-element.76), channel_id=1, source_target_pairs={{0,28},{1,29},{2,30},{3,31},{4,0},{5,1},{6,2},{7,3},{8,4},{9,5},{1... | collective-permute-start | bytes 3080 | tf_op jit(solution)/shard_map/ppermute | solution.py:20
  200.8 5.3 %collective-permute-start.68 = (f32[8,64]{1,0:T(8,128)S(1)}, f32[8,64]{1,0:T(8,128)S(1)}, u32[]{:S(2)}, u32[]{:S(2)}) collective-permute-start(f32[8,64]{1,0:T(8,128)S(1)} %get-tuple-element.58), channel_id=1, source_target_pairs={{0,31},{1,0},{2,1},{3,2},{4,3},{5,4},{6,5},{7,6},{8,7},{9,8},{10,9... | collective-permute-start | bytes 6152 | tf_op jit(solution)/shard_map/ppermute | solution.py:20
  206.1 4.7 %collective-permute-start.70 = (f32[8,64]{1,0:T(8,128)S(1)}, f32[8,64]{1,0:T(8,128)S(1)}, u32[]{:S(2)}, u32[]{:S(2)}) collective-permute-start(f32[8,64]{1,0:T(8,128)S(1)} %get-tuple-element.56), channel_id=1, source_target_pairs={{0,28},{1,29},{2,30},{3,31},{4,0},{5,1},{6,2},{7,3},{8,4},{9,5},{1... | collective-permute-start | bytes 6152 | tf_op jit(solution)/shard_map/ppermute | solution.py:20
  231.0 4.1 %collective-permute-done.78 = f32[2,24,24]{2,1,0:T(8,128)S(1)} collective-permute-done((f32[2,24,24]{2,1,0:T(8,128)S(1)}, f32[2,24,24]{2,1,0:T(8,128)S(1)}, u32[]{:S(2)}, u32[]{:S(2)}) %collective-permute-start.78) | collective-permute-done | bytes 4640 | tf_op jit(solution)/shard_map/ppermute | solution.py:49
  (320 shorter events, 121.0 us)
Async XLA Ops:
  4.5 16.6 %collective-permute-start.4 = (f32[1,2112]{1,0:T(1,128)S(1)}, f32[1,2112]{1,0:T(1,128)S(1)}, u32[]{:S(2)}, u32[]{:S(2)}) collective-permute-start(f32[1,2112]{1,0:T(1,128)S(1)} %pad_maximum_fusion.4), channel_id=1, source_target_pairs={{0,16},{1,17},{2,18},{3,19},{4,20},{5,21},{6,22},{7,23},{8,24},{9,... | collective-permute-start | bytes 25352 | tf_op jit(solution)/shard_map/ppermute | solution.py:20
  8.8 10.9 %collective-permute-start = (f32[1,1056]{1,0:T(1,128)S(1)}, f32[1,1056]{1,0:T(1,128)S(1)}, u32[]{:S(2)}, u32[]{:S(2)}) collective-permute-start(f32[1,1056]{1,0:T(1,128)S(1)} %pad_maximum_fusion.6), channel_id=1, source_target_pairs={{0,1},{1,2},{2,3},{3,4},{4,5},{5,6},{6,7},{7,8},{8,9},{9,10},{10,1... | collective-permute-start | bytes 12680 | tf_op jit(solution)/shard_map/ppermute | solution.py:20
  8.9 10.8 %collective-permute-start.1 = (f32[1,1056]{1,0:T(1,128)S(1)}, f32[1,1056]{1,0:T(1,128)S(1)}, u32[]{:S(2)}, u32[]{:S(2)}) collective-permute-start(f32[1,1056]{1,0:T(1,128)S(1)} %pad_maximum_fusion.7), channel_id=1, source_target_pairs={{0,31},{1,0},{2,1},{3,2},{4,3},{5,4},{6,5},{7,6},{8,7},{9,8},{10,9... | collective-permute-start | bytes 12680 | tf_op jit(solution)/shard_map/ppermute | solution.py:20
  29.5 8.5 %collective-permute-start.10 = (f32[2,8]{1,0:T(2,128)S(1)}, f32[2,8]{1,0:T(2,128)S(1)}, u32[]{:S(2)}, u32[]{:S(2)}) collective-permute-start(f32[2,8]{1,0:T(2,128)S(1)} %pad_maximum_fusion.10), channel_id=1, source_target_pairs={{0,3},{1,2},{2,1},{3,0},{4,7},{5,6},{6,5},{7,4},{8,11},{9,10},{10,... | collective-permute-start | bytes 200 | tf_op jit(solution)/shard_map/ppermute | solution.py:49
  29.6 9.1 %collective-permute-start.11 = (f32[2,8]{1,0:T(2,128)S(1)}, f32[2,8]{1,0:T(2,128)S(1)}, u32[]{:S(2)}, u32[]{:S(2)}) collective-permute-start(f32[2,8]{1,0:T(2,128)S(1)} %pad_maximum_fusion.10), channel_id=1, source_target_pairs={{0,2},{1,3},{2,0},{3,1},{4,6},{5,7},{6,4},{7,5},{8,10},{9,11},{10,... | collective-permute-start | bytes 200 | tf_op jit(solution)/shard_map/ppermute | solution.py:49
  29.6 9.1 %collective-permute-start.12 = (f32[2,8]{1,0:T(2,128)S(1)}, f32[2,8]{1,0:T(2,128)S(1)}, u32[]{:S(2)}, u32[]{:S(2)}) collective-permute-start(f32[2,8]{1,0:T(2,128)S(1)} %pad_maximum_fusion.10), channel_id=1, source_target_pairs={{0,1},{1,0},{2,3},{3,2},{4,5},{5,4},{6,7},{7,6},{8,9},{9,8},{10,11... | collective-permute-start | bytes 200 | tf_op jit(solution)/shard_map/ppermute | solution.py:49
  33.4 18.1 %collective-permute-start.5 = (f32[17,64]{1,0:T(8,128)S(1)}, f32[17,64]{1,0:T(8,128)S(1)}, u32[]{:S(2)}, u32[]{:S(2)}) collective-permute-start(f32[17,64]{1,0:T(8,128)S(1)} %get-tuple-element.20), channel_id=1, source_target_pairs={{0,31},{1,0},{2,1},{3,2},{4,3},{5,4},{6,5},{7,6},{8,7},{9,8},{10,9... | collective-permute-start | bytes 13064 | tf_op jit(solution)/shard_map/ppermute | solution.py:20
  38.0 13.4 %collective-permute-start.6 = (f32[17,64]{1,0:T(8,128)S(1)}, f32[17,64]{1,0:T(8,128)S(1)}, u32[]{:S(2)}, u32[]{:S(2)}) collective-permute-start(f32[17,64]{1,0:T(8,128)S(1)} %get-tuple-element.19), channel_id=1, source_target_pairs={{0,1},{1,2},{2,3},{3,4},{4,5},{5,6},{6,7},{7,8},{8,9},{9,10},{10,1... | collective-permute-start | bytes 13064 | tf_op jit(solution)/shard_map/ppermute | solution.py:20
  38.0 13.4 %collective-permute-start.7 = (f32[17,64]{1,0:T(8,128)S(1)}, f32[17,64]{1,0:T(8,128)S(1)}, u32[]{:S(2)}, u32[]{:S(2)}) collective-permute-start(f32[17,64]{1,0:T(8,128)S(1)} %get-tuple-element.18), channel_id=1, source_target_pairs={{0,28},{1,29},{2,30},{3,31},{4,0},{5,1},{6,2},{7,3},{8,4},{9,5},{1... | collective-permute-start | bytes 13064 | tf_op jit(solution)/shard_map/ppermute | solution.py:20
  57.0 10.1 %collective-permute-start.17 = (f32[8,64]{1,0:T(8,128)S(1)}, f32[8,64]{1,0:T(8,128)S(1)}, u32[]{:S(2)}, u32[]{:S(2)}) collective-permute-start(f32[8,64]{1,0:T(8,128)S(1)} %get-tuple-element.71), channel_id=1, source_target_pairs={{0,1},{1,2},{2,3},{3,4},{4,5},{5,6},{6,7},{7,8},{8,9},{9,10},{10,1... | collective-permute-start | bytes 6152 | tf_op jit(solution)/shard_map/ppermute | solution.py:20
  57.0 10.1 %collective-permute-start.18 = (f32[8,64]{1,0:T(8,128)S(1)}, f32[8,64]{1,0:T(8,128)S(1)}, u32[]{:S(2)}, u32[]{:S(2)}) collective-permute-start(f32[8,64]{1,0:T(8,128)S(1)} %get-tuple-element.70), channel_id=1, source_target_pairs={{0,31},{1,0},{2,1},{3,2},{4,3},{5,4},{6,5},{7,6},{8,7},{9,8},{10,9... | collective-permute-start | bytes 6152 | tf_op jit(solution)/shard_map/ppermute | solution.py:20
  76.7 6.7 %collective-permute-start.23 = (f32[8,64]{1,0:T(8,128)S(1)}, f32[8,64]{1,0:T(8,128)S(1)}, u32[]{:S(2)}, u32[]{:S(2)}) collective-permute-start(f32[8,64]{1,0:T(8,128)S(1)} %get-tuple-element.31), channel_id=1, source_target_pairs={{0,1},{1,2},{2,3},{3,4},{4,5},{5,6},{6,7},{7,8},{8,9},{9,10},{10,1... | collective-permute-start | bytes 6152 | tf_op jit(solution)/shard_map/ppermute | solution.py:20
  86.2 10.2 %collective-permute-start.27 = (f32[8,64]{1,0:T(8,128)S(1)}, f32[8,64]{1,0:T(8,128)S(1)}, u32[]{:S(2)}, u32[]{:S(2)}) collective-permute-start(f32[8,64]{1,0:T(8,128)S(1)} %get-tuple-element.67), channel_id=1, source_target_pairs={{0,1},{1,2},{2,3},{3,4},{4,5},{5,6},{6,7},{7,8},{8,9},{9,10},{10,1... | collective-permute-start | bytes 6152 | tf_op jit(solution)/shard_map/ppermute | solution.py:20
  86.2 10.2 %collective-permute-start.28 = (f32[8,64]{1,0:T(8,128)S(1)}, f32[8,64]{1,0:T(8,128)S(1)}, u32[]{:S(2)}, u32[]{:S(2)}) collective-permute-start(f32[8,64]{1,0:T(8,128)S(1)} %get-tuple-element.66), channel_id=1, source_target_pairs={{0,31},{1,0},{2,1},{3,2},{4,3},{5,4},{6,5},{7,6},{8,7},{9,8},{10,9... | collective-permute-start | bytes 6152 | tf_op jit(solution)/shard_map/ppermute | solution.py:20
  105.9 6.7 %collective-permute-start.33 = (f32[8,64]{1,0:T(8,128)S(1)}, f32[8,64]{1,0:T(8,128)S(1)}, u32[]{:S(2)}, u32[]{:S(2)}) collective-permute-start(f32[8,64]{1,0:T(8,128)S(1)} %get-tuple-element.27), channel_id=1, source_target_pairs={{0,1},{1,2},{2,3},{3,4},{4,5},{5,6},{6,7},{7,8},{8,9},{9,10},{10,1... | collective-permute-start | bytes 6152 | tf_op jit(solution)/shard_map/ppermute | solution.py:20
  115.4 10.2 %collective-permute-start.37 = (f32[8,64]{1,0:T(8,128)S(1)}, f32[8,64]{1,0:T(8,128)S(1)}, u32[]{:S(2)}, u32[]{:S(2)}) collective-permute-start(f32[8,64]{1,0:T(8,128)S(1)} %get-tuple-element.63), channel_id=1, source_target_pairs={{0,1},{1,2},{2,3},{3,4},{4,5},{5,6},{6,7},{7,8},{8,9},{9,10},{10,1... | collective-permute-start | bytes 6152 | tf_op jit(solution)/shard_map/ppermute | solution.py:20
  115.4 10.2 %collective-permute-start.38 = (f32[8,64]{1,0:T(8,128)S(1)}, f32[8,64]{1,0:T(8,128)S(1)}, u32[]{:S(2)}, u32[]{:S(2)}) collective-permute-start(f32[8,64]{1,0:T(8,128)S(1)} %get-tuple-element.62), channel_id=1, source_target_pairs={{0,31},{1,0},{2,1},{3,2},{4,3},{5,4},{6,5},{7,6},{8,7},{9,8},{10,9... | collective-permute-start | bytes 6152 | tf_op jit(solution)/shard_map/ppermute | solution.py:20
  156.5 11.0 %collective-permute-start.52 = (f32[8,32]{1,0:T(8,128)S(1)}, f32[8,32]{1,0:T(8,128)S(1)}, u32[]{:S(2)}, u32[]{:S(2)}) collective-permute-start(f32[8,32]{1,0:T(8,128)S(1)} %get-tuple-element.83), channel_id=1, source_target_pairs={{0,1},{1,2},{2,3},{3,4},{4,5},{5,6},{6,7},{7,8},{8,9},{9,10},{10,1... | collective-permute-start | bytes 3080 | tf_op jit(solution)/shard_map/ppermute | solution.py:20
  156.5 11.0 %collective-permute-start.53 = (f32[8,32]{1,0:T(8,128)S(1)}, f32[8,32]{1,0:T(8,128)S(1)}, u32[]{:S(2)}, u32[]{:S(2)}) collective-permute-start(f32[8,32]{1,0:T(8,128)S(1)} %get-tuple-element.82), channel_id=1, source_target_pairs={{0,31},{1,0},{2,1},{3,2},{4,3},{5,4},{6,5},{7,6},{8,7},{9,8},{10,9... | collective-permute-start | bytes 3080 | tf_op jit(solution)/shard_map/ppermute | solution.py:20
  174.4 8.8 %collective-permute-start.61 = (f32[8,64]{1,0:T(8,128)S(1)}, f32[8,64]{1,0:T(8,128)S(1)}, u32[]{:S(2)}, u32[]{:S(2)}) collective-permute-start(f32[8,64]{1,0:T(8,128)S(1)} %concatenate.231), channel_id=1, source_target_pairs={{0,16},{1,17},{2,18},{3,19},{4,20},{5,21},{6,22},{7,23},{8,24},{9,... | collective-permute-start | bytes 6152 | tf_op jit(solution)/shard_map/ppermute | solution.py:20
  183.8 10.1 %collective-permute-start.62 = (f32[8,32]{1,0:T(8,128)S(1)}, f32[8,32]{1,0:T(8,128)S(1)}, u32[]{:S(2)}, u32[]{:S(2)}) collective-permute-start(f32[8,32]{1,0:T(8,128)S(1)} %get-tuple-element.79), channel_id=1, source_target_pairs={{0,1},{1,2},{2,3},{3,4},{4,5},{5,6},{6,7},{7,8},{8,9},{9,10},{10,1... | collective-permute-start | bytes 3080 | tf_op jit(solution)/shard_map/ppermute | solution.py:20
  183.8 10.1 %collective-permute-start.63 = (f32[8,32]{1,0:T(8,128)S(1)}, f32[8,32]{1,0:T(8,128)S(1)}, u32[]{:S(2)}, u32[]{:S(2)}) collective-permute-start(f32[8,32]{1,0:T(8,128)S(1)} %get-tuple-element.78), channel_id=1, source_target_pairs={{0,31},{1,0},{2,1},{3,2},{4,3},{5,4},{6,5},{7,6},{8,7},{9,8},{10,9... | collective-permute-start | bytes 3080 | tf_op jit(solution)/shard_map/ppermute | solution.py:20
  200.8 10.1 %collective-permute-start.67 = (f32[8,64]{1,0:T(8,128)S(1)}, f32[8,64]{1,0:T(8,128)S(1)}, u32[]{:S(2)}, u32[]{:S(2)}) collective-permute-start(f32[8,64]{1,0:T(8,128)S(1)} %get-tuple-element.59), channel_id=1, source_target_pairs={{0,1},{1,2},{2,3},{3,4},{4,5},{5,6},{6,7},{7,8},{8,9},{9,10},{10,1... | collective-permute-start | bytes 6152 | tf_op jit(solution)/shard_map/ppermute | solution.py:20
  200.8 10.1 %collective-permute-start.68 = (f32[8,64]{1,0:T(8,128)S(1)}, f32[8,64]{1,0:T(8,128)S(1)}, u32[]{:S(2)}, u32[]{:S(2)}) collective-permute-start(f32[8,64]{1,0:T(8,128)S(1)} %get-tuple-element.58), channel_id=1, source_target_pairs={{0,31},{1,0},{2,1},{3,2},{4,3},{5,4},{6,5},{7,6},{8,7},{9,8},{10,9... | collective-permute-start | bytes 6152 | tf_op jit(solution)/shard_map/ppermute | solution.py:20
  (63 other events, 390.6 us)

commit v6 on v5

--- a/solution.py
+++ b/solution.py
@@ -87,7 +87,7 @@
     groups = hi_mask.shape[0]
     rows = terms.shape[0]
     spread = terms[:, None, :] * hi_mask[None]
-    summed = jnp.einsum("ran,nb->rab", spread, lo_hot, precision=lax.Precision.HIGH)
+    summed = jnp.einsum("ran,nb->rab", spread, lo_hot, precision=highest)
     return summed.reshape(rows, groups * LANES)[:, :length]
 
 

time: 236 us -> 239 us (1.013)
  matrix products: 34.4 us -> 37.8 us
    dot_general x14, matrix products: 9.56 us -> 13 us  [scatter_cols(): summed = jnp.einsum('ran,nb->rab', spread, lo_hot, precision=highest)]
where the time goes in v6:
time: 239 us
  starting transfers between devices  112 us (47%)
  waiting for transfers between devices  75.6 us (32%)
  matrix products  37.8 us (16%)
  local copies, waits for them, and re-layouts  8.56 us (4%)
  other arithmetic  3.83 us (2%)
    ppermute x65, starting transfers between devices, from_behind(): lax.ppermute(shard, axis, [(i, (i + by) % length) for i in range(length)])  99.1 us
    ppermute x65, waiting for transfers between devices, from_behind(): lax.ppermute(shard, axis, [(i, (i + by) % length) for i in range(length)])  60.6 us
    dot_general x14, matrix products, gather_cols(): jnp.einsum('rab,nb->ran', split, lo_hot, precision=lax.Precision.HIGH)  22.6 us
    ppermute x14, waiting for transfers between devices, all_sum(): lax.ppermute(value, 'dom', [(i, i ^ t << shift) for i in range(length)])  15 us
    dot_general x14, matrix products, scatter_cols(): summed = jnp.einsum('ran,nb->rab', spread, lo_hot, precision=highest)  13 us
    ppermute x14, starting transfers between devices, all_sum(): lax.ppermute(value, 'dom', [(i, i ^ t << shift) for i in range(length)])  12.5 us
  transfers between devices with their start and end apart: 79, of which 32 were waited for; matrix products, arithmetic and copies ran while one was open for 2% of the time, Pallas kernels for 0%

profile of v6, /device:TPU:0, one launch (start us, length us, event | category | flops | bytes accessed | tf_op | source)
XLA Modules:
  0.0 239.1 jit_solution(910863010368062007)
XLA Ops:
  4.6 4.1 %collective-permute-start.4 = (f32[1,2112]{1,0:T(1,128)S(1)}, f32[1,2112]{1,0:T(1,128)S(1)}, u32[]{:S(2)}, u32[]{:S(2)}) collective-permute-start(f32[1,2112]{1,0:T(1,128)S(1)} %pad_maximum_fusion.4), channel_id=1, source_target_pairs={{0,16},{1,17},{2,18},{3,19},{4,20},{5,21},{6,22},{7,23},{8,24},{9,... | collective-permute-start | bytes 25352 | tf_op jit(solution)/shard_map/ppermute | solution.py:20
  9.0 5.4 %collective-permute-start.1 = (f32[1,1056]{1,0:T(1,128)S(1)}, f32[1,1056]{1,0:T(1,128)S(1)}, u32[]{:S(2)}, u32[]{:S(2)}) collective-permute-start(f32[1,1056]{1,0:T(1,128)S(1)} %pad_maximum_fusion.7), channel_id=1, source_target_pairs={{0,31},{1,0},{2,1},{3,2},{4,3},{5,4},{6,5},{7,6},{8,7},{9,8},{10,9... | collective-permute-start | bytes 12680 | tf_op jit(solution)/shard_map/ppermute | solution.py:20
  14.6 4.8 %collective-permute-start.3 = (f32[1,1056]{1,0:T(1,128)S(1)}, f32[1,1056]{1,0:T(1,128)S(1)}, u32[]{:S(2)}, u32[]{:S(2)}) collective-permute-start(f32[1,1056]{1,0:T(1,128)S(1)} %pad_maximum_fusion.9), channel_id=1, source_target_pairs={{0,28},{1,29},{2,30},{3,31},{4,0},{5,1},{6,2},{7,3},{8,4},{9,5},{1... | collective-permute-start | bytes 12680 | tf_op jit(solution)/shard_map/ppermute | solution.py:20
  21.4 3.7 %fusion.20 = f32[16,5120]{1,0:T(8,128)S(1)} fusion(f32[15,5120]{1,0:T(8,128)S(1)} %fusion.109, s32[5120]{0:T(1024)S(1)} %get-tuple-element.49, f32[16,1920]{1,0:T(8,128)S(1)} %concatenate.178), kind=kOutput, calls=%fused_computation.28 | convolution fusion | flops 946749440 | bytes 778240 | tf_op jit(solution)/shard_map/rab,nb->ran/dot_general | solution.py:81
  34.9 4.6 %collective-permute-start.5 = (f32[17,64]{1,0:T(8,128)S(1)}, f32[17,64]{1,0:T(8,128)S(1)}, u32[]{:S(2)}, u32[]{:S(2)}) collective-permute-start(f32[17,64]{1,0:T(8,128)S(1)} %get-tuple-element.20), channel_id=1, source_target_pairs={{0,31},{1,0},{2,1},{3,2},{4,3},{5,4},{6,5},{7,6},{8,7},{9,8},{10,9... | collective-permute-start | bytes 13064 | tf_op jit(solution)/shard_map/ppermute | solution.py:20
  58.6 5.3 %collective-permute-start.18 = (f32[8,64]{1,0:T(8,128)S(1)}, f32[8,64]{1,0:T(8,128)S(1)}, u32[]{:S(2)}, u32[]{:S(2)}) collective-permute-start(f32[8,64]{1,0:T(8,128)S(1)} %get-tuple-element.70), channel_id=1, source_target_pairs={{0,31},{1,0},{2,1},{3,2},{4,3},{5,4},{6,5},{7,6},{8,7},{9,8},{10,9... | collective-permute-start | bytes 6152 | tf_op jit(solution)/shard_map/ppermute | solution.py:20
  63.9 4.7 %collective-permute-start.20 = (f32[8,64]{1,0:T(8,128)S(1)}, f32[8,64]{1,0:T(8,128)S(1)}, u32[]{:S(2)}, u32[]{:S(2)}) collective-permute-start(f32[8,64]{1,0:T(8,128)S(1)} %get-tuple-element.68), channel_id=1, source_target_pairs={{0,28},{1,29},{2,30},{3,31},{4,0},{5,1},{6,2},{7,3},{8,4},{9,5},{1... | collective-permute-start | bytes 6152 | tf_op jit(solution)/shard_map/ppermute | solution.py:20
  81.4 4.1 %collective-permute-done.23 = f32[8,64]{1,0:T(8,128)S(1)} collective-permute-done((f32[8,64]{1,0:T(8,128)S(1)}, f32[8,64]{1,0:T(8,128)S(1)}, u32[]{:S(2)}, u32[]{:S(2)}) %collective-permute-start.23) | collective-permute-done | bytes 2080 | tf_op jit(solution)/shard_map/ppermute | solution.py:20
  88.3 5.3 %collective-permute-start.28 = (f32[8,64]{1,0:T(8,128)S(1)}, f32[8,64]{1,0:T(8,128)S(1)}, u32[]{:S(2)}, u32[]{:S(2)}) collective-permute-start(f32[8,64]{1,0:T(8,128)S(1)} %get-tuple-element.66), channel_id=1, source_target_pairs={{0,31},{1,0},{2,1},{3,2},{4,3},{5,4},{6,5},{7,6},{8,7},{9,8},{10,9... | collective-permute-start | bytes 6152 | tf_op jit(solution)/shard_map/ppermute | solution.py:20
  93.6 4.7 %collective-permute-start.30 = (f32[8,64]{1,0:T(8,128)S(1)}, f32[8,64]{1,0:T(8,128)S(1)}, u32[]{:S(2)}, u32[]{:S(2)}) collective-permute-start(f32[8,64]{1,0:T(8,128)S(1)} %get-tuple-element.64), channel_id=1, source_target_pairs={{0,28},{1,29},{2,30},{3,31},{4,0},{5,1},{6,2},{7,3},{8,4},{9,5},{1... | collective-permute-start | bytes 6152 | tf_op jit(solution)/shard_map/ppermute | solution.py:20
  111.1 4.1 %collective-permute-done.33 = f32[8,64]{1,0:T(8,128)S(1)} collective-permute-done((f32[8,64]{1,0:T(8,128)S(1)}, f32[8,64]{1,0:T(8,128)S(1)}, u32[]{:S(2)}, u32[]{:S(2)}) %collective-permute-start.33) | collective-permute-done | bytes 2080 | tf_op jit(solution)/shard_map/ppermute | solution.py:20
  118.0 5.3 %collective-permute-start.38 = (f32[8,64]{1,0:T(8,128)S(1)}, f32[8,64]{1,0:T(8,128)S(1)}, u32[]{:S(2)}, u32[]{:S(2)}) collective-permute-start(f32[8,64]{1,0:T(8,128)S(1)} %get-tuple-element.62), channel_id=1, source_target_pairs={{0,31},{1,0},{2,1},{3,2},{4,3},{5,4},{6,5},{7,6},{8,7},{9,8},{10,9... | collective-permute-start | bytes 6152 | tf_op jit(solution)/shard_map/ppermute | solution.py:20
  123.4 4.7 %collective-permute-start.40 = (f32[8,64]{1,0:T(8,128)S(1)}, f32[8,64]{1,0:T(8,128)S(1)}, u32[]{:S(2)}, u32[]{:S(2)}) collective-permute-start(f32[8,64]{1,0:T(8,128)S(1)} %get-tuple-element.60), channel_id=1, source_target_pairs={{0,28},{1,29},{2,30},{3,31},{4,0},{5,1},{6,2},{7,3},{8,4},{9,5},{1... | collective-permute-start | bytes 6152 | tf_op jit(solution)/shard_map/ppermute | solution.py:20
  141.0 3.9 %collective-permute-done.43 = f32[8,64]{1,0:T(8,128)S(1)} collective-permute-done((f32[8,64]{1,0:T(8,128)S(1)}, f32[8,64]{1,0:T(8,128)S(1)}, u32[]{:S(2)}, u32[]{:S(2)}) %collective-permute-start.43) | collective-permute-done | bytes 2080 | tf_op jit(solution)/shard_map/ppermute | solution.py:20
  148.2 4.3 %collective-permute-start.47 = (f32[8,32]{1,0:T(8,128)S(1)}, f32[8,32]{1,0:T(8,128)S(1)}, u32[]{:S(2)}, u32[]{:S(2)}) collective-permute-start(f32[8,32]{1,0:T(8,128)S(1)} %get-tuple-element.48), channel_id=1, source_target_pairs={{0,31},{1,0},{2,1},{3,2},{4,3},{5,4},{6,5},{7,6},{8,7},{9,8},{10,9... | collective-permute-start | bytes 3080 | tf_op jit(solution)/shard_map/ppermute | solution.py:20
  154.6 4.6 %collective-permute-done.48 = f32[8,32]{1,0:T(8,128)S(1)} collective-permute-done((f32[8,32]{1,0:T(8,128)S(1)}, f32[8,32]{1,0:T(8,128)S(1)}, u32[]{:S(2)}, u32[]{:S(2)}) %collective-permute-start.48) | collective-permute-done | bytes 1056 | tf_op jit(solution)/shard_map/ppermute | solution.py:20
  159.8 6.3 %collective-permute-start.53 = (f32[8,32]{1,0:T(8,128)S(1)}, f32[8,32]{1,0:T(8,128)S(1)}, u32[]{:S(2)}, u32[]{:S(2)}) collective-permute-start(f32[8,32]{1,0:T(8,128)S(1)} %get-tuple-element.82), channel_id=1, source_target_pairs={{0,31},{1,0},{2,1},{3,2},{4,3},{5,4},{6,5},{7,6},{8,7},{9,8},{10,9... | collective-permute-start | bytes 3080 | tf_op jit(solution)/shard_map/ppermute | solution.py:20
  166.1 4.7 %collective-permute-start.55 = (f32[8,32]{1,0:T(8,128)S(1)}, f32[8,32]{1,0:T(8,128)S(1)}, u32[]{:S(2)}, u32[]{:S(2)}) collective-permute-start(f32[8,32]{1,0:T(8,128)S(1)} %get-tuple-element.80), channel_id=1, source_target_pairs={{0,28},{1,29},{2,30},{3,31},{4,0},{5,1},{6,2},{7,3},{8,4},{9,5},{1... | collective-permute-start | bytes 3080 | tf_op jit(solution)/shard_map/ppermute | solution.py:20
  180.5 4.1 %collective-permute-done.58 = f32[8,32]{1,0:T(8,128)S(1)} collective-permute-done((f32[8,32]{1,0:T(8,128)S(1)}, f32[8,32]{1,0:T(8,128)S(1)}, u32[]{:S(2)}, u32[]{:S(2)}) %collective-permute-start.58) | collective-permute-done | bytes 1056 | tf_op jit(solution)/shard_map/ppermute | solution.py:20
  187.3 5.3 %collective-permute-start.63 = (f32[8,32]{1,0:T(8,128)S(1)}, f32[8,32]{1,0:T(8,128)S(1)}, u32[]{:S(2)}, u32[]{:S(2)}) collective-permute-start(f32[8,32]{1,0:T(8,128)S(1)} %get-tuple-element.78), channel_id=1, source_target_pairs={{0,31},{1,0},{2,1},{3,2},{4,3},{5,4},{6,5},{7,6},{8,7},{9,8},{10,9... | collective-permute-start | bytes 3080 | tf_op jit(solution)/shard_map/ppermute | solution.py:20
  192.6 4.7 %collective-permute-start.65 = (f32[8,32]{1,0:T(8,128)S(1)}, f32[8,32]{1,0:T(8,128)S(1)}, u32[]{:S(2)}, u32[]{:S(2)}) collective-permute-start(f32[8,32]{1,0:T(8,128)S(1)} %get-tuple-element.76), channel_id=1, source_target_pairs={{0,28},{1,29},{2,30},{3,31},{4,0},{5,1},{6,2},{7,3},{8,4},{9,5},{1... | collective-permute-start | bytes 3080 | tf_op jit(solution)/shard_map/ppermute | solution.py:20
  204.3 5.3 %collective-permute-start.68 = (f32[8,64]{1,0:T(8,128)S(1)}, f32[8,64]{1,0:T(8,128)S(1)}, u32[]{:S(2)}, u32[]{:S(2)}) collective-permute-start(f32[8,64]{1,0:T(8,128)S(1)} %get-tuple-element.58), channel_id=1, source_target_pairs={{0,31},{1,0},{2,1},{3,2},{4,3},{5,4},{6,5},{7,6},{8,7},{9,8},{10,9... | collective-permute-start | bytes 6152 | tf_op jit(solution)/shard_map/ppermute | solution.py:20
  209.6 4.7 %collective-permute-start.70 = (f32[8,64]{1,0:T(8,128)S(1)}, f32[8,64]{1,0:T(8,128)S(1)}, u32[]{:S(2)}, u32[]{:S(2)}) collective-permute-start(f32[8,64]{1,0:T(8,128)S(1)} %get-tuple-element.56), channel_id=1, source_target_pairs={{0,28},{1,29},{2,30},{3,31},{4,0},{5,1},{6,2},{7,3},{8,4},{9,5},{1... | collective-permute-start | bytes 6152 | tf_op jit(solution)/shard_map/ppermute | solution.py:20
  234.4 4.1 %collective-permute-done.78 = f32[2,24,24]{2,1,0:T(8,128)S(1)} collective-permute-done((f32[2,24,24]{2,1,0:T(8,128)S(1)}, f32[2,24,24]{2,1,0:T(8,128)S(1)}, u32[]{:S(2)}, u32[]{:S(2)}) %collective-permute-start.78) | collective-permute-done | bytes 4640 | tf_op jit(solution)/shard_map/ppermute | solution.py:49
  (320 shorter events, 124.4 us)
Async XLA Ops:
  4.6 16.6 %collective-permute-start.4 = (f32[1,2112]{1,0:T(1,128)S(1)}, f32[1,2112]{1,0:T(1,128)S(1)}, u32[]{:S(2)}, u32[]{:S(2)}) collective-permute-start(f32[1,2112]{1,0:T(1,128)S(1)} %pad_maximum_fusion.4), channel_id=1, source_target_pairs={{0,16},{1,17},{2,18},{3,19},{4,20},{5,21},{6,22},{7,23},{8,24},{9,... | collective-permute-start | bytes 25352 | tf_op jit(solution)/shard_map/ppermute | solution.py:20
  8.8 10.9 %collective-permute-start = (f32[1,1056]{1,0:T(1,128)S(1)}, f32[1,1056]{1,0:T(1,128)S(1)}, u32[]{:S(2)}, u32[]{:S(2)}) collective-permute-start(f32[1,1056]{1,0:T(1,128)S(1)} %pad_maximum_fusion.6), channel_id=1, source_target_pairs={{0,1},{1,2},{2,3},{3,4},{4,5},{5,6},{6,7},{7,8},{8,9},{9,10},{10,1... | collective-permute-start | bytes 12680 | tf_op jit(solution)/shard_map/ppermute | solution.py:20
  9.0 10.8 %collective-permute-start.1 = (f32[1,1056]{1,0:T(1,128)S(1)}, f32[1,1056]{1,0:T(1,128)S(1)}, u32[]{:S(2)}, u32[]{:S(2)}) collective-permute-start(f32[1,1056]{1,0:T(1,128)S(1)} %pad_maximum_fusion.7), channel_id=1, source_target_pairs={{0,31},{1,0},{2,1},{3,2},{4,3},{5,4},{6,5},{7,6},{8,7},{9,8},{10,9... | collective-permute-start | bytes 12680 | tf_op jit(solution)/shard_map/ppermute | solution.py:20
  29.6 9.9 %collective-permute-start.10 = (f32[2,8]{1,0:T(2,128)S(1)}, f32[2,8]{1,0:T(2,128)S(1)}, u32[]{:S(2)}, u32[]{:S(2)}) collective-permute-start(f32[2,8]{1,0:T(2,128)S(1)} %pad_maximum_fusion.10), channel_id=1, source_target_pairs={{0,3},{1,2},{2,1},{3,0},{4,7},{5,6},{6,5},{7,4},{8,11},{9,10},{10,... | collective-permute-start | bytes 200 | tf_op jit(solution)/shard_map/ppermute | solution.py:49
  29.6 10.6 %collective-permute-start.11 = (f32[2,8]{1,0:T(2,128)S(1)}, f32[2,8]{1,0:T(2,128)S(1)}, u32[]{:S(2)}, u32[]{:S(2)}) collective-permute-start(f32[2,8]{1,0:T(2,128)S(1)} %pad_maximum_fusion.10), channel_id=1, source_target_pairs={{0,2},{1,3},{2,0},{3,1},{4,6},{5,7},{6,4},{7,5},{8,10},{9,11},{10,... | collective-permute-start | bytes 200 | tf_op jit(solution)/shard_map/ppermute | solution.py:49
  29.7 10.5 %collective-permute-start.12 = (f32[2,8]{1,0:T(2,128)S(1)}, f32[2,8]{1,0:T(2,128)S(1)}, u32[]{:S(2)}, u32[]{:S(2)}) collective-permute-start(f32[2,8]{1,0:T(2,128)S(1)} %pad_maximum_fusion.10), channel_id=1, source_target_pairs={{0,1},{1,0},{2,3},{3,2},{4,5},{5,4},{6,7},{7,6},{8,9},{9,8},{10,11... | collective-permute-start | bytes 200 | tf_op jit(solution)/shard_map/ppermute | solution.py:49
  34.9 18.1 %collective-permute-start.5 = (f32[17,64]{1,0:T(8,128)S(1)}, f32[17,64]{1,0:T(8,128)S(1)}, u32[]{:S(2)}, u32[]{:S(2)}) collective-permute-start(f32[17,64]{1,0:T(8,128)S(1)} %get-tuple-element.20), channel_id=1, source_target_pairs={{0,31},{1,0},{2,1},{3,2},{4,3},{5,4},{6,5},{7,6},{8,7},{9,8},{10,9... | collective-permute-start | bytes 13064 | tf_op jit(solution)/shard_map/ppermute | solution.py:20
  39.5 13.4 %collective-permute-start.6 = (f32[17,64]{1,0:T(8,128)S(1)}, f32[17,64]{1,0:T(8,128)S(1)}, u32[]{:S(2)}, u32[]{:S(2)}) collective-permute-start(f32[17,64]{1,0:T(8,128)S(1)} %get-tuple-element.19), channel_id=1, source_target_pairs={{0,1},{1,2},{2,3},{3,4},{4,5},{5,6},{6,7},{7,8},{8,9},{9,10},{10,1... | collective-permute-start | bytes 13064 | tf_op jit(solution)/shard_map/ppermute | solution.py:20
  39.5 13.4 %collective-permute-start.7 = (f32[17,64]{1,0:T(8,128)S(1)}, f32[17,64]{1,0:T(8,128)S(1)}, u32[]{:S(2)}, u32[]{:S(2)}) collective-permute-start(f32[17,64]{1,0:T(8,128)S(1)} %get-tuple-element.18), channel_id=1, source_target_pairs={{0,28},{1,29},{2,30},{3,31},{4,0},{5,1},{6,2},{7,3},{8,4},{9,5},{1... | collective-permute-start | bytes 13064 | tf_op jit(solution)/shard_map/ppermute | solution.py:20
  58.6 10.1 %collective-permute-start.17 = (f32[8,64]{1,0:T(8,128)S(1)}, f32[8,64]{1,0:T(8,128)S(1)}, u32[]{:S(2)}, u32[]{:S(2)}) collective-permute-start(f32[8,64]{1,0:T(8,128)S(1)} %get-tuple-element.71), channel_id=1, source_target_pairs={{0,1},{1,2},{2,3},{3,4},{4,5},{5,6},{6,7},{7,8},{8,9},{9,10},{10,1... | collective-permute-start | bytes 6152 | tf_op jit(solution)/shard_map/ppermute | solution.py:20
  58.6 10.1 %collective-permute-start.18 = (f32[8,64]{1,0:T(8,128)S(1)}, f32[8,64]{1,0:T(8,128)S(1)}, u32[]{:S(2)}, u32[]{:S(2)}) collective-permute-start(f32[8,64]{1,0:T(8,128)S(1)} %get-tuple-element.70), channel_id=1, source_target_pairs={{0,31},{1,0},{2,1},{3,2},{4,3},{5,4},{6,5},{7,6},{8,7},{9,8},{10,9... | collective-permute-start | bytes 6152 | tf_op jit(solution)/shard_map/ppermute | solution.py:20
  78.8 6.7 %collective-permute-start.23 = (f32[8,64]{1,0:T(8,128)S(1)}, f32[8,64]{1,0:T(8,128)S(1)}, u32[]{:S(2)}, u32[]{:S(2)}) collective-permute-start(f32[8,64]{1,0:T(8,128)S(1)} %get-tuple-element.31), channel_id=1, source_target_pairs={{0,1},{1,2},{2,3},{3,4},{4,5},{5,6},{6,7},{7,8},{8,9},{9,10},{10,1... | collective-permute-start | bytes 6152 | tf_op jit(solution)/shard_map/ppermute | solution.py:20
  88.3 10.2 %collective-permute-start.27 = (f32[8,64]{1,0:T(8,128)S(1)}, f32[8,64]{1,0:T(8,128)S(1)}, u32[]{:S(2)}, u32[]{:S(2)}) collective-permute-start(f32[8,64]{1,0:T(8,128)S(1)} %get-tuple-element.67), channel_id=1, source_target_pairs={{0,1},{1,2},{2,3},{3,4},{4,5},{5,6},{6,7},{7,8},{8,9},{9,10},{10,1... | collective-permute-start | bytes 6152 | tf_op jit(solution)/shard_map/ppermute | solution.py:20
  88.3 10.2 %collective-permute-start.28 = (f32[8,64]{1,0:T(8,128)S(1)}, f32[8,64]{1,0:T(8,128)S(1)}, u32[]{:S(2)}, u32[]{:S(2)}) collective-permute-start(f32[8,64]{1,0:T(8,128)S(1)} %get-tuple-element.66), channel_id=1, source_target_pairs={{0,31},{1,0},{2,1},{3,2},{4,3},{5,4},{6,5},{7,6},{8,7},{9,8},{10,9... | collective-permute-start | bytes 6152 | tf_op jit(solution)/shard_map/ppermute | solution.py:20
  108.5 6.7 %collective-permute-start.33 = (f32[8,64]{1,0:T(8,128)S(1)}, f32[8,64]{1,0:T(8,128)S(1)}, u32[]{:S(2)}, u32[]{:S(2)}) collective-permute-start(f32[8,64]{1,0:T(8,128)S(1)} %get-tuple-element.27), channel_id=1, source_target_pairs={{0,1},{1,2},{2,3},{3,4},{4,5},{5,6},{6,7},{7,8},{8,9},{9,10},{10,1... | collective-permute-start | bytes 6152 | tf_op jit(solution)/shard_map/ppermute | solution.py:20
  118.0 10.2 %collective-permute-start.37 = (f32[8,64]{1,0:T(8,128)S(1)}, f32[8,64]{1,0:T(8,128)S(1)}, u32[]{:S(2)}, u32[]{:S(2)}) collective-permute-start(f32[8,64]{1,0:T(8,128)S(1)} %get-tuple-element.63), channel_id=1, source_target_pairs={{0,1},{1,2},{2,3},{3,4},{4,5},{5,6},{6,7},{7,8},{8,9},{9,10},{10,1... | collective-permute-start | bytes 6152 | tf_op jit(solution)/shard_map/ppermute | solution.py:20
  118.0 10.2 %collective-permute-start.38 = (f32[8,64]{1,0:T(8,128)S(1)}, f32[8,64]{1,0:T(8,128)S(1)}, u32[]{:S(2)}, u32[]{:S(2)}) collective-permute-start(f32[8,64]{1,0:T(8,128)S(1)} %get-tuple-element.62), channel_id=1, source_target_pairs={{0,31},{1,0},{2,1},{3,2},{4,3},{5,4},{6,5},{7,6},{8,7},{9,8},{10,9... | collective-permute-start | bytes 6152 | tf_op jit(solution)/shard_map/ppermute | solution.py:20
  159.8 11.0 %collective-permute-start.52 = (f32[8,32]{1,0:T(8,128)S(1)}, f32[8,32]{1,0:T(8,128)S(1)}, u32[]{:S(2)}, u32[]{:S(2)}) collective-permute-start(f32[8,32]{1,0:T(8,128)S(1)} %get-tuple-element.83), channel_id=1, source_target_pairs={{0,1},{1,2},{2,3},{3,4},{4,5},{5,6},{6,7},{7,8},{8,9},{9,10},{10,1... | collective-permute-start | bytes 3080 | tf_op jit(solution)/shard_map/ppermute | solution.py:20
  159.8 11.0 %collective-permute-start.53 = (f32[8,32]{1,0:T(8,128)S(1)}, f32[8,32]{1,0:T(8,128)S(1)}, u32[]{:S(2)}, u32[]{:S(2)}) collective-permute-start(f32[8,32]{1,0:T(8,128)S(1)} %get-tuple-element.82), channel_id=1, source_target_pairs={{0,31},{1,0},{2,1},{3,2},{4,3},{5,4},{6,5},{7,6},{8,7},{9,8},{10,9... | collective-permute-start | bytes 3080 | tf_op jit(solution)/shard_map/ppermute | solution.py:20
  177.8 8.8 %collective-permute-start.61 = (f32[8,64]{1,0:T(8,128)S(1)}, f32[8,64]{1,0:T(8,128)S(1)}, u32[]{:S(2)}, u32[]{:S(2)}) collective-permute-start(f32[8,64]{1,0:T(8,128)S(1)} %concatenate.231), channel_id=1, source_target_pairs={{0,16},{1,17},{2,18},{3,19},{4,20},{5,21},{6,22},{7,23},{8,24},{9,... | collective-permute-start | bytes 6152 | tf_op jit(solution)/shard_map/ppermute | solution.py:20
  187.3 10.1 %collective-permute-start.62 = (f32[8,32]{1,0:T(8,128)S(1)}, f32[8,32]{1,0:T(8,128)S(1)}, u32[]{:S(2)}, u32[]{:S(2)}) collective-permute-start(f32[8,32]{1,0:T(8,128)S(1)} %get-tuple-element.79), channel_id=1, source_target_pairs={{0,1},{1,2},{2,3},{3,4},{4,5},{5,6},{6,7},{7,8},{8,9},{9,10},{10,1... | collective-permute-start | bytes 3080 | tf_op jit(solution)/shard_map/ppermute | solution.py:20
  187.3 10.1 %collective-permute-start.63 = (f32[8,32]{1,0:T(8,128)S(1)}, f32[8,32]{1,0:T(8,128)S(1)}, u32[]{:S(2)}, u32[]{:S(2)}) collective-permute-start(f32[8,32]{1,0:T(8,128)S(1)} %get-tuple-element.78), channel_id=1, source_target_pairs={{0,31},{1,0},{2,1},{3,2},{4,3},{5,4},{6,5},{7,6},{8,7},{9,8},{10,9... | collective-permute-start | bytes 3080 | tf_op jit(solution)/shard_map/ppermute | solution.py:20
  204.2 10.1 %collective-permute-start.67 = (f32[8,64]{1,0:T(8,128)S(1)}, f32[8,64]{1,0:T(8,128)S(1)}, u32[]{:S(2)}, u32[]{:S(2)}) collective-permute-start(f32[8,64]{1,0:T(8,128)S(1)} %get-tuple-element.59), channel_id=1, source_target_pairs={{0,1},{1,2},{2,3},{3,4},{4,5},{5,6},{6,7},{7,8},{8,9},{9,10},{10,1... | collective-permute-start | bytes 6152 | tf_op jit(solution)/shard_map/ppermute | solution.py:20
  204.3 10.1 %collective-permute-start.68 = (f32[8,64]{1,0:T(8,128)S(1)}, f32[8,64]{1,0:T(8,128)S(1)}, u32[]{:S(2)}, u32[]{:S(2)}) collective-permute-start(f32[8,64]{1,0:T(8,128)S(1)} %get-tuple-element.58), channel_id=1, source_target_pairs={{0,31},{1,0},{2,1},{3,2},{4,3},{5,4},{6,5},{7,6},{8,7},{9,8},{10,9... | collective-permute-start | bytes 6152 | tf_op jit(solution)/shard_map/ppermute | solution.py:20
  (63 other events, 390.9 us)

commit v7 on v5

--- a/solution.py
+++ b/solution.py
@@ -72,13 +72,13 @@
     return lo_hot, hi_mask, length
 
 
-def gather_cols(values, table):
+def gather_cols(values, table, precision=lax.Precision.HIGH):
     lo_hot, hi_mask, length = table
     groups = hi_mask.shape[0]
     rows = values.shape[0]
     padded = jnp.pad(values, ((0, 0), (0, groups * LANES - length)))
     split = padded.reshape(rows, groups, LANES)
-    picked = jnp.einsum("rab,nb->ran", split, lo_hot, precision=lax.Precision.HIGH)
+    picked = jnp.einsum("rab,nb->ran", split, lo_hot, precision=precision)
     return jnp.sum(picked * hi_mask[None], axis=1)
 
 
@@ -195,7 +195,9 @@
     pair_moved, node_diag_moved = exchange(
         extend_pieces(pair, send_edge_table), give_back_pieces(node_diag_local, send_node_table)
     )
-    pair_values = edge_values(extend_finish(pair, pair_moved))
+    pair_values = gather_cols(extend_finish(pair, pair_moved), edge_table, highest).reshape(
+        2 * modes, edofs, elements
+    )
     node_diag = give_back_finish(node_diag_local, node_diag_moved, send_node_table)[0]
     stiff_pair = element_terms(stiff_elem, pair_values)
     mass_pair = element_terms(mass_elem, pair_values)

time: 236 us -> 237 us (level)
  no operation moved by 1% of the time
where the time goes in v7:
time: 237 us; the launch traced here: 236 us
  starting transfers between devices  112 us (47%)
  waiting for transfers between devices  75.6 us (32%)
  matrix products  35 us (15%)
  local copies, waits for them, and re-layouts  8.56 us (4%)
  other arithmetic  3.83 us (2%)
    ppermute x65, starting transfers between devices, from_behind(): lax.ppermute(shard, axis, [(i, (i + by) % length) for i in range(length)])  99.1 us
    ppermute x65, waiting for transfers between devices, from_behind(): lax.ppermute(shard, axis, [(i, (i + by) % length) for i in range(length)])  60.6 us
    dot_general x14, matrix products, gather_cols(): picked = jnp.einsum('rab,nb->ran', split, lo_hot, precision=precision)  23.2 us
    ppermute x14, waiting for transfers between devices, all_sum(): lax.ppermute(value, 'dom', [(i, i ^ t << shift) for i in range(length)])  15 us
    ppermute x14, starting transfers between devices, all_sum(): lax.ppermute(value, 'dom', [(i, i ^ t << shift) for i in range(length)])  12.5 us
    dot_general x14, matrix products, scatter_cols(): jnp.einsum('ran,nb->rab', spread, lo_hot, precision=lax.Precision.HIGH)  9.56 us
  transfers between devices with their start and end apart: 79, of which 32 were waited for; matrix products, arithmetic and copies ran while one was open for 2% of the time, Pallas kernels for 0%

profile of v7, /device:TPU:0, one launch (start us, length us, event | category | flops | bytes accessed | tf_op | source)
XLA Modules:
  0.0 236.3 jit_solution(10397275965711023816)
XLA Ops:
  4.5 4.1 %collective-permute-start.4 = (f32[1,2112]{1,0:T(1,128)S(1)}, f32[1,2112]{1,0:T(1,128)S(1)}, u32[]{:S(2)}, u32[]{:S(2)}) collective-permute-start(f32[1,2112]{1,0:T(1,128)S(1)} %pad_maximum_fusion.4), channel_id=1, source_target_pairs={{0,16},{1,17},{2,18},{3,19},{4,20},{5,21},{6,22},{7,23},{8,24},{9,... | collective-permute-start | bytes 25352 | tf_op jit(solution)/shard_map/ppermute | solution.py:20
  8.9 5.4 %collective-permute-start.1 = (f32[1,1056]{1,0:T(1,128)S(1)}, f32[1,1056]{1,0:T(1,128)S(1)}, u32[]{:S(2)}, u32[]{:S(2)}) collective-permute-start(f32[1,1056]{1,0:T(1,128)S(1)} %pad_maximum_fusion.7), channel_id=1, source_target_pairs={{0,31},{1,0},{2,1},{3,2},{4,3},{5,4},{6,5},{7,6},{8,7},{9,8},{10,9... | collective-permute-start | bytes 12680 | tf_op jit(solution)/shard_map/ppermute | solution.py:20
  14.5 4.8 %collective-permute-start.3 = (f32[1,1056]{1,0:T(1,128)S(1)}, f32[1,1056]{1,0:T(1,128)S(1)}, u32[]{:S(2)}, u32[]{:S(2)}) collective-permute-start(f32[1,1056]{1,0:T(1,128)S(1)} %pad_maximum_fusion.9), channel_id=1, source_target_pairs={{0,28},{1,29},{2,30},{3,31},{4,0},{5,1},{6,2},{7,3},{8,4},{9,5},{1... | collective-permute-start | bytes 12680 | tf_op jit(solution)/shard_map/ppermute | solution.py:20
  21.3 4.3 %fusion.20 = f32[16,5120]{1,0:T(8,128)S(1)} fusion(f32[15,5120]{1,0:T(8,128)S(1)} %fusion.109, s32[5120]{0:T(1024)S(1)} %get-tuple-element.49, f32[16,1920]{1,0:T(8,128)S(1)} %concatenate.178), kind=kOutput, calls=%fused_computation.28 | convolution fusion | flops 1890467840 | bytes 778240 | tf_op jit(solution)/shard_map/rab,nb->ran/dot_general | solution.py:81
  34.0 4.6 %collective-permute-start.5 = (f32[17,64]{1,0:T(8,128)S(1)}, f32[17,64]{1,0:T(8,128)S(1)}, u32[]{:S(2)}, u32[]{:S(2)}) collective-permute-start(f32[17,64]{1,0:T(8,128)S(1)} %get-tuple-element.20), channel_id=1, source_target_pairs={{0,31},{1,0},{2,1},{3,2},{4,3},{5,4},{6,5},{7,6},{8,7},{9,8},{10,9... | collective-permute-start | bytes 13064 | tf_op jit(solution)/shard_map/ppermute | solution.py:20
  57.7 5.3 %collective-permute-start.18 = (f32[8,64]{1,0:T(8,128)S(1)}, f32[8,64]{1,0:T(8,128)S(1)}, u32[]{:S(2)}, u32[]{:S(2)}) collective-permute-start(f32[8,64]{1,0:T(8,128)S(1)} %get-tuple-element.70), channel_id=1, source_target_pairs={{0,31},{1,0},{2,1},{3,2},{4,3},{5,4},{6,5},{7,6},{8,7},{9,8},{10,9... | collective-permute-start | bytes 6152 | tf_op jit(solution)/shard_map/ppermute | solution.py:20
  63.0 4.7 %collective-permute-start.20 = (f32[8,64]{1,0:T(8,128)S(1)}, f32[8,64]{1,0:T(8,128)S(1)}, u32[]{:S(2)}, u32[]{:S(2)}) collective-permute-start(f32[8,64]{1,0:T(8,128)S(1)} %get-tuple-element.68), channel_id=1, source_target_pairs={{0,28},{1,29},{2,30},{3,31},{4,0},{5,1},{6,2},{7,3},{8,4},{9,5},{1... | collective-permute-start | bytes 6152 | tf_op jit(solution)/shard_map/ppermute | solution.py:20
  80.0 4.1 %collective-permute-done.23 = f32[8,64]{1,0:T(8,128)S(1)} collective-permute-done((f32[8,64]{1,0:T(8,128)S(1)}, f32[8,64]{1,0:T(8,128)S(1)}, u32[]{:S(2)}, u32[]{:S(2)}) %collective-permute-start.23) | collective-permute-done | bytes 2080 | tf_op jit(solution)/shard_map/ppermute | solution.py:20
  86.8 5.3 %collective-permute-start.28 = (f32[8,64]{1,0:T(8,128)S(1)}, f32[8,64]{1,0:T(8,128)S(1)}, u32[]{:S(2)}, u32[]{:S(2)}) collective-permute-start(f32[8,64]{1,0:T(8,128)S(1)} %get-tuple-element.66), channel_id=1, source_target_pairs={{0,31},{1,0},{2,1},{3,2},{4,3},{5,4},{6,5},{7,6},{8,7},{9,8},{10,9... | collective-permute-start | bytes 6152 | tf_op jit(solution)/shard_map/ppermute | solution.py:20
  92.2 4.7 %collective-permute-start.30 = (f32[8,64]{1,0:T(8,128)S(1)}, f32[8,64]{1,0:T(8,128)S(1)}, u32[]{:S(2)}, u32[]{:S(2)}) collective-permute-start(f32[8,64]{1,0:T(8,128)S(1)} %get-tuple-element.64), channel_id=1, source_target_pairs={{0,28},{1,29},{2,30},{3,31},{4,0},{5,1},{6,2},{7,3},{8,4},{9,5},{1... | collective-permute-start | bytes 6152 | tf_op jit(solution)/shard_map/ppermute | solution.py:20
  109.1 4.1 %collective-permute-done.33 = f32[8,64]{1,0:T(8,128)S(1)} collective-permute-done((f32[8,64]{1,0:T(8,128)S(1)}, f32[8,64]{1,0:T(8,128)S(1)}, u32[]{:S(2)}, u32[]{:S(2)}) %collective-permute-start.33) | collective-permute-done | bytes 2080 | tf_op jit(solution)/shard_map/ppermute | solution.py:20
  116.0 5.3 %collective-permute-start.38 = (f32[8,64]{1,0:T(8,128)S(1)}, f32[8,64]{1,0:T(8,128)S(1)}, u32[]{:S(2)}, u32[]{:S(2)}) collective-permute-start(f32[8,64]{1,0:T(8,128)S(1)} %get-tuple-element.62), channel_id=1, source_target_pairs={{0,31},{1,0},{2,1},{3,2},{4,3},{5,4},{6,5},{7,6},{8,7},{9,8},{10,9... | collective-permute-start | bytes 6152 | tf_op jit(solution)/shard_map/ppermute | solution.py:20
  121.3 4.7 %collective-permute-start.40 = (f32[8,64]{1,0:T(8,128)S(1)}, f32[8,64]{1,0:T(8,128)S(1)}, u32[]{:S(2)}, u32[]{:S(2)}) collective-permute-start(f32[8,64]{1,0:T(8,128)S(1)} %get-tuple-element.60), channel_id=1, source_target_pairs={{0,28},{1,29},{2,30},{3,31},{4,0},{5,1},{6,2},{7,3},{8,4},{9,5},{1... | collective-permute-start | bytes 6152 | tf_op jit(solution)/shard_map/ppermute | solution.py:20
  138.5 3.9 %collective-permute-done.43 = f32[8,64]{1,0:T(8,128)S(1)} collective-permute-done((f32[8,64]{1,0:T(8,128)S(1)}, f32[8,64]{1,0:T(8,128)S(1)}, u32[]{:S(2)}, u32[]{:S(2)}) %collective-permute-start.43) | collective-permute-done | bytes 2080 | tf_op jit(solution)/shard_map/ppermute | solution.py:20
  145.5 4.3 %collective-permute-start.47 = (f32[8,32]{1,0:T(8,128)S(1)}, f32[8,32]{1,0:T(8,128)S(1)}, u32[]{:S(2)}, u32[]{:S(2)}) collective-permute-start(f32[8,32]{1,0:T(8,128)S(1)} %get-tuple-element.48), channel_id=1, source_target_pairs={{0,31},{1,0},{2,1},{3,2},{4,3},{5,4},{6,5},{7,6},{8,7},{9,8},{10,9... | collective-permute-start | bytes 3080 | tf_op jit(solution)/shard_map/ppermute | solution.py:20
  151.9 4.6 %collective-permute-done.48 = f32[8,32]{1,0:T(8,128)S(1)} collective-permute-done((f32[8,32]{1,0:T(8,128)S(1)}, f32[8,32]{1,0:T(8,128)S(1)}, u32[]{:S(2)}, u32[]{:S(2)}) %collective-permute-start.48) | collective-permute-done | bytes 1056 | tf_op jit(solution)/shard_map/ppermute | solution.py:20
  157.1 6.3 %collective-permute-start.53 = (f32[8,32]{1,0:T(8,128)S(1)}, f32[8,32]{1,0:T(8,128)S(1)}, u32[]{:S(2)}, u32[]{:S(2)}) collective-permute-start(f32[8,32]{1,0:T(8,128)S(1)} %get-tuple-element.82), channel_id=1, source_target_pairs={{0,31},{1,0},{2,1},{3,2},{4,3},{5,4},{6,5},{7,6},{8,7},{9,8},{10,9... | collective-permute-start | bytes 3080 | tf_op jit(solution)/shard_map/ppermute | solution.py:20
  163.4 4.7 %collective-permute-start.55 = (f32[8,32]{1,0:T(8,128)S(1)}, f32[8,32]{1,0:T(8,128)S(1)}, u32[]{:S(2)}, u32[]{:S(2)}) collective-permute-start(f32[8,32]{1,0:T(8,128)S(1)} %get-tuple-element.80), channel_id=1, source_target_pairs={{0,28},{1,29},{2,30},{3,31},{4,0},{5,1},{6,2},{7,3},{8,4},{9,5},{1... | collective-permute-start | bytes 3080 | tf_op jit(solution)/shard_map/ppermute | solution.py:20
  177.8 4.3 %collective-permute-done.58 = f32[8,32]{1,0:T(8,128)S(1)} collective-permute-done((f32[8,32]{1,0:T(8,128)S(1)}, f32[8,32]{1,0:T(8,128)S(1)}, u32[]{:S(2)}, u32[]{:S(2)}) %collective-permute-start.58) | collective-permute-done | bytes 1056 | tf_op jit(solution)/shard_map/ppermute | solution.py:20
  184.5 5.3 %collective-permute-start.63 = (f32[8,32]{1,0:T(8,128)S(1)}, f32[8,32]{1,0:T(8,128)S(1)}, u32[]{:S(2)}, u32[]{:S(2)}) collective-permute-start(f32[8,32]{1,0:T(8,128)S(1)} %get-tuple-element.78), channel_id=1, source_target_pairs={{0,31},{1,0},{2,1},{3,2},{4,3},{5,4},{6,5},{7,6},{8,7},{9,8},{10,9... | collective-permute-start | bytes 3080 | tf_op jit(solution)/shard_map/ppermute | solution.py:20
  189.8 4.7 %collective-permute-start.65 = (f32[8,32]{1,0:T(8,128)S(1)}, f32[8,32]{1,0:T(8,128)S(1)}, u32[]{:S(2)}, u32[]{:S(2)}) collective-permute-start(f32[8,32]{1,0:T(8,128)S(1)} %get-tuple-element.76), channel_id=1, source_target_pairs={{0,28},{1,29},{2,30},{3,31},{4,0},{5,1},{6,2},{7,3},{8,4},{9,5},{1... | collective-permute-start | bytes 3080 | tf_op jit(solution)/shard_map/ppermute | solution.py:20
  201.5 5.3 %collective-permute-start.68 = (f32[8,64]{1,0:T(8,128)S(1)}, f32[8,64]{1,0:T(8,128)S(1)}, u32[]{:S(2)}, u32[]{:S(2)}) collective-permute-start(f32[8,64]{1,0:T(8,128)S(1)} %get-tuple-element.58), channel_id=1, source_target_pairs={{0,31},{1,0},{2,1},{3,2},{4,3},{5,4},{6,5},{7,6},{8,7},{9,8},{10,9... | collective-permute-start | bytes 6152 | tf_op jit(solution)/shard_map/ppermute | solution.py:20
  206.8 4.7 %collective-permute-start.70 = (f32[8,64]{1,0:T(8,128)S(1)}, f32[8,64]{1,0:T(8,128)S(1)}, u32[]{:S(2)}, u32[]{:S(2)}) collective-permute-start(f32[8,64]{1,0:T(8,128)S(1)} %get-tuple-element.56), channel_id=1, source_target_pairs={{0,28},{1,29},{2,30},{3,31},{4,0},{5,1},{6,2},{7,3},{8,4},{9,5},{1... | collective-permute-start | bytes 6152 | tf_op jit(solution)/shard_map/ppermute | solution.py:20
  231.6 4.1 %collective-permute-done.78 = f32[2,24,24]{2,1,0:T(8,128)S(1)} collective-permute-done((f32[2,24,24]{2,1,0:T(8,128)S(1)}, f32[2,24,24]{2,1,0:T(8,128)S(1)}, u32[]{:S(2)}, u32[]{:S(2)}) %collective-permute-start.78) | collective-permute-done | bytes 4640 | tf_op jit(solution)/shard_map/ppermute | solution.py:49
  (320 shorter events, 120.8 us)
Async XLA Ops:
  4.5 16.6 %collective-permute-start.4 = (f32[1,2112]{1,0:T(1,128)S(1)}, f32[1,2112]{1,0:T(1,128)S(1)}, u32[]{:S(2)}, u32[]{:S(2)}) collective-permute-start(f32[1,2112]{1,0:T(1,128)S(1)} %pad_maximum_fusion.4), channel_id=1, source_target_pairs={{0,16},{1,17},{2,18},{3,19},{4,20},{5,21},{6,22},{7,23},{8,24},{9,... | collective-permute-start | bytes 25352 | tf_op jit(solution)/shard_map/ppermute | solution.py:20
  8.8 10.9 %collective-permute-start = (f32[1,1056]{1,0:T(1,128)S(1)}, f32[1,1056]{1,0:T(1,128)S(1)}, u32[]{:S(2)}, u32[]{:S(2)}) collective-permute-start(f32[1,1056]{1,0:T(1,128)S(1)} %pad_maximum_fusion.6), channel_id=1, source_target_pairs={{0,1},{1,2},{2,3},{3,4},{4,5},{5,6},{6,7},{7,8},{8,9},{9,10},{10,1... | collective-permute-start | bytes 12680 | tf_op jit(solution)/shard_map/ppermute | solution.py:20
  8.9 10.8 %collective-permute-start.1 = (f32[1,1056]{1,0:T(1,128)S(1)}, f32[1,1056]{1,0:T(1,128)S(1)}, u32[]{:S(2)}, u32[]{:S(2)}) collective-permute-start(f32[1,1056]{1,0:T(1,128)S(1)} %pad_maximum_fusion.7), channel_id=1, source_target_pairs={{0,31},{1,0},{2,1},{3,2},{4,3},{5,4},{6,5},{7,6},{8,7},{9,8},{10,9... | collective-permute-start | bytes 12680 | tf_op jit(solution)/shard_map/ppermute | solution.py:20
  30.1 8.5 %collective-permute-start.10 = (f32[2,8]{1,0:T(2,128)S(1)}, f32[2,8]{1,0:T(2,128)S(1)}, u32[]{:S(2)}, u32[]{:S(2)}) collective-permute-start(f32[2,8]{1,0:T(2,128)S(1)} %pad_maximum_fusion.10), channel_id=1, source_target_pairs={{0,3},{1,2},{2,1},{3,0},{4,7},{5,6},{6,5},{7,4},{8,11},{9,10},{10,... | collective-permute-start | bytes 200 | tf_op jit(solution)/shard_map/ppermute | solution.py:49
  30.2 9.1 %collective-permute-start.11 = (f32[2,8]{1,0:T(2,128)S(1)}, f32[2,8]{1,0:T(2,128)S(1)}, u32[]{:S(2)}, u32[]{:S(2)}) collective-permute-start(f32[2,8]{1,0:T(2,128)S(1)} %pad_maximum_fusion.10), channel_id=1, source_target_pairs={{0,2},{1,3},{2,0},{3,1},{4,6},{5,7},{6,4},{7,5},{8,10},{9,11},{10,... | collective-permute-start | bytes 200 | tf_op jit(solution)/shard_map/ppermute | solution.py:49
  30.3 9.1 %collective-permute-start.12 = (f32[2,8]{1,0:T(2,128)S(1)}, f32[2,8]{1,0:T(2,128)S(1)}, u32[]{:S(2)}, u32[]{:S(2)}) collective-permute-start(f32[2,8]{1,0:T(2,128)S(1)} %pad_maximum_fusion.10), channel_id=1, source_target_pairs={{0,1},{1,0},{2,3},{3,2},{4,5},{5,4},{6,7},{7,6},{8,9},{9,8},{10,11... | collective-permute-start | bytes 200 | tf_op jit(solution)/shard_map/ppermute | solution.py:49
  34.0 18.1 %collective-permute-start.5 = (f32[17,64]{1,0:T(8,128)S(1)}, f32[17,64]{1,0:T(8,128)S(1)}, u32[]{:S(2)}, u32[]{:S(2)}) collective-permute-start(f32[17,64]{1,0:T(8,128)S(1)} %get-tuple-element.20), channel_id=1, source_target_pairs={{0,31},{1,0},{2,1},{3,2},{4,3},{5,4},{6,5},{7,6},{8,7},{9,8},{10,9... | collective-permute-start | bytes 13064 | tf_op jit(solution)/shard_map/ppermute | solution.py:20
  38.6 13.4 %collective-permute-start.6 = (f32[17,64]{1,0:T(8,128)S(1)}, f32[17,64]{1,0:T(8,128)S(1)}, u32[]{:S(2)}, u32[]{:S(2)}) collective-permute-start(f32[17,64]{1,0:T(8,128)S(1)} %get-tuple-element.19), channel_id=1, source_target_pairs={{0,1},{1,2},{2,3},{3,4},{4,5},{5,6},{6,7},{7,8},{8,9},{9,10},{10,1... | collective-permute-start | bytes 13064 | tf_op jit(solution)/shard_map/ppermute | solution.py:20
  38.6 13.4 %collective-permute-start.7 = (f32[17,64]{1,0:T(8,128)S(1)}, f32[17,64]{1,0:T(8,128)S(1)}, u32[]{:S(2)}, u32[]{:S(2)}) collective-permute-start(f32[17,64]{1,0:T(8,128)S(1)} %get-tuple-element.18), channel_id=1, source_target_pairs={{0,28},{1,29},{2,30},{3,31},{4,0},{5,1},{6,2},{7,3},{8,4},{9,5},{1... | collective-permute-start | bytes 13064 | tf_op jit(solution)/shard_map/ppermute | solution.py:20
  57.7 10.1 %collective-permute-start.17 = (f32[8,64]{1,0:T(8,128)S(1)}, f32[8,64]{1,0:T(8,128)S(1)}, u32[]{:S(2)}, u32[]{:S(2)}) collective-permute-start(f32[8,64]{1,0:T(8,128)S(1)} %get-tuple-element.71), channel_id=1, source_target_pairs={{0,1},{1,2},{2,3},{3,4},{4,5},{5,6},{6,7},{7,8},{8,9},{9,10},{10,1... | collective-permute-start | bytes 6152 | tf_op jit(solution)/shard_map/ppermute | solution.py:20
  57.7 10.1 %collective-permute-start.18 = (f32[8,64]{1,0:T(8,128)S(1)}, f32[8,64]{1,0:T(8,128)S(1)}, u32[]{:S(2)}, u32[]{:S(2)}) collective-permute-start(f32[8,64]{1,0:T(8,128)S(1)} %get-tuple-element.70), channel_id=1, source_target_pairs={{0,31},{1,0},{2,1},{3,2},{4,3},{5,4},{6,5},{7,6},{8,7},{9,8},{10,9... | collective-permute-start | bytes 6152 | tf_op jit(solution)/shard_map/ppermute | solution.py:20
  77.4 6.7 %collective-permute-start.23 = (f32[8,64]{1,0:T(8,128)S(1)}, f32[8,64]{1,0:T(8,128)S(1)}, u32[]{:S(2)}, u32[]{:S(2)}) collective-permute-start(f32[8,64]{1,0:T(8,128)S(1)} %get-tuple-element.31), channel_id=1, source_target_pairs={{0,1},{1,2},{2,3},{3,4},{4,5},{5,6},{6,7},{7,8},{8,9},{9,10},{10,1... | collective-permute-start | bytes 6152 | tf_op jit(solution)/shard_map/ppermute | solution.py:20
  86.8 10.2 %collective-permute-start.27 = (f32[8,64]{1,0:T(8,128)S(1)}, f32[8,64]{1,0:T(8,128)S(1)}, u32[]{:S(2)}, u32[]{:S(2)}) collective-permute-start(f32[8,64]{1,0:T(8,128)S(1)} %get-tuple-element.67), channel_id=1, source_target_pairs={{0,1},{1,2},{2,3},{3,4},{4,5},{5,6},{6,7},{7,8},{8,9},{9,10},{10,1... | collective-permute-start | bytes 6152 | tf_op jit(solution)/shard_map/ppermute | solution.py:20
  86.8 10.2 %collective-permute-start.28 = (f32[8,64]{1,0:T(8,128)S(1)}, f32[8,64]{1,0:T(8,128)S(1)}, u32[]{:S(2)}, u32[]{:S(2)}) collective-permute-start(f32[8,64]{1,0:T(8,128)S(1)} %get-tuple-element.66), channel_id=1, source_target_pairs={{0,31},{1,0},{2,1},{3,2},{4,3},{5,4},{6,5},{7,6},{8,7},{9,8},{10,9... | collective-permute-start | bytes 6152 | tf_op jit(solution)/shard_map/ppermute | solution.py:20
  116.0 10.2 %collective-permute-start.37 = (f32[8,64]{1,0:T(8,128)S(1)}, f32[8,64]{1,0:T(8,128)S(1)}, u32[]{:S(2)}, u32[]{:S(2)}) collective-permute-start(f32[8,64]{1,0:T(8,128)S(1)} %get-tuple-element.63), channel_id=1, source_target_pairs={{0,1},{1,2},{2,3},{3,4},{4,5},{5,6},{6,7},{7,8},{8,9},{9,10},{10,1... | collective-permute-start | bytes 6152 | tf_op jit(solution)/shard_map/ppermute | solution.py:20
  116.0 10.2 %collective-permute-start.38 = (f32[8,64]{1,0:T(8,128)S(1)}, f32[8,64]{1,0:T(8,128)S(1)}, u32[]{:S(2)}, u32[]{:S(2)}) collective-permute-start(f32[8,64]{1,0:T(8,128)S(1)} %get-tuple-element.62), channel_id=1, source_target_pairs={{0,31},{1,0},{2,1},{3,2},{4,3},{5,4},{6,5},{7,6},{8,7},{9,8},{10,9... | collective-permute-start | bytes 6152 | tf_op jit(solution)/shard_map/ppermute | solution.py:20
  157.1 11.0 %collective-permute-start.52 = (f32[8,32]{1,0:T(8,128)S(1)}, f32[8,32]{1,0:T(8,128)S(1)}, u32[]{:S(2)}, u32[]{:S(2)}) collective-permute-start(f32[8,32]{1,0:T(8,128)S(1)} %get-tuple-element.83), channel_id=1, source_target_pairs={{0,1},{1,2},{2,3},{3,4},{4,5},{5,6},{6,7},{7,8},{8,9},{9,10},{10,1... | collective-permute-start | bytes 3080 | tf_op jit(solution)/shard_map/ppermute | solution.py:20
  157.1 11.0 %collective-permute-start.53 = (f32[8,32]{1,0:T(8,128)S(1)}, f32[8,32]{1,0:T(8,128)S(1)}, u32[]{:S(2)}, u32[]{:S(2)}) collective-permute-start(f32[8,32]{1,0:T(8,128)S(1)} %get-tuple-element.82), channel_id=1, source_target_pairs={{0,31},{1,0},{2,1},{3,2},{4,3},{5,4},{6,5},{7,6},{8,7},{9,8},{10,9... | collective-permute-start | bytes 3080 | tf_op jit(solution)/shard_map/ppermute | solution.py:20
  175.0 8.8 %collective-permute-start.61 = (f32[8,64]{1,0:T(8,128)S(1)}, f32[8,64]{1,0:T(8,128)S(1)}, u32[]{:S(2)}, u32[]{:S(2)}) collective-permute-start(f32[8,64]{1,0:T(8,128)S(1)} %concatenate.231), channel_id=1, source_target_pairs={{0,16},{1,17},{2,18},{3,19},{4,20},{5,21},{6,22},{7,23},{8,24},{9,... | collective-permute-start | bytes 6152 | tf_op jit(solution)/shard_map/ppermute | solution.py:20
  175.2 6.9 %collective-permute-start.58 = (f32[8,32]{1,0:T(8,128)S(1)}, f32[8,32]{1,0:T(8,128)S(1)}, u32[]{:S(2)}, u32[]{:S(2)}) collective-permute-start(f32[8,32]{1,0:T(8,128)S(1)} %get-tuple-element.43), channel_id=1, source_target_pairs={{0,1},{1,2},{2,3},{3,4},{4,5},{5,6},{6,7},{7,8},{8,9},{9,10},{10,1... | collective-permute-start | bytes 3080 | tf_op jit(solution)/shard_map/ppermute | solution.py:20
  184.4 10.1 %collective-permute-start.62 = (f32[8,32]{1,0:T(8,128)S(1)}, f32[8,32]{1,0:T(8,128)S(1)}, u32[]{:S(2)}, u32[]{:S(2)}) collective-permute-start(f32[8,32]{1,0:T(8,128)S(1)} %get-tuple-element.79), channel_id=1, source_target_pairs={{0,1},{1,2},{2,3},{3,4},{4,5},{5,6},{6,7},{7,8},{8,9},{9,10},{10,1... | collective-permute-start | bytes 3080 | tf_op jit(solution)/shard_map/ppermute | solution.py:20
  184.5 10.1 %collective-permute-start.63 = (f32[8,32]{1,0:T(8,128)S(1)}, f32[8,32]{1,0:T(8,128)S(1)}, u32[]{:S(2)}, u32[]{:S(2)}) collective-permute-start(f32[8,32]{1,0:T(8,128)S(1)} %get-tuple-element.78), channel_id=1, source_target_pairs={{0,31},{1,0},{2,1},{3,2},{4,3},{5,4},{6,5},{7,6},{8,7},{9,8},{10,9... | collective-permute-start | bytes 3080 | tf_op jit(solution)/shard_map/ppermute | solution.py:20
  201.4 10.1 %collective-permute-start.67 = (f32[8,64]{1,0:T(8,128)S(1)}, f32[8,64]{1,0:T(8,128)S(1)}, u32[]{:S(2)}, u32[]{:S(2)}) collective-permute-start(f32[8,64]{1,0:T(8,128)S(1)} %get-tuple-element.59), channel_id=1, source_target_pairs={{0,1},{1,2},{2,3},{3,4},{4,5},{5,6},{6,7},{7,8},{8,9},{9,10},{10,1... | collective-permute-start | bytes 6152 | tf_op jit(solution)/shard_map/ppermute | solution.py:20
  201.5 10.1 %collective-permute-start.68 = (f32[8,64]{1,0:T(8,128)S(1)}, f32[8,64]{1,0:T(8,128)S(1)}, u32[]{:S(2)}, u32[]{:S(2)}) collective-permute-start(f32[8,64]{1,0:T(8,128)S(1)} %get-tuple-element.58), channel_id=1, source_target_pairs={{0,31},{1,0},{2,1},{3,2},{4,3},{5,4},{6,5},{7,6},{8,7},{9,8},{10,9... | collective-permute-start | bytes 6152 | tf_op jit(solution)/shard_map/ppermute | solution.py:20
  (63 other events, 390.9 us)

commit v8 on v7

--- a/solution.py
+++ b/solution.py
@@ -69,21 +69,22 @@
     hi = index // LANES
     lo_hot = (lo[:, None] == jnp.arange(LANES, dtype=jnp.int32)[None, :]).astype(jnp.float32)
     hi_mask = (hi[None, :] == jnp.arange(groups, dtype=jnp.int32)[:, None]).astype(jnp.float32)
-    return lo_hot, hi_mask, length
+    lo_hot_t = (jnp.arange(LANES, dtype=jnp.int32)[:, None] == lo[None, :]).astype(jnp.float32)
+    return lo_hot, hi_mask, length, lo_hot_t
 
 
 def gather_cols(values, table, precision=lax.Precision.HIGH):
-    lo_hot, hi_mask, length = table
+    lo_hot, hi_mask, length, lo_hot_t = table
     groups = hi_mask.shape[0]
     rows = values.shape[0]
     padded = jnp.pad(values, ((0, 0), (0, groups * LANES - length)))
     split = padded.reshape(rows, groups, LANES)
-    picked = jnp.einsum("rab,nb->ran", split, lo_hot, precision=precision)
+    picked = jnp.einsum("rab,bn->ran", split, lo_hot_t, precision=precision)
     return jnp.sum(picked * hi_mask[None], axis=1)
 
 
 def scatter_cols(terms, table):
-    lo_hot, hi_mask, length = table
+    lo_hot, hi_mask, length, lo_hot_t = table
     groups = hi_mask.shape[0]
     rows = terms.shape[0]
     spread = terms[:, None, :] * hi_mask[None]

time: 237 us -> 224 us (0.945)
  matrix products: 35 us -> 22.5 us
    dot_general x14, matrix products: 23.2 us -> 10.8 us  [gather_cols(): picked = jnp.einsum('rab,bn->ran', split, lo_hot_t, precision=precision)]
where the time goes in v8:
time: 224 us
  starting transfers between devices  112 us (50%)
  waiting for transfers between devices  75.6 us (34%)
  matrix products  22.5 us (10%)
  local copies, waits for them, and re-layouts  8.56 us (4%)
  other arithmetic  3.83 us (2%)
    ppermute x65, starting transfers between devices, from_behind(): lax.ppermute(shard, axis, [(i, (i + by) % length) for i in range(length)])  99.3 us
    ppermute x65, waiting for transfers between devices, from_behind(): lax.ppermute(shard, axis, [(i, (i + by) % length) for i in range(length)])  60.6 us
    ppermute x14, waiting for transfers between devices, all_sum(): lax.ppermute(value, 'dom', [(i, i ^ t << shift) for i in range(length)])  15 us
    ppermute x14, starting transfers between devices, all_sum(): lax.ppermute(value, 'dom', [(i, i ^ t << shift) for i in range(length)])  12.5 us
    dot_general x14, matrix products, gather_cols(): picked = jnp.einsum('rab,bn->ran', split, lo_hot_t, precision=precision)  10.8 us
    dot_general x14, matrix products, scatter_cols(): jnp.einsum('ran,nb->rab', spread, lo_hot, precision=lax.Precision.HIGH)  9.56 us
  transfers between devices with their start and end apart: 79, of which 32 were waited for; matrix products, arithmetic and copies ran while one was open for 2% of the time, Pallas kernels for 0%

profile of v8, /device:TPU:0, one launch (start us, length us, event | category | flops | bytes accessed | tf_op | source)
XLA Modules:
  0.0 224.1 jit_solution(5953370364101089228)
XLA Ops:
  4.4 4.1 %collective-permute-start.4 = (f32[1,2112]{1,0:T(1,128)S(1)}, f32[1,2112]{1,0:T(1,128)S(1)}, u32[]{:S(2)}, u32[]{:S(2)}) collective-permute-start(f32[1,2112]{1,0:T(1,128)S(1)} %pad_maximum_fusion.4), channel_id=1, source_target_pairs={{0,16},{1,17},{2,18},{3,19},{4,20},{5,21},{6,22},{7,23},{8,24},{9,... | collective-permute-start | bytes 25352 | tf_op jit(solution)/shard_map/ppermute | solution.py:20
  8.8 5.4 %collective-permute-start.1 = (f32[1,1056]{1,0:T(1,128)S(1)}, f32[1,1056]{1,0:T(1,128)S(1)}, u32[]{:S(2)}, u32[]{:S(2)}) collective-permute-start(f32[1,1056]{1,0:T(1,128)S(1)} %pad_maximum_fusion.7), channel_id=1, source_target_pairs={{0,31},{1,0},{2,1},{3,2},{4,3},{5,4},{6,5},{7,6},{8,7},{9,8},{10,9... | collective-permute-start | bytes 12680 | tf_op jit(solution)/shard_map/ppermute | solution.py:20
  14.5 4.8 %collective-permute-start.3 = (f32[1,1056]{1,0:T(1,128)S(1)}, f32[1,1056]{1,0:T(1,128)S(1)}, u32[]{:S(2)}, u32[]{:S(2)}) collective-permute-start(f32[1,1056]{1,0:T(1,128)S(1)} %pad_maximum_fusion.9), channel_id=1, source_target_pairs={{0,28},{1,29},{2,30},{3,31},{4,0},{5,1},{6,2},{7,3},{8,4},{9,5},{1... | collective-permute-start | bytes 12680 | tf_op jit(solution)/shard_map/ppermute | solution.py:20
  31.9 4.6 %collective-permute-start.5 = (f32[17,64]{1,0:T(8,128)S(1)}, f32[17,64]{1,0:T(8,128)S(1)}, u32[]{:S(2)}, u32[]{:S(2)}) collective-permute-start(f32[17,64]{1,0:T(8,128)S(1)} %get-tuple-element.20), channel_id=1, source_target_pairs={{0,31},{1,0},{2,1},{3,2},{4,3},{5,4},{6,5},{7,6},{8,7},{9,8},{10,9... | collective-permute-start | bytes 13064 | tf_op jit(solution)/shard_map/ppermute | solution.py:20
  55.5 5.3 %collective-permute-start.18 = (f32[8,64]{1,0:T(8,128)S(1)}, f32[8,64]{1,0:T(8,128)S(1)}, u32[]{:S(2)}, u32[]{:S(2)}) collective-permute-start(f32[8,64]{1,0:T(8,128)S(1)} %get-tuple-element.70), channel_id=1, source_target_pairs={{0,31},{1,0},{2,1},{3,2},{4,3},{5,4},{6,5},{7,6},{8,7},{9,8},{10,9... | collective-permute-start | bytes 6152 | tf_op jit(solution)/shard_map/ppermute | solution.py:20
  60.8 4.7 %collective-permute-start.20 = (f32[8,64]{1,0:T(8,128)S(1)}, f32[8,64]{1,0:T(8,128)S(1)}, u32[]{:S(2)}, u32[]{:S(2)}) collective-permute-start(f32[8,64]{1,0:T(8,128)S(1)} %get-tuple-element.68), channel_id=1, source_target_pairs={{0,28},{1,29},{2,30},{3,31},{4,0},{5,1},{6,2},{7,3},{8,4},{9,5},{1... | collective-permute-start | bytes 6152 | tf_op jit(solution)/shard_map/ppermute | solution.py:20
  75.9 4.1 %collective-permute-done.23 = f32[8,64]{1,0:T(8,128)S(1)} collective-permute-done((f32[8,64]{1,0:T(8,128)S(1)}, f32[8,64]{1,0:T(8,128)S(1)}, u32[]{:S(2)}, u32[]{:S(2)}) %collective-permute-start.23) | collective-permute-done | bytes 2080 | tf_op jit(solution)/shard_map/ppermute | solution.py:20
  82.7 5.3 %collective-permute-start.28 = (f32[8,64]{1,0:T(8,128)S(1)}, f32[8,64]{1,0:T(8,128)S(1)}, u32[]{:S(2)}, u32[]{:S(2)}) collective-permute-start(f32[8,64]{1,0:T(8,128)S(1)} %get-tuple-element.66), channel_id=1, source_target_pairs={{0,31},{1,0},{2,1},{3,2},{4,3},{5,4},{6,5},{7,6},{8,7},{9,8},{10,9... | collective-permute-start | bytes 6152 | tf_op jit(solution)/shard_map/ppermute | solution.py:20
  88.0 4.7 %collective-permute-start.30 = (f32[8,64]{1,0:T(8,128)S(1)}, f32[8,64]{1,0:T(8,128)S(1)}, u32[]{:S(2)}, u32[]{:S(2)}) collective-permute-start(f32[8,64]{1,0:T(8,128)S(1)} %get-tuple-element.64), channel_id=1, source_target_pairs={{0,28},{1,29},{2,30},{3,31},{4,0},{5,1},{6,2},{7,3},{8,4},{9,5},{1... | collective-permute-start | bytes 6152 | tf_op jit(solution)/shard_map/ppermute | solution.py:20
  103.1 4.1 %collective-permute-done.33 = f32[8,64]{1,0:T(8,128)S(1)} collective-permute-done((f32[8,64]{1,0:T(8,128)S(1)}, f32[8,64]{1,0:T(8,128)S(1)}, u32[]{:S(2)}, u32[]{:S(2)}) %collective-permute-start.33) | collective-permute-done | bytes 2080 | tf_op jit(solution)/shard_map/ppermute | solution.py:20
  109.9 5.3 %collective-permute-start.38 = (f32[8,64]{1,0:T(8,128)S(1)}, f32[8,64]{1,0:T(8,128)S(1)}, u32[]{:S(2)}, u32[]{:S(2)}) collective-permute-start(f32[8,64]{1,0:T(8,128)S(1)} %get-tuple-element.62), channel_id=1, source_target_pairs={{0,31},{1,0},{2,1},{3,2},{4,3},{5,4},{6,5},{7,6},{8,7},{9,8},{10,9... | collective-permute-start | bytes 6152 | tf_op jit(solution)/shard_map/ppermute | solution.py:20
  115.3 4.7 %collective-permute-start.40 = (f32[8,64]{1,0:T(8,128)S(1)}, f32[8,64]{1,0:T(8,128)S(1)}, u32[]{:S(2)}, u32[]{:S(2)}) collective-permute-start(f32[8,64]{1,0:T(8,128)S(1)} %get-tuple-element.60), channel_id=1, source_target_pairs={{0,28},{1,29},{2,30},{3,31},{4,0},{5,1},{6,2},{7,3},{8,4},{9,5},{1... | collective-permute-start | bytes 6152 | tf_op jit(solution)/shard_map/ppermute | solution.py:20
  130.7 3.9 %collective-permute-done.43 = f32[8,64]{1,0:T(8,128)S(1)} collective-permute-done((f32[8,64]{1,0:T(8,128)S(1)}, f32[8,64]{1,0:T(8,128)S(1)}, u32[]{:S(2)}, u32[]{:S(2)}) %collective-permute-start.43) | collective-permute-done | bytes 2080 | tf_op jit(solution)/shard_map/ppermute | solution.py:20
  137.8 4.3 %collective-permute-start.47 = (f32[8,32]{1,0:T(8,128)S(1)}, f32[8,32]{1,0:T(8,128)S(1)}, u32[]{:S(2)}, u32[]{:S(2)}) collective-permute-start(f32[8,32]{1,0:T(8,128)S(1)} %get-tuple-element.48), channel_id=1, source_target_pairs={{0,31},{1,0},{2,1},{3,2},{4,3},{5,4},{6,5},{7,6},{8,7},{9,8},{10,9... | collective-permute-start | bytes 3080 | tf_op jit(solution)/shard_map/ppermute | solution.py:20
  144.1 4.6 %collective-permute-done.48 = f32[8,32]{1,0:T(8,128)S(1)} collective-permute-done((f32[8,32]{1,0:T(8,128)S(1)}, f32[8,32]{1,0:T(8,128)S(1)}, u32[]{:S(2)}, u32[]{:S(2)}) %collective-permute-start.48) | collective-permute-done | bytes 1056 | tf_op jit(solution)/shard_map/ppermute | solution.py:20
  149.4 6.3 %collective-permute-start.53 = (f32[8,32]{1,0:T(8,128)S(1)}, f32[8,32]{1,0:T(8,128)S(1)}, u32[]{:S(2)}, u32[]{:S(2)}) collective-permute-start(f32[8,32]{1,0:T(8,128)S(1)} %get-tuple-element.82), channel_id=1, source_target_pairs={{0,31},{1,0},{2,1},{3,2},{4,3},{5,4},{6,5},{7,6},{8,7},{9,8},{10,9... | collective-permute-start | bytes 3080 | tf_op jit(solution)/shard_map/ppermute | solution.py:20
  155.6 4.7 %collective-permute-start.55 = (f32[8,32]{1,0:T(8,128)S(1)}, f32[8,32]{1,0:T(8,128)S(1)}, u32[]{:S(2)}, u32[]{:S(2)}) collective-permute-start(f32[8,32]{1,0:T(8,128)S(1)} %get-tuple-element.80), channel_id=1, source_target_pairs={{0,28},{1,29},{2,30},{3,31},{4,0},{5,1},{6,2},{7,3},{8,4},{9,5},{1... | collective-permute-start | bytes 3080 | tf_op jit(solution)/shard_map/ppermute | solution.py:20
  168.8 4.1 %collective-permute-done.58 = f32[8,32]{1,0:T(8,128)S(1)} collective-permute-done((f32[8,32]{1,0:T(8,128)S(1)}, f32[8,32]{1,0:T(8,128)S(1)}, u32[]{:S(2)}, u32[]{:S(2)}) %collective-permute-start.58) | collective-permute-done | bytes 1056 | tf_op jit(solution)/shard_map/ppermute | solution.py:20
  175.5 5.3 %collective-permute-start.63 = (f32[8,32]{1,0:T(8,128)S(1)}, f32[8,32]{1,0:T(8,128)S(1)}, u32[]{:S(2)}, u32[]{:S(2)}) collective-permute-start(f32[8,32]{1,0:T(8,128)S(1)} %get-tuple-element.78), channel_id=1, source_target_pairs={{0,31},{1,0},{2,1},{3,2},{4,3},{5,4},{6,5},{7,6},{8,7},{9,8},{10,9... | collective-permute-start | bytes 3080 | tf_op jit(solution)/shard_map/ppermute | solution.py:20
  180.9 4.7 %collective-permute-start.65 = (f32[8,32]{1,0:T(8,128)S(1)}, f32[8,32]{1,0:T(8,128)S(1)}, u32[]{:S(2)}, u32[]{:S(2)}) collective-permute-start(f32[8,32]{1,0:T(8,128)S(1)} %get-tuple-element.76), channel_id=1, source_target_pairs={{0,28},{1,29},{2,30},{3,31},{4,0},{5,1},{6,2},{7,3},{8,4},{9,5},{1... | collective-permute-start | bytes 3080 | tf_op jit(solution)/shard_map/ppermute | solution.py:20
  191.1 5.3 %collective-permute-start.68 = (f32[8,64]{1,0:T(8,128)S(1)}, f32[8,64]{1,0:T(8,128)S(1)}, u32[]{:S(2)}, u32[]{:S(2)}) collective-permute-start(f32[8,64]{1,0:T(8,128)S(1)} %get-tuple-element.58), channel_id=1, source_target_pairs={{0,31},{1,0},{2,1},{3,2},{4,3},{5,4},{6,5},{7,6},{8,7},{9,8},{10,9... | collective-permute-start | bytes 6152 | tf_op jit(solution)/shard_map/ppermute | solution.py:20
  196.4 4.7 %collective-permute-start.70 = (f32[8,64]{1,0:T(8,128)S(1)}, f32[8,64]{1,0:T(8,128)S(1)}, u32[]{:S(2)}, u32[]{:S(2)}) collective-permute-start(f32[8,64]{1,0:T(8,128)S(1)} %get-tuple-element.56), channel_id=1, source_target_pairs={{0,28},{1,29},{2,30},{3,31},{4,0},{5,1},{6,2},{7,3},{8,4},{9,5},{1... | collective-permute-start | bytes 6152 | tf_op jit(solution)/shard_map/ppermute | solution.py:20
  213.2 3.4 %collective-permute-start.77 = (f32[2,24,24]{2,1,0:T(8,128)S(1)}, f32[2,24,24]{2,1,0:T(8,128)S(1)}, u32[]{:S(2)}, u32[]{:S(2)}) collective-permute-start(f32[2,24,24]{2,1,0:T(8,128)S(1)} %add_add_fusion.1), channel_id=1, source_target_pairs={{0,4},{1,5},{2,6},{3,7},{4,0},{5,1},{6,2},{7,3},{8,12},{9,13},{10,... | collective-permute-start | bytes 13832 | tf_op jit(solution)/shard_map/ppermute | solution.py:49
  219.4 4.1 %collective-permute-done.78 = f32[2,24,24]{2,1,0:T(8,128)S(1)} collective-permute-done((f32[2,24,24]{2,1,0:T(8,128)S(1)}, f32[2,24,24]{2,1,0:T(8,128)S(1)}, u32[]{:S(2)}, u32[]{:S(2)}) %collective-permute-start.78) | collective-permute-done | bytes 4640 | tf_op jit(solution)/shard_map/ppermute | solution.py:49
  (320 shorter events, 109.7 us)
Async XLA Ops:
  4.4 16.6 %collective-permute-start.4 = (f32[1,2112]{1,0:T(1,128)S(1)}, f32[1,2112]{1,0:T(1,128)S(1)}, u32[]{:S(2)}, u32[]{:S(2)}) collective-permute-start(f32[1,2112]{1,0:T(1,128)S(1)} %pad_maximum_fusion.4), channel_id=1, source_target_pairs={{0,16},{1,17},{2,18},{3,19},{4,20},{5,21},{6,22},{7,23},{8,24},{9,... | collective-permute-start | bytes 25352 | tf_op jit(solution)/shard_map/ppermute | solution.py:20
  8.7 10.9 %collective-permute-start = (f32[1,1056]{1,0:T(1,128)S(1)}, f32[1,1056]{1,0:T(1,128)S(1)}, u32[]{:S(2)}, u32[]{:S(2)}) collective-permute-start(f32[1,1056]{1,0:T(1,128)S(1)} %pad_maximum_fusion.6), channel_id=1, source_target_pairs={{0,1},{1,2},{2,3},{3,4},{4,5},{5,6},{6,7},{7,8},{8,9},{9,10},{10,1... | collective-permute-start | bytes 12680 | tf_op jit(solution)/shard_map/ppermute | solution.py:20
  8.8 10.8 %collective-permute-start.1 = (f32[1,1056]{1,0:T(1,128)S(1)}, f32[1,1056]{1,0:T(1,128)S(1)}, u32[]{:S(2)}, u32[]{:S(2)}) collective-permute-start(f32[1,1056]{1,0:T(1,128)S(1)} %pad_maximum_fusion.7), channel_id=1, source_target_pairs={{0,31},{1,0},{2,1},{3,2},{4,3},{5,4},{6,5},{7,6},{8,7},{9,8},{10,9... | collective-permute-start | bytes 12680 | tf_op jit(solution)/shard_map/ppermute | solution.py:20
  28.0 8.5 %collective-permute-start.10 = (f32[2,8]{1,0:T(2,128)S(1)}, f32[2,8]{1,0:T(2,128)S(1)}, u32[]{:S(2)}, u32[]{:S(2)}) collective-permute-start(f32[2,8]{1,0:T(2,128)S(1)} %pad_maximum_fusion.10), channel_id=1, source_target_pairs={{0,3},{1,2},{2,1},{3,0},{4,7},{5,6},{6,5},{7,4},{8,11},{9,10},{10,... | collective-permute-start | bytes 200 | tf_op jit(solution)/shard_map/ppermute | solution.py:49
  28.1 9.1 %collective-permute-start.11 = (f32[2,8]{1,0:T(2,128)S(1)}, f32[2,8]{1,0:T(2,128)S(1)}, u32[]{:S(2)}, u32[]{:S(2)}) collective-permute-start(f32[2,8]{1,0:T(2,128)S(1)} %pad_maximum_fusion.10), channel_id=1, source_target_pairs={{0,2},{1,3},{2,0},{3,1},{4,6},{5,7},{6,4},{7,5},{8,10},{9,11},{10,... | collective-permute-start | bytes 200 | tf_op jit(solution)/shard_map/ppermute | solution.py:49
  28.2 9.1 %collective-permute-start.12 = (f32[2,8]{1,0:T(2,128)S(1)}, f32[2,8]{1,0:T(2,128)S(1)}, u32[]{:S(2)}, u32[]{:S(2)}) collective-permute-start(f32[2,8]{1,0:T(2,128)S(1)} %pad_maximum_fusion.10), channel_id=1, source_target_pairs={{0,1},{1,0},{2,3},{3,2},{4,5},{5,4},{6,7},{7,6},{8,9},{9,8},{10,11... | collective-permute-start | bytes 200 | tf_op jit(solution)/shard_map/ppermute | solution.py:49
  31.9 18.1 %collective-permute-start.5 = (f32[17,64]{1,0:T(8,128)S(1)}, f32[17,64]{1,0:T(8,128)S(1)}, u32[]{:S(2)}, u32[]{:S(2)}) collective-permute-start(f32[17,64]{1,0:T(8,128)S(1)} %get-tuple-element.20), channel_id=1, source_target_pairs={{0,31},{1,0},{2,1},{3,2},{4,3},{5,4},{6,5},{7,6},{8,7},{9,8},{10,9... | collective-permute-start | bytes 13064 | tf_op jit(solution)/shard_map/ppermute | solution.py:20
  36.5 13.4 %collective-permute-start.6 = (f32[17,64]{1,0:T(8,128)S(1)}, f32[17,64]{1,0:T(8,128)S(1)}, u32[]{:S(2)}, u32[]{:S(2)}) collective-permute-start(f32[17,64]{1,0:T(8,128)S(1)} %get-tuple-element.19), channel_id=1, source_target_pairs={{0,1},{1,2},{2,3},{3,4},{4,5},{5,6},{6,7},{7,8},{8,9},{9,10},{10,1... | collective-permute-start | bytes 13064 | tf_op jit(solution)/shard_map/ppermute | solution.py:20
  36.5 13.4 %collective-permute-start.7 = (f32[17,64]{1,0:T(8,128)S(1)}, f32[17,64]{1,0:T(8,128)S(1)}, u32[]{:S(2)}, u32[]{:S(2)}) collective-permute-start(f32[17,64]{1,0:T(8,128)S(1)} %get-tuple-element.18), channel_id=1, source_target_pairs={{0,28},{1,29},{2,30},{3,31},{4,0},{5,1},{6,2},{7,3},{8,4},{9,5},{1... | collective-permute-start | bytes 13064 | tf_op jit(solution)/shard_map/ppermute | solution.py:20
  55.5 10.1 %collective-permute-start.17 = (f32[8,64]{1,0:T(8,128)S(1)}, f32[8,64]{1,0:T(8,128)S(1)}, u32[]{:S(2)}, u32[]{:S(2)}) collective-permute-start(f32[8,64]{1,0:T(8,128)S(1)} %get-tuple-element.71), channel_id=1, source_target_pairs={{0,1},{1,2},{2,3},{3,4},{4,5},{5,6},{6,7},{7,8},{8,9},{9,10},{10,1... | collective-permute-start | bytes 6152 | tf_op jit(solution)/shard_map/ppermute | solution.py:20
  55.5 10.1 %collective-permute-start.18 = (f32[8,64]{1,0:T(8,128)S(1)}, f32[8,64]{1,0:T(8,128)S(1)}, u32[]{:S(2)}, u32[]{:S(2)}) collective-permute-start(f32[8,64]{1,0:T(8,128)S(1)} %get-tuple-element.70), channel_id=1, source_target_pairs={{0,31},{1,0},{2,1},{3,2},{4,3},{5,4},{6,5},{7,6},{8,7},{9,8},{10,9... | collective-permute-start | bytes 6152 | tf_op jit(solution)/shard_map/ppermute | solution.py:20
  73.3 6.7 %collective-permute-start.23 = (f32[8,64]{1,0:T(8,128)S(1)}, f32[8,64]{1,0:T(8,128)S(1)}, u32[]{:S(2)}, u32[]{:S(2)}) collective-permute-start(f32[8,64]{1,0:T(8,128)S(1)} %get-tuple-element.31), channel_id=1, source_target_pairs={{0,1},{1,2},{2,3},{3,4},{4,5},{5,6},{6,7},{7,8},{8,9},{9,10},{10,1... | collective-permute-start | bytes 6152 | tf_op jit(solution)/shard_map/ppermute | solution.py:20
  82.7 10.2 %collective-permute-start.27 = (f32[8,64]{1,0:T(8,128)S(1)}, f32[8,64]{1,0:T(8,128)S(1)}, u32[]{:S(2)}, u32[]{:S(2)}) collective-permute-start(f32[8,64]{1,0:T(8,128)S(1)} %get-tuple-element.67), channel_id=1, source_target_pairs={{0,1},{1,2},{2,3},{3,4},{4,5},{5,6},{6,7},{7,8},{8,9},{9,10},{10,1... | collective-permute-start | bytes 6152 | tf_op jit(solution)/shard_map/ppermute | solution.py:20
  82.7 10.2 %collective-permute-start.28 = (f32[8,64]{1,0:T(8,128)S(1)}, f32[8,64]{1,0:T(8,128)S(1)}, u32[]{:S(2)}, u32[]{:S(2)}) collective-permute-start(f32[8,64]{1,0:T(8,128)S(1)} %get-tuple-element.66), channel_id=1, source_target_pairs={{0,31},{1,0},{2,1},{3,2},{4,3},{5,4},{6,5},{7,6},{8,7},{9,8},{10,9... | collective-permute-start | bytes 6152 | tf_op jit(solution)/shard_map/ppermute | solution.py:20
  100.5 6.7 %collective-permute-start.33 = (f32[8,64]{1,0:T(8,128)S(1)}, f32[8,64]{1,0:T(8,128)S(1)}, u32[]{:S(2)}, u32[]{:S(2)}) collective-permute-start(f32[8,64]{1,0:T(8,128)S(1)} %get-tuple-element.27), channel_id=1, source_target_pairs={{0,1},{1,2},{2,3},{3,4},{4,5},{5,6},{6,7},{7,8},{8,9},{9,10},{10,1... | collective-permute-start | bytes 6152 | tf_op jit(solution)/shard_map/ppermute | solution.py:20
  109.9 10.2 %collective-permute-start.37 = (f32[8,64]{1,0:T(8,128)S(1)}, f32[8,64]{1,0:T(8,128)S(1)}, u32[]{:S(2)}, u32[]{:S(2)}) collective-permute-start(f32[8,64]{1,0:T(8,128)S(1)} %get-tuple-element.63), channel_id=1, source_target_pairs={{0,1},{1,2},{2,3},{3,4},{4,5},{5,6},{6,7},{7,8},{8,9},{9,10},{10,1... | collective-permute-start | bytes 6152 | tf_op jit(solution)/shard_map/ppermute | solution.py:20
  109.9 10.2 %collective-permute-start.38 = (f32[8,64]{1,0:T(8,128)S(1)}, f32[8,64]{1,0:T(8,128)S(1)}, u32[]{:S(2)}, u32[]{:S(2)}) collective-permute-start(f32[8,64]{1,0:T(8,128)S(1)} %get-tuple-element.62), channel_id=1, source_target_pairs={{0,31},{1,0},{2,1},{3,2},{4,3},{5,4},{6,5},{7,6},{8,7},{9,8},{10,9... | collective-permute-start | bytes 6152 | tf_op jit(solution)/shard_map/ppermute | solution.py:20
  149.3 11.0 %collective-permute-start.52 = (f32[8,32]{1,0:T(8,128)S(1)}, f32[8,32]{1,0:T(8,128)S(1)}, u32[]{:S(2)}, u32[]{:S(2)}) collective-permute-start(f32[8,32]{1,0:T(8,128)S(1)} %get-tuple-element.83), channel_id=1, source_target_pairs={{0,1},{1,2},{2,3},{3,4},{4,5},{5,6},{6,7},{7,8},{8,9},{9,10},{10,1... | collective-permute-start | bytes 3080 | tf_op jit(solution)/shard_map/ppermute | solution.py:20
  149.4 11.0 %collective-permute-start.53 = (f32[8,32]{1,0:T(8,128)S(1)}, f32[8,32]{1,0:T(8,128)S(1)}, u32[]{:S(2)}, u32[]{:S(2)}) collective-permute-start(f32[8,32]{1,0:T(8,128)S(1)} %get-tuple-element.82), channel_id=1, source_target_pairs={{0,31},{1,0},{2,1},{3,2},{4,3},{5,4},{6,5},{7,6},{8,7},{9,8},{10,9... | collective-permute-start | bytes 3080 | tf_op jit(solution)/shard_map/ppermute | solution.py:20
  166.1 8.8 %collective-permute-start.61 = (f32[8,64]{1,0:T(8,128)S(1)}, f32[8,64]{1,0:T(8,128)S(1)}, u32[]{:S(2)}, u32[]{:S(2)}) collective-permute-start(f32[8,64]{1,0:T(8,128)S(1)} %concatenate.241), channel_id=1, source_target_pairs={{0,16},{1,17},{2,18},{3,19},{4,20},{5,21},{6,22},{7,23},{8,24},{9,... | collective-permute-start | bytes 6152 | tf_op jit(solution)/shard_map/ppermute | solution.py:20
  175.5 10.1 %collective-permute-start.62 = (f32[8,32]{1,0:T(8,128)S(1)}, f32[8,32]{1,0:T(8,128)S(1)}, u32[]{:S(2)}, u32[]{:S(2)}) collective-permute-start(f32[8,32]{1,0:T(8,128)S(1)} %get-tuple-element.79), channel_id=1, source_target_pairs={{0,1},{1,2},{2,3},{3,4},{4,5},{5,6},{6,7},{7,8},{8,9},{9,10},{10,1... | collective-permute-start | bytes 3080 | tf_op jit(solution)/shard_map/ppermute | solution.py:20
  175.5 10.1 %collective-permute-start.63 = (f32[8,32]{1,0:T(8,128)S(1)}, f32[8,32]{1,0:T(8,128)S(1)}, u32[]{:S(2)}, u32[]{:S(2)}) collective-permute-start(f32[8,32]{1,0:T(8,128)S(1)} %get-tuple-element.78), channel_id=1, source_target_pairs={{0,31},{1,0},{2,1},{3,2},{4,3},{5,4},{6,5},{7,6},{8,7},{9,8},{10,9... | collective-permute-start | bytes 3080 | tf_op jit(solution)/shard_map/ppermute | solution.py:20
  191.1 10.1 %collective-permute-start.67 = (f32[8,64]{1,0:T(8,128)S(1)}, f32[8,64]{1,0:T(8,128)S(1)}, u32[]{:S(2)}, u32[]{:S(2)}) collective-permute-start(f32[8,64]{1,0:T(8,128)S(1)} %get-tuple-element.59), channel_id=1, source_target_pairs={{0,1},{1,2},{2,3},{3,4},{4,5},{5,6},{6,7},{7,8},{8,9},{9,10},{10,1... | collective-permute-start | bytes 6152 | tf_op jit(solution)/shard_map/ppermute | solution.py:20
  191.1 10.1 %collective-permute-start.68 = (f32[8,64]{1,0:T(8,128)S(1)}, f32[8,64]{1,0:T(8,128)S(1)}, u32[]{:S(2)}, u32[]{:S(2)}) collective-permute-start(f32[8,64]{1,0:T(8,128)S(1)} %get-tuple-element.58), channel_id=1, source_target_pairs={{0,31},{1,0},{2,1},{3,2},{4,3},{5,4},{6,5},{7,6},{8,7},{9,8},{10,9... | collective-permute-start | bytes 6152 | tf_op jit(solution)/shard_map/ppermute | solution.py:20
  (63 other events, 388.7 us)

commit v9 on v8

--- a/solution.py
+++ b/solution.py
@@ -116,15 +116,15 @@
 
 def exchange(*groups):
     pieces, offsets, bounds = [], [], []
-    flat = len({piece.shape[0] for group_pieces, _ in groups for piece in group_pieces}) > 1
+    rows = max(piece.shape[0] for group_pieces, _ in groups for piece in group_pieces)
     for group_pieces, group_offsets in groups:
         bounds.append((len(pieces), len(group_pieces)))
-        pieces += [piece.reshape(1, -1) if flat else piece for piece in group_pieces]
+        pieces += [jnp.pad(piece, ((0, rows - piece.shape[0]), (0, 0))) for piece in group_pieces]
         offsets += group_offsets
     moved = shift_pieces(pieces, offsets)
     out = []
     for (start, count), (group_pieces, _) in zip(bounds, groups):
-        out.append([m.reshape(p.shape) for m, p in zip(moved[start : start + count], group_pieces)])
+        out.append([m[: p.shape[0]] for m, p in zip(moved[start : start + count], group_pieces)])
     return out
 
 

time: 224 us -> 224 us (level)
  no operation moved by 1% of the time
where the time goes in v9:
time: 224 us
  starting transfers between devices  112 us (50%)
  waiting for transfers between devices  75.5 us (34%)
  matrix products  22.5 us (10%)
  local copies, waits for them, and re-layouts  8.57 us (4%)
  other arithmetic  4.16 us (2%)
    ppermute x65, starting transfers between devices, from_behind(): lax.ppermute(shard, axis, [(i, (i + by) % length) for i in range(length)])  99 us
    ppermute x65, waiting for transfers between devices, from_behind(): lax.ppermute(shard, axis, [(i, (i + by) % length) for i in range(length)])  60.5 us
    ppermute x14, waiting for transfers between devices, all_sum(): lax.ppermute(value, 'dom', [(i, i ^ t << shift) for i in range(length)])  15 us
    ppermute x14, starting transfers between devices, all_sum(): lax.ppermute(value, 'dom', [(i, i ^ t << shift) for i in range(length)])  12.5 us
    dot_general x14, matrix products, gather_cols(): picked = jnp.einsum('rab,bn->ran', split, lo_hot_t, precision=precision)  10.8 us
    dot_general x14, matrix products, scatter_cols(): jnp.einsum('ran,nb->rab', spread, lo_hot, precision=lax.Precision.HIGH)  9.56 us
  transfers between devices with their start and end apart: 79, of which 32 were waited for; matrix products, arithmetic and copies ran while one was open for 2% of the time, Pallas kernels for 0%

profile of v9, /device:TPU:0, one launch (start us, length us, event | category | flops | bytes accessed | tf_op | source)
XLA Modules:
  0.0 223.9 jit_solution(11007547280525767453)
XLA Ops:
  5.0 4.0 %collective-permute-start.4 = (f32[16,192]{1,0:T(8,128)S(1)}, f32[16,192]{1,0:T(8,128)S(1)}, u32[]{:S(2)}, u32[]{:S(2)}) collective-permute-start(f32[16,192]{1,0:T(8,128)S(1)} %select_maximum_fusion.1), channel_id=1, source_target_pairs={{0,16},{1,17},{2,18},{3,19},{4,20},{5,21},{6,22},{7,23},{8,24},{9,... | collective-permute-start | bytes 36872 | tf_op jit(solution)/shard_map/ppermute | solution.py:20
  9.3 5.3 %collective-permute-start.1 = (f32[16,96]{1,0:T(8,128)S(1)}, f32[16,96]{1,0:T(8,128)S(1)}, u32[]{:S(2)}, u32[]{:S(2)}) collective-permute-start(f32[16,96]{1,0:T(8,128)S(1)} %select_maximum_fusion.5), channel_id=1, source_target_pairs={{0,31},{1,0},{2,1},{3,2},{4,3},{5,4},{6,5},{7,6},{8,7},{9,8},{10,9... | collective-permute-start | bytes 18440 | tf_op jit(solution)/shard_map/ppermute | solution.py:20
  14.8 4.7 %collective-permute-start.3 = (f32[16,96]{1,0:T(8,128)S(1)}, f32[16,96]{1,0:T(8,128)S(1)}, u32[]{:S(2)}, u32[]{:S(2)}) collective-permute-start(f32[16,96]{1,0:T(8,128)S(1)} %select_maximum_fusion.3), channel_id=1, source_target_pairs={{0,28},{1,29},{2,30},{3,31},{4,0},{5,1},{6,2},{7,3},{8,4},{9,5},{1... | collective-permute-start | bytes 18440 | tf_op jit(solution)/shard_map/ppermute | solution.py:20
  31.8 4.6 %collective-permute-start.5 = (f32[17,64]{1,0:T(8,128)S(1)}, f32[17,64]{1,0:T(8,128)S(1)}, u32[]{:S(2)}, u32[]{:S(2)}) collective-permute-start(f32[17,64]{1,0:T(8,128)S(1)} %get-tuple-element.18), channel_id=1, source_target_pairs={{0,31},{1,0},{2,1},{3,2},{4,3},{5,4},{6,5},{7,6},{8,7},{9,8},{10,9... | collective-permute-start | bytes 13064 | tf_op jit(solution)/shard_map/ppermute | solution.py:20
  55.3 5.3 %collective-permute-start.18 = (f32[8,64]{1,0:T(8,128)S(1)}, f32[8,64]{1,0:T(8,128)S(1)}, u32[]{:S(2)}, u32[]{:S(2)}) collective-permute-start(f32[8,64]{1,0:T(8,128)S(1)} %get-tuple-element.66), channel_id=1, source_target_pairs={{0,31},{1,0},{2,1},{3,2},{4,3},{5,4},{6,5},{7,6},{8,7},{9,8},{10,9... | collective-permute-start | bytes 6152 | tf_op jit(solution)/shard_map/ppermute | solution.py:20
  60.7 4.7 %collective-permute-start.20 = (f32[8,64]{1,0:T(8,128)S(1)}, f32[8,64]{1,0:T(8,128)S(1)}, u32[]{:S(2)}, u32[]{:S(2)}) collective-permute-start(f32[8,64]{1,0:T(8,128)S(1)} %get-tuple-element.64), channel_id=1, source_target_pairs={{0,28},{1,29},{2,30},{3,31},{4,0},{5,1},{6,2},{7,3},{8,4},{9,5},{1... | collective-permute-start | bytes 6152 | tf_op jit(solution)/shard_map/ppermute | solution.py:20
  75.8 4.1 %collective-permute-done.23 = f32[8,64]{1,0:T(8,128)S(1)} collective-permute-done((f32[8,64]{1,0:T(8,128)S(1)}, f32[8,64]{1,0:T(8,128)S(1)}, u32[]{:S(2)}, u32[]{:S(2)}) %collective-permute-start.23) | collective-permute-done | bytes 2080 | tf_op jit(solution)/shard_map/ppermute | solution.py:20
  82.6 5.3 %collective-permute-start.28 = (f32[8,64]{1,0:T(8,128)S(1)}, f32[8,64]{1,0:T(8,128)S(1)}, u32[]{:S(2)}, u32[]{:S(2)}) collective-permute-start(f32[8,64]{1,0:T(8,128)S(1)} %get-tuple-element.62), channel_id=1, source_target_pairs={{0,31},{1,0},{2,1},{3,2},{4,3},{5,4},{6,5},{7,6},{8,7},{9,8},{10,9... | collective-permute-start | bytes 6152 | tf_op jit(solution)/shard_map/ppermute | solution.py:20
  87.9 4.7 %collective-permute-start.30 = (f32[8,64]{1,0:T(8,128)S(1)}, f32[8,64]{1,0:T(8,128)S(1)}, u32[]{:S(2)}, u32[]{:S(2)}) collective-permute-start(f32[8,64]{1,0:T(8,128)S(1)} %get-tuple-element.60), channel_id=1, source_target_pairs={{0,28},{1,29},{2,30},{3,31},{4,0},{5,1},{6,2},{7,3},{8,4},{9,5},{1... | collective-permute-start | bytes 6152 | tf_op jit(solution)/shard_map/ppermute | solution.py:20
  103.0 4.1 %collective-permute-done.33 = f32[8,64]{1,0:T(8,128)S(1)} collective-permute-done((f32[8,64]{1,0:T(8,128)S(1)}, f32[8,64]{1,0:T(8,128)S(1)}, u32[]{:S(2)}, u32[]{:S(2)}) %collective-permute-start.33) | collective-permute-done | bytes 2080 | tf_op jit(solution)/shard_map/ppermute | solution.py:20
  109.8 5.3 %collective-permute-start.38 = (f32[8,64]{1,0:T(8,128)S(1)}, f32[8,64]{1,0:T(8,128)S(1)}, u32[]{:S(2)}, u32[]{:S(2)}) collective-permute-start(f32[8,64]{1,0:T(8,128)S(1)} %get-tuple-element.58), channel_id=1, source_target_pairs={{0,31},{1,0},{2,1},{3,2},{4,3},{5,4},{6,5},{7,6},{8,7},{9,8},{10,9... | collective-permute-start | bytes 6152 | tf_op jit(solution)/shard_map/ppermute | solution.py:20
  115.1 4.7 %collective-permute-start.40 = (f32[8,64]{1,0:T(8,128)S(1)}, f32[8,64]{1,0:T(8,128)S(1)}, u32[]{:S(2)}, u32[]{:S(2)}) collective-permute-start(f32[8,64]{1,0:T(8,128)S(1)} %get-tuple-element.56), channel_id=1, source_target_pairs={{0,28},{1,29},{2,30},{3,31},{4,0},{5,1},{6,2},{7,3},{8,4},{9,5},{1... | collective-permute-start | bytes 6152 | tf_op jit(solution)/shard_map/ppermute | solution.py:20
  130.6 3.9 %collective-permute-done.43 = f32[8,64]{1,0:T(8,128)S(1)} collective-permute-done((f32[8,64]{1,0:T(8,128)S(1)}, f32[8,64]{1,0:T(8,128)S(1)}, u32[]{:S(2)}, u32[]{:S(2)}) %collective-permute-start.43) | collective-permute-done | bytes 2080 | tf_op jit(solution)/shard_map/ppermute | solution.py:20
  137.6 4.3 %collective-permute-start.47 = (f32[8,32]{1,0:T(8,128)S(1)}, f32[8,32]{1,0:T(8,128)S(1)}, u32[]{:S(2)}, u32[]{:S(2)}) collective-permute-start(f32[8,32]{1,0:T(8,128)S(1)} %get-tuple-element.44), channel_id=1, source_target_pairs={{0,31},{1,0},{2,1},{3,2},{4,3},{5,4},{6,5},{7,6},{8,7},{9,8},{10,9... | collective-permute-start | bytes 3080 | tf_op jit(solution)/shard_map/ppermute | solution.py:20
  144.0 4.6 %collective-permute-done.48 = f32[8,32]{1,0:T(8,128)S(1)} collective-permute-done((f32[8,32]{1,0:T(8,128)S(1)}, f32[8,32]{1,0:T(8,128)S(1)}, u32[]{:S(2)}, u32[]{:S(2)}) %collective-permute-start.48) | collective-permute-done | bytes 1056 | tf_op jit(solution)/shard_map/ppermute | solution.py:20
  149.2 6.3 %collective-permute-start.53 = (f32[8,32]{1,0:T(8,128)S(1)}, f32[8,32]{1,0:T(8,128)S(1)}, u32[]{:S(2)}, u32[]{:S(2)}) collective-permute-start(f32[8,32]{1,0:T(8,128)S(1)} %get-tuple-element.78), channel_id=1, source_target_pairs={{0,31},{1,0},{2,1},{3,2},{4,3},{5,4},{6,5},{7,6},{8,7},{9,8},{10,9... | collective-permute-start | bytes 3080 | tf_op jit(solution)/shard_map/ppermute | solution.py:20
  155.5 4.7 %collective-permute-start.55 = (f32[8,32]{1,0:T(8,128)S(1)}, f32[8,32]{1,0:T(8,128)S(1)}, u32[]{:S(2)}, u32[]{:S(2)}) collective-permute-start(f32[8,32]{1,0:T(8,128)S(1)} %get-tuple-element.76), channel_id=1, source_target_pairs={{0,28},{1,29},{2,30},{3,31},{4,0},{5,1},{6,2},{7,3},{8,4},{9,5},{1... | collective-permute-start | bytes 3080 | tf_op jit(solution)/shard_map/ppermute | solution.py:20
  168.7 4.1 %collective-permute-done.58 = f32[8,32]{1,0:T(8,128)S(1)} collective-permute-done((f32[8,32]{1,0:T(8,128)S(1)}, f32[8,32]{1,0:T(8,128)S(1)}, u32[]{:S(2)}, u32[]{:S(2)}) %collective-permute-start.58) | collective-permute-done | bytes 1056 | tf_op jit(solution)/shard_map/ppermute | solution.py:20
  175.4 5.3 %collective-permute-start.63 = (f32[8,32]{1,0:T(8,128)S(1)}, f32[8,32]{1,0:T(8,128)S(1)}, u32[]{:S(2)}, u32[]{:S(2)}) collective-permute-start(f32[8,32]{1,0:T(8,128)S(1)} %get-tuple-element.74), channel_id=1, source_target_pairs={{0,31},{1,0},{2,1},{3,2},{4,3},{5,4},{6,5},{7,6},{8,7},{9,8},{10,9... | collective-permute-start | bytes 3080 | tf_op jit(solution)/shard_map/ppermute | solution.py:20
  180.7 4.7 %collective-permute-start.65 = (f32[8,32]{1,0:T(8,128)S(1)}, f32[8,32]{1,0:T(8,128)S(1)}, u32[]{:S(2)}, u32[]{:S(2)}) collective-permute-start(f32[8,32]{1,0:T(8,128)S(1)} %get-tuple-element.72), channel_id=1, source_target_pairs={{0,28},{1,29},{2,30},{3,31},{4,0},{5,1},{6,2},{7,3},{8,4},{9,5},{1... | collective-permute-start | bytes 3080 | tf_op jit(solution)/shard_map/ppermute | solution.py:20
  191.0 5.3 %collective-permute-start.68 = (f32[8,64]{1,0:T(8,128)S(1)}, f32[8,64]{1,0:T(8,128)S(1)}, u32[]{:S(2)}, u32[]{:S(2)}) collective-permute-start(f32[8,64]{1,0:T(8,128)S(1)} %get-tuple-element.54), channel_id=1, source_target_pairs={{0,31},{1,0},{2,1},{3,2},{4,3},{5,4},{6,5},{7,6},{8,7},{9,8},{10,9... | collective-permute-start | bytes 6152 | tf_op jit(solution)/shard_map/ppermute | solution.py:20
  196.3 4.7 %collective-permute-start.70 = (f32[8,64]{1,0:T(8,128)S(1)}, f32[8,64]{1,0:T(8,128)S(1)}, u32[]{:S(2)}, u32[]{:S(2)}) collective-permute-start(f32[8,64]{1,0:T(8,128)S(1)} %get-tuple-element.52), channel_id=1, source_target_pairs={{0,28},{1,29},{2,30},{3,31},{4,0},{5,1},{6,2},{7,3},{8,4},{9,5},{1... | collective-permute-start | bytes 6152 | tf_op jit(solution)/shard_map/ppermute | solution.py:20
  213.0 3.4 %collective-permute-start.77 = (f32[2,24,24]{2,1,0:T(8,128)S(1)}, f32[2,24,24]{2,1,0:T(8,128)S(1)}, u32[]{:S(2)}, u32[]{:S(2)}) collective-permute-start(f32[2,24,24]{2,1,0:T(8,128)S(1)} %add_add_fusion.1), channel_id=1, source_target_pairs={{0,4},{1,5},{2,6},{3,7},{4,0},{5,1},{6,2},{7,3},{8,12},{9,13},{10,... | collective-permute-start | bytes 13832 | tf_op jit(solution)/shard_map/ppermute | solution.py:49
  219.2 4.1 %collective-permute-done.78 = f32[2,24,24]{2,1,0:T(8,128)S(1)} collective-permute-done((f32[2,24,24]{2,1,0:T(8,128)S(1)}, f32[2,24,24]{2,1,0:T(8,128)S(1)}, u32[]{:S(2)}, u32[]{:S(2)}) %collective-permute-start.78) | collective-permute-done | bytes 4640 | tf_op jit(solution)/shard_map/ppermute | solution.py:49
  (302 shorter events, 109.8 us)
Async XLA Ops:
  5.0 14.9 %collective-permute-start.4 = (f32[16,192]{1,0:T(8,128)S(1)}, f32[16,192]{1,0:T(8,128)S(1)}, u32[]{:S(2)}, u32[]{:S(2)}) collective-permute-start(f32[16,192]{1,0:T(8,128)S(1)} %select_maximum_fusion.1), channel_id=1, source_target_pairs={{0,16},{1,17},{2,18},{3,19},{4,20},{5,21},{6,22},{7,23},{8,24},{9,... | collective-permute-start | bytes 36872 | tf_op jit(solution)/shard_map/ppermute | solution.py:20
  9.2 10.7 %collective-permute-start = (f32[16,96]{1,0:T(8,128)S(1)}, f32[16,96]{1,0:T(8,128)S(1)}, u32[]{:S(2)}, u32[]{:S(2)}) collective-permute-start(f32[16,96]{1,0:T(8,128)S(1)} %select_maximum_fusion.6), channel_id=1, source_target_pairs={{0,1},{1,2},{2,3},{3,4},{4,5},{5,6},{6,7},{7,8},{8,9},{9,10},{10,1... | collective-permute-start | bytes 18440 | tf_op jit(solution)/shard_map/ppermute | solution.py:20
  9.3 10.6 %collective-permute-start.1 = (f32[16,96]{1,0:T(8,128)S(1)}, f32[16,96]{1,0:T(8,128)S(1)}, u32[]{:S(2)}, u32[]{:S(2)}) collective-permute-start(f32[16,96]{1,0:T(8,128)S(1)} %select_maximum_fusion.5), channel_id=1, source_target_pairs={{0,31},{1,0},{2,1},{3,2},{4,3},{5,4},{6,5},{7,6},{8,7},{9,8},{10,9... | collective-permute-start | bytes 18440 | tf_op jit(solution)/shard_map/ppermute | solution.py:20
  27.9 8.5 %collective-permute-start.10 = (f32[2,8]{1,0:T(2,128)S(1)}, f32[2,8]{1,0:T(2,128)S(1)}, u32[]{:S(2)}, u32[]{:S(2)}) collective-permute-start(f32[2,8]{1,0:T(2,128)S(1)} %pad_maximum_fusion.5), channel_id=1, source_target_pairs={{0,3},{1,2},{2,1},{3,0},{4,7},{5,6},{6,5},{7,4},{8,11},{9,10},{10,... | collective-permute-start | bytes 200 | tf_op jit(solution)/shard_map/ppermute | solution.py:49
  28.0 9.1 %collective-permute-start.11 = (f32[2,8]{1,0:T(2,128)S(1)}, f32[2,8]{1,0:T(2,128)S(1)}, u32[]{:S(2)}, u32[]{:S(2)}) collective-permute-start(f32[2,8]{1,0:T(2,128)S(1)} %pad_maximum_fusion.5), channel_id=1, source_target_pairs={{0,2},{1,3},{2,0},{3,1},{4,6},{5,7},{6,4},{7,5},{8,10},{9,11},{10,... | collective-permute-start | bytes 200 | tf_op jit(solution)/shard_map/ppermute | solution.py:49
  28.1 9.0 %collective-permute-start.12 = (f32[2,8]{1,0:T(2,128)S(1)}, f32[2,8]{1,0:T(2,128)S(1)}, u32[]{:S(2)}, u32[]{:S(2)}) collective-permute-start(f32[2,8]{1,0:T(2,128)S(1)} %pad_maximum_fusion.5), channel_id=1, source_target_pairs={{0,1},{1,0},{2,3},{3,2},{4,5},{5,4},{6,7},{7,6},{8,9},{9,8},{10,11... | collective-permute-start | bytes 200 | tf_op jit(solution)/shard_map/ppermute | solution.py:49
  31.8 18.0 %collective-permute-start.5 = (f32[17,64]{1,0:T(8,128)S(1)}, f32[17,64]{1,0:T(8,128)S(1)}, u32[]{:S(2)}, u32[]{:S(2)}) collective-permute-start(f32[17,64]{1,0:T(8,128)S(1)} %get-tuple-element.18), channel_id=1, source_target_pairs={{0,31},{1,0},{2,1},{3,2},{4,3},{5,4},{6,5},{7,6},{8,7},{9,8},{10,9... | collective-permute-start | bytes 13064 | tf_op jit(solution)/shard_map/ppermute | solution.py:20
  36.4 13.4 %collective-permute-start.6 = (f32[17,64]{1,0:T(8,128)S(1)}, f32[17,64]{1,0:T(8,128)S(1)}, u32[]{:S(2)}, u32[]{:S(2)}) collective-permute-start(f32[17,64]{1,0:T(8,128)S(1)} %get-tuple-element.17), channel_id=1, source_target_pairs={{0,1},{1,2},{2,3},{3,4},{4,5},{5,6},{6,7},{7,8},{8,9},{9,10},{10,1... | collective-permute-start | bytes 13064 | tf_op jit(solution)/shard_map/ppermute | solution.py:20
  36.4 13.4 %collective-permute-start.7 = (f32[17,64]{1,0:T(8,128)S(1)}, f32[17,64]{1,0:T(8,128)S(1)}, u32[]{:S(2)}, u32[]{:S(2)}) collective-permute-start(f32[17,64]{1,0:T(8,128)S(1)} %get-tuple-element.16), channel_id=1, source_target_pairs={{0,28},{1,29},{2,30},{3,31},{4,0},{5,1},{6,2},{7,3},{8,4},{9,5},{1... | collective-permute-start | bytes 13064 | tf_op jit(solution)/shard_map/ppermute | solution.py:20
  55.3 10.1 %collective-permute-start.17 = (f32[8,64]{1,0:T(8,128)S(1)}, f32[8,64]{1,0:T(8,128)S(1)}, u32[]{:S(2)}, u32[]{:S(2)}) collective-permute-start(f32[8,64]{1,0:T(8,128)S(1)} %get-tuple-element.67), channel_id=1, source_target_pairs={{0,1},{1,2},{2,3},{3,4},{4,5},{5,6},{6,7},{7,8},{8,9},{9,10},{10,1... | collective-permute-start | bytes 6152 | tf_op jit(solution)/shard_map/ppermute | solution.py:20
  55.3 10.1 %collective-permute-start.18 = (f32[8,64]{1,0:T(8,128)S(1)}, f32[8,64]{1,0:T(8,128)S(1)}, u32[]{:S(2)}, u32[]{:S(2)}) collective-permute-start(f32[8,64]{1,0:T(8,128)S(1)} %get-tuple-element.66), channel_id=1, source_target_pairs={{0,31},{1,0},{2,1},{3,2},{4,3},{5,4},{6,5},{7,6},{8,7},{9,8},{10,9... | collective-permute-start | bytes 6152 | tf_op jit(solution)/shard_map/ppermute | solution.py:20
  73.2 6.7 %collective-permute-start.23 = (f32[8,64]{1,0:T(8,128)S(1)}, f32[8,64]{1,0:T(8,128)S(1)}, u32[]{:S(2)}, u32[]{:S(2)}) collective-permute-start(f32[8,64]{1,0:T(8,128)S(1)} %get-tuple-element.29), channel_id=1, source_target_pairs={{0,1},{1,2},{2,3},{3,4},{4,5},{5,6},{6,7},{7,8},{8,9},{9,10},{10,1... | collective-permute-start | bytes 6152 | tf_op jit(solution)/shard_map/ppermute | solution.py:20
  82.5 10.2 %collective-permute-start.27 = (f32[8,64]{1,0:T(8,128)S(1)}, f32[8,64]{1,0:T(8,128)S(1)}, u32[]{:S(2)}, u32[]{:S(2)}) collective-permute-start(f32[8,64]{1,0:T(8,128)S(1)} %get-tuple-element.63), channel_id=1, source_target_pairs={{0,1},{1,2},{2,3},{3,4},{4,5},{5,6},{6,7},{7,8},{8,9},{9,10},{10,1... | collective-permute-start | bytes 6152 | tf_op jit(solution)/shard_map/ppermute | solution.py:20
  82.6 10.2 %collective-permute-start.28 = (f32[8,64]{1,0:T(8,128)S(1)}, f32[8,64]{1,0:T(8,128)S(1)}, u32[]{:S(2)}, u32[]{:S(2)}) collective-permute-start(f32[8,64]{1,0:T(8,128)S(1)} %get-tuple-element.62), channel_id=1, source_target_pairs={{0,31},{1,0},{2,1},{3,2},{4,3},{5,4},{6,5},{7,6},{8,7},{9,8},{10,9... | collective-permute-start | bytes 6152 | tf_op jit(solution)/shard_map/ppermute | solution.py:20
  100.4 6.7 %collective-permute-start.33 = (f32[8,64]{1,0:T(8,128)S(1)}, f32[8,64]{1,0:T(8,128)S(1)}, u32[]{:S(2)}, u32[]{:S(2)}) collective-permute-start(f32[8,64]{1,0:T(8,128)S(1)} %get-tuple-element.25), channel_id=1, source_target_pairs={{0,1},{1,2},{2,3},{3,4},{4,5},{5,6},{6,7},{7,8},{8,9},{9,10},{10,1... | collective-permute-start | bytes 6152 | tf_op jit(solution)/shard_map/ppermute | solution.py:20
  109.8 10.5 %collective-permute-start.37 = (f32[8,64]{1,0:T(8,128)S(1)}, f32[8,64]{1,0:T(8,128)S(1)}, u32[]{:S(2)}, u32[]{:S(2)}) collective-permute-start(f32[8,64]{1,0:T(8,128)S(1)} %get-tuple-element.59), channel_id=1, source_target_pairs={{0,1},{1,2},{2,3},{3,4},{4,5},{5,6},{6,7},{7,8},{8,9},{9,10},{10,1... | collective-permute-start | bytes 6152 | tf_op jit(solution)/shard_map/ppermute | solution.py:20
  109.8 10.5 %collective-permute-start.38 = (f32[8,64]{1,0:T(8,128)S(1)}, f32[8,64]{1,0:T(8,128)S(1)}, u32[]{:S(2)}, u32[]{:S(2)}) collective-permute-start(f32[8,64]{1,0:T(8,128)S(1)} %get-tuple-element.58), channel_id=1, source_target_pairs={{0,31},{1,0},{2,1},{3,2},{4,3},{5,4},{6,5},{7,6},{8,7},{9,8},{10,9... | collective-permute-start | bytes 6152 | tf_op jit(solution)/shard_map/ppermute | solution.py:20
  149.2 11.0 %collective-permute-start.52 = (f32[8,32]{1,0:T(8,128)S(1)}, f32[8,32]{1,0:T(8,128)S(1)}, u32[]{:S(2)}, u32[]{:S(2)}) collective-permute-start(f32[8,32]{1,0:T(8,128)S(1)} %get-tuple-element.79), channel_id=1, source_target_pairs={{0,1},{1,2},{2,3},{3,4},{4,5},{5,6},{6,7},{7,8},{8,9},{9,10},{10,1... | collective-permute-start | bytes 3080 | tf_op jit(solution)/shard_map/ppermute | solution.py:20
  149.2 11.0 %collective-permute-start.53 = (f32[8,32]{1,0:T(8,128)S(1)}, f32[8,32]{1,0:T(8,128)S(1)}, u32[]{:S(2)}, u32[]{:S(2)}) collective-permute-start(f32[8,32]{1,0:T(8,128)S(1)} %get-tuple-element.78), channel_id=1, source_target_pairs={{0,31},{1,0},{2,1},{3,2},{4,3},{5,4},{6,5},{7,6},{8,7},{9,8},{10,9... | collective-permute-start | bytes 3080 | tf_op jit(solution)/shard_map/ppermute | solution.py:20
  166.0 8.8 %collective-permute-start.61 = (f32[8,64]{1,0:T(8,128)S(1)}, f32[8,64]{1,0:T(8,128)S(1)}, u32[]{:S(2)}, u32[]{:S(2)}) collective-permute-start(f32[8,64]{1,0:T(8,128)S(1)} %concatenate.242), channel_id=1, source_target_pairs={{0,16},{1,17},{2,18},{3,19},{4,20},{5,21},{6,22},{7,23},{8,24},{9,... | collective-permute-start | bytes 6152 | tf_op jit(solution)/shard_map/ppermute | solution.py:20
  175.4 10.1 %collective-permute-start.62 = (f32[8,32]{1,0:T(8,128)S(1)}, f32[8,32]{1,0:T(8,128)S(1)}, u32[]{:S(2)}, u32[]{:S(2)}) collective-permute-start(f32[8,32]{1,0:T(8,128)S(1)} %get-tuple-element.75), channel_id=1, source_target_pairs={{0,1},{1,2},{2,3},{3,4},{4,5},{5,6},{6,7},{7,8},{8,9},{9,10},{10,1... | collective-permute-start | bytes 3080 | tf_op jit(solution)/shard_map/ppermute | solution.py:20
  175.4 10.1 %collective-permute-start.63 = (f32[8,32]{1,0:T(8,128)S(1)}, f32[8,32]{1,0:T(8,128)S(1)}, u32[]{:S(2)}, u32[]{:S(2)}) collective-permute-start(f32[8,32]{1,0:T(8,128)S(1)} %get-tuple-element.74), channel_id=1, source_target_pairs={{0,31},{1,0},{2,1},{3,2},{4,3},{5,4},{6,5},{7,6},{8,7},{9,8},{10,9... | collective-permute-start | bytes 3080 | tf_op jit(solution)/shard_map/ppermute | solution.py:20
  190.9 10.1 %collective-permute-start.67 = (f32[8,64]{1,0:T(8,128)S(1)}, f32[8,64]{1,0:T(8,128)S(1)}, u32[]{:S(2)}, u32[]{:S(2)}) collective-permute-start(f32[8,64]{1,0:T(8,128)S(1)} %get-tuple-element.55), channel_id=1, source_target_pairs={{0,1},{1,2},{2,3},{3,4},{4,5},{5,6},{6,7},{7,8},{8,9},{9,10},{10,1... | collective-permute-start | bytes 6152 | tf_op jit(solution)/shard_map/ppermute | solution.py:20
  191.0 10.1 %collective-permute-start.68 = (f32[8,64]{1,0:T(8,128)S(1)}, f32[8,64]{1,0:T(8,128)S(1)}, u32[]{:S(2)}, u32[]{:S(2)}) collective-permute-start(f32[8,64]{1,0:T(8,128)S(1)} %get-tuple-element.54), channel_id=1, source_target_pairs={{0,31},{1,0},{2,1},{3,2},{4,3},{5,4},{6,5},{7,6},{8,7},{9,8},{10,9... | collective-permute-start | bytes 6152 | tf_op jit(solution)/shard_map/ppermute | solution.py:20
  (62 other events, 386.1 us)

commit v10 on v9

--- a/solution.py
+++ b/solution.py
@@ -193,8 +193,11 @@
 
     pair = jnp.concatenate([x_block, p_block], axis=0)
     node_diag_local = scatter_cols(jnp.einsum("jje->je", node_elem).reshape(1, -1), node_table)
+    x_out, edge_offsets = extend_pieces(x_block, send_edge_table)
+    p_out, _ = extend_pieces(p_block, send_edge_table)
+    pair_out = [jnp.concatenate([a, b], axis=0) for a, b in zip(x_out, p_out)]
     pair_moved, node_diag_moved = exchange(
-        extend_pieces(pair, send_edge_table), give_back_pieces(node_diag_local, send_node_table)
+        (pair_out, edge_offsets), give_back_pieces(node_diag_local, send_node_table)
     )
     pair_values = gather_cols(extend_finish(pair, pair_moved), edge_table, highest).reshape(
         2 * modes, edofs, elements

time: 224 us -> 224 us (level)
  waiting for transfers between devices: 75.5 us -> 72.9 us
  local copies, waits for them, and re-layouts: 8.57 us -> 6.29 us
    dot_general x14 -> x15, matrix products: 10.8 us -> 12.6 us  [gather_cols(): picked = jnp.einsum('rab,bn->ran', split, lo_hot_t, precision=precision)]
  transfers between devices with their start and end apart: 79 -> 79, of which waited for: 32 -> 33; matrix products, arithmetic and copies ran while one was open for 2% -> 2% of each run, Pallas kernels for 0% -> 0%
where the time goes in v10:
time: 224 us
  starting transfers between devices  114 us (51%)
  waiting for transfers between devices  72.9 us (33%)
  matrix products  24.4 us (11%)
  local copies, waits for them, and re-layouts  6.29 us (3%)
  other arithmetic  4.17 us (2%)
    ppermute x65, starting transfers between devices, from_behind(): lax.ppermute(shard, axis, [(i, (i + by) % length) for i in range(length)])  100 us
    ppermute x65, waiting for transfers between devices, from_behind(): lax.ppermute(shard, axis, [(i, (i + by) % length) for i in range(length)])  59.9 us
    ppermute x14, starting transfers between devices, all_sum(): lax.ppermute(value, 'dom', [(i, i ^ t << shift) for i in range(length)])  13.9 us
    ppermute x14, waiting for transfers between devices, all_sum(): lax.ppermute(value, 'dom', [(i, i ^ t << shift) for i in range(length)])  13 us
    dot_general x15, matrix products, gather_cols(): picked = jnp.einsum('rab,bn->ran', split, lo_hot_t, precision=precision)  12.6 us
    dot_general x14, matrix products, scatter_cols(): jnp.einsum('ran,nb->rab', spread, lo_hot, precision=lax.Precision.HIGH)  9.55 us
  transfers between devices with their start and end apart: 79, of which 33 were waited for; matrix products, arithmetic and copies ran while one was open for 2% of the time, Pallas kernels for 0%

profile of v10, /device:TPU:0, one launch (start us, length us, event | category | flops | bytes accessed | tf_op | source)
XLA Modules:
  0.0 223.7 jit_solution(693437652609686882)
XLA Ops:
  4.6 4.0 %collective-permute-start.4 = (f32[16,192]{1,0:T(8,128)S(1)}, f32[16,192]{1,0:T(8,128)S(1)}, u32[]{:S(2)}, u32[]{:S(2)}) collective-permute-start(f32[16,192]{1,0:T(8,128)S(1)} %select_maximum_fusion.1), channel_id=1, source_target_pairs={{0,16},{1,17},{2,18},{3,19},{4,20},{5,21},{6,22},{7,23},{8,24},{9,... | collective-permute-start | bytes 36872 | tf_op jit(solution)/shard_map/ppermute | solution.py:20
  13.7 5.3 %collective-permute-start.1 = (f32[16,96]{1,0:T(8,128)S(1)}, f32[16,96]{1,0:T(8,128)S(1)}, u32[]{:S(2)}, u32[]{:S(2)}) collective-permute-start(f32[16,96]{1,0:T(8,128)S(1)} %select_maximum_fusion.5), channel_id=1, source_target_pairs={{0,31},{1,0},{2,1},{3,2},{4,3},{5,4},{6,5},{7,6},{8,7},{9,8},{10,9... | collective-permute-start | bytes 18440 | tf_op jit(solution)/shard_map/ppermute | solution.py:20
  31.1 5.6 %collective-permute-start.5 = (f32[17,64]{1,0:T(8,128)S(1)}, f32[17,64]{1,0:T(8,128)S(1)}, u32[]{:S(2)}, u32[]{:S(2)}) collective-permute-start(f32[17,64]{1,0:T(8,128)S(1)} %get-tuple-element.18), channel_id=1, source_target_pairs={{0,31},{1,0},{2,1},{3,2},{4,3},{5,4},{6,5},{7,6},{8,7},{9,8},{10,9... | collective-permute-start | bytes 13064 | tf_op jit(solution)/shard_map/ppermute | solution.py:20
  36.9 3.4 %collective-permute-start.14 = (f32[2,8]{1,0:T(2,128)S(1)}, f32[2,8]{1,0:T(2,128)S(1)}, u32[]{:S(2)}, u32[]{:S(2)}) collective-permute-start(f32[2,8]{1,0:T(2,128)S(1)} %add_add_fusion.3), channel_id=1, source_target_pairs={{0,8},{1,9},{2,10},{3,11},{4,12},{5,13},{6,14},{7,15},{8,0},{9,1},... | collective-permute-start | bytes 200 | tf_op jit(solution)/shard_map/ppermute | solution.py:49
  55.1 5.3 %collective-permute-start.18 = (f32[8,64]{1,0:T(8,128)S(1)}, f32[8,64]{1,0:T(8,128)S(1)}, u32[]{:S(2)}, u32[]{:S(2)}) collective-permute-start(f32[8,64]{1,0:T(8,128)S(1)} %get-tuple-element.62), channel_id=1, source_target_pairs={{0,31},{1,0},{2,1},{3,2},{4,3},{5,4},{6,5},{7,6},{8,7},{9,8},{10,9... | collective-permute-start | bytes 6152 | tf_op jit(solution)/shard_map/ppermute | solution.py:20
  60.5 4.7 %collective-permute-start.20 = (f32[8,64]{1,0:T(8,128)S(1)}, f32[8,64]{1,0:T(8,128)S(1)}, u32[]{:S(2)}, u32[]{:S(2)}) collective-permute-start(f32[8,64]{1,0:T(8,128)S(1)} %get-tuple-element.60), channel_id=1, source_target_pairs={{0,28},{1,29},{2,30},{3,31},{4,0},{5,1},{6,2},{7,3},{8,4},{9,5},{1... | collective-permute-start | bytes 6152 | tf_op jit(solution)/shard_map/ppermute | solution.py:20
  75.6 4.1 %collective-permute-done.23 = f32[8,64]{1,0:T(8,128)S(1)} collective-permute-done((f32[8,64]{1,0:T(8,128)S(1)}, f32[8,64]{1,0:T(8,128)S(1)}, u32[]{:S(2)}, u32[]{:S(2)}) %collective-permute-start.23) | collective-permute-done | bytes 2080 | tf_op jit(solution)/shard_map/ppermute | solution.py:20
  82.3 5.3 %collective-permute-start.28 = (f32[8,64]{1,0:T(8,128)S(1)}, f32[8,64]{1,0:T(8,128)S(1)}, u32[]{:S(2)}, u32[]{:S(2)}) collective-permute-start(f32[8,64]{1,0:T(8,128)S(1)} %get-tuple-element.58), channel_id=1, source_target_pairs={{0,31},{1,0},{2,1},{3,2},{4,3},{5,4},{6,5},{7,6},{8,7},{9,8},{10,9... | collective-permute-start | bytes 6152 | tf_op jit(solution)/shard_map/ppermute | solution.py:20
  87.7 4.7 %collective-permute-start.30 = (f32[8,64]{1,0:T(8,128)S(1)}, f32[8,64]{1,0:T(8,128)S(1)}, u32[]{:S(2)}, u32[]{:S(2)}) collective-permute-start(f32[8,64]{1,0:T(8,128)S(1)} %get-tuple-element.56), channel_id=1, source_target_pairs={{0,28},{1,29},{2,30},{3,31},{4,0},{5,1},{6,2},{7,3},{8,4},{9,5},{1... | collective-permute-start | bytes 6152 | tf_op jit(solution)/shard_map/ppermute | solution.py:20
  102.8 4.1 %collective-permute-done.33 = f32[8,64]{1,0:T(8,128)S(1)} collective-permute-done((f32[8,64]{1,0:T(8,128)S(1)}, f32[8,64]{1,0:T(8,128)S(1)}, u32[]{:S(2)}, u32[]{:S(2)}) %collective-permute-start.33) | collective-permute-done | bytes 2080 | tf_op jit(solution)/shard_map/ppermute | solution.py:20
  109.6 5.3 %collective-permute-start.38 = (f32[8,64]{1,0:T(8,128)S(1)}, f32[8,64]{1,0:T(8,128)S(1)}, u32[]{:S(2)}, u32[]{:S(2)}) collective-permute-start(f32[8,64]{1,0:T(8,128)S(1)} %get-tuple-element.54), channel_id=1, source_target_pairs={{0,31},{1,0},{2,1},{3,2},{4,3},{5,4},{6,5},{7,6},{8,7},{9,8},{10,9... | collective-permute-start | bytes 6152 | tf_op jit(solution)/shard_map/ppermute | solution.py:20
  114.9 4.7 %collective-permute-start.40 = (f32[8,64]{1,0:T(8,128)S(1)}, f32[8,64]{1,0:T(8,128)S(1)}, u32[]{:S(2)}, u32[]{:S(2)}) collective-permute-start(f32[8,64]{1,0:T(8,128)S(1)} %get-tuple-element.52), channel_id=1, source_target_pairs={{0,28},{1,29},{2,30},{3,31},{4,0},{5,1},{6,2},{7,3},{8,4},{9,5},{1... | collective-permute-start | bytes 6152 | tf_op jit(solution)/shard_map/ppermute | solution.py:20
  130.4 3.9 %collective-permute-done.43 = f32[8,64]{1,0:T(8,128)S(1)} collective-permute-done((f32[8,64]{1,0:T(8,128)S(1)}, f32[8,64]{1,0:T(8,128)S(1)}, u32[]{:S(2)}, u32[]{:S(2)}) %collective-permute-start.43) | collective-permute-done | bytes 2080 | tf_op jit(solution)/shard_map/ppermute | solution.py:20
  137.4 4.3 %collective-permute-start.47 = (f32[8,32]{1,0:T(8,128)S(1)}, f32[8,32]{1,0:T(8,128)S(1)}, u32[]{:S(2)}, u32[]{:S(2)}) collective-permute-start(f32[8,32]{1,0:T(8,128)S(1)} %get-tuple-element.40), channel_id=1, source_target_pairs={{0,31},{1,0},{2,1},{3,2},{4,3},{5,4},{6,5},{7,6},{8,7},{9,8},{10,9... | collective-permute-start | bytes 3080 | tf_op jit(solution)/shard_map/ppermute | solution.py:20
  143.8 4.6 %collective-permute-done.48 = f32[8,32]{1,0:T(8,128)S(1)} collective-permute-done((f32[8,32]{1,0:T(8,128)S(1)}, f32[8,32]{1,0:T(8,128)S(1)}, u32[]{:S(2)}, u32[]{:S(2)}) %collective-permute-start.48) | collective-permute-done | bytes 1056 | tf_op jit(solution)/shard_map/ppermute | solution.py:20
  149.0 6.3 %collective-permute-start.53 = (f32[8,32]{1,0:T(8,128)S(1)}, f32[8,32]{1,0:T(8,128)S(1)}, u32[]{:S(2)}, u32[]{:S(2)}) collective-permute-start(f32[8,32]{1,0:T(8,128)S(1)} %get-tuple-element.86), channel_id=1, source_target_pairs={{0,31},{1,0},{2,1},{3,2},{4,3},{5,4},{6,5},{7,6},{8,7},{9,8},{10,9... | collective-permute-start | bytes 3080 | tf_op jit(solution)/shard_map/ppermute | solution.py:20
  155.3 4.7 %collective-permute-start.55 = (f32[8,32]{1,0:T(8,128)S(1)}, f32[8,32]{1,0:T(8,128)S(1)}, u32[]{:S(2)}, u32[]{:S(2)}) collective-permute-start(f32[8,32]{1,0:T(8,128)S(1)} %get-tuple-element.84), channel_id=1, source_target_pairs={{0,28},{1,29},{2,30},{3,31},{4,0},{5,1},{6,2},{7,3},{8,4},{9,5},{1... | collective-permute-start | bytes 3080 | tf_op jit(solution)/shard_map/ppermute | solution.py:20
  168.5 4.1 %collective-permute-done.58 = f32[8,32]{1,0:T(8,128)S(1)} collective-permute-done((f32[8,32]{1,0:T(8,128)S(1)}, f32[8,32]{1,0:T(8,128)S(1)}, u32[]{:S(2)}, u32[]{:S(2)}) %collective-permute-start.58) | collective-permute-done | bytes 1056 | tf_op jit(solution)/shard_map/ppermute | solution.py:20
  175.2 5.3 %collective-permute-start.63 = (f32[8,32]{1,0:T(8,128)S(1)}, f32[8,32]{1,0:T(8,128)S(1)}, u32[]{:S(2)}, u32[]{:S(2)}) collective-permute-start(f32[8,32]{1,0:T(8,128)S(1)} %get-tuple-element.82), channel_id=1, source_target_pairs={{0,31},{1,0},{2,1},{3,2},{4,3},{5,4},{6,5},{7,6},{8,7},{9,8},{10,9... | collective-permute-start | bytes 3080 | tf_op jit(solution)/shard_map/ppermute | solution.py:20
  180.5 4.7 %collective-permute-start.65 = (f32[8,32]{1,0:T(8,128)S(1)}, f32[8,32]{1,0:T(8,128)S(1)}, u32[]{:S(2)}, u32[]{:S(2)}) collective-permute-start(f32[8,32]{1,0:T(8,128)S(1)} %get-tuple-element.80), channel_id=1, source_target_pairs={{0,28},{1,29},{2,30},{3,31},{4,0},{5,1},{6,2},{7,3},{8,4},{9,5},{1... | collective-permute-start | bytes 3080 | tf_op jit(solution)/shard_map/ppermute | solution.py:20
  190.7 5.3 %collective-permute-start.68 = (f32[8,64]{1,0:T(8,128)S(1)}, f32[8,64]{1,0:T(8,128)S(1)}, u32[]{:S(2)}, u32[]{:S(2)}) collective-permute-start(f32[8,64]{1,0:T(8,128)S(1)} %get-tuple-element.50), channel_id=1, source_target_pairs={{0,31},{1,0},{2,1},{3,2},{4,3},{5,4},{6,5},{7,6},{8,7},{9,8},{10,9... | collective-permute-start | bytes 6152 | tf_op jit(solution)/shard_map/ppermute | solution.py:20
  196.1 4.7 %collective-permute-start.70 = (f32[8,64]{1,0:T(8,128)S(1)}, f32[8,64]{1,0:T(8,128)S(1)}, u32[]{:S(2)}, u32[]{:S(2)}) collective-permute-start(f32[8,64]{1,0:T(8,128)S(1)} %get-tuple-element.48), channel_id=1, source_target_pairs={{0,28},{1,29},{2,30},{3,31},{4,0},{5,1},{6,2},{7,3},{8,4},{9,5},{1... | collective-permute-start | bytes 6152 | tf_op jit(solution)/shard_map/ppermute | solution.py:20
  212.8 3.4 %collective-permute-start.77 = (f32[2,24,24]{2,1,0:T(8,128)S(1)}, f32[2,24,24]{2,1,0:T(8,128)S(1)}, u32[]{:S(2)}, u32[]{:S(2)}) collective-permute-start(f32[2,24,24]{2,1,0:T(8,128)S(1)} %add_add_fusion.1), channel_id=1, source_target_pairs={{0,4},{1,5},{2,6},{3,7},{4,0},{5,1},{6,2},{7,3},{8,12},{9,13},{10,... | collective-permute-start | bytes 13832 | tf_op jit(solution)/shard_map/ppermute | solution.py:49
  219.0 4.1 %collective-permute-done.78 = f32[2,24,24]{2,1,0:T(8,128)S(1)} collective-permute-done((f32[2,24,24]{2,1,0:T(8,128)S(1)}, f32[2,24,24]{2,1,0:T(8,128)S(1)}, u32[]{:S(2)}, u32[]{:S(2)}) %collective-permute-start.78) | collective-permute-done | bytes 4640 | tf_op jit(solution)/shard_map/ppermute | solution.py:49
  (308 shorter events, 109.8 us)
Async XLA Ops:
  4.6 14.8 %collective-permute-start.4 = (f32[16,192]{1,0:T(8,128)S(1)}, f32[16,192]{1,0:T(8,128)S(1)}, u32[]{:S(2)}, u32[]{:S(2)}) collective-permute-start(f32[16,192]{1,0:T(8,128)S(1)} %select_maximum_fusion.1), channel_id=1, source_target_pairs={{0,16},{1,17},{2,18},{3,19},{4,20},{5,21},{6,22},{7,23},{8,24},{9,... | collective-permute-start | bytes 36872 | tf_op jit(solution)/shard_map/ppermute | solution.py:20
  8.8 10.7 %collective-permute-start.2 = (f32[16,96]{1,0:T(8,128)S(1)}, f32[16,96]{1,0:T(8,128)S(1)}, u32[]{:S(2)}, u32[]{:S(2)}) collective-permute-start(f32[16,96]{1,0:T(8,128)S(1)} %select_maximum_fusion.4), channel_id=1, source_target_pairs={{0,4},{1,5},{2,6},{3,7},{4,8},{5,9},{6,10},{7,11},{8,12},{9,13},{1... | collective-permute-start | bytes 18440 | tf_op jit(solution)/shard_map/ppermute | solution.py:20
  10.4 9.2 %collective-permute-start.3 = (f32[16,96]{1,0:T(8,128)S(1)}, f32[16,96]{1,0:T(8,128)S(1)}, u32[]{:S(2)}, u32[]{:S(2)}) collective-permute-start(f32[16,96]{1,0:T(8,128)S(1)} %select_maximum_fusion.3), channel_id=1, source_target_pairs={{0,28},{1,29},{2,30},{3,31},{4,0},{5,1},{6,2},{7,3},{8,4},{9,5},{1... | collective-permute-start | bytes 18440 | tf_op jit(solution)/shard_map/ppermute | solution.py:20
  13.7 6.7 %collective-permute-start.1 = (f32[16,96]{1,0:T(8,128)S(1)}, f32[16,96]{1,0:T(8,128)S(1)}, u32[]{:S(2)}, u32[]{:S(2)}) collective-permute-start(f32[16,96]{1,0:T(8,128)S(1)} %select_maximum_fusion.5), channel_id=1, source_target_pairs={{0,31},{1,0},{2,1},{3,2},{4,3},{5,4},{6,5},{7,6},{8,7},{9,8},{10,9... | collective-permute-start | bytes 18440 | tf_op jit(solution)/shard_map/ppermute | solution.py:20
  27.3 9.5 %collective-permute-start.10 = (f32[2,8]{1,0:T(2,128)S(1)}, f32[2,8]{1,0:T(2,128)S(1)}, u32[]{:S(2)}, u32[]{:S(2)}) collective-permute-start(f32[2,8]{1,0:T(2,128)S(1)} %pad_maximum_fusion.6), channel_id=1, source_target_pairs={{0,3},{1,2},{2,1},{3,0},{4,7},{5,6},{6,5},{7,4},{8,11},{9,10},{10,... | collective-permute-start | bytes 200 | tf_op jit(solution)/shard_map/ppermute | solution.py:49
  27.4 9.4 %collective-permute-start.11 = (f32[2,8]{1,0:T(2,128)S(1)}, f32[2,8]{1,0:T(2,128)S(1)}, u32[]{:S(2)}, u32[]{:S(2)}) collective-permute-start(f32[2,8]{1,0:T(2,128)S(1)} %pad_maximum_fusion.6), channel_id=1, source_target_pairs={{0,2},{1,3},{2,0},{3,1},{4,6},{5,7},{6,4},{7,5},{8,10},{9,11},{10,... | collective-permute-start | bytes 200 | tf_op jit(solution)/shard_map/ppermute | solution.py:49
  27.4 9.3 %collective-permute-start.12 = (f32[2,8]{1,0:T(2,128)S(1)}, f32[2,8]{1,0:T(2,128)S(1)}, u32[]{:S(2)}, u32[]{:S(2)}) collective-permute-start(f32[2,8]{1,0:T(2,128)S(1)} %pad_maximum_fusion.6), channel_id=1, source_target_pairs={{0,1},{1,0},{2,3},{3,2},{4,5},{5,4},{6,7},{7,6},{8,9},{9,8},{10,11... | collective-permute-start | bytes 200 | tf_op jit(solution)/shard_map/ppermute | solution.py:49
  31.1 18.8 %collective-permute-start.5 = (f32[17,64]{1,0:T(8,128)S(1)}, f32[17,64]{1,0:T(8,128)S(1)}, u32[]{:S(2)}, u32[]{:S(2)}) collective-permute-start(f32[17,64]{1,0:T(8,128)S(1)} %get-tuple-element.18), channel_id=1, source_target_pairs={{0,31},{1,0},{2,1},{3,2},{4,3},{5,4},{6,5},{7,6},{8,7},{9,8},{10,9... | collective-permute-start | bytes 13064 | tf_op jit(solution)/shard_map/ppermute | solution.py:20
  36.7 13.2 %collective-permute-start.6 = (f32[17,64]{1,0:T(8,128)S(1)}, f32[17,64]{1,0:T(8,128)S(1)}, u32[]{:S(2)}, u32[]{:S(2)}) collective-permute-start(f32[17,64]{1,0:T(8,128)S(1)} %get-tuple-element.17), channel_id=1, source_target_pairs={{0,1},{1,2},{2,3},{3,4},{4,5},{5,6},{6,7},{7,8},{8,9},{9,10},{10,1... | collective-permute-start | bytes 13064 | tf_op jit(solution)/shard_map/ppermute | solution.py:20
  36.7 13.2 %collective-permute-start.7 = (f32[17,64]{1,0:T(8,128)S(1)}, f32[17,64]{1,0:T(8,128)S(1)}, u32[]{:S(2)}, u32[]{:S(2)}) collective-permute-start(f32[17,64]{1,0:T(8,128)S(1)} %get-tuple-element.16), channel_id=1, source_target_pairs={{0,28},{1,29},{2,30},{3,31},{4,0},{5,1},{6,2},{7,3},{8,4},{9,5},{1... | collective-permute-start | bytes 13064 | tf_op jit(solution)/shard_map/ppermute | solution.py:20
  55.1 10.1 %collective-permute-start.17 = (f32[8,64]{1,0:T(8,128)S(1)}, f32[8,64]{1,0:T(8,128)S(1)}, u32[]{:S(2)}, u32[]{:S(2)}) collective-permute-start(f32[8,64]{1,0:T(8,128)S(1)} %get-tuple-element.63), channel_id=1, source_target_pairs={{0,1},{1,2},{2,3},{3,4},{4,5},{5,6},{6,7},{7,8},{8,9},{9,10},{10,1... | collective-permute-start | bytes 6152 | tf_op jit(solution)/shard_map/ppermute | solution.py:20
  55.1 10.1 %collective-permute-start.18 = (f32[8,64]{1,0:T(8,128)S(1)}, f32[8,64]{1,0:T(8,128)S(1)}, u32[]{:S(2)}, u32[]{:S(2)}) collective-permute-start(f32[8,64]{1,0:T(8,128)S(1)} %get-tuple-element.62), channel_id=1, source_target_pairs={{0,31},{1,0},{2,1},{3,2},{4,3},{5,4},{6,5},{7,6},{8,7},{9,8},{10,9... | collective-permute-start | bytes 6152 | tf_op jit(solution)/shard_map/ppermute | solution.py:20
  73.0 6.7 %collective-permute-start.23 = (f32[8,64]{1,0:T(8,128)S(1)}, f32[8,64]{1,0:T(8,128)S(1)}, u32[]{:S(2)}, u32[]{:S(2)}) collective-permute-start(f32[8,64]{1,0:T(8,128)S(1)} %get-tuple-element.29), channel_id=1, source_target_pairs={{0,1},{1,2},{2,3},{3,4},{4,5},{5,6},{6,7},{7,8},{8,9},{9,10},{10,1... | collective-permute-start | bytes 6152 | tf_op jit(solution)/shard_map/ppermute | solution.py:20
  82.3 10.2 %collective-permute-start.27 = (f32[8,64]{1,0:T(8,128)S(1)}, f32[8,64]{1,0:T(8,128)S(1)}, u32[]{:S(2)}, u32[]{:S(2)}) collective-permute-start(f32[8,64]{1,0:T(8,128)S(1)} %get-tuple-element.59), channel_id=1, source_target_pairs={{0,1},{1,2},{2,3},{3,4},{4,5},{5,6},{6,7},{7,8},{8,9},{9,10},{10,1... | collective-permute-start | bytes 6152 | tf_op jit(solution)/shard_map/ppermute | solution.py:20
  82.3 10.2 %collective-permute-start.28 = (f32[8,64]{1,0:T(8,128)S(1)}, f32[8,64]{1,0:T(8,128)S(1)}, u32[]{:S(2)}, u32[]{:S(2)}) collective-permute-start(f32[8,64]{1,0:T(8,128)S(1)} %get-tuple-element.58), channel_id=1, source_target_pairs={{0,31},{1,0},{2,1},{3,2},{4,3},{5,4},{6,5},{7,6},{8,7},{9,8},{10,9... | collective-permute-start | bytes 6152 | tf_op jit(solution)/shard_map/ppermute | solution.py:20
  109.6 10.5 %collective-permute-start.37 = (f32[8,64]{1,0:T(8,128)S(1)}, f32[8,64]{1,0:T(8,128)S(1)}, u32[]{:S(2)}, u32[]{:S(2)}) collective-permute-start(f32[8,64]{1,0:T(8,128)S(1)} %get-tuple-element.55), channel_id=1, source_target_pairs={{0,1},{1,2},{2,3},{3,4},{4,5},{5,6},{6,7},{7,8},{8,9},{9,10},{10,1... | collective-permute-start | bytes 6152 | tf_op jit(solution)/shard_map/ppermute | solution.py:20
  109.6 10.5 %collective-permute-start.38 = (f32[8,64]{1,0:T(8,128)S(1)}, f32[8,64]{1,0:T(8,128)S(1)}, u32[]{:S(2)}, u32[]{:S(2)}) collective-permute-start(f32[8,64]{1,0:T(8,128)S(1)} %get-tuple-element.54), channel_id=1, source_target_pairs={{0,31},{1,0},{2,1},{3,2},{4,3},{5,4},{6,5},{7,6},{8,7},{9,8},{10,9... | collective-permute-start | bytes 6152 | tf_op jit(solution)/shard_map/ppermute | solution.py:20
  149.0 11.0 %collective-permute-start.52 = (f32[8,32]{1,0:T(8,128)S(1)}, f32[8,32]{1,0:T(8,128)S(1)}, u32[]{:S(2)}, u32[]{:S(2)}) collective-permute-start(f32[8,32]{1,0:T(8,128)S(1)} %get-tuple-element.87), channel_id=1, source_target_pairs={{0,1},{1,2},{2,3},{3,4},{4,5},{5,6},{6,7},{7,8},{8,9},{9,10},{10,1... | collective-permute-start | bytes 3080 | tf_op jit(solution)/shard_map/ppermute | solution.py:20
  149.0 11.0 %collective-permute-start.53 = (f32[8,32]{1,0:T(8,128)S(1)}, f32[8,32]{1,0:T(8,128)S(1)}, u32[]{:S(2)}, u32[]{:S(2)}) collective-permute-start(f32[8,32]{1,0:T(8,128)S(1)} %get-tuple-element.86), channel_id=1, source_target_pairs={{0,31},{1,0},{2,1},{3,2},{4,3},{5,4},{6,5},{7,6},{8,7},{9,8},{10,9... | collective-permute-start | bytes 3080 | tf_op jit(solution)/shard_map/ppermute | solution.py:20
  165.8 8.8 %collective-permute-start.61 = (f32[8,64]{1,0:T(8,128)S(1)}, f32[8,64]{1,0:T(8,128)S(1)}, u32[]{:S(2)}, u32[]{:S(2)}) collective-permute-start(f32[8,64]{1,0:T(8,128)S(1)} %concatenate.265), channel_id=1, source_target_pairs={{0,16},{1,17},{2,18},{3,19},{4,20},{5,21},{6,22},{7,23},{8,24},{9,... | collective-permute-start | bytes 6152 | tf_op jit(solution)/shard_map/ppermute | solution.py:20
  175.2 10.1 %collective-permute-start.62 = (f32[8,32]{1,0:T(8,128)S(1)}, f32[8,32]{1,0:T(8,128)S(1)}, u32[]{:S(2)}, u32[]{:S(2)}) collective-permute-start(f32[8,32]{1,0:T(8,128)S(1)} %get-tuple-element.83), channel_id=1, source_target_pairs={{0,1},{1,2},{2,3},{3,4},{4,5},{5,6},{6,7},{7,8},{8,9},{9,10},{10,1... | collective-permute-start | bytes 3080 | tf_op jit(solution)/shard_map/ppermute | solution.py:20
  175.2 10.1 %collective-permute-start.63 = (f32[8,32]{1,0:T(8,128)S(1)}, f32[8,32]{1,0:T(8,128)S(1)}, u32[]{:S(2)}, u32[]{:S(2)}) collective-permute-start(f32[8,32]{1,0:T(8,128)S(1)} %get-tuple-element.82), channel_id=1, source_target_pairs={{0,31},{1,0},{2,1},{3,2},{4,3},{5,4},{6,5},{7,6},{8,7},{9,8},{10,9... | collective-permute-start | bytes 3080 | tf_op jit(solution)/shard_map/ppermute | solution.py:20
  190.7 10.1 %collective-permute-start.67 = (f32[8,64]{1,0:T(8,128)S(1)}, f32[8,64]{1,0:T(8,128)S(1)}, u32[]{:S(2)}, u32[]{:S(2)}) collective-permute-start(f32[8,64]{1,0:T(8,128)S(1)} %get-tuple-element.51), channel_id=1, source_target_pairs={{0,1},{1,2},{2,3},{3,4},{4,5},{5,6},{6,7},{7,8},{8,9},{9,10},{10,1... | collective-permute-start | bytes 6152 | tf_op jit(solution)/shard_map/ppermute | solution.py:20
  190.7 10.1 %collective-permute-start.68 = (f32[8,64]{1,0:T(8,128)S(1)}, f32[8,64]{1,0:T(8,128)S(1)}, u32[]{:S(2)}, u32[]{:S(2)}) collective-permute-start(f32[8,64]{1,0:T(8,128)S(1)} %get-tuple-element.50), channel_id=1, source_target_pairs={{0,31},{1,0},{2,1},{3,2},{4,3},{5,4},{6,5},{7,6},{8,7},{9,8},{10,9... | collective-permute-start | bytes 6152 | tf_op jit(solution)/shard_map/ppermute | solution.py:20
  (65 other events, 419.0 us)

commit v11 on v9

--- a/solution.py
+++ b/solution.py
@@ -83,6 +83,20 @@
     return jnp.sum(picked * hi_mask[None], axis=1)
 
 
+def gather_split(owned, ghosts, table):
+    lo_hot, hi_mask, length, lo_hot_t = table
+    rows, width = owned.shape
+    if width % LANES:
+        return gather_cols(jnp.concatenate([owned, ghosts], axis=1), table)
+    split = width // LANES
+    groups = hi_mask.shape[0]
+    high = lax.Precision.HIGH
+    near = jnp.einsum("rab,bn->ran", owned.reshape(rows, split, LANES), lo_hot_t, precision=high)
+    far = jnp.pad(ghosts, ((0, 0), (0, (groups - split) * LANES - ghosts.shape[1])))
+    far = jnp.einsum("rab,bn->ran", far.reshape(rows, groups - split, LANES), lo_hot_t, precision=high)
+    return jnp.sum(near * hi_mask[None, :split], axis=1) + jnp.sum(far * hi_mask[None, split:], axis=1)
+
+
 def scatter_cols(terms, table):
     lo_hot, hi_mask, length, lo_hot_t = table
     groups = hi_mask.shape[0]
@@ -246,7 +260,10 @@
     second = first + jacobi_weight * (nodal_res - node_image) / node_diag
     ends = gather_cols(extend(second, send_node_table), grad_table)
     w_block = smooth + ends[:, :owned_edges] - ends[:, owned_edges:]
-    w_values = edge_values(extend(w_block, send_edge_table))
+    (w_moved,) = exchange(extend_pieces(w_block, send_edge_table))
+    w_values = gather_split(w_block, jnp.concatenate(w_moved, axis=1), edge_table).reshape(
+        modes, edofs, elements
+    )
     stiff_wterm = element_terms(stiff_elem, w_values)
     mass_wterm = element_terms(mass_elem, w_values)
     basis_values = jnp.concatenate([pair_values[:modes], w_values, pair_values[modes:]], axis=0)

time: 224 us -> 224 us (level)
    dot_general x14 -> x13, matrix products: 10.8 us -> 9.37 us  [gather_cols(): picked = jnp.einsum('rab,bn->ran', split, lo_hot_t, precision=precision)]
where the time goes in v11:
time: 224 us; the launch traced here: 223 us
  starting transfers between devices  111 us (50%)
  waiting for transfers between devices  74 us (33%)
  matrix products  23.3 us (10%)
  local copies, waits for them, and re-layouts  8.59 us (4%)
  other arithmetic  4.18 us (2%)
    ppermute x65, starting transfers between devices, from_behind(): lax.ppermute(shard, axis, [(i, (i + by) % length) for i in range(length)])  98.9 us
    ppermute x65, waiting for transfers between devices, from_behind(): lax.ppermute(shard, axis, [(i, (i + by) % length) for i in range(length)])  59 us
    ppermute x14, waiting for transfers between devices, all_sum(): lax.ppermute(value, 'dom', [(i, i ^ t << shift) for i in range(length)])  15 us
    ppermute x14, starting transfers between devices, all_sum(): lax.ppermute(value, 'dom', [(i, i ^ t << shift) for i in range(length)])  12.5 us
    dot_general x14, matrix products, scatter_cols(): jnp.einsum('ran,nb->rab', spread, lo_hot, precision=lax.Precision.HIGH)  9.57 us
    dot_general x13, matrix products, gather_cols(): picked = jnp.einsum('rab,bn->ran', split, lo_hot_t, precision=precision)  9.37 us
  transfers between devices with their start and end apart: 79, of which 32 were waited for; matrix products, arithmetic and copies ran while one was open for 2% of the time, Pallas kernels for 0%

profile of v11, /device:TPU:0, one launch (start us, length us, event | category | flops | bytes accessed | tf_op | source)
XLA Modules:
  0.0 223.2 jit_solution(10416508034295048489)
XLA Ops:
  5.0 4.0 %collective-permute-start.4 = (f32[16,192]{1,0:T(8,128)S(1)}, f32[16,192]{1,0:T(8,128)S(1)}, u32[]{:S(2)}, u32[]{:S(2)}) collective-permute-start(f32[16,192]{1,0:T(8,128)S(1)} %select_maximum_fusion.1), channel_id=1, source_target_pairs={{0,16},{1,17},{2,18},{3,19},{4,20},{5,21},{6,22},{7,23},{8,24},{9,... | collective-permute-start | bytes 36872 | tf_op jit(solution)/shard_map/ppermute | solution.py:20
  9.3 5.3 %collective-permute-start.1 = (f32[16,96]{1,0:T(8,128)S(1)}, f32[16,96]{1,0:T(8,128)S(1)}, u32[]{:S(2)}, u32[]{:S(2)}) collective-permute-start(f32[16,96]{1,0:T(8,128)S(1)} %select_maximum_fusion.5), channel_id=1, source_target_pairs={{0,31},{1,0},{2,1},{3,2},{4,3},{5,4},{6,5},{7,6},{8,7},{9,8},{10,9... | collective-permute-start | bytes 18440 | tf_op jit(solution)/shard_map/ppermute | solution.py:20
  14.8 4.7 %collective-permute-start.3 = (f32[16,96]{1,0:T(8,128)S(1)}, f32[16,96]{1,0:T(8,128)S(1)}, u32[]{:S(2)}, u32[]{:S(2)}) collective-permute-start(f32[16,96]{1,0:T(8,128)S(1)} %select_maximum_fusion.3), channel_id=1, source_target_pairs={{0,28},{1,29},{2,30},{3,31},{4,0},{5,1},{6,2},{7,3},{8,4},{9,5},{1... | collective-permute-start | bytes 18440 | tf_op jit(solution)/shard_map/ppermute | solution.py:20
  31.8 4.6 %collective-permute-start.5 = (f32[17,64]{1,0:T(8,128)S(1)}, f32[17,64]{1,0:T(8,128)S(1)}, u32[]{:S(2)}, u32[]{:S(2)}) collective-permute-start(f32[17,64]{1,0:T(8,128)S(1)} %get-tuple-element.18), channel_id=1, source_target_pairs={{0,31},{1,0},{2,1},{3,2},{4,3},{5,4},{6,5},{7,6},{8,7},{9,8},{10,9... | collective-permute-start | bytes 13064 | tf_op jit(solution)/shard_map/ppermute | solution.py:20
  55.3 5.3 %collective-permute-start.18 = (f32[8,64]{1,0:T(8,128)S(1)}, f32[8,64]{1,0:T(8,128)S(1)}, u32[]{:S(2)}, u32[]{:S(2)}) collective-permute-start(f32[8,64]{1,0:T(8,128)S(1)} %get-tuple-element.66), channel_id=1, source_target_pairs={{0,31},{1,0},{2,1},{3,2},{4,3},{5,4},{6,5},{7,6},{8,7},{9,8},{10,9... | collective-permute-start | bytes 6152 | tf_op jit(solution)/shard_map/ppermute | solution.py:20
  60.7 4.7 %collective-permute-start.20 = (f32[8,64]{1,0:T(8,128)S(1)}, f32[8,64]{1,0:T(8,128)S(1)}, u32[]{:S(2)}, u32[]{:S(2)}) collective-permute-start(f32[8,64]{1,0:T(8,128)S(1)} %get-tuple-element.64), channel_id=1, source_target_pairs={{0,28},{1,29},{2,30},{3,31},{4,0},{5,1},{6,2},{7,3},{8,4},{9,5},{1... | collective-permute-start | bytes 6152 | tf_op jit(solution)/shard_map/ppermute | solution.py:20
  75.8 4.1 %collective-permute-done.23 = f32[8,64]{1,0:T(8,128)S(1)} collective-permute-done((f32[8,64]{1,0:T(8,128)S(1)}, f32[8,64]{1,0:T(8,128)S(1)}, u32[]{:S(2)}, u32[]{:S(2)}) %collective-permute-start.23) | collective-permute-done | bytes 2080 | tf_op jit(solution)/shard_map/ppermute | solution.py:20
  82.6 5.3 %collective-permute-start.28 = (f32[8,64]{1,0:T(8,128)S(1)}, f32[8,64]{1,0:T(8,128)S(1)}, u32[]{:S(2)}, u32[]{:S(2)}) collective-permute-start(f32[8,64]{1,0:T(8,128)S(1)} %get-tuple-element.62), channel_id=1, source_target_pairs={{0,31},{1,0},{2,1},{3,2},{4,3},{5,4},{6,5},{7,6},{8,7},{9,8},{10,9... | collective-permute-start | bytes 6152 | tf_op jit(solution)/shard_map/ppermute | solution.py:20
  87.9 4.7 %collective-permute-start.30 = (f32[8,64]{1,0:T(8,128)S(1)}, f32[8,64]{1,0:T(8,128)S(1)}, u32[]{:S(2)}, u32[]{:S(2)}) collective-permute-start(f32[8,64]{1,0:T(8,128)S(1)} %get-tuple-element.60), channel_id=1, source_target_pairs={{0,28},{1,29},{2,30},{3,31},{4,0},{5,1},{6,2},{7,3},{8,4},{9,5},{1... | collective-permute-start | bytes 6152 | tf_op jit(solution)/shard_map/ppermute | solution.py:20
  103.0 4.1 %collective-permute-done.33 = f32[8,64]{1,0:T(8,128)S(1)} collective-permute-done((f32[8,64]{1,0:T(8,128)S(1)}, f32[8,64]{1,0:T(8,128)S(1)}, u32[]{:S(2)}, u32[]{:S(2)}) %collective-permute-start.33) | collective-permute-done | bytes 2080 | tf_op jit(solution)/shard_map/ppermute | solution.py:20
  109.8 5.3 %collective-permute-start.38 = (f32[8,64]{1,0:T(8,128)S(1)}, f32[8,64]{1,0:T(8,128)S(1)}, u32[]{:S(2)}, u32[]{:S(2)}) collective-permute-start(f32[8,64]{1,0:T(8,128)S(1)} %get-tuple-element.58), channel_id=1, source_target_pairs={{0,31},{1,0},{2,1},{3,2},{4,3},{5,4},{6,5},{7,6},{8,7},{9,8},{10,9... | collective-permute-start | bytes 6152 | tf_op jit(solution)/shard_map/ppermute | solution.py:20
  115.1 4.7 %collective-permute-start.40 = (f32[8,64]{1,0:T(8,128)S(1)}, f32[8,64]{1,0:T(8,128)S(1)}, u32[]{:S(2)}, u32[]{:S(2)}) collective-permute-start(f32[8,64]{1,0:T(8,128)S(1)} %get-tuple-element.56), channel_id=1, source_target_pairs={{0,28},{1,29},{2,30},{3,31},{4,0},{5,1},{6,2},{7,3},{8,4},{9,5},{1... | collective-permute-start | bytes 6152 | tf_op jit(solution)/shard_map/ppermute | solution.py:20
  130.6 3.9 %collective-permute-done.43 = f32[8,64]{1,0:T(8,128)S(1)} collective-permute-done((f32[8,64]{1,0:T(8,128)S(1)}, f32[8,64]{1,0:T(8,128)S(1)}, u32[]{:S(2)}, u32[]{:S(2)}) %collective-permute-start.43) | collective-permute-done | bytes 2080 | tf_op jit(solution)/shard_map/ppermute | solution.py:20
  137.6 4.3 %collective-permute-start.47 = (f32[8,32]{1,0:T(8,128)S(1)}, f32[8,32]{1,0:T(8,128)S(1)}, u32[]{:S(2)}, u32[]{:S(2)}) collective-permute-start(f32[8,32]{1,0:T(8,128)S(1)} %get-tuple-element.44), channel_id=1, source_target_pairs={{0,31},{1,0},{2,1},{3,2},{4,3},{5,4},{6,5},{7,6},{8,7},{9,8},{10,9... | collective-permute-start | bytes 3080 | tf_op jit(solution)/shard_map/ppermute | solution.py:20
  144.0 4.6 %collective-permute-done.48 = f32[8,32]{1,0:T(8,128)S(1)} collective-permute-done((f32[8,32]{1,0:T(8,128)S(1)}, f32[8,32]{1,0:T(8,128)S(1)}, u32[]{:S(2)}, u32[]{:S(2)}) %collective-permute-start.48) | collective-permute-done | bytes 1056 | tf_op jit(solution)/shard_map/ppermute | solution.py:20
  149.2 6.3 %collective-permute-start.53 = (f32[8,32]{1,0:T(8,128)S(1)}, f32[8,32]{1,0:T(8,128)S(1)}, u32[]{:S(2)}, u32[]{:S(2)}) collective-permute-start(f32[8,32]{1,0:T(8,128)S(1)} %get-tuple-element.78), channel_id=1, source_target_pairs={{0,31},{1,0},{2,1},{3,2},{4,3},{5,4},{6,5},{7,6},{8,7},{9,8},{10,9... | collective-permute-start | bytes 3080 | tf_op jit(solution)/shard_map/ppermute | solution.py:20
  155.5 4.7 %collective-permute-start.55 = (f32[8,32]{1,0:T(8,128)S(1)}, f32[8,32]{1,0:T(8,128)S(1)}, u32[]{:S(2)}, u32[]{:S(2)}) collective-permute-start(f32[8,32]{1,0:T(8,128)S(1)} %get-tuple-element.76), channel_id=1, source_target_pairs={{0,28},{1,29},{2,30},{3,31},{4,0},{5,1},{6,2},{7,3},{8,4},{9,5},{1... | collective-permute-start | bytes 3080 | tf_op jit(solution)/shard_map/ppermute | solution.py:20
  168.6 4.1 %collective-permute-done.58 = f32[8,32]{1,0:T(8,128)S(1)} collective-permute-done((f32[8,32]{1,0:T(8,128)S(1)}, f32[8,32]{1,0:T(8,128)S(1)}, u32[]{:S(2)}, u32[]{:S(2)}) %collective-permute-start.58) | collective-permute-done | bytes 1056 | tf_op jit(solution)/shard_map/ppermute | solution.py:20
  175.3 5.3 %collective-permute-start.63 = (f32[8,32]{1,0:T(8,128)S(1)}, f32[8,32]{1,0:T(8,128)S(1)}, u32[]{:S(2)}, u32[]{:S(2)}) collective-permute-start(f32[8,32]{1,0:T(8,128)S(1)} %get-tuple-element.74), channel_id=1, source_target_pairs={{0,31},{1,0},{2,1},{3,2},{4,3},{5,4},{6,5},{7,6},{8,7},{9,8},{10,9... | collective-permute-start | bytes 3080 | tf_op jit(solution)/shard_map/ppermute | solution.py:20
  180.6 4.7 %collective-permute-start.65 = (f32[8,32]{1,0:T(8,128)S(1)}, f32[8,32]{1,0:T(8,128)S(1)}, u32[]{:S(2)}, u32[]{:S(2)}) collective-permute-start(f32[8,32]{1,0:T(8,128)S(1)} %get-tuple-element.72), channel_id=1, source_target_pairs={{0,28},{1,29},{2,30},{3,31},{4,0},{5,1},{6,2},{7,3},{8,4},{9,5},{1... | collective-permute-start | bytes 3080 | tf_op jit(solution)/shard_map/ppermute | solution.py:20
  190.9 5.3 %collective-permute-start.68 = (f32[8,64]{1,0:T(8,128)S(1)}, f32[8,64]{1,0:T(8,128)S(1)}, u32[]{:S(2)}, u32[]{:S(2)}) collective-permute-start(f32[8,64]{1,0:T(8,128)S(1)} %get-tuple-element.54), channel_id=1, source_target_pairs={{0,31},{1,0},{2,1},{3,2},{4,3},{5,4},{6,5},{7,6},{8,7},{9,8},{10,9... | collective-permute-start | bytes 6152 | tf_op jit(solution)/shard_map/ppermute | solution.py:20
  196.2 4.7 %collective-permute-start.70 = (f32[8,64]{1,0:T(8,128)S(1)}, f32[8,64]{1,0:T(8,128)S(1)}, u32[]{:S(2)}, u32[]{:S(2)}) collective-permute-start(f32[8,64]{1,0:T(8,128)S(1)} %get-tuple-element.52), channel_id=1, source_target_pairs={{0,28},{1,29},{2,30},{3,31},{4,0},{5,1},{6,2},{7,3},{8,4},{9,5},{1... | collective-permute-start | bytes 6152 | tf_op jit(solution)/shard_map/ppermute | solution.py:20
  212.3 3.4 %collective-permute-start.77 = (f32[2,24,24]{2,1,0:T(8,128)S(1)}, f32[2,24,24]{2,1,0:T(8,128)S(1)}, u32[]{:S(2)}, u32[]{:S(2)}) collective-permute-start(f32[2,24,24]{2,1,0:T(8,128)S(1)} %add_add_fusion.1), channel_id=1, source_target_pairs={{0,4},{1,5},{2,6},{3,7},{4,0},{5,1},{6,2},{7,3},{8,12},{9,13},{10,... | collective-permute-start | bytes 13832 | tf_op jit(solution)/shard_map/ppermute | solution.py:49
  218.5 4.1 %collective-permute-done.78 = f32[2,24,24]{2,1,0:T(8,128)S(1)} collective-permute-done((f32[2,24,24]{2,1,0:T(8,128)S(1)}, f32[2,24,24]{2,1,0:T(8,128)S(1)}, u32[]{:S(2)}, u32[]{:S(2)}) %collective-permute-start.78) | collective-permute-done | bytes 4640 | tf_op jit(solution)/shard_map/ppermute | solution.py:49
  (305 shorter events, 109.1 us)
Async XLA Ops:
  5.0 14.9 %collective-permute-start.4 = (f32[16,192]{1,0:T(8,128)S(1)}, f32[16,192]{1,0:T(8,128)S(1)}, u32[]{:S(2)}, u32[]{:S(2)}) collective-permute-start(f32[16,192]{1,0:T(8,128)S(1)} %select_maximum_fusion.1), channel_id=1, source_target_pairs={{0,16},{1,17},{2,18},{3,19},{4,20},{5,21},{6,22},{7,23},{8,24},{9,... | collective-permute-start | bytes 36872 | tf_op jit(solution)/shard_map/ppermute | solution.py:20
  9.2 10.7 %collective-permute-start = (f32[16,96]{1,0:T(8,128)S(1)}, f32[16,96]{1,0:T(8,128)S(1)}, u32[]{:S(2)}, u32[]{:S(2)}) collective-permute-start(f32[16,96]{1,0:T(8,128)S(1)} %select_maximum_fusion.6), channel_id=1, source_target_pairs={{0,1},{1,2},{2,3},{3,4},{4,5},{5,6},{6,7},{7,8},{8,9},{9,10},{10,1... | collective-permute-start | bytes 18440 | tf_op jit(solution)/shard_map/ppermute | solution.py:20
  9.3 10.6 %collective-permute-start.1 = (f32[16,96]{1,0:T(8,128)S(1)}, f32[16,96]{1,0:T(8,128)S(1)}, u32[]{:S(2)}, u32[]{:S(2)}) collective-permute-start(f32[16,96]{1,0:T(8,128)S(1)} %select_maximum_fusion.5), channel_id=1, source_target_pairs={{0,31},{1,0},{2,1},{3,2},{4,3},{5,4},{6,5},{7,6},{8,7},{9,8},{10,9... | collective-permute-start | bytes 18440 | tf_op jit(solution)/shard_map/ppermute | solution.py:20
  27.9 8.5 %collective-permute-start.10 = (f32[2,8]{1,0:T(2,128)S(1)}, f32[2,8]{1,0:T(2,128)S(1)}, u32[]{:S(2)}, u32[]{:S(2)}) collective-permute-start(f32[2,8]{1,0:T(2,128)S(1)} %pad_maximum_fusion.5), channel_id=1, source_target_pairs={{0,3},{1,2},{2,1},{3,0},{4,7},{5,6},{6,5},{7,4},{8,11},{9,10},{10,... | collective-permute-start | bytes 200 | tf_op jit(solution)/shard_map/ppermute | solution.py:49
  28.0 9.1 %collective-permute-start.11 = (f32[2,8]{1,0:T(2,128)S(1)}, f32[2,8]{1,0:T(2,128)S(1)}, u32[]{:S(2)}, u32[]{:S(2)}) collective-permute-start(f32[2,8]{1,0:T(2,128)S(1)} %pad_maximum_fusion.5), channel_id=1, source_target_pairs={{0,2},{1,3},{2,0},{3,1},{4,6},{5,7},{6,4},{7,5},{8,10},{9,11},{10,... | collective-permute-start | bytes 200 | tf_op jit(solution)/shard_map/ppermute | solution.py:49
  28.1 9.0 %collective-permute-start.12 = (f32[2,8]{1,0:T(2,128)S(1)}, f32[2,8]{1,0:T(2,128)S(1)}, u32[]{:S(2)}, u32[]{:S(2)}) collective-permute-start(f32[2,8]{1,0:T(2,128)S(1)} %pad_maximum_fusion.5), channel_id=1, source_target_pairs={{0,1},{1,0},{2,3},{3,2},{4,5},{5,4},{6,7},{7,6},{8,9},{9,8},{10,11... | collective-permute-start | bytes 200 | tf_op jit(solution)/shard_map/ppermute | solution.py:49
  31.8 18.0 %collective-permute-start.5 = (f32[17,64]{1,0:T(8,128)S(1)}, f32[17,64]{1,0:T(8,128)S(1)}, u32[]{:S(2)}, u32[]{:S(2)}) collective-permute-start(f32[17,64]{1,0:T(8,128)S(1)} %get-tuple-element.18), channel_id=1, source_target_pairs={{0,31},{1,0},{2,1},{3,2},{4,3},{5,4},{6,5},{7,6},{8,7},{9,8},{10,9... | collective-permute-start | bytes 13064 | tf_op jit(solution)/shard_map/ppermute | solution.py:20
  36.4 13.4 %collective-permute-start.6 = (f32[17,64]{1,0:T(8,128)S(1)}, f32[17,64]{1,0:T(8,128)S(1)}, u32[]{:S(2)}, u32[]{:S(2)}) collective-permute-start(f32[17,64]{1,0:T(8,128)S(1)} %get-tuple-element.17), channel_id=1, source_target_pairs={{0,1},{1,2},{2,3},{3,4},{4,5},{5,6},{6,7},{7,8},{8,9},{9,10},{10,1... | collective-permute-start | bytes 13064 | tf_op jit(solution)/shard_map/ppermute | solution.py:20
  36.4 13.4 %collective-permute-start.7 = (f32[17,64]{1,0:T(8,128)S(1)}, f32[17,64]{1,0:T(8,128)S(1)}, u32[]{:S(2)}, u32[]{:S(2)}) collective-permute-start(f32[17,64]{1,0:T(8,128)S(1)} %get-tuple-element.16), channel_id=1, source_target_pairs={{0,28},{1,29},{2,30},{3,31},{4,0},{5,1},{6,2},{7,3},{8,4},{9,5},{1... | collective-permute-start | bytes 13064 | tf_op jit(solution)/shard_map/ppermute | solution.py:20
  55.3 10.1 %collective-permute-start.17 = (f32[8,64]{1,0:T(8,128)S(1)}, f32[8,64]{1,0:T(8,128)S(1)}, u32[]{:S(2)}, u32[]{:S(2)}) collective-permute-start(f32[8,64]{1,0:T(8,128)S(1)} %get-tuple-element.67), channel_id=1, source_target_pairs={{0,1},{1,2},{2,3},{3,4},{4,5},{5,6},{6,7},{7,8},{8,9},{9,10},{10,1... | collective-permute-start | bytes 6152 | tf_op jit(solution)/shard_map/ppermute | solution.py:20
  55.3 10.1 %collective-permute-start.18 = (f32[8,64]{1,0:T(8,128)S(1)}, f32[8,64]{1,0:T(8,128)S(1)}, u32[]{:S(2)}, u32[]{:S(2)}) collective-permute-start(f32[8,64]{1,0:T(8,128)S(1)} %get-tuple-element.66), channel_id=1, source_target_pairs={{0,31},{1,0},{2,1},{3,2},{4,3},{5,4},{6,5},{7,6},{8,7},{9,8},{10,9... | collective-permute-start | bytes 6152 | tf_op jit(solution)/shard_map/ppermute | solution.py:20
  73.2 6.7 %collective-permute-start.23 = (f32[8,64]{1,0:T(8,128)S(1)}, f32[8,64]{1,0:T(8,128)S(1)}, u32[]{:S(2)}, u32[]{:S(2)}) collective-permute-start(f32[8,64]{1,0:T(8,128)S(1)} %get-tuple-element.29), channel_id=1, source_target_pairs={{0,1},{1,2},{2,3},{3,4},{4,5},{5,6},{6,7},{7,8},{8,9},{9,10},{10,1... | collective-permute-start | bytes 6152 | tf_op jit(solution)/shard_map/ppermute | solution.py:20
  82.5 10.2 %collective-permute-start.27 = (f32[8,64]{1,0:T(8,128)S(1)}, f32[8,64]{1,0:T(8,128)S(1)}, u32[]{:S(2)}, u32[]{:S(2)}) collective-permute-start(f32[8,64]{1,0:T(8,128)S(1)} %get-tuple-element.63), channel_id=1, source_target_pairs={{0,1},{1,2},{2,3},{3,4},{4,5},{5,6},{6,7},{7,8},{8,9},{9,10},{10,1... | collective-permute-start | bytes 6152 | tf_op jit(solution)/shard_map/ppermute | solution.py:20
  82.6 10.2 %collective-permute-start.28 = (f32[8,64]{1,0:T(8,128)S(1)}, f32[8,64]{1,0:T(8,128)S(1)}, u32[]{:S(2)}, u32[]{:S(2)}) collective-permute-start(f32[8,64]{1,0:T(8,128)S(1)} %get-tuple-element.62), channel_id=1, source_target_pairs={{0,31},{1,0},{2,1},{3,2},{4,3},{5,4},{6,5},{7,6},{8,7},{9,8},{10,9... | collective-permute-start | bytes 6152 | tf_op jit(solution)/shard_map/ppermute | solution.py:20
  100.4 6.7 %collective-permute-start.33 = (f32[8,64]{1,0:T(8,128)S(1)}, f32[8,64]{1,0:T(8,128)S(1)}, u32[]{:S(2)}, u32[]{:S(2)}) collective-permute-start(f32[8,64]{1,0:T(8,128)S(1)} %get-tuple-element.25), channel_id=1, source_target_pairs={{0,1},{1,2},{2,3},{3,4},{4,5},{5,6},{6,7},{7,8},{8,9},{9,10},{10,1... | collective-permute-start | bytes 6152 | tf_op jit(solution)/shard_map/ppermute | solution.py:20
  109.8 10.5 %collective-permute-start.37 = (f32[8,64]{1,0:T(8,128)S(1)}, f32[8,64]{1,0:T(8,128)S(1)}, u32[]{:S(2)}, u32[]{:S(2)}) collective-permute-start(f32[8,64]{1,0:T(8,128)S(1)} %get-tuple-element.59), channel_id=1, source_target_pairs={{0,1},{1,2},{2,3},{3,4},{4,5},{5,6},{6,7},{7,8},{8,9},{9,10},{10,1... | collective-permute-start | bytes 6152 | tf_op jit(solution)/shard_map/ppermute | solution.py:20
  109.8 10.5 %collective-permute-start.38 = (f32[8,64]{1,0:T(8,128)S(1)}, f32[8,64]{1,0:T(8,128)S(1)}, u32[]{:S(2)}, u32[]{:S(2)}) collective-permute-start(f32[8,64]{1,0:T(8,128)S(1)} %get-tuple-element.58), channel_id=1, source_target_pairs={{0,31},{1,0},{2,1},{3,2},{4,3},{5,4},{6,5},{7,6},{8,7},{9,8},{10,9... | collective-permute-start | bytes 6152 | tf_op jit(solution)/shard_map/ppermute | solution.py:20
  127.8 6.7 %collective-permute-start.43 = (f32[8,64]{1,0:T(8,128)S(1)}, f32[8,64]{1,0:T(8,128)S(1)}, u32[]{:S(2)}, u32[]{:S(2)}) collective-permute-start(f32[8,64]{1,0:T(8,128)S(1)} %get-tuple-element.21), channel_id=1, source_target_pairs={{0,1},{1,2},{2,3},{3,4},{4,5},{5,6},{6,7},{7,8},{8,9},{9,10},{10,1... | collective-permute-start | bytes 6152 | tf_op jit(solution)/shard_map/ppermute | solution.py:20
  149.2 11.1 %collective-permute-start.52 = (f32[8,32]{1,0:T(8,128)S(1)}, f32[8,32]{1,0:T(8,128)S(1)}, u32[]{:S(2)}, u32[]{:S(2)}) collective-permute-start(f32[8,32]{1,0:T(8,128)S(1)} %get-tuple-element.79), channel_id=1, source_target_pairs={{0,1},{1,2},{2,3},{3,4},{4,5},{5,6},{6,7},{7,8},{8,9},{9,10},{10,1... | collective-permute-start | bytes 3080 | tf_op jit(solution)/shard_map/ppermute | solution.py:20
  149.2 11.1 %collective-permute-start.53 = (f32[8,32]{1,0:T(8,128)S(1)}, f32[8,32]{1,0:T(8,128)S(1)}, u32[]{:S(2)}, u32[]{:S(2)}) collective-permute-start(f32[8,32]{1,0:T(8,128)S(1)} %get-tuple-element.78), channel_id=1, source_target_pairs={{0,31},{1,0},{2,1},{3,2},{4,3},{5,4},{6,5},{7,6},{8,7},{9,8},{10,9... | collective-permute-start | bytes 3080 | tf_op jit(solution)/shard_map/ppermute | solution.py:20
  175.3 10.1 %collective-permute-start.62 = (f32[8,32]{1,0:T(8,128)S(1)}, f32[8,32]{1,0:T(8,128)S(1)}, u32[]{:S(2)}, u32[]{:S(2)}) collective-permute-start(f32[8,32]{1,0:T(8,128)S(1)} %get-tuple-element.75), channel_id=1, source_target_pairs={{0,1},{1,2},{2,3},{3,4},{4,5},{5,6},{6,7},{7,8},{8,9},{9,10},{10,1... | collective-permute-start | bytes 3080 | tf_op jit(solution)/shard_map/ppermute | solution.py:20
  175.3 10.1 %collective-permute-start.63 = (f32[8,32]{1,0:T(8,128)S(1)}, f32[8,32]{1,0:T(8,128)S(1)}, u32[]{:S(2)}, u32[]{:S(2)}) collective-permute-start(f32[8,32]{1,0:T(8,128)S(1)} %get-tuple-element.74), channel_id=1, source_target_pairs={{0,31},{1,0},{2,1},{3,2},{4,3},{5,4},{6,5},{7,6},{8,7},{9,8},{10,9... | collective-permute-start | bytes 3080 | tf_op jit(solution)/shard_map/ppermute | solution.py:20
  190.8 11.5 %collective-permute-start.67 = (f32[8,64]{1,0:T(8,128)S(1)}, f32[8,64]{1,0:T(8,128)S(1)}, u32[]{:S(2)}, u32[]{:S(2)}) collective-permute-start(f32[8,64]{1,0:T(8,128)S(1)} %get-tuple-element.55), channel_id=1, source_target_pairs={{0,1},{1,2},{2,3},{3,4},{4,5},{5,6},{6,7},{7,8},{8,9},{9,10},{10,1... | collective-permute-start | bytes 6152 | tf_op jit(solution)/shard_map/ppermute | solution.py:20
  190.9 11.5 %collective-permute-start.68 = (f32[8,64]{1,0:T(8,128)S(1)}, f32[8,64]{1,0:T(8,128)S(1)}, u32[]{:S(2)}, u32[]{:S(2)}) collective-permute-start(f32[8,64]{1,0:T(8,128)S(1)} %get-tuple-element.54), channel_id=1, source_target_pairs={{0,31},{1,0},{2,1},{3,2},{4,3},{5,4},{6,5},{7,6},{8,7},{9,8},{10,9... | collective-permute-start | bytes 6152 | tf_op jit(solution)/shard_map/ppermute | solution.py:20
  (62 other events, 381.0 us)

commit v12 on v9

--- a/solution.py
+++ b/solution.py
@@ -250,9 +250,8 @@
     stiff_wterm = element_terms(stiff_elem, w_values)
     mass_wterm = element_terms(mass_elem, w_values)
     basis_values = jnp.concatenate([pair_values[:modes], w_values, pair_values[modes:]], axis=0)
-    w_rows = jnp.stack(
-        [inner_elements(stiff_wterm, basis_values), inner_elements(mass_wterm, basis_values)]
-    )
+    w_rows = inner_elements(jnp.concatenate([stiff_wterm, mass_wterm], axis=0), basis_values)
+    w_rows = w_rows.reshape(2, modes, -1)
     full_gram = all_sum(arrange(jnp.stack([stiff_part, mass_part]), w_rows, modes))
     total_edges = owned_edges * lax.axis_size("dom")
     return (w_block, full_gram[0] / total_edges, full_gram[1] / total_edges)

time: 224 us -> 224 us (level)
  no operation moved by 1% of the time
where the time goes in v12:
time: 224 us; the launch traced here: 223 us
  starting transfers between devices  112 us (50%)
  waiting for transfers between devices  75.5 us (34%)
  matrix products  21.9 us (10%)
  local copies, waits for them, and re-layouts  8.65 us (4%)
  other arithmetic  4.05 us (2%)
    ppermute x65, starting transfers between devices, from_behind(): lax.ppermute(shard, axis, [(i, (i + by) % length) for i in range(length)])  99 us
    ppermute x65, waiting for transfers between devices, from_behind(): lax.ppermute(shard, axis, [(i, (i + by) % length) for i in range(length)])  60.5 us
    ppermute x14, waiting for transfers between devices, all_sum(): lax.ppermute(value, 'dom', [(i, i ^ t << shift) for i in range(length)])  15 us
    ppermute x14, starting transfers between devices, all_sum(): lax.ppermute(value, 'dom', [(i, i ^ t << shift) for i in range(length)])  12.5 us
    dot_general x14, matrix products, gather_cols(): picked = jnp.einsum('rab,bn->ran', split, lo_hot_t, precision=precision)  10.7 us
    dot_general x14, matrix products, scatter_cols(): jnp.einsum('ran,nb->rab', spread, lo_hot, precision=lax.Precision.HIGH)  9.56 us
  transfers between devices with their start and end apart: 79, of which 32 were waited for; matrix products, arithmetic and copies ran while one was open for 2% of the time, Pallas kernels for 0%

profile of v12, /device:TPU:0, one launch (start us, length us, event | category | flops | bytes accessed | tf_op | source)
XLA Modules:
  0.0 223.2 jit_solution(7953038244917939951)
XLA Ops:
  5.0 4.0 %collective-permute-start.4 = (f32[16,192]{1,0:T(8,128)S(1)}, f32[16,192]{1,0:T(8,128)S(1)}, u32[]{:S(2)}, u32[]{:S(2)}) collective-permute-start(f32[16,192]{1,0:T(8,128)S(1)} %select_maximum_fusion.1), channel_id=1, source_target_pairs={{0,16},{1,17},{2,18},{3,19},{4,20},{5,21},{6,22},{7,23},{8,24},{9,... | collective-permute-start | bytes 36872 | tf_op jit(solution)/shard_map/ppermute | solution.py:20
  9.3 5.3 %collective-permute-start.1 = (f32[16,96]{1,0:T(8,128)S(1)}, f32[16,96]{1,0:T(8,128)S(1)}, u32[]{:S(2)}, u32[]{:S(2)}) collective-permute-start(f32[16,96]{1,0:T(8,128)S(1)} %select_maximum_fusion.5), channel_id=1, source_target_pairs={{0,31},{1,0},{2,1},{3,2},{4,3},{5,4},{6,5},{7,6},{8,7},{9,8},{10,9... | collective-permute-start | bytes 18440 | tf_op jit(solution)/shard_map/ppermute | solution.py:20
  14.8 4.7 %collective-permute-start.3 = (f32[16,96]{1,0:T(8,128)S(1)}, f32[16,96]{1,0:T(8,128)S(1)}, u32[]{:S(2)}, u32[]{:S(2)}) collective-permute-start(f32[16,96]{1,0:T(8,128)S(1)} %select_maximum_fusion.3), channel_id=1, source_target_pairs={{0,28},{1,29},{2,30},{3,31},{4,0},{5,1},{6,2},{7,3},{8,4},{9,5},{1... | collective-permute-start | bytes 18440 | tf_op jit(solution)/shard_map/ppermute | solution.py:20
  31.8 4.6 %collective-permute-start.5 = (f32[17,64]{1,0:T(8,128)S(1)}, f32[17,64]{1,0:T(8,128)S(1)}, u32[]{:S(2)}, u32[]{:S(2)}) collective-permute-start(f32[17,64]{1,0:T(8,128)S(1)} %get-tuple-element.18), channel_id=1, source_target_pairs={{0,31},{1,0},{2,1},{3,2},{4,3},{5,4},{6,5},{7,6},{8,7},{9,8},{10,9... | collective-permute-start | bytes 13064 | tf_op jit(solution)/shard_map/ppermute | solution.py:20
  55.3 5.3 %collective-permute-start.18 = (f32[8,64]{1,0:T(8,128)S(1)}, f32[8,64]{1,0:T(8,128)S(1)}, u32[]{:S(2)}, u32[]{:S(2)}) collective-permute-start(f32[8,64]{1,0:T(8,128)S(1)} %get-tuple-element.66), channel_id=1, source_target_pairs={{0,31},{1,0},{2,1},{3,2},{4,3},{5,4},{6,5},{7,6},{8,7},{9,8},{10,9... | collective-permute-start | bytes 6152 | tf_op jit(solution)/shard_map/ppermute | solution.py:20
  60.7 4.7 %collective-permute-start.20 = (f32[8,64]{1,0:T(8,128)S(1)}, f32[8,64]{1,0:T(8,128)S(1)}, u32[]{:S(2)}, u32[]{:S(2)}) collective-permute-start(f32[8,64]{1,0:T(8,128)S(1)} %get-tuple-element.64), channel_id=1, source_target_pairs={{0,28},{1,29},{2,30},{3,31},{4,0},{5,1},{6,2},{7,3},{8,4},{9,5},{1... | collective-permute-start | bytes 6152 | tf_op jit(solution)/shard_map/ppermute | solution.py:20
  75.7 4.1 %collective-permute-done.23 = f32[8,64]{1,0:T(8,128)S(1)} collective-permute-done((f32[8,64]{1,0:T(8,128)S(1)}, f32[8,64]{1,0:T(8,128)S(1)}, u32[]{:S(2)}, u32[]{:S(2)}) %collective-permute-start.23) | collective-permute-done | bytes 2080 | tf_op jit(solution)/shard_map/ppermute | solution.py:20
  82.5 5.3 %collective-permute-start.28 = (f32[8,64]{1,0:T(8,128)S(1)}, f32[8,64]{1,0:T(8,128)S(1)}, u32[]{:S(2)}, u32[]{:S(2)}) collective-permute-start(f32[8,64]{1,0:T(8,128)S(1)} %get-tuple-element.62), channel_id=1, source_target_pairs={{0,31},{1,0},{2,1},{3,2},{4,3},{5,4},{6,5},{7,6},{8,7},{9,8},{10,9... | collective-permute-start | bytes 6152 | tf_op jit(solution)/shard_map/ppermute | solution.py:20
  87.8 4.7 %collective-permute-start.30 = (f32[8,64]{1,0:T(8,128)S(1)}, f32[8,64]{1,0:T(8,128)S(1)}, u32[]{:S(2)}, u32[]{:S(2)}) collective-permute-start(f32[8,64]{1,0:T(8,128)S(1)} %get-tuple-element.60), channel_id=1, source_target_pairs={{0,28},{1,29},{2,30},{3,31},{4,0},{5,1},{6,2},{7,3},{8,4},{9,5},{1... | collective-permute-start | bytes 6152 | tf_op jit(solution)/shard_map/ppermute | solution.py:20
  102.9 4.1 %collective-permute-done.33 = f32[8,64]{1,0:T(8,128)S(1)} collective-permute-done((f32[8,64]{1,0:T(8,128)S(1)}, f32[8,64]{1,0:T(8,128)S(1)}, u32[]{:S(2)}, u32[]{:S(2)}) %collective-permute-start.33) | collective-permute-done | bytes 2080 | tf_op jit(solution)/shard_map/ppermute | solution.py:20
  109.7 5.3 %collective-permute-start.38 = (f32[8,64]{1,0:T(8,128)S(1)}, f32[8,64]{1,0:T(8,128)S(1)}, u32[]{:S(2)}, u32[]{:S(2)}) collective-permute-start(f32[8,64]{1,0:T(8,128)S(1)} %get-tuple-element.58), channel_id=1, source_target_pairs={{0,31},{1,0},{2,1},{3,2},{4,3},{5,4},{6,5},{7,6},{8,7},{9,8},{10,9... | collective-permute-start | bytes 6152 | tf_op jit(solution)/shard_map/ppermute | solution.py:20
  115.0 4.7 %collective-permute-start.40 = (f32[8,64]{1,0:T(8,128)S(1)}, f32[8,64]{1,0:T(8,128)S(1)}, u32[]{:S(2)}, u32[]{:S(2)}) collective-permute-start(f32[8,64]{1,0:T(8,128)S(1)} %get-tuple-element.56), channel_id=1, source_target_pairs={{0,28},{1,29},{2,30},{3,31},{4,0},{5,1},{6,2},{7,3},{8,4},{9,5},{1... | collective-permute-start | bytes 6152 | tf_op jit(solution)/shard_map/ppermute | solution.py:20
  130.5 3.9 %collective-permute-done.43 = f32[8,64]{1,0:T(8,128)S(1)} collective-permute-done((f32[8,64]{1,0:T(8,128)S(1)}, f32[8,64]{1,0:T(8,128)S(1)}, u32[]{:S(2)}, u32[]{:S(2)}) %collective-permute-start.43) | collective-permute-done | bytes 2080 | tf_op jit(solution)/shard_map/ppermute | solution.py:20
  137.5 4.3 %collective-permute-start.47 = (f32[8,32]{1,0:T(8,128)S(1)}, f32[8,32]{1,0:T(8,128)S(1)}, u32[]{:S(2)}, u32[]{:S(2)}) collective-permute-start(f32[8,32]{1,0:T(8,128)S(1)} %get-tuple-element.44), channel_id=1, source_target_pairs={{0,31},{1,0},{2,1},{3,2},{4,3},{5,4},{6,5},{7,6},{8,7},{9,8},{10,9... | collective-permute-start | bytes 3080 | tf_op jit(solution)/shard_map/ppermute | solution.py:20
  143.9 4.6 %collective-permute-done.48 = f32[8,32]{1,0:T(8,128)S(1)} collective-permute-done((f32[8,32]{1,0:T(8,128)S(1)}, f32[8,32]{1,0:T(8,128)S(1)}, u32[]{:S(2)}, u32[]{:S(2)}) %collective-permute-start.48) | collective-permute-done | bytes 1056 | tf_op jit(solution)/shard_map/ppermute | solution.py:20
  149.1 6.3 %collective-permute-start.53 = (f32[8,32]{1,0:T(8,128)S(1)}, f32[8,32]{1,0:T(8,128)S(1)}, u32[]{:S(2)}, u32[]{:S(2)}) collective-permute-start(f32[8,32]{1,0:T(8,128)S(1)} %get-tuple-element.78), channel_id=1, source_target_pairs={{0,31},{1,0},{2,1},{3,2},{4,3},{5,4},{6,5},{7,6},{8,7},{9,8},{10,9... | collective-permute-start | bytes 3080 | tf_op jit(solution)/shard_map/ppermute | solution.py:20
  155.4 4.7 %collective-permute-start.55 = (f32[8,32]{1,0:T(8,128)S(1)}, f32[8,32]{1,0:T(8,128)S(1)}, u32[]{:S(2)}, u32[]{:S(2)}) collective-permute-start(f32[8,32]{1,0:T(8,128)S(1)} %get-tuple-element.76), channel_id=1, source_target_pairs={{0,28},{1,29},{2,30},{3,31},{4,0},{5,1},{6,2},{7,3},{8,4},{9,5},{1... | collective-permute-start | bytes 3080 | tf_op jit(solution)/shard_map/ppermute | solution.py:20
  168.6 4.1 %collective-permute-done.58 = f32[8,32]{1,0:T(8,128)S(1)} collective-permute-done((f32[8,32]{1,0:T(8,128)S(1)}, f32[8,32]{1,0:T(8,128)S(1)}, u32[]{:S(2)}, u32[]{:S(2)}) %collective-permute-start.58) | collective-permute-done | bytes 1056 | tf_op jit(solution)/shard_map/ppermute | solution.py:20
  175.3 5.3 %collective-permute-start.63 = (f32[8,32]{1,0:T(8,128)S(1)}, f32[8,32]{1,0:T(8,128)S(1)}, u32[]{:S(2)}, u32[]{:S(2)}) collective-permute-start(f32[8,32]{1,0:T(8,128)S(1)} %get-tuple-element.74), channel_id=1, source_target_pairs={{0,31},{1,0},{2,1},{3,2},{4,3},{5,4},{6,5},{7,6},{8,7},{9,8},{10,9... | collective-permute-start | bytes 3080 | tf_op jit(solution)/shard_map/ppermute | solution.py:20
  180.6 4.7 %collective-permute-start.65 = (f32[8,32]{1,0:T(8,128)S(1)}, f32[8,32]{1,0:T(8,128)S(1)}, u32[]{:S(2)}, u32[]{:S(2)}) collective-permute-start(f32[8,32]{1,0:T(8,128)S(1)} %get-tuple-element.72), channel_id=1, source_target_pairs={{0,28},{1,29},{2,30},{3,31},{4,0},{5,1},{6,2},{7,3},{8,4},{9,5},{1... | collective-permute-start | bytes 3080 | tf_op jit(solution)/shard_map/ppermute | solution.py:20
  190.9 5.3 %collective-permute-start.68 = (f32[8,64]{1,0:T(8,128)S(1)}, f32[8,64]{1,0:T(8,128)S(1)}, u32[]{:S(2)}, u32[]{:S(2)}) collective-permute-start(f32[8,64]{1,0:T(8,128)S(1)} %get-tuple-element.54), channel_id=1, source_target_pairs={{0,31},{1,0},{2,1},{3,2},{4,3},{5,4},{6,5},{7,6},{8,7},{9,8},{10,9... | collective-permute-start | bytes 6152 | tf_op jit(solution)/shard_map/ppermute | solution.py:20
  196.2 4.7 %collective-permute-start.70 = (f32[8,64]{1,0:T(8,128)S(1)}, f32[8,64]{1,0:T(8,128)S(1)}, u32[]{:S(2)}, u32[]{:S(2)}) collective-permute-start(f32[8,64]{1,0:T(8,128)S(1)} %get-tuple-element.52), channel_id=1, source_target_pairs={{0,28},{1,29},{2,30},{3,31},{4,0},{5,1},{6,2},{7,3},{8,4},{9,5},{1... | collective-permute-start | bytes 6152 | tf_op jit(solution)/shard_map/ppermute | solution.py:20
  212.3 3.4 %collective-permute-start.77 = (f32[2,24,24]{2,1,0:T(8,128)S(1)}, f32[2,24,24]{2,1,0:T(8,128)S(1)}, u32[]{:S(2)}, u32[]{:S(2)}) collective-permute-start(f32[2,24,24]{2,1,0:T(8,128)S(1)} %add_add_fusion.1), channel_id=1, source_target_pairs={{0,4},{1,5},{2,6},{3,7},{4,0},{5,1},{6,2},{7,3},{8,12},{9,13},{10,... | collective-permute-start | bytes 13832 | tf_op jit(solution)/shard_map/ppermute | solution.py:49
  218.5 4.1 %collective-permute-done.78 = f32[2,24,24]{2,1,0:T(8,128)S(1)} collective-permute-done((f32[2,24,24]{2,1,0:T(8,128)S(1)}, f32[2,24,24]{2,1,0:T(8,128)S(1)}, u32[]{:S(2)}, u32[]{:S(2)}) %collective-permute-start.78) | collective-permute-done | bytes 4640 | tf_op jit(solution)/shard_map/ppermute | solution.py:49
  (301 shorter events, 109.1 us)
Async XLA Ops:
  5.0 14.9 %collective-permute-start.4 = (f32[16,192]{1,0:T(8,128)S(1)}, f32[16,192]{1,0:T(8,128)S(1)}, u32[]{:S(2)}, u32[]{:S(2)}) collective-permute-start(f32[16,192]{1,0:T(8,128)S(1)} %select_maximum_fusion.1), channel_id=1, source_target_pairs={{0,16},{1,17},{2,18},{3,19},{4,20},{5,21},{6,22},{7,23},{8,24},{9,... | collective-permute-start | bytes 36872 | tf_op jit(solution)/shard_map/ppermute | solution.py:20
  9.2 10.7 %collective-permute-start = (f32[16,96]{1,0:T(8,128)S(1)}, f32[16,96]{1,0:T(8,128)S(1)}, u32[]{:S(2)}, u32[]{:S(2)}) collective-permute-start(f32[16,96]{1,0:T(8,128)S(1)} %select_maximum_fusion.6), channel_id=1, source_target_pairs={{0,1},{1,2},{2,3},{3,4},{4,5},{5,6},{6,7},{7,8},{8,9},{9,10},{10,1... | collective-permute-start | bytes 18440 | tf_op jit(solution)/shard_map/ppermute | solution.py:20
  9.3 10.6 %collective-permute-start.1 = (f32[16,96]{1,0:T(8,128)S(1)}, f32[16,96]{1,0:T(8,128)S(1)}, u32[]{:S(2)}, u32[]{:S(2)}) collective-permute-start(f32[16,96]{1,0:T(8,128)S(1)} %select_maximum_fusion.5), channel_id=1, source_target_pairs={{0,31},{1,0},{2,1},{3,2},{4,3},{5,4},{6,5},{7,6},{8,7},{9,8},{10,9... | collective-permute-start | bytes 18440 | tf_op jit(solution)/shard_map/ppermute | solution.py:20
  27.9 8.5 %collective-permute-start.10 = (f32[2,8]{1,0:T(2,128)S(1)}, f32[2,8]{1,0:T(2,128)S(1)}, u32[]{:S(2)}, u32[]{:S(2)}) collective-permute-start(f32[2,8]{1,0:T(2,128)S(1)} %pad_maximum_fusion.1), channel_id=1, source_target_pairs={{0,3},{1,2},{2,1},{3,0},{4,7},{5,6},{6,5},{7,4},{8,11},{9,10},{10,... | collective-permute-start | bytes 200 | tf_op jit(solution)/shard_map/ppermute | solution.py:49
  28.0 9.1 %collective-permute-start.11 = (f32[2,8]{1,0:T(2,128)S(1)}, f32[2,8]{1,0:T(2,128)S(1)}, u32[]{:S(2)}, u32[]{:S(2)}) collective-permute-start(f32[2,8]{1,0:T(2,128)S(1)} %pad_maximum_fusion.1), channel_id=1, source_target_pairs={{0,2},{1,3},{2,0},{3,1},{4,6},{5,7},{6,4},{7,5},{8,10},{9,11},{10,... | collective-permute-start | bytes 200 | tf_op jit(solution)/shard_map/ppermute | solution.py:49
  28.1 9.0 %collective-permute-start.12 = (f32[2,8]{1,0:T(2,128)S(1)}, f32[2,8]{1,0:T(2,128)S(1)}, u32[]{:S(2)}, u32[]{:S(2)}) collective-permute-start(f32[2,8]{1,0:T(2,128)S(1)} %pad_maximum_fusion.1), channel_id=1, source_target_pairs={{0,1},{1,0},{2,3},{3,2},{4,5},{5,4},{6,7},{7,6},{8,9},{9,8},{10,11... | collective-permute-start | bytes 200 | tf_op jit(solution)/shard_map/ppermute | solution.py:49
  31.8 18.0 %collective-permute-start.5 = (f32[17,64]{1,0:T(8,128)S(1)}, f32[17,64]{1,0:T(8,128)S(1)}, u32[]{:S(2)}, u32[]{:S(2)}) collective-permute-start(f32[17,64]{1,0:T(8,128)S(1)} %get-tuple-element.18), channel_id=1, source_target_pairs={{0,31},{1,0},{2,1},{3,2},{4,3},{5,4},{6,5},{7,6},{8,7},{9,8},{10,9... | collective-permute-start | bytes 13064 | tf_op jit(solution)/shard_map/ppermute | solution.py:20
  36.4 13.4 %collective-permute-start.6 = (f32[17,64]{1,0:T(8,128)S(1)}, f32[17,64]{1,0:T(8,128)S(1)}, u32[]{:S(2)}, u32[]{:S(2)}) collective-permute-start(f32[17,64]{1,0:T(8,128)S(1)} %get-tuple-element.17), channel_id=1, source_target_pairs={{0,1},{1,2},{2,3},{3,4},{4,5},{5,6},{6,7},{7,8},{8,9},{9,10},{10,1... | collective-permute-start | bytes 13064 | tf_op jit(solution)/shard_map/ppermute | solution.py:20
  36.4 13.4 %collective-permute-start.7 = (f32[17,64]{1,0:T(8,128)S(1)}, f32[17,64]{1,0:T(8,128)S(1)}, u32[]{:S(2)}, u32[]{:S(2)}) collective-permute-start(f32[17,64]{1,0:T(8,128)S(1)} %get-tuple-element.16), channel_id=1, source_target_pairs={{0,28},{1,29},{2,30},{3,31},{4,0},{5,1},{6,2},{7,3},{8,4},{9,5},{1... | collective-permute-start | bytes 13064 | tf_op jit(solution)/shard_map/ppermute | solution.py:20
  55.3 10.1 %collective-permute-start.17 = (f32[8,64]{1,0:T(8,128)S(1)}, f32[8,64]{1,0:T(8,128)S(1)}, u32[]{:S(2)}, u32[]{:S(2)}) collective-permute-start(f32[8,64]{1,0:T(8,128)S(1)} %get-tuple-element.67), channel_id=1, source_target_pairs={{0,1},{1,2},{2,3},{3,4},{4,5},{5,6},{6,7},{7,8},{8,9},{9,10},{10,1... | collective-permute-start | bytes 6152 | tf_op jit(solution)/shard_map/ppermute | solution.py:20
  55.3 10.1 %collective-permute-start.18 = (f32[8,64]{1,0:T(8,128)S(1)}, f32[8,64]{1,0:T(8,128)S(1)}, u32[]{:S(2)}, u32[]{:S(2)}) collective-permute-start(f32[8,64]{1,0:T(8,128)S(1)} %get-tuple-element.66), channel_id=1, source_target_pairs={{0,31},{1,0},{2,1},{3,2},{4,3},{5,4},{6,5},{7,6},{8,7},{9,8},{10,9... | collective-permute-start | bytes 6152 | tf_op jit(solution)/shard_map/ppermute | solution.py:20
  73.1 6.7 %collective-permute-start.23 = (f32[8,64]{1,0:T(8,128)S(1)}, f32[8,64]{1,0:T(8,128)S(1)}, u32[]{:S(2)}, u32[]{:S(2)}) collective-permute-start(f32[8,64]{1,0:T(8,128)S(1)} %get-tuple-element.29), channel_id=1, source_target_pairs={{0,1},{1,2},{2,3},{3,4},{4,5},{5,6},{6,7},{7,8},{8,9},{9,10},{10,1... | collective-permute-start | bytes 6152 | tf_op jit(solution)/shard_map/ppermute | solution.py:20
  82.5 10.2 %collective-permute-start.27 = (f32[8,64]{1,0:T(8,128)S(1)}, f32[8,64]{1,0:T(8,128)S(1)}, u32[]{:S(2)}, u32[]{:S(2)}) collective-permute-start(f32[8,64]{1,0:T(8,128)S(1)} %get-tuple-element.63), channel_id=1, source_target_pairs={{0,1},{1,2},{2,3},{3,4},{4,5},{5,6},{6,7},{7,8},{8,9},{9,10},{10,1... | collective-permute-start | bytes 6152 | tf_op jit(solution)/shard_map/ppermute | solution.py:20
  82.5 10.2 %collective-permute-start.28 = (f32[8,64]{1,0:T(8,128)S(1)}, f32[8,64]{1,0:T(8,128)S(1)}, u32[]{:S(2)}, u32[]{:S(2)}) collective-permute-start(f32[8,64]{1,0:T(8,128)S(1)} %get-tuple-element.62), channel_id=1, source_target_pairs={{0,31},{1,0},{2,1},{3,2},{4,3},{5,4},{6,5},{7,6},{8,7},{9,8},{10,9... | collective-permute-start | bytes 6152 | tf_op jit(solution)/shard_map/ppermute | solution.py:20
  109.7 10.5 %collective-permute-start.37 = (f32[8,64]{1,0:T(8,128)S(1)}, f32[8,64]{1,0:T(8,128)S(1)}, u32[]{:S(2)}, u32[]{:S(2)}) collective-permute-start(f32[8,64]{1,0:T(8,128)S(1)} %get-tuple-element.59), channel_id=1, source_target_pairs={{0,1},{1,2},{2,3},{3,4},{4,5},{5,6},{6,7},{7,8},{8,9},{9,10},{10,1... | collective-permute-start | bytes 6152 | tf_op jit(solution)/shard_map/ppermute | solution.py:20
  109.7 10.5 %collective-permute-start.38 = (f32[8,64]{1,0:T(8,128)S(1)}, f32[8,64]{1,0:T(8,128)S(1)}, u32[]{:S(2)}, u32[]{:S(2)}) collective-permute-start(f32[8,64]{1,0:T(8,128)S(1)} %get-tuple-element.58), channel_id=1, source_target_pairs={{0,31},{1,0},{2,1},{3,2},{4,3},{5,4},{6,5},{7,6},{8,7},{9,8},{10,9... | collective-permute-start | bytes 6152 | tf_op jit(solution)/shard_map/ppermute | solution.py:20
  127.7 6.7 %collective-permute-start.43 = (f32[8,64]{1,0:T(8,128)S(1)}, f32[8,64]{1,0:T(8,128)S(1)}, u32[]{:S(2)}, u32[]{:S(2)}) collective-permute-start(f32[8,64]{1,0:T(8,128)S(1)} %get-tuple-element.21), channel_id=1, source_target_pairs={{0,1},{1,2},{2,3},{3,4},{4,5},{5,6},{6,7},{7,8},{8,9},{9,10},{10,1... | collective-permute-start | bytes 6152 | tf_op jit(solution)/shard_map/ppermute | solution.py:20
  149.1 11.0 %collective-permute-start.52 = (f32[8,32]{1,0:T(8,128)S(1)}, f32[8,32]{1,0:T(8,128)S(1)}, u32[]{:S(2)}, u32[]{:S(2)}) collective-permute-start(f32[8,32]{1,0:T(8,128)S(1)} %get-tuple-element.79), channel_id=1, source_target_pairs={{0,1},{1,2},{2,3},{3,4},{4,5},{5,6},{6,7},{7,8},{8,9},{9,10},{10,1... | collective-permute-start | bytes 3080 | tf_op jit(solution)/shard_map/ppermute | solution.py:20
  149.1 11.0 %collective-permute-start.53 = (f32[8,32]{1,0:T(8,128)S(1)}, f32[8,32]{1,0:T(8,128)S(1)}, u32[]{:S(2)}, u32[]{:S(2)}) collective-permute-start(f32[8,32]{1,0:T(8,128)S(1)} %get-tuple-element.78), channel_id=1, source_target_pairs={{0,31},{1,0},{2,1},{3,2},{4,3},{5,4},{6,5},{7,6},{8,7},{9,8},{10,9... | collective-permute-start | bytes 3080 | tf_op jit(solution)/shard_map/ppermute | solution.py:20
  165.9 8.8 %collective-permute-start.61 = (f32[8,64]{1,0:T(8,128)S(1)}, f32[8,64]{1,0:T(8,128)S(1)}, u32[]{:S(2)}, u32[]{:S(2)}) collective-permute-start(f32[8,64]{1,0:T(8,128)S(1)} %concatenate.246), channel_id=1, source_target_pairs={{0,16},{1,17},{2,18},{3,19},{4,20},{5,21},{6,22},{7,23},{8,24},{9,... | collective-permute-start | bytes 6152 | tf_op jit(solution)/shard_map/ppermute | solution.py:20
  175.3 10.1 %collective-permute-start.62 = (f32[8,32]{1,0:T(8,128)S(1)}, f32[8,32]{1,0:T(8,128)S(1)}, u32[]{:S(2)}, u32[]{:S(2)}) collective-permute-start(f32[8,32]{1,0:T(8,128)S(1)} %get-tuple-element.75), channel_id=1, source_target_pairs={{0,1},{1,2},{2,3},{3,4},{4,5},{5,6},{6,7},{7,8},{8,9},{9,10},{10,1... | collective-permute-start | bytes 3080 | tf_op jit(solution)/shard_map/ppermute | solution.py:20
  175.3 10.1 %collective-permute-start.63 = (f32[8,32]{1,0:T(8,128)S(1)}, f32[8,32]{1,0:T(8,128)S(1)}, u32[]{:S(2)}, u32[]{:S(2)}) collective-permute-start(f32[8,32]{1,0:T(8,128)S(1)} %get-tuple-element.74), channel_id=1, source_target_pairs={{0,31},{1,0},{2,1},{3,2},{4,3},{5,4},{6,5},{7,6},{8,7},{9,8},{10,9... | collective-permute-start | bytes 3080 | tf_op jit(solution)/shard_map/ppermute | solution.py:20
  190.9 10.1 %collective-permute-start.67 = (f32[8,64]{1,0:T(8,128)S(1)}, f32[8,64]{1,0:T(8,128)S(1)}, u32[]{:S(2)}, u32[]{:S(2)}) collective-permute-start(f32[8,64]{1,0:T(8,128)S(1)} %get-tuple-element.55), channel_id=1, source_target_pairs={{0,1},{1,2},{2,3},{3,4},{4,5},{5,6},{6,7},{7,8},{8,9},{9,10},{10,1... | collective-permute-start | bytes 6152 | tf_op jit(solution)/shard_map/ppermute | solution.py:20
  190.9 10.1 %collective-permute-start.68 = (f32[8,64]{1,0:T(8,128)S(1)}, f32[8,64]{1,0:T(8,128)S(1)}, u32[]{:S(2)}, u32[]{:S(2)}) collective-permute-start(f32[8,64]{1,0:T(8,128)S(1)} %get-tuple-element.54), channel_id=1, source_target_pairs={{0,31},{1,0},{2,1},{3,2},{4,3},{5,4},{6,5},{7,6},{8,7},{9,8},{10,9... | collective-permute-start | bytes 6152 | tf_op jit(solution)/shard_map/ppermute | solution.py:20
  (62 other events, 386.1 us)
